TPU v7x, 32 devices: a whole 2x2x4 slice. The times are simulated.
32 devices in a mesh: veh: 8 (over z, x), req: 4 (over y, core).
Axes of the slice: x: 2, y: 2, z: 4, core: 2. Of those that a mesh axis runs over, the one named last changes fastest.
Arguments:
- vehicle_emb: bfloat16 [8192, 128], P(('veh', 'req')), may hold values from -40 to 40
- request_emb: bfloat16 [16384, 128], P('req'), may hold values from -8 to 8
- request_feat: bfloat16 [16384, 256], P('req'), may hold values from -6 to 6
- log_supply: float32 [8192], P('veh'), may hold values from -1.2 to 1.2
- log_demand: float32 [16384], P('req'), may hold values from -1.2 to 1.2
Outputs:
- assigned: float32 [8192, 256], P(('veh', 'req'))
All inputs are finite; a program needn't handle non-finite values.
Results may differ from a plain program's by a relative error of at most 0.0017.
Values may be sent and summed in bfloat16 or wider, within the bound.
No kernel may reach another device: no remote copies, remote signals or barrier semaphores. Data moves between devices by JAX's collectives and lax.ppermute only.
A program may use at most 64 MiB of HBM per device.

v0:
```python
import math

import jax
import jax.numpy as jnp
from jax import lax
from jax.sharding import PartitionSpec as P


def combined_all(x, axis, combine):
    everything = jax.tree.map(lambda part: lax.all_gather(part, axis), x)
    first = jax.tree.map(lambda part: part[0], everything)

    def turn(k, so_far):
        return combine(so_far, jax.tree.map(lambda part: part[k], everything))

    return lax.fori_loop(1, lax.axis_size(axis), turn, first)


def pair_combine(former, latter):
    highest = jnp.maximum(former[0], latter[0])
    return (
        highest,
        former[1] * jnp.exp(former[0] - highest) + latter[1] * jnp.exp(latter[0] - highest),
    )


def local(vehicle_emb, request_emb, request_feat, log_supply, log_demand):
    own_rows = lax.all_gather(vehicle_emb, "req", axis=0, tiled=True)
    row_count = own_rows.shape[0]
    block_rows = min(256, row_count)
    block_count = row_count // block_rows
    vehicle_blocks = own_rows.reshape(block_count, block_rows, own_rows.shape[1])
    score_scale = 3.0 / math.sqrt(own_rows.shape[1])
    request_count = request_emb.shape[0]

    def block_scores(vehicle_block):
        return (
            lax.dot_general(
                vehicle_block,
                request_emb,
                (((1,), (1,)), ((), ())),
                preferred_element_type=jnp.float32,
            )
            * score_scale
        )

    def column_pot(shift):
        shift_blocks = shift.reshape(block_count, block_rows)

        def column_step(state_pair, element):
            running, accrued = state_pair
            vehicle_block, shift_block = element
            logits = block_scores(vehicle_block) + shift_block[:, None]
            highest = jnp.maximum(running, jnp.max(logits, axis=0))
            accrued = accrued * jnp.exp(running - highest) + jnp.sum(
                jnp.exp(logits - highest[None, :]), axis=0
            )
            return ((highest, accrued), None)

        start_pair = (
            jnp.full((request_count,), -1e30, jnp.float32),
            jnp.zeros((request_count,), jnp.float32),
        )
        (highest, accrued), unused = lax.scan(
            column_step, start_pair, (vehicle_blocks, shift_blocks)
        )
        highest, accrued = combined_all((highest, accrued), "veh", pair_combine)
        return log_demand - (highest + jnp.log(accrued))

    demand_first = column_pot(jnp.zeros((row_count,), jnp.float32))

    def row_block(vehicle_block):
        logits = block_scores(vehicle_block) + demand_first[None, :]
        highest = jnp.max(logits, axis=1)
        return (highest, jnp.sum(jnp.exp(logits - highest[:, None]), axis=1))

    highest, accrued = lax.map(row_block, vehicle_blocks)
    highest = highest.reshape(row_count)
    accrued = accrued.reshape(row_count)
    highest, accrued = combined_all((highest, accrued), "req", pair_combine)
    supply_pot = log_supply - (highest + jnp.log(accrued))
    demand_second = column_pot(supply_pot)

    def assign_block(vehicle_block):
        logits = block_scores(vehicle_block) + demand_second[None, :]
        block_peak = jnp.max(logits, axis=1)
        powers = jnp.exp(logits - block_peak[:, None])
        block_mass = jnp.sum(powers, axis=1)
        weights = powers.astype(jnp.bfloat16)
        block_feat = jnp.dot(weights, request_feat, preferred_element_type=jnp.float32)
        return (block_peak, block_mass, block_feat)

    peaks, masses, features = lax.map(assign_block, vehicle_blocks)
    peaks = peaks.reshape(row_count)
    masses = masses.reshape(row_count)
    features = features.reshape(row_count, request_feat.shape[1])
    summit = lax.pmax(peaks, "req")
    factor = jnp.exp(peaks - summit)
    own_feat, own_mass = (
        lax.psum_scatter(features * factor[:, None], "req", scatter_dimension=0, tiled=True),
        lax.psum_scatter(masses * factor, "req", scatter_dimension=0, tiled=True),
    )
    result = own_feat / own_mass[:, None]
    return result


def solution(mesh):
    in_specs = (P(("veh", "req"), None), P("req", None), P("req", None), P("veh"), P("req"))
    out_specs = P(("veh", "req"), None)
    return jax.shard_map(local, mesh=mesh, in_specs=in_specs, out_specs=out_specs, check_vma=False)
```

profile of v0, /device:TPU:0, one launch (start us, length us, event | category | flops | bytes accessed | tf_op | source)
XLA Modules:
  0.0 278.1 jit_solution(16617239473979468213)
XLA Ops:
  6.5 7.4 %all_gather.33 = bf16[1024,128]{1,0:T(8,128)(2,1)S(1)} all-gather(bf16[256,128]{1,0:T(8,128)(2,1)} %param.19), channel_id=1, replica_groups=mesh['veh'=8,'req'=4] {'req'}, dimensions={0}, use_global_device_ids=true | all-gather | bytes 327680 | tf_op jit(solution)/shard_map/all_gather | solution.py:28
  14.0 26.8 %while.108 = (s32[]{:T(128)}, f32[4096]{0:T(1024)S(1)}, f32[4096]{0:T(1024)S(1)}, bf16[4,256,128]{2,1,0:T(8,128)(2,1)S(1)}, bf16[4096,128]{1,0:T(8,128)(2,1)}, /*index=5*/s32[]{:T(128)}, s32[]{:T(128)}) while((s32[]{:T(128)}, f32[4096]{0:T(1024)S(1)}, f32[4096]{0:T(1024)S(1)}, bf16[4,256,128]{2,1,0:T(8,128)(2,1)S(1)}, ...), condition=%wide.region_3.4_spmd.clone, body=%wide.region_0.3_spmd.clone.sunk | while | flops 272650240 | bytes 9715804 | solution.py:64
  14.0 3.9 %fusion.61 = (f32[4096]{0:T(1024)S(1)}, f32[256,4096]{1,0:T(8,128)}) fusion(bf16[4096,128]{1,0:T(8,128)(2,1)} %get-tuple-element.1003, bf16[4,256,128]{2,1,0:T(8,128)(2,1)S(1)} %get-tuple-element.1002, s32[]{:T(128)} %get-tuple-element.992), kind=kOutput, calls=%fused_computation.56.clone.1 | convolution fusion | flops 270528512 | bytes 5324804 | tf_op jit(solution)/shard_map/while/body/eval_jaxpr/dot_general | solution.py:38
  20.7 3.9 %fusion.61 = (f32[4096]{0:T(1024)S(1)}, f32[256,4096]{1,0:T(8,128)}) fusion(bf16[4096,128]{1,0:T(8,128)(2,1)} %get-tuple-element.1003, bf16[4,256,128]{2,1,0:T(8,128)(2,1)S(1)} %get-tuple-element.1002, s32[]{:T(128)} %get-tuple-element.992), kind=kOutput, calls=%fused_computation.56.clone.1 | convolution fusion | flops 270528512 | bytes 5324804 | tf_op jit(solution)/shard_map/while/body/eval_jaxpr/dot_general | solution.py:38
  27.4 3.9 %fusion.61 = (f32[4096]{0:T(1024)S(1)}, f32[256,4096]{1,0:T(8,128)}) fusion(bf16[4096,128]{1,0:T(8,128)(2,1)} %get-tuple-element.1003, bf16[4,256,128]{2,1,0:T(8,128)(2,1)S(1)} %get-tuple-element.1002, s32[]{:T(128)} %get-tuple-element.992), kind=kOutput, calls=%fused_computation.56.clone.1 | convolution fusion | flops 270528512 | bytes 5324804 | tf_op jit(solution)/shard_map/while/body/eval_jaxpr/dot_general | solution.py:38
  34.1 3.9 %fusion.61 = (f32[4096]{0:T(1024)S(1)}, f32[256,4096]{1,0:T(8,128)}) fusion(bf16[4096,128]{1,0:T(8,128)(2,1)} %get-tuple-element.1003, bf16[4,256,128]{2,1,0:T(8,128)(2,1)S(1)} %get-tuple-element.1002, s32[]{:T(128)} %get-tuple-element.992), kind=kOutput, calls=%fused_computation.56.clone.1 | convolution fusion | flops 270528512 | bytes 5324804 | tf_op jit(solution)/shard_map/while/body/eval_jaxpr/dot_general | solution.py:38
  40.8 30.9 %all-gather = f32[32768]{0:T(1024)S(1)} all-gather(f32[4096]{0:T(1024)S(1)} %get-tuple-element.542), channel_id=2, replica_groups=mesh['veh'=8,'req'=4] {'veh'}, dimensions={0}, use_global_device_ids=true | all-gather | bytes 147456 | tf_op jit(solution)/shard_map/all_gather | solution.py:10
  71.7 30.5 %all-gather.1 = f32[32768]{0:T(1024)S(1)} all-gather(f32[4096]{0:T(1024)S(1)} %get-tuple-element.543), channel_id=3, replica_groups=mesh['veh'=8,'req'=4] {'veh'}, dimensions={0}, use_global_device_ids=true | all-gather | bytes 147456 | tf_op jit(solution)/shard_map/all_gather | solution.py:10
  102.9 11.3 %while.104 = (s32[]{:T(128)}, f32[4,256]{1,0:T(4,128)S(1)}, f32[4,256]{1,0:T(4,128)S(1)}, bf16[4,256,128]{2,1,0:T(8,128)(2,1)S(1)}, bf16[4096,128]{1,0:T(8,128)(...) while((s32[]{:T(128)}, f32[4,256]{1,0:T(4,128)S(1)}, f32[4,256]{1,0:T(4,128)S(1)}, ...), condition=%wide.region_9.10_spmd, body=%wide.region_6.9_spmd.sunk | while | flops 273677824 | bytes 9526369 | solution.py:77
  114.3 5.2 %all-gather.4 = f32[4,1,1024]{2,1,0:T(1,128)S(1)} all-gather(f32[1,1,1024]{2,1,0:T(1,128)S(1)} %reshape.42), channel_id=1, replica_groups=mesh['veh'=8,'req'=4] {'req'}, dimensions={0}, use_global_device_ids=true | all-gather | bytes 20480 | tf_op jit(solution)/shard_map/all_gather | solution.py:10
  119.5 5.2 %all-gather.5 = f32[4,1,1024]{2,1,0:T(1,128)S(1)} all-gather(f32[1,1,1024]{2,1,0:T(1,128)S(1)} %reshape.44), channel_id=1, replica_groups=mesh['veh'=8,'req'=4] {'req'}, dimensions={0}, use_global_device_ids=true | all-gather | bytes 20480 | tf_op jit(solution)/shard_map/all_gather | solution.py:10
  124.9 27.0 %while.109 = (s32[]{:T(128)}, f32[4096]{0:T(1024)S(1)}, f32[4096]{0:T(1024)S(1)}, bf16[4,256,128]{2,1,0:T(8,128)(2,1)S(1)}, bf16[4096,128]{1,0:T(8,128)(2,1)}, /*index=5*/f32[4,256]{1,0:T(4,128)S(1)}, s32[]{:T(128)}, s32[]{:T(128)}) while((s32[]{:T(128)}, f32[4096]{0:T(1024)S(1)}, f32[4096]{0:T(1024)S(1)}, ...), condition=%wide.region_15.16_spmd.clone, body=%wide.region_12.15_spmd.clone.sunk | while | flops 273698816 | bytes 9718888 | solution.py:64
  124.9 4.0 %fusion.64 = (f32[4096]{0:T(1024)S(1)}, f32[256,4096]{1,0:T(8,128)}) fusion(f32[256]{0:T(256)S(1)} %bitcast.109, bf16[4096,128]{1,0:T(8,128)(2,1)} %get-tuple-element.1098, bf16[4,256,128]{2,1,0:T(8,128)(2,1)S(1)} %get-tuple-element.1097, s32[]{:T(128)} %get-tuple-element.1086), kind=kOutput, calls=%fused_computation.57.clone.1 | convolution fusion | flops 271577088 | bytes 5325828 | tf_op jit(solution)/shard_map/while/body/eval_jaxpr/dot_general | solution.py:38
  128.9 2.8 %exponential_reduce_fusion.8 = f32[4096]{0:T(1024)S(1)} fusion(f32[256,4096]{1,0:T(8,128)} %get-tuple-element.984, f32[4096]{0:T(1024)S(1)} %select_maximum_fusion.5), kind=kLoop, calls=%fused_computation.37.clone.1 | loop fusion | flops 2093056 | bytes 4227072 | tf_op jit(solution)/shard_map/while/body/eval_jaxpr/reduce_sum | solution.py:55
  131.8 3.9 %fusion.64 = (f32[4096]{0:T(1024)S(1)}, f32[256,4096]{1,0:T(8,128)}) fusion(f32[256]{0:T(256)S(1)} %bitcast.109, bf16[4096,128]{1,0:T(8,128)(2,1)} %get-tuple-element.1098, bf16[4,256,128]{2,1,0:T(8,128)(2,1)S(1)} %get-tuple-element.1097, s32[]{:T(128)} %get-tuple-element.1086), kind=kOutput, calls=%fused_computation.57.clone.1 | convolution fusion | flops 271577088 | bytes 5325828 | tf_op jit(solution)/shard_map/while/body/eval_jaxpr/dot_general | solution.py:38
  138.5 3.9 %fusion.64 = (f32[4096]{0:T(1024)S(1)}, f32[256,4096]{1,0:T(8,128)}) fusion(f32[256]{0:T(256)S(1)} %bitcast.109, bf16[4096,128]{1,0:T(8,128)(2,1)} %get-tuple-element.1098, bf16[4,256,128]{2,1,0:T(8,128)(2,1)S(1)} %get-tuple-element.1097, s32[]{:T(128)} %get-tuple-element.1086), kind=kOutput, calls=%fused_computation.57.clone.1 | convolution fusion | flops 271577088 | bytes 5325828 | tf_op jit(solution)/shard_map/while/body/eval_jaxpr/dot_general | solution.py:38
  145.2 3.9 %fusion.64 = (f32[4096]{0:T(1024)S(1)}, f32[256,4096]{1,0:T(8,128)}) fusion(f32[256]{0:T(256)S(1)} %bitcast.109, bf16[4096,128]{1,0:T(8,128)(2,1)} %get-tuple-element.1098, bf16[4,256,128]{2,1,0:T(8,128)(2,1)S(1)} %get-tuple-element.1097, s32[]{:T(128)} %get-tuple-element.1086), kind=kOutput, calls=%fused_computation.57.clone.1 | convolution fusion | flops 271577088 | bytes 5325828 | tf_op jit(solution)/shard_map/while/body/eval_jaxpr/dot_general | solution.py:38
  151.9 30.5 %all-gather.2 = f32[32768]{0:T(1024)S(1)} all-gather(f32[4096]{0:T(1024)S(1)} %get-tuple-element.550), channel_id=4, replica_groups=mesh['veh'=8,'req'=4] {'veh'}, dimensions={0}, use_global_device_ids=true | all-gather | bytes 147456 | tf_op jit(solution)/shard_map/all_gather | solution.py:10
  183.2 30.5 %all-gather.3 = f32[32768]{0:T(1024)S(1)} all-gather(f32[4096]{0:T(1024)S(1)} %get-tuple-element.551), channel_id=5, replica_groups=mesh['veh'=8,'req'=4] {'veh'}, dimensions={0}, use_global_device_ids=true | all-gather | bytes 147456 | tf_op jit(solution)/shard_map/all_gather | solution.py:10
  214.3 7.3 %while.106 = (s32[]{:T(128)}, f32[4096]{0:T(1024)S(1)}, f32[4096]{0:T(1024)S(1)}, f32[8,4096]{1,0:T(8,128)}, f32[8,4096]{1,0:T(8,128)}, /*index=5*/s32[]{:T(128)}, s32[]{:T(128)}, s32[]{:T(128)}) while((s32[]{:T(128)}, f32[4096]{0:T(1024)S(1)}, f32[4096]{0:T(1024)S(1)}, f32[8,4096]{1,0:T(8,128)}, f32[8,4096]{1,0:T(8,128)}, ...), condition=%wide.region_17.18_spmd, body=%wide.region_16.17_spmd.sunk | while | flops 24581 | bytes 163971 | solution.py:16
  221.7 14.7 %while.107 = (s32[]{:T(128)}, f32[4,256]{1,0:T(4,128)S(1)}, f32[4,256]{1,0:T(4,128)S(1)}, f32[4,256,256]{2,1,0:T(8,128)S(1)}, bf16[4,256,128]{2,1,0:T(8,128)(2,1...) while((s32[]{:T(128)}, f32[4,256]{1,0:T(4,128)S(1)}, ...), condition=%wide.region_21.22_spmd, body=%wide.region_18.21_spmd.sunk | while | flops 812645888 | bytes 16081013 | solution.py:93
  236.4 5.7 %pmax.7 = f32[1024]{0:T(1024)S(1)} all-reduce(f32[1024]{0:T(1024)S(1)} %bitcast.114), channel_id=1, replica_groups=mesh['veh'=8,'req'=4] {'req'}, use_global_device_ids=true, to_apply=%region_22.23 | all-reduce | flops 1024 | bytes 8192 | tf_op jit(solution)/shard_map/pmax | solution.py:97
  244.5 6.7 %all-reduce = f32[1024]{0:T(1024)S(1)} all-reduce(f32[1024]{0:T(1024)S(1)} %get-tuple-element.682), channel_id=7, replica_groups=mesh['veh'=8,'req'=4] {'req'}, use_global_device_ids=true, to_apply=%region_24.25.clone | all-reduce | flops 1024 | bytes 8192
  251.3 18.2 %reduce-scatter.2.cloned.1.call-done = f32[256,256]{1,0:T(8,128)} async-done(((f32[1024,256]{1,0:T(8,128)}), f32[256,256]{1,0:T(8,128)}) %reduce-scatter.2.cloned.1.call-update) | async-done | bytes 262160 | tf_op jit(solution)/shard_map/reduce_scatter | solution.py:100
  (151 shorter events, 59.0 us)
Async XLA Ops:
  6.5 262.9 %reduce-scatter.2.cloned.1.call-start = ((), (), s32[]{:S(2)}) async-start(), calls=%async_computation.1 | async-start | bytes 1310720 | tf_op jit(solution)/shard_map/reduce_scatter | solution.py:100
  14.0 88.9 %copy-start.1 = (f32[4096]{0:T(1024)S(1)}, f32[4096]{0:T(1024)}, u32[]{:S(2)}) copy-start(f32[4096]{0:T(1024)} %param.23) | copy-start | bytes 49156
  102.9 22.0 %copy-start.2 = (f32[1024]{0:T(1024)S(1)}, f32[1024]{0:T(1024)}, u32[]{:S(2)}) copy-start(f32[1024]{0:T(1024)} %param.22) | copy-start | bytes 12292
  124.9 96.8 %copy-start = (bf16[4096,256]{1,0:T(8,128)(2,1)S(1)}, bf16[4096,256]{1,0:T(8,128)(2,1)}, u32[]{:S(2)}) copy-start(bf16[4096,256]{1,0:T(8,128)(2,1)} %param.21) | copy-start | bytes 6291460
  221.7 21.6 %copy-start.3 = (u32[32]{0:T(128)S(1)}, u32[32]{0:T(128)}, u32[]{:S(2)}) copy-start(u32[32]{0:T(128)} %constant.176) | copy-start | bytes 388
Sparse Core Ops, SparseCore 0:
  243.4 25.9 reduce-scatter.1
where the time goes:
time: 279 us; the launch traced here: 278 us
  blocking collectives  153 us (55%)
  matrix products  50.6 us (18%)
  other arithmetic  31.5 us (11%)
  waiting for transfers between devices  18.2 us (7%)
  between operations  14.3 us (5%)
  local copies, waits for them, and re-layouts  10.1 us (4%)
    all_gather x6, blocking collectives, combined_all(): everything = jax.tree.map(lambda part: lax.all_gather(part, axis), x)  133 us
    dot_general x16, matrix products, block_scores(): lax.dot_general(vehicle_block, request_emb, (((1,), (1,)), ((), ())), pre...  47.3 us
    reduce_sum x8, other arithmetic, column_step(): jnp.sum(jnp.exp(logits - highest[None, :]), axis=0)  22.3 us
    reduce_scatter x1, waiting for transfers between devices, local(): lax.psum_scatter(features * factor[:, None], 'req', scatter_dimension=0,...  18.2 us
    all_gather x1, blocking collectives, local(): own_rows = lax.all_gather(vehicle_emb, 'req', axis=0, tiled=True)  7.42 us
    dynamic_slice x17, local copies, waits for them, and re-layouts, turn(): return combine(so_far, jax.tree.map(lambda part: part[k], everything))  7.21 us
    unnamed x1, blocking collectives  6.65 us
    pmax x1, blocking collectives, local(): summit = lax.pmax(peaks, 'req')  5.67 us
  transfers between devices with their start and end apart: 1, of which 1 were waited for; matrix products, arithmetic and copies ran while one was open for 0% of the time, Pallas kernels for 0%

commit v1 on v0

--- a/solution.py
+++ b/solution.py
@@ -6,22 +6,15 @@
 from jax.sharding import PartitionSpec as P
 
 
-def combined_all(x, axis, combine):
-    everything = jax.tree.map(lambda part: lax.all_gather(part, axis), x)
-    first = jax.tree.map(lambda part: part[0], everything)
-
-    def turn(k, so_far):
-        return combine(so_far, jax.tree.map(lambda part: part[k], everything))
-
-    return lax.fori_loop(1, lax.axis_size(axis), turn, first)
+def gather_by_exchange(x, axis):
+    count = lax.axis_size(axis)
+    spread = jnp.broadcast_to(x[None], (count,) + x.shape)
+    return lax.all_to_all(spread, axis, 0, 0, tiled=True)
 
 
-def pair_combine(former, latter):
-    highest = jnp.maximum(former[0], latter[0])
-    return (
-        highest,
-        former[1] * jnp.exp(former[0] - highest) + latter[1] * jnp.exp(latter[0] - highest),
-    )
+def merge_lse(parts):
+    top = jnp.max(parts, axis=0)
+    return top + jnp.log(jnp.sum(jnp.exp(parts - top[None]), axis=0))
 
 
 def local(vehicle_emb, request_emb, request_feat, log_supply, log_demand):
@@ -64,21 +57,19 @@
         (highest, accrued), unused = lax.scan(
             column_step, start_pair, (vehicle_blocks, shift_blocks)
         )
-        highest, accrued = combined_all((highest, accrued), "veh", pair_combine)
-        return log_demand - (highest + jnp.log(accrued))
+        partial = highest + jnp.log(accrued)
+        return log_demand - merge_lse(gather_by_exchange(partial, "veh"))
 
     demand_first = column_pot(jnp.zeros((row_count,), jnp.float32))
 
     def row_block(vehicle_block):
         logits = block_scores(vehicle_block) + demand_first[None, :]
         highest = jnp.max(logits, axis=1)
-        return (highest, jnp.sum(jnp.exp(logits - highest[:, None]), axis=1))
+        return highest + jnp.log(jnp.sum(jnp.exp(logits - highest[:, None]), axis=1))
 
-    highest, accrued = lax.map(row_block, vehicle_blocks)
-    highest = highest.reshape(row_count)
-    accrued = accrued.reshape(row_count)
-    highest, accrued = combined_all((highest, accrued), "req", pair_combine)
-    supply_pot = log_supply - (highest + jnp.log(accrued))
+    partial = lax.map(row_block, vehicle_blocks).reshape(row_count)
+    parts = lax.all_gather(partial, "req", axis=0, tiled=False)
+    supply_pot = log_supply - merge_lse(parts)
     demand_second = column_pot(supply_pot)
 
     def assign_block(vehicle_block):

time: 279 us -> 166 us (0.59)
  blocking collectives: 153 us -> 24.9 us
  waiting for transfers between devices: 18.2 us -> 30.5 us
  starting transfers between devices: 0.01 us -> 9.23 us
  local copies, waits for them, and re-layouts: 10.1 us -> 2.71 us
    all_gather x6 -> x1, blocking collectives: 133 us -> 5.18 us  [local(): parts = lax.all_gather(partial, 'req', axis=0, tiled=False)]
    all_to_all x0 -> x2, waiting for transfers between devices: none -> 15.1 us  [gather_by_exchange(): return lax.all_to_all(spread, axis, 0, 0, tiled=True)]
    all_to_all x0 -> x2, starting transfers between devices: none -> 9.19 us  [gather_by_exchange(): return lax.all_to_all(spread, axis, 0, 0, tiled=True)]
    dynamic_slice x17 -> x0, local copies, waits for them, and re-layouts: 7.21 us -> none  [turn(): return combine(so_far, jax.tree.map(lambda part: part[k], everything))]
    reduce_scatter x1, waiting for transfers between devices: 18.2 us -> 15.4 us  [local(): lax.psum_scatter(features * factor[:, None], 'req', scatter_dimension=0,...]
  transfers between devices with their start and end apart: 1 -> 3, of which waited for: 1 -> 3; matrix products, arithmetic and copies ran while one was open for 0% -> 0% of each run, Pallas kernels for 0% -> 0%
where the time goes in v1:
time: 166 us; the launch traced here: 165 us
  matrix products  50.6 us (30%)
  other arithmetic  32.4 us (20%)
  waiting for transfers between devices  30.5 us (18%)
  blocking collectives  24.9 us (15%)
  between operations  14.3 us (9%)
  starting transfers between devices  9.23 us (6%)
  local copies, waits for them, and re-layouts  2.71 us (2%)
    dot_general x16, matrix products, block_scores(): lax.dot_general(vehicle_block, request_emb, (((1,), (1,)), ((), ())), pre...  47.3 us
    reduce_sum x8, other arithmetic, column_step(): jnp.sum(jnp.exp(logits - highest[None, :]), axis=0)  22.3 us
    reduce_scatter x1, waiting for transfers between devices, local(): lax.psum_scatter(features * factor[:, None], 'req', scatter_dimension=0,...  15.4 us
    all_to_all x2, waiting for transfers between devices, gather_by_exchange(): return lax.all_to_all(spread, axis, 0, 0, tiled=True)  15.1 us
    all_to_all x2, starting transfers between devices, gather_by_exchange(): return lax.all_to_all(spread, axis, 0, 0, tiled=True)  9.19 us
    all_gather x1, blocking collectives, local(): own_rows = lax.all_gather(vehicle_emb, 'req', axis=0, tiled=True)  7.42 us
    unnamed x1, blocking collectives  6.51 us
    pmax x1, blocking collectives, local(): summit = lax.pmax(peaks, 'req')  5.81 us
  transfers between devices with their start and end apart: 3, of which 3 were waited for; matrix products, arithmetic and copies ran while one was open for 0% of the time, Pallas kernels for 0%

profile of v1, /device:TPU:0, one launch (start us, length us, event | category | flops | bytes accessed | tf_op | source)
XLA Modules:
  0.0 165.0 jit_solution(15575758034844773592)
XLA Ops:
  6.5 7.4 %all_gather.6 = bf16[1024,128]{1,0:T(8,128)(2,1)S(1)} all-gather(bf16[256,128]{1,0:T(8,128)(2,1)} %param.13), channel_id=1, replica_groups=mesh['veh'=8,'req'=4] {'req'}, dimensions={0}, use_global_device_ids=true | all-gather | bytes 327680 | tf_op jit(solution)/shard_map/all_gather | solution.py:21
  14.0 26.8 %while.52 = (s32[]{:T(128)}, f32[4096]{0:T(1024)S(1)}, f32[4096]{0:T(1024)S(1)}, bf16[4,256,128]{2,1,0:T(8,128)(2,1)S(1)}, bf16[4096,128]{1,0:T(8,128)(2,1)}, /*index=5*/s32[]{:T(128)}, s32[]{:T(128)}) while((s32[]{:T(128)}, f32[4096]{0:T(1024)S(1)}, f32[4096]{0:T(1024)S(1)}, bf16[4,256,128]{2,1,0:T(8,128)(2,1)S(1)}, ...), condition=%wide.region_3.4_spmd.clone, body=%wide.region_0.3_spmd.clone.sunk | while | flops 272650240 | bytes 9715804 | solution.py:57
  14.0 3.9 %fusion.67 = (f32[4096]{0:T(1024)S(1)}, f32[256,4096]{1,0:T(8,128)}) fusion(bf16[4096,128]{1,0:T(8,128)(2,1)} %get-tuple-element.424, bf16[4,256,128]{2,1,0:T(8,128)(2,1)S(1)} %get-tuple-element.423, s32[]{:T(128)} %get-tuple-element.413), kind=kOutput, calls=%fused_computation.57.clone.1 | convolution fusion | flops 270528512 | bytes 5324804 | tf_op jit(solution)/shard_map/while/body/eval_jaxpr/dot_general | solution.py:31
  17.8 2.8 %exponential_reduce_fusion.7 = f32[4096]{0:T(1024)S(1)} fusion(f32[256,4096]{1,0:T(8,128)} %get-tuple-element.397, f32[4096]{0:T(1024)S(1)} %select_maximum_fusion.4), kind=kLoop, calls=%fused_computation.20.clone.1 | loop fusion | flops 2093056 | bytes 4227072 | tf_op jit(solution)/shard_map/while/body/eval_jaxpr/reduce_sum | solution.py:48
  20.7 3.9 %fusion.67 = (f32[4096]{0:T(1024)S(1)}, f32[256,4096]{1,0:T(8,128)}) fusion(bf16[4096,128]{1,0:T(8,128)(2,1)} %get-tuple-element.424, bf16[4,256,128]{2,1,0:T(8,128)(2,1)S(1)} %get-tuple-element.423, s32[]{:T(128)} %get-tuple-element.413), kind=kOutput, calls=%fused_computation.57.clone.1 | convolution fusion | flops 270528512 | bytes 5324804 | tf_op jit(solution)/shard_map/while/body/eval_jaxpr/dot_general | solution.py:31
  24.5 2.8 %exponential_reduce_fusion.7 = f32[4096]{0:T(1024)S(1)} fusion(f32[256,4096]{1,0:T(8,128)} %get-tuple-element.397, f32[4096]{0:T(1024)S(1)} %select_maximum_fusion.4), kind=kLoop, calls=%fused_computation.20.clone.1 | loop fusion | flops 2093056 | bytes 4227072 | tf_op jit(solution)/shard_map/while/body/eval_jaxpr/reduce_sum | solution.py:48
  27.4 3.9 %fusion.67 = (f32[4096]{0:T(1024)S(1)}, f32[256,4096]{1,0:T(8,128)}) fusion(bf16[4096,128]{1,0:T(8,128)(2,1)} %get-tuple-element.424, bf16[4,256,128]{2,1,0:T(8,128)(2,1)S(1)} %get-tuple-element.423, s32[]{:T(128)} %get-tuple-element.413), kind=kOutput, calls=%fused_computation.57.clone.1 | convolution fusion | flops 270528512 | bytes 5324804 | tf_op jit(solution)/shard_map/while/body/eval_jaxpr/dot_general | solution.py:31
  31.2 2.8 %exponential_reduce_fusion.7 = f32[4096]{0:T(1024)S(1)} fusion(f32[256,4096]{1,0:T(8,128)} %get-tuple-element.397, f32[4096]{0:T(1024)S(1)} %select_maximum_fusion.4), kind=kLoop, calls=%fused_computation.20.clone.1 | loop fusion | flops 2093056 | bytes 4227072 | tf_op jit(solution)/shard_map/while/body/eval_jaxpr/reduce_sum | solution.py:48
  34.1 3.9 %fusion.67 = (f32[4096]{0:T(1024)S(1)}, f32[256,4096]{1,0:T(8,128)}) fusion(bf16[4096,128]{1,0:T(8,128)(2,1)} %get-tuple-element.424, bf16[4,256,128]{2,1,0:T(8,128)(2,1)S(1)} %get-tuple-element.423, s32[]{:T(128)} %get-tuple-element.413), kind=kOutput, calls=%fused_computation.57.clone.1 | convolution fusion | flops 270528512 | bytes 5324804 | tf_op jit(solution)/shard_map/while/body/eval_jaxpr/dot_general | solution.py:31
  41.5 5.8 %all-to-all-start = ((f32[8,1,4096]{2,1,0:T(1,128)}), f32[8,1,4096]{2,1,0:T(1,128)S(1)}, u32[]{:S(2)}, u32[]{:S(2)}) async-start(f32[8,1,4096]{2,1,0:T(1,128)} %broadcast_in_dim.24), calls=%async_computation | async-start | bytes 262144 | tf_op jit(solution)/shard_map/all_to_all | solution.py:12
  47.3 7.5 %all-to-all-done = f32[8,1,4096]{2,1,0:T(1,128)S(1)} async-done(((f32[8,1,4096]{2,1,0:T(1,128)}), f32[8,1,4096]{2,1,0:T(1,128)S(1)}, u32[]{:S(2)}, u32[]{:S(2)}) %all-to-all-start) | async-done | bytes 131104 | tf_op jit(solution)/shard_map/all_to_all | solution.py:12
  55.1 11.2 %while.50 = (s32[]{:T(128)}, f32[4,256]{1,0:T(4,128)S(1)}, bf16[4,256,128]{2,1,0:T(8,128)(2,1)S(1)}, bf16[4096,128]{1,0:T(8,128)(2,1)}, f32[4096]{0:T(1024)S(1)}, /*index=5*/s32[]{:T(128)}, s32[]{:T(128)}) while((s32[]{:T(128)}, f32[4,256]{1,0:T(4,128)S(1)}, bf16[4,256,128]{2,1,0:T(8,128)(2,1)S(1)}, bf16[4096,128]{1,0:T(8,128)(2,1)}, ...), condition=%wide.region_9.10_spmd, body=%wide.region_6.9_spmd.sunk | while | flops 273678080 | bytes 9527381 | solution.py:70
  66.4 5.2 %all-gather = f32[4,1,1024]{2,1,0:T(1,128)S(1)} all-gather(f32[1,1,1024]{2,1,0:T(1,128)S(1)} %reshape.61), channel_id=1, replica_groups=mesh['veh'=8,'req'=4] {'req'}, dimensions={0}, use_global_device_ids=true | all-gather | bytes 20480 | tf_op jit(solution)/shard_map/all_gather | solution.py:71
  71.6 27.0 %while.53 = (s32[]{:T(128)}, f32[4096]{0:T(1024)S(1)}, f32[4096]{0:T(1024)S(1)}, bf16[4,256,128]{2,1,0:T(8,128)(2,1)S(1)}, bf16[4096,128]{1,0:T(8,128)(2,1)}, /*index=5*/f32[4,256]{1,0:T(4,128)S(1)}, s32[]{:T(128)}, s32[]{:T(128)}) while((s32[]{:T(128)}, f32[4096]{0:T(1024)S(1)}, f32[4096]{0:T(1024)S(1)}, ...), condition=%wide.region_15.16_spmd.clone, body=%wide.region_12.15_spmd.clone.sunk | while | flops 273698816 | bytes 9718888 | solution.py:57
  71.7 4.0 %fusion.70 = (f32[4096]{0:T(1024)S(1)}, f32[256,4096]{1,0:T(8,128)}) fusion(f32[256]{0:T(256)S(1)} %bitcast.89, bf16[4096,128]{1,0:T(8,128)(2,1)} %get-tuple-element.468, bf16[4,256,128]{2,1,0:T(8,128)(2,1)S(1)} %get-tuple-element.467, s32[]{:T(128)} %get-tuple-element.456), kind=kOutput, calls=%fused_computation.58.clone.1 | convolution fusion | flops 271577088 | bytes 5325828 | tf_op jit(solution)/shard_map/while/body/eval_jaxpr/dot_general | solution.py:31
  78.5 3.9 %fusion.70 = (f32[4096]{0:T(1024)S(1)}, f32[256,4096]{1,0:T(8,128)}) fusion(f32[256]{0:T(256)S(1)} %bitcast.89, bf16[4096,128]{1,0:T(8,128)(2,1)} %get-tuple-element.468, bf16[4,256,128]{2,1,0:T(8,128)(2,1)S(1)} %get-tuple-element.467, s32[]{:T(128)} %get-tuple-element.456), kind=kOutput, calls=%fused_computation.58.clone.1 | convolution fusion | flops 271577088 | bytes 5325828 | tf_op jit(solution)/shard_map/while/body/eval_jaxpr/dot_general | solution.py:31
  85.3 3.9 %fusion.70 = (f32[4096]{0:T(1024)S(1)}, f32[256,4096]{1,0:T(8,128)}) fusion(f32[256]{0:T(256)S(1)} %bitcast.89, bf16[4096,128]{1,0:T(8,128)(2,1)} %get-tuple-element.468, bf16[4,256,128]{2,1,0:T(8,128)(2,1)S(1)} %get-tuple-element.467, s32[]{:T(128)} %get-tuple-element.456), kind=kOutput, calls=%fused_computation.58.clone.1 | convolution fusion | flops 271577088 | bytes 5325828 | tf_op jit(solution)/shard_map/while/body/eval_jaxpr/dot_general | solution.py:31
  92.0 3.9 %fusion.70 = (f32[4096]{0:T(1024)S(1)}, f32[256,4096]{1,0:T(8,128)}) fusion(f32[256]{0:T(256)S(1)} %bitcast.89, bf16[4096,128]{1,0:T(8,128)(2,1)} %get-tuple-element.468, bf16[4,256,128]{2,1,0:T(8,128)(2,1)S(1)} %get-tuple-element.467, s32[]{:T(128)} %get-tuple-element.456), kind=kOutput, calls=%fused_computation.58.clone.1 | convolution fusion | flops 271577088 | bytes 5325828 | tf_op jit(solution)/shard_map/while/body/eval_jaxpr/dot_general | solution.py:31
  99.4 3.4 %all-to-all-start.1 = ((f32[8,1,4096]{2,1,0:T(1,128)}), f32[8,1,4096]{2,1,0:T(1,128)S(1)}, u32[]{:S(2)}, u32[]{:S(2)}) async-start(f32[8,1,4096]{2,1,0:T(1,128)} %broadcast_in_dim.25), calls=%async_computation.1 | async-start | bytes 262144 | tf_op jit(solution)/shard_map/all_to_all | solution.py:12
  102.9 7.6 %all-to-all-done.1 = f32[8,1,4096]{2,1,0:T(1,128)S(1)} async-done(((f32[8,1,4096]{2,1,0:T(1,128)}), f32[8,1,4096]{2,1,0:T(1,128)S(1)}, u32[]{:S(2)}, u32[]{:S(2)}) %all-to-all-start.1) | async-done | bytes 131104 | tf_op jit(solution)/shard_map/all_to_all | solution.py:12
  111.5 14.7 %while.51 = (s32[]{:T(128)}, f32[4,256]{1,0:T(4,128)S(1)}, f32[4,256]{1,0:T(4,128)S(1)}, f32[4,256,256]{2,1,0:T(8,128)S(1)}, bf16[4,256,128]{2,1,0:T(8,128)(2,1)...) while((s32[]{:T(128)}, f32[4,256]{1,0:T(4,128)S(1)}, ...), condition=%wide.region_21.22_spmd, body=%wide.region_18.21_spmd.sunk | while | flops 812645888 | bytes 16081013 | solution.py:84
  126.1 5.8 %pmax.7 = f32[1024]{0:T(1024)S(1)} all-reduce(f32[1024]{0:T(1024)S(1)} %bitcast.92), channel_id=1, replica_groups=mesh['veh'=8,'req'=4] {'req'}, use_global_device_ids=true, to_apply=%region_22.23 | all-reduce | flops 1024 | bytes 8192 | tf_op jit(solution)/shard_map/pmax | solution.py:88
  134.4 6.5 %all-reduce = f32[1024]{0:T(1024)S(1)} all-reduce(f32[1024]{0:T(1024)S(1)} %get-tuple-element.232), channel_id=3, replica_groups=mesh['veh'=8,'req'=4] {'req'}, use_global_device_ids=true, to_apply=%region_24.25.clone | all-reduce | flops 1024 | bytes 8192
  141.0 15.4 %reduce-scatter.2.cloned.1.call-done = f32[256,256]{1,0:T(8,128)} async-done(((f32[1024,256]{1,0:T(8,128)}), f32[256,256]{1,0:T(8,128)}) %reduce-scatter.2.cloned.1.call-update) | async-done | bytes 262160 | tf_op jit(solution)/shard_map/reduce_scatter | solution.py:91
  (109 shorter events, 46.3 us)
Async XLA Ops:
  14.0 41.1 %copy-start.1 = (f32[4096]{0:T(1024)S(1)}, f32[4096]{0:T(1024)}, u32[]{:S(2)}) copy-start(f32[4096]{0:T(1024)} %param.17) | copy-start | bytes 49156
  41.5 13.3 %all-to-all-start = ((f32[8,1,4096]{2,1,0:T(1,128)}), f32[8,1,4096]{2,1,0:T(1,128)S(1)}, u32[]{:S(2)}, u32[]{:S(2)}) async-start(f32[8,1,4096]{2,1,0:T(1,128)} %broadcast_in_dim.24), calls=%async_computation | async-start | bytes 262144 | tf_op jit(solution)/shard_map/all_to_all | solution.py:12
  55.1 16.5 %copy-start.2 = (f32[1024]{0:T(1024)S(1)}, f32[1024]{0:T(1024)}, u32[]{:S(2)}) copy-start(f32[1024]{0:T(1024)} %param.16) | copy-start | bytes 12292
  71.6 39.8 %copy-start = (bf16[4096,256]{1,0:T(8,128)(2,1)S(1)}, bf16[4096,256]{1,0:T(8,128)(2,1)}, u32[]{:S(2)}) copy-start(bf16[4096,256]{1,0:T(8,128)(2,1)} %param.15) | copy-start | bytes 6291460
  99.4 11.0 %all-to-all-start.1 = ((f32[8,1,4096]{2,1,0:T(1,128)}), f32[8,1,4096]{2,1,0:T(1,128)S(1)}, u32[]{:S(2)}, u32[]{:S(2)}) async-start(f32[8,1,4096]{2,1,0:T(1,128)} %broadcast_in_dim.25), calls=%async_computation.1 | async-start | bytes 262144 | tf_op jit(solution)/shard_map/all_to_all | solution.py:12
  102.8 53.6 %reduce-scatter.2.cloned.1.call-start = ((), (), s32[]{:S(2)}) async-start(), calls=%async_computation.3 | async-start | bytes 1310720 | tf_op jit(solution)/shard_map/reduce_scatter | solution.py:91
  111.5 21.7 %copy-start.3 = (u32[32]{0:T(128)S(1)}, u32[32]{0:T(128)}, u32[]{:S(2)}) copy-start(u32[32]{0:T(128)} %constant.72) | copy-start | bytes 388
Sparse Core Ops, SparseCore 0:
  133.3 23.0 reduce-scatter.1

commit v2 on v1

v2 whole, which is shorter than its diff:
```python
import functools
import math

import jax
import jax.numpy as jnp
from jax import lax
from jax.experimental import pallas as pl
from jax.sharding import PartitionSpec as P


def gather_by_exchange(x, axis):
    count = lax.axis_size(axis)
    spread = jnp.broadcast_to(x[None], (count,) + x.shape)
    return lax.all_to_all(spread, axis, 0, 0, tiled=True)


def merge_lse(parts):
    top = jnp.max(parts, axis=0)
    return top + jnp.log(jnp.sum(jnp.exp(parts - top[None]), axis=0))


def lse_kernel(a_ref, shift_ref, b_ref, out_ref, *, scale):
    scores = lax.dot_general(
        a_ref[...], b_ref[...], (((1,), (1,)), ((), ())), preferred_element_type=jnp.float32
    )
    logits = scores * scale + shift_ref[...]
    top = jnp.max(logits, axis=0, keepdims=True)
    total = jnp.sum(jnp.exp(logits - top), axis=0, keepdims=True)
    out_ref[...] = top + jnp.log(total)


def lse_over_rows(a, shift, b, scale, tile):
    rows, width = a.shape
    cols = b.shape[0]
    tile = min(tile, cols)
    return pl.pallas_call(
        functools.partial(lse_kernel, scale=scale),
        out_shape=jax.ShapeDtypeStruct((1, cols), jnp.float32),
        grid=(cols // tile,),
        in_specs=[
            pl.BlockSpec((rows, width), lambda j: (0, 0)),
            pl.BlockSpec((rows, 1), lambda j: (0, 0)),
            pl.BlockSpec((tile, width), lambda j: (j, 0)),
        ],
        out_specs=pl.BlockSpec((1, tile), lambda j: (0, j)),
        cost_estimate=pl.CostEstimate(
            flops=2 * rows * cols * width + 5 * rows * cols,
            transcendentals=rows * cols,
            bytes_accessed=2 * (rows + cols) * width + 4 * (rows + cols),
        ),
    )(a, shift.reshape(rows, 1), b)[0]


def assign_kernel(v_ref, r_ref, d_ref, f_ref, peak_ref, mass_ref, feat_ref, *, scale):
    scores = lax.dot_general(
        v_ref[...], r_ref[...], (((1,), (1,)), ((), ())), preferred_element_type=jnp.float32
    )
    logits = scores * scale + d_ref[...]
    top = jnp.max(logits, axis=1, keepdims=True)
    powers = jnp.exp(logits - top)
    peak_ref[...] = top
    mass_ref[...] = jnp.sum(powers, axis=1, keepdims=True)
    feat_ref[...] = jnp.dot(
        powers.astype(jnp.bfloat16), f_ref[...], preferred_element_type=jnp.float32
    )


def assign_rows(v, r, d, f, scale, tile):
    rows, width = v.shape
    cols, feat = f.shape
    tile = min(tile, rows)
    return pl.pallas_call(
        functools.partial(assign_kernel, scale=scale),
        out_shape=(
            jax.ShapeDtypeStruct((rows, 1), jnp.float32),
            jax.ShapeDtypeStruct((rows, 1), jnp.float32),
            jax.ShapeDtypeStruct((rows, feat), jnp.float32),
        ),
        grid=(rows // tile,),
        in_specs=[
            pl.BlockSpec((tile, width), lambda i: (i, 0)),
            pl.BlockSpec((cols, width), lambda i: (0, 0)),
            pl.BlockSpec((1, cols), lambda i: (0, 0)),
            pl.BlockSpec((cols, feat), lambda i: (0, 0)),
        ],
        out_specs=(
            pl.BlockSpec((tile, 1), lambda i: (i, 0)),
            pl.BlockSpec((tile, 1), lambda i: (i, 0)),
            pl.BlockSpec((tile, feat), lambda i: (i, 0)),
        ),
        cost_estimate=pl.CostEstimate(
            flops=2 * rows * cols * (width + feat) + 5 * rows * cols,
            transcendentals=rows * cols,
            bytes_accessed=2 * (rows + cols) * width + 2 * cols * feat + 4 * rows * (feat + 2),
        ),
    )(v, r, d.reshape(1, cols), f)


def local(vehicle_emb, request_emb, request_feat, log_supply, log_demand):
    own_rows = lax.all_gather(vehicle_emb, "req", axis=0, tiled=True)
    row_count = own_rows.shape[0]
    scale = 3.0 / math.sqrt(own_rows.shape[1])

    def column_pot(shift):
        partial = lse_over_rows(own_rows, shift, request_emb, scale, 512)
        return log_demand - merge_lse(gather_by_exchange(partial, "veh"))

    demand_first = column_pot(jnp.zeros((row_count,), jnp.float32))
    partial = lse_over_rows(request_emb, demand_first, own_rows, scale, 256)
    parts = lax.all_gather(partial, "req", axis=0, tiled=False)
    supply_pot = log_supply - merge_lse(parts)
    demand_second = column_pot(supply_pot)

    peaks, masses, features = assign_rows(
        own_rows, request_emb, demand_second, request_feat, scale, 128
    )
    peaks = peaks[:, 0]
    masses = masses[:, 0]
    summit = lax.pmax(peaks, "req")
    factor = jnp.exp(peaks - summit)
    own_feat, own_mass = (
        lax.psum_scatter(features * factor[:, None], "req", scatter_dimension=0, tiled=True),
        lax.psum_scatter(masses * factor, "req", scatter_dimension=0, tiled=True),
    )
    return own_feat / own_mass[:, None]


def solution(mesh):
    in_specs = (P(("veh", "req"), None), P("req", None), P("req", None), P("veh"), P("req"))
    out_specs = P(("veh", "req"), None)
    return jax.shard_map(local, mesh=mesh, in_specs=in_specs, out_specs=out_specs, check_vma=False)
```

time: 166 us -> 137 us (0.83)
  matrix products: 50.6 us -> 0 us
  Pallas kernels: 0 us -> 42.9 us
  other arithmetic: 32.4 us -> 7.84 us
  blocking collectives: 24.9 us -> 49.1 us
  waiting for transfers between devices: 30.5 us -> 15.6 us
  starting transfers between devices: 9.23 us -> 0.01 us
  local copies, waits for them, and re-layouts: 2.71 us -> 6.09 us
    dot_general x20 -> x0, matrix products: 50.6 us -> none  [the longest x16 47.3 us: block_scores(): lax.dot_general(vehicle_block, request_emb, (((1,), (1,)), ((), ())), pre...]
    pallas_call x0 -> x4, Pallas kernels: none -> 42.9 us  [the longest x3 27.2 us: lse_over_rows(): pl.pallas_call(functools.partial(lse_kernel, scale=scale), out_shape=jax....]
    reduce_sum x16 -> x0, other arithmetic: 28 us -> none  [the longest x8 22.3 us: column_step(): jnp.sum(jnp.exp(logits - highest[None, :]), axis=0)]
    all_to_all x0 -> x2, blocking collectives: none -> 23.2 us  [gather_by_exchange(): return lax.all_to_all(spread, axis, 0, 0, tiled=True)]
    all_to_all x2 -> x0, waiting for transfers between devices: 15.1 us -> none  [gather_by_exchange(): return lax.all_to_all(spread, axis, 0, 0, tiled=True)]
    all_to_all x2 -> x0, starting transfers between devices: 9.19 us -> none  [gather_by_exchange(): return lax.all_to_all(spread, axis, 0, 0, tiled=True)]
    reshape x1 -> x3, local copies, waits for them, and re-layouts: 0.01 us -> 3.85 us  [lse_over_rows(): shift.reshape(rows, 1)]
    pallas_call x0 -> x2, other arithmetic: none -> 2.5 us  [assign_rows(): pl.pallas_call(functools.partial(assign_kernel, scale=scale), out_shape=(...]
  transfers between devices with their start and end apart: 3 -> 1, of which waited for: 3 -> 1; matrix products, arithmetic and copies ran while one was open for 0% -> 0% of each run, Pallas kernels for 0% -> 0%
where the time goes in v2:
time: 137 us; the launch traced here: 136 us
  blocking collectives  49.1 us (36%)
  Pallas kernels  42.9 us (31%)
  waiting for transfers between devices  15.6 us (11%)
  between operations  14.1 us (10%)
  other arithmetic  7.84 us (6%)
  local copies, waits for them, and re-layouts  6.09 us (4%)
    pallas_call x3, Pallas kernels, lse_over_rows(): pl.pallas_call(functools.partial(lse_kernel, scale=scale), out_shape=jax....  27.2 us
    all_to_all x2, blocking collectives, gather_by_exchange(): return lax.all_to_all(spread, axis, 0, 0, tiled=True)  23.2 us
    pallas_call x1, Pallas kernels, assign_rows(): pl.pallas_call(functools.partial(assign_kernel, scale=scale), out_shape=(...  15.7 us
    reduce_scatter x1, waiting for transfers between devices, local(): lax.psum_scatter(features * factor[:, None], 'req', scatter_dimension=0,...  15.6 us
    all_gather x1, blocking collectives, local(): own_rows = lax.all_gather(vehicle_emb, 'req', axis=0, tiled=True)  8.81 us
    pmax x1, blocking collectives, local(): summit = lax.pmax(peaks, 'req')  6 us
    unnamed x1, blocking collectives  5.77 us
    all_gather x1, blocking collectives, local(): parts = lax.all_gather(partial, 'req', axis=0, tiled=False)  5.3 us
  transfers between devices with their start and end apart: 1, of which 1 were waited for; matrix products, arithmetic and copies ran while one was open for 0% of the time, Pallas kernels for 0%

profile of v2, /device:TPU:0, one launch (start us, length us, event | category | flops | bytes accessed | tf_op | source)
XLA Modules:
  0.0 135.7 jit_solution(1687246902372815205)
XLA Ops:
  6.5 8.8 %all_gather.6.a_ref.b_ref.v_ref = bf16[1024,128]{1,0:T(8,128)(2,1)} all-gather(bf16[256,128]{1,0:T(8,128)(2,1)} %param.5), channel_id=1, replica_groups=mesh['veh'=8,'req'=4] {'req'}, dimensions={0}, use_global_device_ids=true | all-gather | bytes 327680 | tf_op jit(solution)/shard_map/all_gather | solution.py:100
  15.4 0.8 reshape.29.shift_ref
  16.2 8.8 %shard_map.55 = f32[1,4096]{1,0:T(1,128)} custom-call(bf16[1024,128]{1,0:T(8,128)(2,1)} %all_gather.6.a_ref.b_ref.v_ref, f32[1024,1]{1,0:T(8,128)} %reshape.29.shift_ref, bf16[4096,128]{1,0:T(8,128)(2,1)} %r_ref.1), custom_call_target="tpu_custom_call" | custom-call | flops 1094713344 | bytes 1331200 | tf_op jit(solution)/shard_map/pallas_call | solution.py:36
  25.0 0.8 broadcast_in_dim.4
  25.8 13.1 %all_to_all.18 = f32[8,1,4096]{2,1,0:T(1,128)S(1)} all-to-all(f32[8,1,4096]{2,1,0:T(1,128)S(1)} %broadcast_in_dim.4), channel_id=1, replica_groups=mesh['veh'=8,'req'=4] {'veh'}, dimensions={0} | all-to-all | bytes 262144 | tf_op jit(solution)/shard_map/all_to_all | solution.py:14
  39.0 0.1 fusion.3
  39.1 2.0 %copy.13.shift_ref = f32[4096,1]{1,0:T(8,128)} copy(f32[4096,1]{0,1:T(1,128)S(1)} %bitcast.25) | data formatting | bytes 32768 | tf_op jit(solution)/shard_map/reshape | solution.py:51
  41.1 9.6 %shard_map.56 = f32[1,1024]{1,0:T(1,128)} custom-call(bf16[4096,128]{1,0:T(8,128)(2,1)} %r_ref.1, f32[4096,1]{1,0:T(8,128)} %copy.13.shift_ref, bf16[1024,128]{1,0:T(8,128)(2,1)} %all_gather.6.a_ref.b_ref.v_ref), custom_call_target="tpu_custom_call" | custom-call | flops 1094713344 | bytes 1331200 | tf_op jit(solution)/shard_map/pallas_call | solution.py:36
  50.7 5.3 %all-gather = f32[4,1,1024]{2,1,0:T(1,128)S(1)} all-gather(f32[1,1,1024]{2,1,0:T(1,128)} %bitcast.30), channel_id=1, replica_groups=mesh['veh'=8,'req'=4] {'req'}, dimensions={0}, use_global_device_ids=true | all-gather | bytes 20480 | tf_op jit(solution)/shard_map/all_gather | solution.py:110
  56.1 1.0 copy.14.shift_ref
  57.1 8.8 %shard_map.57 = f32[1,4096]{1,0:T(1,128)} custom-call(bf16[1024,128]{1,0:T(8,128)(2,1)} %all_gather.6.a_ref.b_ref.v_ref, f32[1024,1]{1,0:T(8,128)} %copy.14.shift_ref, bf16[4096,128]{1,0:T(8,128)(2,1)} %r_ref.1), custom_call_target="tpu_custom_call" | custom-call | flops 1094713344 | bytes 1331200 | tf_op jit(solution)/shard_map/pallas_call | solution.py:36
  65.9 0.8 broadcast_in_dim.5
  66.7 10.1 %all_to_all.19 = f32[8,1,4096]{2,1,0:T(1,128)S(1)} all-to-all(f32[8,1,4096]{2,1,0:T(1,128)S(1)} %broadcast_in_dim.5), channel_id=1, replica_groups=mesh['veh'=8,'req'=4] {'veh'}, dimensions={0} | all-to-all | bytes 262144 | tf_op jit(solution)/shard_map/all_to_all | solution.py:14
  76.9 0.1 fusion.1
  77.0 0.6 add_subtract_fusion
  77.7 15.7 %shard_map.58 = (f32[1024,1]{1,0:T(8,128)}, f32[1024,1]{1,0:T(8,128)}, f32[1024,256]{1,0:T(8,128)}) custom-call(bf16[1024,128]{1,0:T(8,128)(2,1)} %all_gather.6.a_ref.b_ref.v_ref, bf16[4096,128]{1,0:T(8,128)(2,1)} %r_ref.1, f32[1,4096]{1,0:T(1,128)} %bitcast.29, bf16[4096,256]{1,0:T(8,128)(2,1)} %f_ref.1), custom_call_target="tpu_custom_call" | custom-call | flops 3242196992 | bytes 4464640 | tf_op jit(solution)/shard_map/pallas_call | solution.py:72
  93.4 1.3 reduce.3
  94.6 6.0 %pmax.7 = f32[1024]{0:T(1024)S(1)} all-reduce(f32[1024]{0:T(1024)S(1)} %reduce.3), channel_id=1, replica_groups=mesh['veh'=8,'req'=4] {'req'}, use_global_device_ids=true, to_apply=%region_6.0 | all-reduce | flops 1024 | bytes 8192 | tf_op jit(solution)/shard_map/pmax | solution.py:119
  100.6 1.2 reduce.4
  101.9 2.5 %broadcast_multiply_fusion = f32[1024,256]{1,0:T(8,128)} fusion(f32[1024,256]{1,0:T(8,128)} %get-tuple-element.8, f32[1024]{0:T(1024)S(1)} %get-tuple-element.12), kind=kLoop, calls=%fused_computation | loop fusion | flops 262144 | bytes 2101248 | tf_op jit(solution)/shard_map/mul | solution.py:122
  104.4 0.6 dynamic-slice
  105.6 5.8 %all-reduce = f32[1024]{0:T(1024)S(1)} all-reduce(f32[1024]{0:T(1024)S(1)} %get-tuple-element.11), channel_id=3, replica_groups=mesh['veh'=8,'req'=4] {'req'}, use_global_device_ids=true, to_apply=%region_8.0.clone | all-reduce | flops 1024 | bytes 8192
  111.5 15.6 %reduce-scatter.2.cloned.1.call-done = f32[256,256]{1,0:T(8,128)} async-done(((f32[1024,256]{1,0:T(8,128)}), f32[256,256]{1,0:T(8,128)}) %reduce-scatter.2.cloned.1.call-update) | async-done | bytes 262160 | tf_op jit(solution)/shard_map/reduce_scatter | solution.py:122
  127.1 1.8 %broadcast_divide_fusion = f32[256,256]{1,0:T(8,128)} fusion(f32[256,256]{1,0:T(8,128)} %reduce-scatter.2.cloned.1.call-done, f32[256]{0:T(256)S(1)} %dynamic-slice.1), kind=kLoop, calls=%fused_computation.7 | loop fusion | flops 65536 | bytes 525312 | tf_op jit(solution)/shard_map/div | solution.py:125
  (16 shorter events, 0.4 us)
Async XLA Ops:
  6.5 120.6 %reduce-scatter.2.cloned.1.call-start = ((), (), s32[]{:S(2)}) async-start(), calls=%async_computation.3 | async-start | bytes 1310720 | tf_op jit(solution)/shard_map/reduce_scatter | solution.py:122
  16.2 22.9 %copy-start = (f32[4096]{0:T(1024)S(1)}, f32[4096]{0:T(1024)}, u32[]{:S(2)}) copy-start(f32[4096]{0:T(1024)} %param.9) | copy-start | bytes 49156
  41.1 14.9 %copy-start.1 = (f32[1024]{0:T(1024)S(1)}, f32[1024]{0:T(1024)}, u32[]{:S(2)}) copy-start(f32[1024]{0:T(1024)} %param.8) | copy-start | bytes 12292
  93.4 11.0 %copy-start.2 = (u32[32]{0:T(128)S(1)}, u32[32]{0:T(128)}, u32[]{:S(2)}) copy-start(u32[32]{0:T(128)} %constant.7) | copy-start | bytes 388
Sparse Core Ops, SparseCore 0:
  104.5 22.5 reduce-scatter.1

commit v3 on v2

--- a/solution.py
+++ b/solution.py
@@ -51,18 +51,20 @@
     )(a, shift.reshape(rows, 1), b)[0]
 
 
-def assign_kernel(v_ref, r_ref, d_ref, f_ref, peak_ref, mass_ref, feat_ref, *, scale):
+def assign_kernel(v_ref, r_ref, d_ref, f_ref, out_ref, *, scale):
     scores = lax.dot_general(
         v_ref[...], r_ref[...], (((1,), (1,)), ((), ())), preferred_element_type=jnp.float32
     )
     logits = scores * scale + d_ref[...]
     top = jnp.max(logits, axis=1, keepdims=True)
     powers = jnp.exp(logits - top)
-    peak_ref[...] = top
-    mass_ref[...] = jnp.sum(powers, axis=1, keepdims=True)
-    feat_ref[...] = jnp.dot(
+    mass = jnp.sum(powers, axis=1, keepdims=True)
+    feat = f_ref.shape[1]
+    out_ref[:, :feat] = jnp.dot(
         powers.astype(jnp.bfloat16), f_ref[...], preferred_element_type=jnp.float32
     )
+    lane = lax.broadcasted_iota(jnp.int32, (top.shape[0], 128), 1)
+    out_ref[:, feat:] = jnp.where(lane == 0, mass, jnp.where(lane == 1, top, 0.0))
 
 
 def assign_rows(v, r, d, f, scale, tile):
@@ -71,11 +73,7 @@
     tile = min(tile, rows)
     return pl.pallas_call(
         functools.partial(assign_kernel, scale=scale),
-        out_shape=(
-            jax.ShapeDtypeStruct((rows, 1), jnp.float32),
-            jax.ShapeDtypeStruct((rows, 1), jnp.float32),
-            jax.ShapeDtypeStruct((rows, feat), jnp.float32),
-        ),
+        out_shape=jax.ShapeDtypeStruct((rows, feat + 128), jnp.float32),
         grid=(rows // tile,),
         in_specs=[
             pl.BlockSpec((tile, width), lambda i: (i, 0)),
@@ -83,11 +81,7 @@
             pl.BlockSpec((1, cols), lambda i: (0, 0)),
             pl.BlockSpec((cols, feat), lambda i: (0, 0)),
         ],
-        out_specs=(
-            pl.BlockSpec((tile, 1), lambda i: (i, 0)),
-            pl.BlockSpec((tile, 1), lambda i: (i, 0)),
-            pl.BlockSpec((tile, feat), lambda i: (i, 0)),
-        ),
+        out_specs=pl.BlockSpec((tile, feat + 128), lambda i: (i, 0)),
         cost_estimate=pl.CostEstimate(
             flops=2 * rows * cols * (width + feat) + 5 * rows * cols,
             transcendentals=rows * cols,
@@ -111,18 +105,17 @@
     supply_pot = log_supply - merge_lse(parts)
     demand_second = column_pot(supply_pot)
 
-    peaks, masses, features = assign_rows(
-        own_rows, request_emb, demand_second, request_feat, scale, 128
-    )
-    peaks = peaks[:, 0]
-    masses = masses[:, 0]
-    summit = lax.pmax(peaks, "req")
-    factor = jnp.exp(peaks - summit)
-    own_feat, own_mass = (
-        lax.psum_scatter(features * factor[:, None], "req", scatter_dimension=0, tiled=True),
-        lax.psum_scatter(masses * factor, "req", scatter_dimension=0, tiled=True),
-    )
-    return own_feat / own_mass[:, None]
+    packed = assign_rows(own_rows, request_emb, demand_second, request_feat, scale, 128)
+    owners = lax.axis_size("req")
+    feat = request_feat.shape[1]
+    packed = packed.reshape(owners, row_count // owners, feat + 128)
+    arrived = lax.all_to_all(packed, "req", 0, 0, tiled=True)
+    peaks = arrived[:, :, feat + 1]
+    masses = arrived[:, :, feat]
+    factor = jnp.exp(peaks - jnp.max(peaks, axis=0, keepdims=True))
+    numerator = jnp.sum(arrived[:, :, :feat] * factor[:, :, None], axis=0)
+    denominator = jnp.sum(masses * factor, axis=0)
+    return numerator / denominator[:, None]
 
 
 def solution(mesh):

time: 137 us -> 113 us (0.82)
  waiting for transfers between devices: 15.6 us -> 0 us
  between operations: 14.1 us -> 0.1 us
  blocking collectives: 49.1 us -> 59.9 us
  other arithmetic: 7.84 us -> 1.27 us
  local copies, waits for them, and re-layouts: 6.09 us -> 8.14 us
    all_to_all x0 -> x1, blocking collectives: none -> 22.5 us  [local(): arrived = lax.all_to_all(packed, 'req', 0, 0, tiled=True)]
    reduce_scatter x1 -> x0, waiting for transfers between devices: 15.6 us -> none  [local(): lax.psum_scatter(features * factor[:, None], 'req', scatter_dimension=0,...]
    pmax x1 -> x0, blocking collectives: 6 us -> none  [local(): summit = lax.pmax(peaks, 'req')]
    unnamed x1 -> x0, blocking collectives: 5.77 us -> none
    pallas_call x2 -> x0, other arithmetic: 2.5 us -> none  [assign_rows(): pl.pallas_call(functools.partial(assign_kernel, scale=scale), out_shape=(...]
    mul x2 -> x1, other arithmetic: 2.47 us -> 0.01 us  [local(): numerator = jnp.sum(arrived[:, :, :feat] * factor[:, :, None], axis=0)]
    reshape x0 -> x1, local copies, waits for them, and re-layouts: none -> 1.87 us  [local(): packed = packed.reshape(owners, row_count // owners, feat + 128)]
    div x1, other arithmetic: 1.76 us -> 0.03 us  [local(): return numerator / denominator[:, None]]
  transfers between devices with their start and end apart: 1 -> 0, of which waited for: 1 -> 0; matrix products, arithmetic and copies ran while one was open for 0% -> 0% of each run, Pallas kernels for 0% -> 0%
where the time goes in v3:
time: 113 us; the launch traced here: 112 us
  blocking collectives  59.9 us (53%)
  Pallas kernels  42.9 us (38%)
  local copies, waits for them, and re-layouts  8.14 us (7%)
  other arithmetic  1.27 us (1%)
    pallas_call x3, Pallas kernels, lse_over_rows(): pl.pallas_call(functools.partial(lse_kernel, scale=scale), out_shape=jax....  27.2 us
    all_to_all x2, blocking collectives, gather_by_exchange(): return lax.all_to_all(spread, axis, 0, 0, tiled=True)  23.2 us
    all_to_all x1, blocking collectives, local(): arrived = lax.all_to_all(packed, 'req', 0, 0, tiled=True)  22.5 us
    pallas_call x1, Pallas kernels, assign_rows(): pl.pallas_call(functools.partial(assign_kernel, scale=scale), out_shape=j...  15.7 us
    all_gather x1, blocking collectives, local(): own_rows = lax.all_gather(vehicle_emb, 'req', axis=0, tiled=True)  8.81 us
    all_gather x1, blocking collectives, local(): parts = lax.all_gather(partial, 'req', axis=0, tiled=False)  5.3 us
    reshape x3, local copies, waits for them, and re-layouts, lse_over_rows(): shift.reshape(rows, 1)  3.85 us

profile of v3, /device:TPU:0, one launch (start us, length us, event | category | flops | bytes accessed | tf_op | source)
XLA Modules:
  0.0 112.3 jit_solution(9003169141217313359)
XLA Ops:
  0.0 8.8 %all_gather.6.a_ref.b_ref.v_ref = bf16[1024,128]{1,0:T(8,128)(2,1)} all-gather(bf16[256,128]{1,0:T(8,128)(2,1)} %param.5), channel_id=1, replica_groups=mesh['veh'=8,'req'=4] {'req'}, dimensions={0}, use_global_device_ids=true | all-gather | bytes 327680 | tf_op jit(solution)/shard_map/all_gather | solution.py:94
  8.8 0.8 reshape.37.shift_ref
  9.6 8.8 %shard_map.55 = f32[1,4096]{1,0:T(1,128)} custom-call(bf16[1024,128]{1,0:T(8,128)(2,1)} %all_gather.6.a_ref.b_ref.v_ref, f32[1024,1]{1,0:T(8,128)} %reshape.37.shift_ref, bf16[4096,128]{1,0:T(8,128)(2,1)} %r_ref.1), custom_call_target="tpu_custom_call" | custom-call | flops 1094713344 | bytes 1331200 | tf_op jit(solution)/shard_map/pallas_call | solution.py:36
  18.4 0.8 broadcast_in_dim.4
  19.2 13.1 %all_to_all.23 = f32[8,1,4096]{2,1,0:T(1,128)S(1)} all-to-all(f32[8,1,4096]{2,1,0:T(1,128)S(1)} %broadcast_in_dim.4), channel_id=1, replica_groups=mesh['veh'=8,'req'=4] {'veh'}, dimensions={0} | all-to-all | bytes 262144 | tf_op jit(solution)/shard_map/all_to_all | solution.py:14
  32.3 0.1 reduce_max.36
  32.4 0.1 fusion.4
  32.5 0.0 copy-done
  32.6 2.0 %copy.23.shift_ref = f32[4096,1]{1,0:T(8,128)} copy(f32[4096,1]{0,1:T(1,128)S(1)} %bitcast.38) | data formatting | bytes 32768 | tf_op jit(solution)/shard_map/reshape | solution.py:51
  34.6 9.6 %shard_map.56 = f32[1,1024]{1,0:T(1,128)} custom-call(bf16[4096,128]{1,0:T(8,128)(2,1)} %r_ref.1, f32[4096,1]{1,0:T(8,128)} %copy.23.shift_ref, bf16[1024,128]{1,0:T(8,128)(2,1)} %all_gather.6.a_ref.b_ref.v_ref), custom_call_target="tpu_custom_call" | custom-call | flops 1094713344 | bytes 1331200 | tf_op jit(solution)/shard_map/pallas_call | solution.py:36
  44.2 5.3 %all-gather = f32[4,1,1024]{2,1,0:T(1,128)S(1)} all-gather(f32[1,1,1024]{2,1,0:T(1,128)} %bitcast.43), channel_id=1, replica_groups=mesh['veh'=8,'req'=4] {'req'}, dimensions={0}, use_global_device_ids=true | all-gather | bytes 20480 | tf_op jit(solution)/shard_map/all_gather | solution.py:104
  49.5 0.0 copy-done.1
  49.6 1.0 copy.24.shift_ref
  50.6 8.8 %shard_map.57 = f32[1,4096]{1,0:T(1,128)} custom-call(bf16[1024,128]{1,0:T(8,128)(2,1)} %all_gather.6.a_ref.b_ref.v_ref, f32[1024,1]{1,0:T(8,128)} %copy.24.shift_ref, bf16[4096,128]{1,0:T(8,128)(2,1)} %r_ref.1), custom_call_target="tpu_custom_call" | custom-call | flops 1094713344 | bytes 1331200 | tf_op jit(solution)/shard_map/pallas_call | solution.py:36
  59.4 0.8 broadcast_in_dim.5
  60.2 10.1 %all_to_all.24 = f32[8,1,4096]{2,1,0:T(1,128)S(1)} all-to-all(f32[8,1,4096]{2,1,0:T(1,128)S(1)} %broadcast_in_dim.5), channel_id=1, replica_groups=mesh['veh'=8,'req'=4] {'veh'}, dimensions={0} | all-to-all | bytes 262144 | tf_op jit(solution)/shard_map/all_to_all | solution.py:14
  70.3 0.1 reduce_max.38
  70.4 0.1 fusion.2
  70.5 0.6 add_subtract_fusion
  71.1 15.7 %shard_map.58 = f32[1024,384]{1,0:T(8,128)} custom-call(bf16[1024,128]{1,0:T(8,128)(2,1)} %all_gather.6.a_ref.b_ref.v_ref, bf16[4096,128]{1,0:T(8,128)(2,1)} %r_ref.1, f32[1,4096]{1,0:T(1,128)} %bitcast.42, bf16[4096,256]{1,0:T(8,128)(2,1)} %f_ref.1), custom_call_target="tpu_custom_call" | custom-call | flops 3242196992 | bytes 4464640 | tf_op jit(solution)/shard_map/pallas_call | solution.py:74
  86.8 1.9 %copy.26 = f32[4,256,384]{1,2,0:T(8,128)S(1)} copy(f32[4,256,384]{2,1,0:T(8,128)} %bitcast.37) | data formatting | bytes 3145728 | tf_op jit(solution)/shard_map/reshape | solution.py:111
  88.7 22.5 %all_to_all.25 = f32[4,256,384]{1,2,0:T(8,128)S(1)} all-to-all(f32[4,256,384]{1,2,0:T(8,128)S(1)} %copy.26), channel_id=1, replica_groups=mesh['veh'=8,'req'=4] {'req'}, dimensions={0} | all-to-all | bytes 3145728 | tf_op jit(solution)/shard_map/all_to_all | solution.py:112
  111.3 0.1 fusion
  111.4 0.8 copy.29
  (10 shorter events, 0.2 us)
Async XLA Ops:
  9.6 22.9 %copy-start = (f32[4096]{0:T(1024)S(1)}, f32[4096]{0:T(1024)}, u32[]{:S(2)}) copy-start(f32[4096]{0:T(1024)} %param.9) | copy-start | bytes 49156
  34.6 15.0 %copy-start.1 = (f32[1024]{0:T(1024)S(1)}, f32[1024]{0:T(1024)}, u32[]{:S(2)}) copy-start(f32[1024]{0:T(1024)} %param.8) | copy-start | bytes 12292

commit v4 on v3

--- a/solution.py
+++ b/solution.py
@@ -5,6 +5,7 @@
 import jax.numpy as jnp
 from jax import lax
 from jax.experimental import pallas as pl
+from jax.experimental.pallas import tpu as pltpu
 from jax.sharding import PartitionSpec as P
 
 
@@ -51,7 +52,7 @@
     )(a, shift.reshape(rows, 1), b)[0]
 
 
-def assign_kernel(v_ref, r_ref, d_ref, f_ref, out_ref, *, scale):
+def assign_kernel(rot_ref, v_ref, r_ref, d_ref, f_ref, out_ref, *, scale):
     scores = lax.dot_general(
         v_ref[...], r_ref[...], (((1,), (1,)), ((), ())), preferred_element_type=jnp.float32
     )
@@ -60,38 +61,51 @@
     powers = jnp.exp(logits - top)
     mass = jnp.sum(powers, axis=1, keepdims=True)
     feat = f_ref.shape[1]
-    out_ref[:, :feat] = jnp.dot(
+    block_feat = jnp.dot(
         powers.astype(jnp.bfloat16), f_ref[...], preferred_element_type=jnp.float32
     )
+    out_ref[:feat, :] = block_feat.T
     lane = lax.broadcasted_iota(jnp.int32, (top.shape[0], 128), 1)
-    out_ref[:, feat:] = jnp.where(lane == 0, mass, jnp.where(lane == 1, top, 0.0))
+    extra = jnp.where(lane == 0, mass, jnp.where(lane == 1, top, 0.0))
+    out_ref[feat:, :] = extra.T[:8, :]
 
 
-def assign_rows(v, r, d, f, scale, tile):
+def assign_rows(v, r, d, f, scale, tile, rotation):
     rows, width = v.shape
     cols, feat = f.shape
     tile = min(tile, rows)
+    tiles = rows // tile
+    grid_spec = pltpu.PrefetchScalarGridSpec(
+        num_scalar_prefetch=1,
+        grid=(tiles,),
+        in_specs=[
+            pl.BlockSpec((tile, width), lambda i, rot: ((i + rot[0]) % tiles, 0)),
+            pl.BlockSpec((cols, width), lambda i, rot: (0, 0)),
+            pl.BlockSpec((1, cols), lambda i, rot: (0, 0)),
+            pl.BlockSpec((cols, feat), lambda i, rot: (0, 0)),
+        ],
+        out_specs=pl.BlockSpec((feat + 8, tile), lambda i, rot: (0, i)),
+    )
     return pl.pallas_call(
         functools.partial(assign_kernel, scale=scale),
-        out_shape=jax.ShapeDtypeStruct((rows, feat + 128), jnp.float32),
-        grid=(rows // tile,),
-        in_specs=[
-            pl.BlockSpec((tile, width), lambda i: (i, 0)),
-            pl.BlockSpec((cols, width), lambda i: (0, 0)),
-            pl.BlockSpec((1, cols), lambda i: (0, 0)),
-            pl.BlockSpec((cols, feat), lambda i: (0, 0)),
-        ],
-        out_specs=pl.BlockSpec((tile, feat + 128), lambda i: (i, 0)),
+        out_shape=jax.ShapeDtypeStruct((feat + 8, rows), jnp.float32),
+        grid_spec=grid_spec,
         cost_estimate=pl.CostEstimate(
             flops=2 * rows * cols * (width + feat) + 5 * rows * cols,
             transcendentals=rows * cols,
-            bytes_accessed=2 * (rows + cols) * width + 2 * cols * feat + 4 * rows * (feat + 2),
+            bytes_accessed=2 * (rows + cols) * width + 2 * cols * feat + 4 * rows * (feat + 8),
         ),
-    )(v, r, d.reshape(1, cols), f)
+    )(rotation, v, r, d.reshape(1, cols), f)
 
 
 def local(vehicle_emb, request_emb, request_feat, log_supply, log_demand):
-    own_rows = lax.all_gather(vehicle_emb, "req", axis=0, tiled=True)
+    placed = lax.dynamic_update_slice_in_dim(
+        jnp.zeros((lax.axis_size("req") * vehicle_emb.shape[0], vehicle_emb.shape[1]), vehicle_emb.dtype),
+        vehicle_emb,
+        lax.axis_index("req") * vehicle_emb.shape[0],
+        axis=0,
+    )
+    own_rows = lax.psum(placed, "req")
     row_count = own_rows.shape[0]
     scale = 3.0 / math.sqrt(own_rows.shape[1])
 
@@ -105,17 +119,29 @@
     supply_pot = log_supply - merge_lse(parts)
     demand_second = column_pot(supply_pot)
 
-    packed = assign_rows(own_rows, request_emb, demand_second, request_feat, scale, 128)
     owners = lax.axis_size("req")
+    chunk = row_count // owners
+    tile = min(128, chunk)
+    me = lax.axis_index("req")
+    rotation = jnp.reshape(me * (chunk // tile), (1,)).astype(jnp.int32)
+    packed = assign_rows(own_rows, request_emb, demand_second, request_feat, scale, tile, rotation)
     feat = request_feat.shape[1]
-    packed = packed.reshape(owners, row_count // owners, feat + 128)
-    arrived = lax.all_to_all(packed, "req", 0, 0, tiled=True)
-    peaks = arrived[:, :, feat + 1]
-    masses = arrived[:, :, feat]
+    pieces = [packed[:, :chunk]]
+    for step in range(1, owners):
+        pieces.append(
+            lax.ppermute(
+                packed[:, step * chunk : (step + 1) * chunk],
+                "req",
+                [(i, (i + step) % owners) for i in range(owners)],
+            )
+        )
+    arrived = jnp.stack(pieces)
+    peaks = arrived[:, feat + 1, :]
+    masses = arrived[:, feat, :]
     factor = jnp.exp(peaks - jnp.max(peaks, axis=0, keepdims=True))
-    numerator = jnp.sum(arrived[:, :, :feat] * factor[:, :, None], axis=0)
+    numerator = jnp.sum(arrived[:, :feat, :] * factor[:, None, :], axis=0)
     denominator = jnp.sum(masses * factor, axis=0)
-    return numerator / denominator[:, None]
+    return (numerator / denominator[None, :]).T
 
 
 def solution(mesh):

time: 113 us -> 148 us (1.31)
  waiting for transfers between devices: 0 us -> 57 us
  blocking collectives: 59.9 us -> 18 us
  between operations: 0.1 us -> 13.5 us
  starting transfers between devices: 0 us -> 4.09 us
  local copies, waits for them, and re-layouts: 8.14 us -> 9.81 us
    psum x0 -> x1, waiting for transfers between devices: none -> 36.2 us  [local(): own_rows = lax.psum(placed, 'req')]
    all_to_all x1 -> x0, blocking collectives: 22.5 us -> none  [local(): arrived = lax.all_to_all(packed, 'req', 0, 0, tiled=True)]
    ppermute x0 -> x3, waiting for transfers between devices: none -> 13.1 us  [local(): lax.ppermute(packed[:, step * chunk:(step + 1) * chunk], 'req', [(i, (i +...]
    all_to_all x2 -> x1, blocking collectives: 23.2 us -> 12.6 us  [gather_by_exchange(): return lax.all_to_all(spread, axis, 0, 0, tiled=True)]
    all_gather x1 -> x0, blocking collectives: 8.81 us -> none  [local(): own_rows = lax.all_gather(vehicle_emb, 'req', axis=0, tiled=True)]
    all_to_all x0 -> x1, waiting for transfers between devices: none -> 7.67 us  [gather_by_exchange(): return lax.all_to_all(spread, axis, 0, 0, tiled=True)]
    all_to_all x0 -> x1, starting transfers between devices: none -> 3.37 us  [gather_by_exchange(): return lax.all_to_all(spread, axis, 0, 0, tiled=True)]
    reshape x1 -> x0, local copies, waits for them, and re-layouts: 1.87 us -> none  [local(): packed = packed.reshape(owners, row_count // owners, feat + 128)]
  transfers between devices with their start and end apart: 0 -> 5, of which waited for: 0 -> 5; matrix products, arithmetic and copies ran while one was open for 0% -> 0% of each run, Pallas kernels for 0% -> 0%
where the time goes in v4:
time: 148 us; the launch traced here: 147 us
  waiting for transfers between devices  57 us (39%)
  Pallas kernels  43.5 us (29%)
  blocking collectives  18 us (12%)
  between operations  13.5 us (9%)
  local copies, waits for them, and re-layouts  9.81 us (7%)
  starting transfers between devices  4.09 us (3%)
    psum x1, waiting for transfers between devices, local(): own_rows = lax.psum(placed, 'req')  36.2 us
    pallas_call x3, Pallas kernels, lse_over_rows(): pl.pallas_call(functools.partial(lse_kernel, scale=scale), out_shape=jax....  27.2 us
    pallas_call x1, Pallas kernels, assign_rows(): pl.pallas_call(functools.partial(assign_kernel, scale=scale), out_shape=j...  16.3 us
    ppermute x3, waiting for transfers between devices, local(): lax.ppermute(packed[:, step * chunk:(step + 1) * chunk], 'req', [(i, (i +...  13.1 us
    all_to_all x1, blocking collectives, gather_by_exchange(): return lax.all_to_all(spread, axis, 0, 0, tiled=True)  12.6 us
    all_to_all x1, waiting for transfers between devices, gather_by_exchange(): return lax.all_to_all(spread, axis, 0, 0, tiled=True)  7.67 us
    all_gather x1, blocking collectives, local(): parts = lax.all_gather(partial, 'req', axis=0, tiled=False)  5.3 us
    reshape x3, local copies, waits for them, and re-layouts, lse_over_rows(): shift.reshape(rows, 1)  3.85 us
  transfers between devices with their start and end apart: 5, of which 5 were waited for; matrix products, arithmetic and copies ran while one was open for 0% of the time, Pallas kernels for 0%

profile of v4, /device:TPU:0, one launch (start us, length us, event | category | flops | bytes accessed | tf_op | source)
XLA Modules:
  0.0 147.3 jit_solution(17037176244321539478)
XLA Ops:
  6.6 0.9 constant_dynamic-update-slice_fusion
  7.4 0.7 copy-done
  8.2 36.2 %all-reduce.2.cloned.1.call-done.a_ref.b_ref.v_ref = bf16[1024,128]{1,0:T(8,128)(2,1)} async-done(((bf16[1024,128]{1,0:T(8,128)(2,1)}), bf16[1024,128]{1,0:T(8,128)(2,1)}) %all-reduce.2.cloned.1.call-update) | async-done | bytes 262160 | tf_op jit(solution)/shard_map/psum | solution.py:108
  44.4 0.8 reshape.38.shift_ref
  45.2 8.8 %shard_map.55 = f32[1,4096]{1,0:T(1,128)} custom-call(bf16[1024,128]{1,0:T(8,128)(2,1)} %all-reduce.2.cloned.1.call-done.a_ref.b_ref.v_ref, f32[1024,1]{1,0:T(8,128)} %reshape.38.shift_ref, bf16[4096,128]{1,0:T(8,128)(2,1)} %r_ref.1), custom_call_target="tpu_custom_call" | custom-call | flops 1094713344 | bytes 1331200 | tf_op jit(solution)/shard_map/pallas_call | solution.py:37
  54.0 0.8 broadcast_in_dim.7
  54.8 12.6 %all_to_all.18 = f32[8,1,4096]{2,1,0:T(1,128)S(1)} all-to-all(f32[8,1,4096]{2,1,0:T(1,128)S(1)} %broadcast_in_dim.7), channel_id=1, replica_groups=mesh['veh'=8,'req'=4] {'veh'}, dimensions={0} | all-to-all | bytes 262144 | tf_op jit(solution)/shard_map/all_to_all | solution.py:15
  67.6 0.1 fusion.4
  67.7 2.0 %copy.19.shift_ref = f32[4096,1]{1,0:T(8,128)} copy(f32[4096,1]{0,1:T(1,128)S(1)} %bitcast.50) | data formatting | bytes 32768 | tf_op jit(solution)/shard_map/reshape | solution.py:52
  69.7 9.6 %shard_map.56 = f32[1,1024]{1,0:T(1,128)} custom-call(bf16[4096,128]{1,0:T(8,128)(2,1)} %r_ref.1, f32[4096,1]{1,0:T(8,128)} %copy.19.shift_ref, bf16[1024,128]{1,0:T(8,128)(2,1)} %all-reduce.2.cloned.1.call-done.a_ref.b_ref.v_ref), custom_call_target="tpu_custom_call" | custom-call | flops 1094713344 | bytes 1331200 | tf_op jit(solution)/shard_map/pallas_call | solution.py:37
  79.3 5.3 %all-gather = f32[4,1,1024]{2,1,0:T(1,128)S(1)} all-gather(f32[1,1,1024]{2,1,0:T(1,128)} %bitcast.55), channel_id=1, replica_groups=mesh['veh'=8,'req'=4] {'req'}, dimensions={0}, use_global_device_ids=true | all-gather | bytes 20480 | tf_op jit(solution)/shard_map/all_gather | solution.py:118
  84.7 1.0 copy.20.shift_ref
  85.7 8.8 %shard_map.57 = f32[1,4096]{1,0:T(1,128)} custom-call(bf16[1024,128]{1,0:T(8,128)(2,1)} %all-reduce.2.cloned.1.call-done.a_ref.b_ref.v_ref, f32[1024,1]{1,0:T(8,128)} %copy.20.shift_ref, bf16[4096,128]{1,0:T(8,128)(2,1)} %r_ref.1), custom_call_target="tpu_custom_call" | custom-call | flops 1094713344 | bytes 1331200 | tf_op jit(solution)/shard_map/pallas_call | solution.py:37
  94.5 1.4 broadcast_in_dim.8
  96.0 3.4 %all-to-all-start.1 = ((f32[8,1,4096]{2,1,0:T(1,128)}), f32[8,1,4096]{2,1,0:T(1,128)S(1)}, u32[]{:S(2)}, u32[]{:S(2)}) async-start(f32[8,1,4096]{2,1,0:T(1,128)} %broadcast_in_dim.8), calls=%async_computation.1 | async-start | bytes 262144 | tf_op jit(solution)/shard_map/all_to_all | solution.py:15
  99.3 7.7 %all-to-all-done.1 = f32[8,1,4096]{2,1,0:T(1,128)S(1)} async-done(((f32[8,1,4096]{2,1,0:T(1,128)}), f32[8,1,4096]{2,1,0:T(1,128)S(1)}, u32[]{:S(2)}, u32[]{:S(2)}) %all-to-all-start.1) | async-done | bytes 131104 | tf_op jit(solution)/shard_map/all_to_all | solution.py:15
  107.2 0.6 add_subtract_fusion
  107.9 16.3 %shard_map.58 = f32[264,1024]{1,0:T(8,128)} custom-call(s32[1]{0:T(128)} %bitcast.rot_ref, bf16[1024,128]{1,0:T(8,128)(2,1)} %all-reduce.2.cloned.1.call-done.a_ref.b_ref.v_ref, bf16[4096,128]{1,0:T(8,128)(2,1)} %r_ref.1, f32[1,4096]{1,0:T(1,128)} %bitcast.54, bf16[4096,256]{1,0:T(8,128)(2,1)} %f_ref.1), custom_call_target="tpu_custom_call" | custom-call | flops 3242196992 | bytes 4489216 | tf_op jit(solution)/shard_map/pallas_call | solution.py:89
  124.2 1.3 slice_bitcast_fusion
  125.6 0.7 collective-permute-start.1
  126.2 6.2 %collective-permute-done.2 = f32[264,256]{1,0:T(8,128)S(1)} collective-permute-done((f32[264,256]{1,0:T(8,128)S(1)}, f32[264,256]{1,0:T(8,128)S(1)}, u32[]{:S(2)}, u32[]{:S(2)}) %collective-permute-start.2) | collective-permute-done | bytes 270368 | tf_op jit(solution)/shard_map/ppermute | solution.py:132
  132.4 6.0 %collective-permute-done.1 = f32[264,256]{1,0:T(8,128)S(1)} collective-permute-done((f32[264,256]{1,0:T(8,128)S(1)}, f32[264,256]{1,0:T(8,128)S(1)}, u32[]{:S(2)}, u32[]{:S(2)}) %collective-permute-start.1) | collective-permute-done | bytes 270368 | tf_op jit(solution)/shard_map/ppermute | solution.py:132
  138.4 0.9 collective-permute-done
  139.6 0.8 copy.23
  (23 shorter events, 0.8 us)
Async XLA Ops:
  6.5 37.9 %all-reduce.2.cloned.1.call-start = ((), (), s32[]{:S(2)}) async-start(), calls=%async_computation.2 | async-start | bytes 524288 | tf_op jit(solution)/shard_map/psum | solution.py:108
  7.4 0.7 copy-start
  45.2 22.5 %copy-start.1 = (f32[4096]{0:T(1024)S(1)}, f32[4096]{0:T(1024)}, u32[]{:S(2)}) copy-start(f32[4096]{0:T(1024)} %param.9) | copy-start | bytes 49156
  69.7 15.0 %copy-start.2 = (f32[1024]{0:T(1024)S(1)}, f32[1024]{0:T(1024)}, u32[]{:S(2)}) copy-start(f32[1024]{0:T(1024)} %param.8) | copy-start | bytes 12292
  96.0 11.1 %all-to-all-start.1 = ((f32[8,1,4096]{2,1,0:T(1,128)}), f32[8,1,4096]{2,1,0:T(1,128)S(1)}, u32[]{:S(2)}, u32[]{:S(2)}) async-start(f32[8,1,4096]{2,1,0:T(1,128)} %broadcast_in_dim.8), calls=%async_computation.1 | async-start | bytes 262144 | tf_op jit(solution)/shard_map/all_to_all | solution.py:15
  125.5 6.9 %collective-permute-start.2 = (f32[264,256]{1,0:T(8,128)S(1)}, f32[264,256]{1,0:T(8,128)S(1)}, u32[]{:S(2)}, u32[]{:S(2)}) collective-permute-start(f32[264,256]{1,0:T(8,128)S(1)} %get-tuple-element.9), channel_id=1, source_target_pairs={{0,3},{1,0},{2,1},{3,2},{4,7},{5,4},{6,5},{7,6},{8,11},{9,8},{10,9... | collective-permute-start | bytes 811016 | tf_op jit(solution)/shard_map/ppermute | solution.py:132
  125.6 12.9 %collective-permute-start.1 = (f32[264,256]{1,0:T(8,128)S(1)}, f32[264,256]{1,0:T(8,128)S(1)}, u32[]{:S(2)}, u32[]{:S(2)}) collective-permute-start(f32[264,256]{1,0:T(8,128)S(1)} %get-tuple-element.10), channel_id=1, source_target_pairs={{0,2},{1,3},{2,0},{3,1},{4,6},{5,7},{6,4},{7,5},{8,10},{9,11},{10,... | collective-permute-start | bytes 811016 | tf_op jit(solution)/shard_map/ppermute | solution.py:132
  126.2 13.1 %collective-permute-start = (f32[264,256]{1,0:T(8,128)S(1)}, f32[264,256]{1,0:T(8,128)S(1)}, u32[]{:S(2)}, u32[]{:S(2)}) collective-permute-start(f32[264,256]{1,0:T(8,128)S(1)} %get-tuple-element.11), channel_id=1, source_target_pairs={{0,1},{1,2},{2,3},{3,0},{4,5},{5,6},{6,7},{7,4},{8,9},{9,10},{10,1... | collective-permute-start | bytes 811016 | tf_op jit(solution)/shard_map/ppermute | solution.py:132
Sparse Core Ops, SparseCore 0:
  9.7 34.6 all-reduce.1

commit v5 on v4

--- a/solution.py
+++ b/solution.py
@@ -99,13 +99,7 @@
 
 
 def local(vehicle_emb, request_emb, request_feat, log_supply, log_demand):
-    placed = lax.dynamic_update_slice_in_dim(
-        jnp.zeros((lax.axis_size("req") * vehicle_emb.shape[0], vehicle_emb.shape[1]), vehicle_emb.dtype),
-        vehicle_emb,
-        lax.axis_index("req") * vehicle_emb.shape[0],
-        axis=0,
-    )
-    own_rows = lax.psum(placed, "req")
+    own_rows = lax.all_gather(vehicle_emb, "req", axis=0, tiled=True)
     row_count = own_rows.shape[0]
     scale = 3.0 / math.sqrt(own_rows.shape[1])
 

time: 148 us -> 105 us (0.71)
  waiting for transfers between devices: 57 us -> 19.5 us
  between operations: 13.5 us -> 0.13 us
  blocking collectives: 18 us -> 27.2 us
  local copies, waits for them, and re-layouts: 9.81 us -> 8.22 us
    psum x1 -> x0, waiting for transfers between devices: 36.2 us -> none  [local(): own_rows = lax.psum(placed, 'req')]
    all_gather x0 -> x1, blocking collectives: none -> 8.81 us  [local(): own_rows = lax.all_gather(vehicle_emb, 'req', axis=0, tiled=True)]
  transfers between devices with their start and end apart: 5 -> 4, of which waited for: 5 -> 4; matrix products, arithmetic and copies ran while one was open for 0% -> 0% of each run, Pallas kernels for 0% -> 0%
where the time goes in v5:
time: 105 us; the launch traced here: 104 us
  Pallas kernels  43.5 us (41%)
  blocking collectives  27.2 us (26%)
  waiting for transfers between devices  19.5 us (19%)
  local copies, waits for them, and re-layouts  8.22 us (8%)
  starting transfers between devices  4.5 us (4%)
  other arithmetic  1.35 us (1%)
    pallas_call x3, Pallas kernels, lse_over_rows(): pl.pallas_call(functools.partial(lse_kernel, scale=scale), out_shape=jax....  27.2 us
    pallas_call x1, Pallas kernels, assign_rows(): pl.pallas_call(functools.partial(assign_kernel, scale=scale), out_shape=j...  16.3 us
    all_to_all x1, blocking collectives, gather_by_exchange(): return lax.all_to_all(spread, axis, 0, 0, tiled=True)  13.1 us
    ppermute x3, waiting for transfers between devices, local(): lax.ppermute(packed[:, step * chunk:(step + 1) * chunk], 'req', [(i, (i +...  11.9 us
    all_gather x1, blocking collectives, local(): own_rows = lax.all_gather(vehicle_emb, 'req', axis=0, tiled=True)  8.81 us
    all_to_all x1, waiting for transfers between devices, gather_by_exchange(): return lax.all_to_all(spread, axis, 0, 0, tiled=True)  7.66 us
    all_gather x1, blocking collectives, local(): parts = lax.all_gather(partial, 'req', axis=0, tiled=False)  5.3 us
    reshape x3, local copies, waits for them, and re-layouts, lse_over_rows(): shift.reshape(rows, 1)  3.85 us
  transfers between devices with their start and end apart: 4, of which 4 were waited for; matrix products, arithmetic and copies ran while one was open for 0% of the time, Pallas kernels for 0%

profile of v5, /device:TPU:0, one launch (start us, length us, event | category | flops | bytes accessed | tf_op | source)
XLA Modules:
  0.0 104.5 jit_solution(3556502557328070937)
XLA Ops:
  0.0 8.8 %all_gather.6.a_ref.b_ref.v_ref = bf16[1024,128]{1,0:T(8,128)(2,1)} all-gather(bf16[256,128]{1,0:T(8,128)(2,1)} %param.5), channel_id=1, replica_groups=mesh['veh'=8,'req'=4] {'req'}, dimensions={0}, use_global_device_ids=true | all-gather | bytes 327680 | tf_op jit(solution)/shard_map/all_gather | solution.py:102
  8.8 0.8 reshape.38.shift_ref
  9.6 8.8 %shard_map.55 = f32[1,4096]{1,0:T(1,128)} custom-call(bf16[1024,128]{1,0:T(8,128)(2,1)} %all_gather.6.a_ref.b_ref.v_ref, f32[1024,1]{1,0:T(8,128)} %reshape.38.shift_ref, bf16[4096,128]{1,0:T(8,128)(2,1)} %r_ref.1), custom_call_target="tpu_custom_call" | custom-call | flops 1094713344 | bytes 1331200 | tf_op jit(solution)/shard_map/pallas_call | solution.py:37
  18.4 0.8 broadcast_in_dim.4
  19.2 13.1 %all_to_all.18 = f32[8,1,4096]{2,1,0:T(1,128)S(1)} all-to-all(f32[8,1,4096]{2,1,0:T(1,128)S(1)} %broadcast_in_dim.4), channel_id=1, replica_groups=mesh['veh'=8,'req'=4] {'veh'}, dimensions={0} | all-to-all | bytes 262144 | tf_op jit(solution)/shard_map/all_to_all | solution.py:15
  32.4 0.1 fusion.4
  32.6 2.0 %copy.19.shift_ref = f32[4096,1]{1,0:T(8,128)} copy(f32[4096,1]{0,1:T(1,128)S(1)} %bitcast.50) | data formatting | bytes 32768 | tf_op jit(solution)/shard_map/reshape | solution.py:52
  34.6 9.6 %shard_map.56 = f32[1,1024]{1,0:T(1,128)} custom-call(bf16[4096,128]{1,0:T(8,128)(2,1)} %r_ref.1, f32[4096,1]{1,0:T(8,128)} %copy.19.shift_ref, bf16[1024,128]{1,0:T(8,128)(2,1)} %all_gather.6.a_ref.b_ref.v_ref), custom_call_target="tpu_custom_call" | custom-call | flops 1094713344 | bytes 1331200 | tf_op jit(solution)/shard_map/pallas_call | solution.py:37
  44.2 5.3 %all-gather = f32[4,1,1024]{2,1,0:T(1,128)S(1)} all-gather(f32[1,1,1024]{2,1,0:T(1,128)} %bitcast.55), channel_id=1, replica_groups=mesh['veh'=8,'req'=4] {'req'}, dimensions={0}, use_global_device_ids=true | all-gather | bytes 20480 | tf_op jit(solution)/shard_map/all_gather | solution.py:112
  49.6 1.0 copy.20.shift_ref
  50.6 8.8 %shard_map.57 = f32[1,4096]{1,0:T(1,128)} custom-call(bf16[1024,128]{1,0:T(8,128)(2,1)} %all_gather.6.a_ref.b_ref.v_ref, f32[1024,1]{1,0:T(8,128)} %copy.20.shift_ref, bf16[4096,128]{1,0:T(8,128)(2,1)} %r_ref.1), custom_call_target="tpu_custom_call" | custom-call | flops 1094713344 | bytes 1331200 | tf_op jit(solution)/shard_map/pallas_call | solution.py:37
  59.4 1.4 %broadcast_in_dim.5 = f32[8,1,4096]{2,1,0:T(1,128)} broadcast(f32[4096]{0:T(1024)} %bitcast.53), dimensions={2} | broadcast | bytes 147456 | tf_op jit(solution)/shard_map/broadcast_in_dim | solution.py:14
  60.8 3.4 %all-to-all-start.1 = ((f32[8,1,4096]{2,1,0:T(1,128)}), f32[8,1,4096]{2,1,0:T(1,128)S(1)}, u32[]{:S(2)}, u32[]{:S(2)}) async-start(f32[8,1,4096]{2,1,0:T(1,128)} %broadcast_in_dim.5), calls=%async_computation.1 | async-start | bytes 262144 | tf_op jit(solution)/shard_map/all_to_all | solution.py:15
  64.2 7.7 %all-to-all-done.1 = f32[8,1,4096]{2,1,0:T(1,128)S(1)} async-done(((f32[8,1,4096]{2,1,0:T(1,128)}), f32[8,1,4096]{2,1,0:T(1,128)S(1)}, u32[]{:S(2)}, u32[]{:S(2)}) %all-to-all-start.1) | async-done | bytes 131104 | tf_op jit(solution)/shard_map/all_to_all | solution.py:15
  72.0 0.1 fusion.2
  72.1 0.6 add_subtract_fusion
  72.7 16.3 %shard_map.58 = f32[264,1024]{1,0:T(8,128)} custom-call(s32[1]{0:T(128)} %bitcast.rot_ref, bf16[1024,128]{1,0:T(8,128)(2,1)} %all_gather.6.a_ref.b_ref.v_ref, bf16[4096,128]{1,0:T(8,128)(2,1)} %r_ref.1, f32[1,4096]{1,0:T(1,128)} %bitcast.54, bf16[4096,256]{1,0:T(8,128)(2,1)} %f_ref.1), custom_call_target="tpu_custom_call" | custom-call | flops 3242196992 | bytes 4489216 | tf_op jit(solution)/shard_map/pallas_call | solution.py:89
  89.1 1.3 %slice_bitcast_fusion = (f32[1,264,256]{2,1,0:T(8,128)S(1)}, f32[264,256]{1,0:T(8,128)S(1)}, f32[264,256]{1,0:T(8,128)S(1)}, f32[264,256]{1,0:T(8,128)S(1)}) fusion(f32[264,1024]{1,0:T(8,128)} %shard_map.58), kind=kLoop, calls=%fused_computation.3 | loop fusion | bytes 2162688 | tf_op jit(solution)/shard_map/stack | solution.py:132
  90.4 0.5 collective-permute-start
  90.9 0.6 collective-permute-start.1
  91.5 5.7 %collective-permute-done.2 = f32[264,256]{1,0:T(8,128)S(1)} collective-permute-done((f32[264,256]{1,0:T(8,128)S(1)}, f32[264,256]{1,0:T(8,128)S(1)}, u32[]{:S(2)}, u32[]{:S(2)}) %collective-permute-start.2) | collective-permute-done | bytes 270368 | tf_op jit(solution)/shard_map/ppermute | solution.py:126
  97.2 2.0 %collective-permute-done = f32[264,256]{1,0:T(8,128)S(1)} collective-permute-done((f32[264,256]{1,0:T(8,128)S(1)}, f32[264,256]{1,0:T(8,128)S(1)}, u32[]{:S(2)}, u32[]{:S(2)}) %collective-permute-start) | collective-permute-done | bytes 270368 | tf_op jit(solution)/shard_map/ppermute | solution.py:126
  99.2 4.1 %collective-permute-done.1 = f32[264,256]{1,0:T(8,128)S(1)} collective-permute-done((f32[264,256]{1,0:T(8,128)S(1)}, f32[264,256]{1,0:T(8,128)S(1)}, u32[]{:S(2)}, u32[]{:S(2)}) %collective-permute-start.1) | collective-permute-done | bytes 270368 | tf_op jit(solution)/shard_map/ppermute | solution.py:126
  103.6 0.8 copy.23
  (17 shorter events, 0.6 us)
Async XLA Ops:
  9.6 22.9 %copy-start = (f32[4096]{0:T(1024)S(1)}, f32[4096]{0:T(1024)}, u32[]{:S(2)}) copy-start(f32[4096]{0:T(1024)} %param.9) | copy-start | bytes 49156
  34.6 15.0 %copy-start.1 = (f32[1024]{0:T(1024)S(1)}, f32[1024]{0:T(1024)}, u32[]{:S(2)}) copy-start(f32[1024]{0:T(1024)} %param.8) | copy-start | bytes 12292
  60.8 11.0 %all-to-all-start.1 = ((f32[8,1,4096]{2,1,0:T(1,128)}), f32[8,1,4096]{2,1,0:T(1,128)S(1)}, u32[]{:S(2)}, u32[]{:S(2)}) async-start(f32[8,1,4096]{2,1,0:T(1,128)} %broadcast_in_dim.5), calls=%async_computation.1 | async-start | bytes 262144 | tf_op jit(solution)/shard_map/all_to_all | solution.py:15
  90.4 6.9 %collective-permute-start.2 = (f32[264,256]{1,0:T(8,128)S(1)}, f32[264,256]{1,0:T(8,128)S(1)}, u32[]{:S(2)}, u32[]{:S(2)}) collective-permute-start(f32[264,256]{1,0:T(8,128)S(1)} %get-tuple-element.9), channel_id=1, source_target_pairs={{0,3},{1,0},{2,1},{3,2},{4,7},{5,4},{6,5},{7,6},{8,11},{9,8},{10,9... | collective-permute-start | bytes 811016 | tf_op jit(solution)/shard_map/ppermute | solution.py:126
  90.4 8.8 %collective-permute-start = (f32[264,256]{1,0:T(8,128)S(1)}, f32[264,256]{1,0:T(8,128)S(1)}, u32[]{:S(2)}, u32[]{:S(2)}) collective-permute-start(f32[264,256]{1,0:T(8,128)S(1)} %get-tuple-element.11), channel_id=1, source_target_pairs={{0,1},{1,2},{2,3},{3,0},{4,5},{5,6},{6,7},{7,4},{8,9},{9,10},{10,1... | collective-permute-start | bytes 811016 | tf_op jit(solution)/shard_map/ppermute | solution.py:126
  90.9 12.4 %collective-permute-start.1 = (f32[264,256]{1,0:T(8,128)S(1)}, f32[264,256]{1,0:T(8,128)S(1)}, u32[]{:S(2)}, u32[]{:S(2)}) collective-permute-start(f32[264,256]{1,0:T(8,128)S(1)} %get-tuple-element.10), channel_id=1, source_target_pairs={{0,2},{1,3},{2,0},{3,1},{4,6},{5,7},{6,4},{7,5},{8,10},{9,11},{10,... | collective-permute-start | bytes 811016 | tf_op jit(solution)/shard_map/ppermute | solution.py:126

commit v6 on v5

--- a/solution.py
+++ b/solution.py
@@ -104,18 +104,18 @@
     scale = 3.0 / math.sqrt(own_rows.shape[1])
 
     def column_pot(shift):
-        partial = lse_over_rows(own_rows, shift, request_emb, scale, 512)
+        partial = lse_over_rows(own_rows, shift, request_emb, scale, 2048)
         return log_demand - merge_lse(gather_by_exchange(partial, "veh"))
 
     demand_first = column_pot(jnp.zeros((row_count,), jnp.float32))
-    partial = lse_over_rows(request_emb, demand_first, own_rows, scale, 256)
+    partial = lse_over_rows(request_emb, demand_first, own_rows, scale, 1024)
     parts = lax.all_gather(partial, "req", axis=0, tiled=False)
     supply_pot = log_supply - merge_lse(parts)
     demand_second = column_pot(supply_pot)
 
     owners = lax.axis_size("req")
     chunk = row_count // owners
-    tile = min(128, chunk)
+    tile = min(256, chunk)
     me = lax.axis_index("req")
     rotation = jnp.reshape(me * (chunk // tile), (1,)).astype(jnp.int32)
     packed = assign_rows(own_rows, request_emb, demand_second, request_feat, scale, tile, rotation)

time: 105 us -> 99.8 us (0.950)
  Pallas kernels: 43.5 us -> 38 us
    pallas_call x3, Pallas kernels: 27.2 us -> 22.9 us  [lse_over_rows(): pl.pallas_call(functools.partial(lse_kernel, scale=scale), out_shape=jax....]
    pallas_call x1, Pallas kernels: 16.3 us -> 15 us  [assign_rows(): pl.pallas_call(functools.partial(assign_kernel, scale=scale), out_shape=j...]
where the time goes in v6:
time: 99.8 us; the launch traced here: 99.1 us
  Pallas kernels  38 us (38%)
  blocking collectives  27.4 us (27%)
  waiting for transfers between devices  19.5 us (20%)
  local copies, waits for them, and re-layouts  8.22 us (8%)
  starting transfers between devices  4.5 us (5%)
  other arithmetic  1.35 us (1%)
    pallas_call x3, Pallas kernels, lse_over_rows(): pl.pallas_call(functools.partial(lse_kernel, scale=scale), out_shape=jax....  22.9 us
    pallas_call x1, Pallas kernels, assign_rows(): pl.pallas_call(functools.partial(assign_kernel, scale=scale), out_shape=j...  15 us
    all_to_all x1, blocking collectives, gather_by_exchange(): return lax.all_to_all(spread, axis, 0, 0, tiled=True)  13.1 us
    ppermute x3, waiting for transfers between devices, local(): lax.ppermute(packed[:, step * chunk:(step + 1) * chunk], 'req', [(i, (i +...  11.9 us
    all_gather x1, blocking collectives, local(): own_rows = lax.all_gather(vehicle_emb, 'req', axis=0, tiled=True)  8.81 us
    all_to_all x1, waiting for transfers between devices, gather_by_exchange(): return lax.all_to_all(spread, axis, 0, 0, tiled=True)  7.67 us
    all_gather x1, blocking collectives, local(): parts = lax.all_gather(partial, 'req', axis=0, tiled=False)  5.49 us
    reshape x3, local copies, waits for them, and re-layouts, lse_over_rows(): shift.reshape(rows, 1)  3.85 us
  transfers between devices with their start and end apart: 4, of which 4 were waited for; matrix products, arithmetic and copies ran while one was open for 0% of the time, Pallas kernels for 0%

profile of v6, /device:TPU:0, one launch (start us, length us, event | category | flops | bytes accessed | tf_op | source)
XLA Modules:
  0.0 99.1 jit_solution(6225632290053403083)
XLA Ops:
  0.0 8.8 %all_gather.6.a_ref.b_ref.v_ref = bf16[1024,128]{1,0:T(8,128)(2,1)} all-gather(bf16[256,128]{1,0:T(8,128)(2,1)} %param.5), channel_id=1, replica_groups=mesh['veh'=8,'req'=4] {'req'}, dimensions={0}, use_global_device_ids=true | all-gather | bytes 327680 | tf_op jit(solution)/shard_map/all_gather | solution.py:102
  8.8 0.8 reshape.38.shift_ref
  9.6 7.4 %shard_map.55 = f32[1,4096]{1,0:T(1,128)} custom-call(bf16[1024,128]{1,0:T(8,128)(2,1)} %all_gather.6.a_ref.b_ref.v_ref, f32[1024,1]{1,0:T(8,128)} %reshape.38.shift_ref, bf16[4096,128]{1,0:T(8,128)(2,1)} %r_ref.1), custom_call_target="tpu_custom_call" | custom-call | flops 1094713344 | bytes 1331200 | tf_op jit(solution)/shard_map/pallas_call | solution.py:37
  17.0 0.8 broadcast_in_dim.4
  17.8 13.1 %all_to_all.18 = f32[8,1,4096]{2,1,0:T(1,128)S(1)} all-to-all(f32[8,1,4096]{2,1,0:T(1,128)S(1)} %broadcast_in_dim.4), channel_id=1, replica_groups=mesh['veh'=8,'req'=4] {'veh'}, dimensions={0} | all-to-all | bytes 262144 | tf_op jit(solution)/shard_map/all_to_all | solution.py:15
  31.0 0.1 fusion.4
  31.1 2.0 %copy.19.shift_ref = f32[4096,1]{1,0:T(8,128)} copy(f32[4096,1]{0,1:T(1,128)S(1)} %bitcast.50) | data formatting | bytes 32768 | tf_op jit(solution)/shard_map/reshape | solution.py:52
  33.2 8.2 %shard_map.56 = f32[1,1024]{1,0:T(1,128)} custom-call(bf16[4096,128]{1,0:T(8,128)(2,1)} %r_ref.1, f32[4096,1]{1,0:T(8,128)} %copy.19.shift_ref, bf16[1024,128]{1,0:T(8,128)(2,1)} %all_gather.6.a_ref.b_ref.v_ref), custom_call_target="tpu_custom_call" | custom-call | flops 1094713344 | bytes 1331200 | tf_op jit(solution)/shard_map/pallas_call | solution.py:37
  41.4 5.5 %all-gather = f32[4,1,1024]{2,1,0:T(1,128)S(1)} all-gather(f32[1,1,1024]{2,1,0:T(1,128)} %bitcast.55), channel_id=1, replica_groups=mesh['veh'=8,'req'=4] {'req'}, dimensions={0}, use_global_device_ids=true | all-gather | bytes 20480 | tf_op jit(solution)/shard_map/all_gather | solution.py:112
  46.9 1.0 %copy.20.shift_ref = f32[1024,1]{1,0:T(8,128)} copy(f32[1024,1]{0,1:T(1,128)S(1)} %bitcast.51) | data formatting | bytes 8192 | tf_op jit(solution)/shard_map/reshape | solution.py:52
  48.0 7.4 %shard_map.57 = f32[1,4096]{1,0:T(1,128)} custom-call(bf16[1024,128]{1,0:T(8,128)(2,1)} %all_gather.6.a_ref.b_ref.v_ref, f32[1024,1]{1,0:T(8,128)} %copy.20.shift_ref, bf16[4096,128]{1,0:T(8,128)(2,1)} %r_ref.1), custom_call_target="tpu_custom_call" | custom-call | flops 1094713344 | bytes 1331200 | tf_op jit(solution)/shard_map/pallas_call | solution.py:37
  55.3 1.4 %broadcast_in_dim.5 = f32[8,1,4096]{2,1,0:T(1,128)} broadcast(f32[4096]{0:T(1024)} %bitcast.53), dimensions={2} | broadcast | bytes 147456 | tf_op jit(solution)/shard_map/broadcast_in_dim | solution.py:14
  56.8 3.4 %all-to-all-start.1 = ((f32[8,1,4096]{2,1,0:T(1,128)}), f32[8,1,4096]{2,1,0:T(1,128)S(1)}, u32[]{:S(2)}, u32[]{:S(2)}) async-start(f32[8,1,4096]{2,1,0:T(1,128)} %broadcast_in_dim.5), calls=%async_computation.1 | async-start | bytes 262144 | tf_op jit(solution)/shard_map/all_to_all | solution.py:15
  60.1 7.7 %all-to-all-done.1 = f32[8,1,4096]{2,1,0:T(1,128)S(1)} async-done(((f32[8,1,4096]{2,1,0:T(1,128)}), f32[8,1,4096]{2,1,0:T(1,128)S(1)}, u32[]{:S(2)}, u32[]{:S(2)}) %all-to-all-start.1) | async-done | bytes 131104 | tf_op jit(solution)/shard_map/all_to_all | solution.py:15
  67.9 0.1 fusion.2
  68.0 0.6 add_subtract_fusion
  68.6 15.0 %shard_map.58 = f32[264,1024]{1,0:T(8,128)} custom-call(s32[1]{0:T(128)} %bitcast.rot_ref, bf16[1024,128]{1,0:T(8,128)(2,1)} %all_gather.6.a_ref.b_ref.v_ref, bf16[4096,128]{1,0:T(8,128)(2,1)} %r_ref.1, f32[1,4096]{1,0:T(1,128)} %bitcast.54, bf16[4096,256]{1,0:T(8,128)(2,1)} %f_ref.1), custom_call_target="tpu_custom_call" | custom-call | flops 3242196992 | bytes 4489216 | tf_op jit(solution)/shard_map/pallas_call | solution.py:89
  83.7 1.3 %slice_bitcast_fusion = (f32[1,264,256]{2,1,0:T(8,128)S(1)}, f32[264,256]{1,0:T(8,128)S(1)}, f32[264,256]{1,0:T(8,128)S(1)}, f32[264,256]{1,0:T(8,128)S(1)}) fusion(f32[264,1024]{1,0:T(8,128)} %shard_map.58), kind=kLoop, calls=%fused_computation.3 | loop fusion | bytes 2162688 | tf_op jit(solution)/shard_map/stack | solution.py:132
  85.0 0.5 collective-permute-start
  85.5 0.6 collective-permute-start.1
  86.1 5.7 %collective-permute-done.2 = f32[264,256]{1,0:T(8,128)S(1)} collective-permute-done((f32[264,256]{1,0:T(8,128)S(1)}, f32[264,256]{1,0:T(8,128)S(1)}, u32[]{:S(2)}, u32[]{:S(2)}) %collective-permute-start.2) | collective-permute-done | bytes 270368 | tf_op jit(solution)/shard_map/ppermute | solution.py:126
  91.8 2.0 %collective-permute-done = f32[264,256]{1,0:T(8,128)S(1)} collective-permute-done((f32[264,256]{1,0:T(8,128)S(1)}, f32[264,256]{1,0:T(8,128)S(1)}, u32[]{:S(2)}, u32[]{:S(2)}) %collective-permute-start) | collective-permute-done | bytes 270368 | tf_op jit(solution)/shard_map/ppermute | solution.py:126
  93.9 4.1 %collective-permute-done.1 = f32[264,256]{1,0:T(8,128)S(1)} collective-permute-done((f32[264,256]{1,0:T(8,128)S(1)}, f32[264,256]{1,0:T(8,128)S(1)}, u32[]{:S(2)}, u32[]{:S(2)}) %collective-permute-start.1) | collective-permute-done | bytes 270368 | tf_op jit(solution)/shard_map/ppermute | solution.py:126
  98.3 0.8 copy.23
  (17 shorter events, 0.6 us)
Async XLA Ops:
  9.6 21.5 %copy-start = (f32[4096]{0:T(1024)S(1)}, f32[4096]{0:T(1024)}, u32[]{:S(2)}) copy-start(f32[4096]{0:T(1024)} %param.9) | copy-start | bytes 49156
  33.2 13.8 %copy-start.1 = (f32[1024]{0:T(1024)S(1)}, f32[1024]{0:T(1024)}, u32[]{:S(2)}) copy-start(f32[1024]{0:T(1024)} %param.8) | copy-start | bytes 12292
  56.8 11.1 %all-to-all-start.1 = ((f32[8,1,4096]{2,1,0:T(1,128)}), f32[8,1,4096]{2,1,0:T(1,128)S(1)}, u32[]{:S(2)}, u32[]{:S(2)}) async-start(f32[8,1,4096]{2,1,0:T(1,128)} %broadcast_in_dim.5), calls=%async_computation.1 | async-start | bytes 262144 | tf_op jit(solution)/shard_map/all_to_all | solution.py:15
  85.0 6.8 %collective-permute-start.2 = (f32[264,256]{1,0:T(8,128)S(1)}, f32[264,256]{1,0:T(8,128)S(1)}, u32[]{:S(2)}, u32[]{:S(2)}) collective-permute-start(f32[264,256]{1,0:T(8,128)S(1)} %get-tuple-element.9), channel_id=1, source_target_pairs={{0,3},{1,0},{2,1},{3,2},{4,7},{5,4},{6,5},{7,6},{8,11},{9,8},{10,9... | collective-permute-start | bytes 811016 | tf_op jit(solution)/shard_map/ppermute | solution.py:126
  85.0 8.8 %collective-permute-start = (f32[264,256]{1,0:T(8,128)S(1)}, f32[264,256]{1,0:T(8,128)S(1)}, u32[]{:S(2)}, u32[]{:S(2)}) collective-permute-start(f32[264,256]{1,0:T(8,128)S(1)} %get-tuple-element.11), channel_id=1, source_target_pairs={{0,1},{1,2},{2,3},{3,0},{4,5},{5,6},{6,7},{7,4},{8,9},{9,10},{10,1... | collective-permute-start | bytes 811016 | tf_op jit(solution)/shard_map/ppermute | solution.py:126
  85.5 12.4 %collective-permute-start.1 = (f32[264,256]{1,0:T(8,128)S(1)}, f32[264,256]{1,0:T(8,128)S(1)}, u32[]{:S(2)}, u32[]{:S(2)}) collective-permute-start(f32[264,256]{1,0:T(8,128)S(1)} %get-tuple-element.10), channel_id=1, source_target_pairs={{0,2},{1,3},{2,0},{3,1},{4,6},{5,7},{6,4},{7,5},{8,10},{9,11},{10,... | collective-permute-start | bytes 811016 | tf_op jit(solution)/shard_map/ppermute | solution.py:126

commit v7 on v6

v7 whole, which is shorter than its diff:
```python
import functools
import math

import jax
import jax.numpy as jnp
from jax import lax
from jax.experimental import pallas as pl
from jax.experimental.pallas import tpu as pltpu
from jax.sharding import PartitionSpec as P


def merged_lse(parts):
    top = jnp.max(parts, axis=0, keepdims=True)
    return top + jnp.log(jnp.sum(jnp.exp(parts - top), axis=0, keepdims=True))


def lse_kernel(*refs, scale, shifted, copies):
    if shifted:
        a_ref, parts_ref, base_ref, b_ref, out_ref, column_ref = refs

        @pl.when(pl.program_id(0) == 0)
        def _():
            row = base_ref[...] - merged_lse(parts_ref[...])
            wide = jnp.broadcast_to(row, (128, row.shape[1]))
            column_ref[...] = jnp.transpose(wide)[:, :1]

    else:
        a_ref, b_ref, out_ref = refs
    scores = lax.dot_general(
        a_ref[...], b_ref[...], (((1,), (1,)), ((), ())), preferred_element_type=jnp.float32
    )
    logits = scores * scale
    if shifted:
        logits = logits + column_ref[...]
    top = jnp.max(logits, axis=0, keepdims=True)
    total = jnp.sum(jnp.exp(logits - top), axis=0, keepdims=True)
    result = top + jnp.log(total)
    out_ref[...] = jnp.broadcast_to(result, (copies, result.shape[1]))


def lse_over_rows(a, b, scale, tile, copies, parts=None, base=None):
    rows, width = a.shape
    cols = b.shape[0]
    tile = min(tile, cols)
    shifted = parts is not None
    in_specs = [pl.BlockSpec((rows, width), lambda j: (0, 0))]
    operands = [a]
    scratch = []
    if shifted:
        in_specs += [
            pl.BlockSpec(parts.shape, lambda j: (0, 0)),
            pl.BlockSpec((1, rows), lambda j: (0, 0)),
        ]
        operands += [parts, base.reshape(1, rows)]
        scratch = [pltpu.VMEM((rows, 1), jnp.float32)]
    in_specs.append(pl.BlockSpec((tile, width), lambda j: (j, 0)))
    operands.append(b)
    return pl.pallas_call(
        functools.partial(lse_kernel, scale=scale, shifted=shifted, copies=copies),
        out_shape=jax.ShapeDtypeStruct((copies, cols), jnp.float32),
        grid=(cols // tile,),
        in_specs=in_specs,
        out_specs=pl.BlockSpec((copies, tile), lambda j: (0, j)),
        scratch_shapes=scratch,
        cost_estimate=pl.CostEstimate(
            flops=2 * rows * cols * width + 5 * rows * cols,
            transcendentals=rows * cols,
            bytes_accessed=2 * (rows + cols) * width + 4 * (rows + copies * cols),
        ),
    )(*operands)


def assign_kernel(rot_ref, v_ref, r_ref, parts_ref, base_ref, f_ref, out_ref, *, scale):
    demand = base_ref[...] - merged_lse(parts_ref[...])
    scores = lax.dot_general(
        v_ref[...], r_ref[...], (((1,), (1,)), ((), ())), preferred_element_type=jnp.float32
    )
    logits = scores * scale + demand
    top = jnp.max(logits, axis=1, keepdims=True)
    powers = jnp.exp(logits - top)
    mass = jnp.sum(powers, axis=1, keepdims=True)
    feat = f_ref.shape[1]
    block_feat = jnp.dot(
        powers.astype(jnp.bfloat16), f_ref[...], preferred_element_type=jnp.float32
    )
    out_ref[:feat, :] = block_feat.T
    lane = lax.broadcasted_iota(jnp.int32, (top.shape[0], 128), 1)
    extra = jnp.where(lane == 0, mass, jnp.where(lane == 1, top, 0.0))
    out_ref[feat:, :] = extra.T[:8, :]


def assign_rows(v, r, parts, base, f, scale, tile, owners, rotation):
    rows, width = v.shape
    cols, feat = f.shape
    chunk = rows // owners
    tiles = rows // tile
    per_chunk = chunk // tile
    grid_spec = pltpu.PrefetchScalarGridSpec(
        num_scalar_prefetch=1,
        grid=(tiles,),
        in_specs=[
            pl.BlockSpec((tile, width), lambda i, rot: ((i + rot[0]) % tiles, 0)),
            pl.BlockSpec((cols, width), lambda i, rot: (0, 0)),
            pl.BlockSpec(parts.shape, lambda i, rot: (0, 0)),
            pl.BlockSpec((1, cols), lambda i, rot: (0, 0)),
            pl.BlockSpec((cols, feat), lambda i, rot: (0, 0)),
        ],
        out_specs=pl.BlockSpec(
            (None, feat + 8, tile), lambda i, rot: (i // per_chunk, 0, i % per_chunk)
        ),
    )
    return pl.pallas_call(
        functools.partial(assign_kernel, scale=scale),
        out_shape=jax.ShapeDtypeStruct((owners, feat + 8, chunk), jnp.float32),
        grid_spec=grid_spec,
        cost_estimate=pl.CostEstimate(
            flops=2 * rows * cols * (width + feat) + 5 * rows * cols,
            transcendentals=rows * cols,
            bytes_accessed=2 * (rows + cols) * width + 2 * cols * feat + 4 * rows * (feat + 8),
        ),
    )(rotation, v, r, parts, base.reshape(1, cols), f)


def local(vehicle_emb, request_emb, request_feat, log_supply, log_demand):
    own_rows = lax.all_gather(vehicle_emb, "req", axis=0, tiled=True)
    row_count = own_rows.shape[0]
    scale = 3.0 / math.sqrt(own_rows.shape[1])
    spread = lax.axis_size("veh")

    def exchange(block):
        return lax.all_to_all(block, "veh", 0, 0, tiled=True)

    first = exchange(lse_over_rows(own_rows, request_emb, scale, 2048, spread))
    partial = lse_over_rows(request_emb, own_rows, scale, 1024, 1, first, log_demand)
    row_parts = lax.all_gather(partial[0], "req", axis=0, tiled=False)
    second = exchange(
        lse_over_rows(own_rows, request_emb, scale, 2048, spread, row_parts, log_supply)
    )

    owners = lax.axis_size("req")
    chunk = row_count // owners
    tile = min(256, chunk)
    me = lax.axis_index("req")
    rotation = jnp.reshape(me * (chunk // tile), (1,)).astype(jnp.int32)
    packed = assign_rows(
        own_rows, request_emb, second, log_demand, request_feat, scale, tile, owners, rotation
    )
    feat = request_feat.shape[1]
    pieces = [packed[0]]
    for step in range(1, owners):
        pieces.append(
            lax.ppermute(packed[step], "req", [(i, (i + step) % owners) for i in range(owners)])
        )
    arrived = jnp.stack(pieces)
    peaks = arrived[:, feat + 1, :]
    masses = arrived[:, feat, :]
    factor = jnp.exp(peaks - jnp.max(peaks, axis=0, keepdims=True))
    numerator = jnp.sum(arrived[:, :feat, :] * factor[:, None, :], axis=0)
    denominator = jnp.sum(masses * factor, axis=0)
    return (numerator / denominator[None, :]).T


def solution(mesh):
    in_specs = (P(("veh", "req"), None), P("req", None), P("req", None), P("veh"), P("req"))
    out_specs = P(("veh", "req"), None)
    return jax.shard_map(local, mesh=mesh, in_specs=in_specs, out_specs=out_specs, check_vma=False)
```

time: 99.8 us -> 97.1 us (0.973)
  local copies, waits for them, and re-layouts: 8.22 us -> 6.91 us
  waiting for transfers between devices: 19.5 us -> 20.6 us
  other arithmetic: 1.35 us -> 0.25 us
    reshape x3 -> x0, local copies, waits for them, and re-layouts: 3.85 us -> none  [lse_over_rows(): shift.reshape(rows, 1)]
    all_to_all x0 -> x2, local copies, waits for them, and re-layouts: none -> 2.71 us  [exchange(): return lax.all_to_all(block, 'veh', 0, 0, tiled=True)]
    broadcast_in_dim x2 -> x0, local copies, waits for them, and re-layouts: 2.22 us -> none  [gather_by_exchange(): spread = jnp.broadcast_to(x[None], (count,) + x.shape)]
    unnamed x4 -> x3, local copies, waits for them, and re-layouts: 0.01 us -> 2.07 us
    another operation x1 -> x0, local copies, waits for them, and re-layouts: 1.3 us -> none  [local(): arrived = jnp.stack(pieces)]
    slice x0 -> x1, local copies, waits for them, and re-layouts: none -> 1.29 us  [local(): pieces = [packed[0]]]
    ppermute x3, waiting for transfers between devices: 11.9 us -> 13 us  [local(): lax.ppermute(packed[step], 'req', [(i, (i + step) % owners) for i in rang...]
where the time goes in v7:
time: 97.1 us; the launch traced here: 96.6 us
  Pallas kernels  37.1 us (38%)
  blocking collectives  27.5 us (28%)
  waiting for transfers between devices  20.6 us (21%)
  local copies, waits for them, and re-layouts  6.91 us (7%)
  starting transfers between devices  4.23 us (4%)
    pallas_call x3, Pallas kernels, lse_over_rows(): pl.pallas_call(functools.partial(lse_kernel, scale=scale, shifted=shifted...  22 us
    pallas_call x1, Pallas kernels, assign_rows(): pl.pallas_call(functools.partial(assign_kernel, scale=scale), out_shape=j...  15 us
    all_to_all x1, blocking collectives, exchange(): return lax.all_to_all(block, 'veh', 0, 0, tiled=True)  13.1 us
    ppermute x3, waiting for transfers between devices, local(): lax.ppermute(packed[step], 'req', [(i, (i + step) % owners) for i in rang...  13 us
    all_gather x1, blocking collectives, local(): own_rows = lax.all_gather(vehicle_emb, 'req', axis=0, tiled=True)  8.82 us
    all_to_all x1, waiting for transfers between devices, exchange(): return lax.all_to_all(block, 'veh', 0, 0, tiled=True)  7.67 us
    all_gather x1, blocking collectives, local(): row_parts = lax.all_gather(partial[0], 'req', axis=0, tiled=False)  5.54 us
    all_to_all x1, starting transfers between devices, exchange(): return lax.all_to_all(block, 'veh', 0, 0, tiled=True)  3.37 us
  transfers between devices with their start and end apart: 4, of which 4 were waited for; matrix products, arithmetic and copies ran while one was open for 0% of the time, Pallas kernels for 0%

profile of v7, /device:TPU:0, one launch (start us, length us, event | category | flops | bytes accessed | tf_op | source)
XLA Modules:
  0.0 96.6 jit_solution(367374739540195428)
XLA Ops:
  0.0 8.8 %all_gather.6.refs_0_.refs_3_.v_ref = bf16[1024,128]{1,0:T(8,128)(2,1)} all-gather(bf16[256,128]{1,0:T(8,128)(2,1)} %param.5), channel_id=1, replica_groups=mesh['veh'=8,'req'=4] {'req'}, dimensions={0}, use_global_device_ids=true | all-gather | bytes 327680 | tf_op jit(solution)/shard_map/all_gather | solution.py:125
  8.8 7.1 %shard_map.55 = f32[8,4096]{1,0:T(8,128)} custom-call(bf16[1024,128]{1,0:T(8,128)(2,1)} %all_gather.6.refs_0_.refs_3_.v_ref, bf16[4096,128]{1,0:T(8,128)(2,1)} %r_ref.1), custom_call_target="tpu_custom_call" | custom-call | flops 1094713344 | bytes 1445888 | tf_op jit(solution)/shard_map/pallas_call | solution.py:58
  15.9 1.0 %copy.7 = f32[8,1,4096]{2,1,0:T(1,128)S(1)} copy(f32[8,1,4096]{2,0,1:T(8,128)} %bitcast.47) | data formatting | bytes 262144 | tf_op jit(solution)/shard_map/all_to_all | solution.py:131
  16.9 13.1 %all_to_all.22 = f32[8,1,4096]{2,1,0:T(1,128)S(1)} all-to-all(f32[8,1,4096]{2,1,0:T(1,128)S(1)} %copy.7), channel_id=1, replica_groups=mesh['veh'=8,'req'=4] {'veh'}, dimensions={0} | all-to-all | bytes 262144 | tf_op jit(solution)/shard_map/all_to_all | solution.py:131
  30.0 0.7 copy.24
  30.8 7.7 %shard_map.56 = f32[1,1024]{1,0:T(1,128)} custom-call(bf16[4096,128]{1,0:T(8,128)(2,1)} %r_ref.1, f32[8,4096]{1,0:T(8,128)} %bitcast.45, f32[1,4096]{1,0:T(1,128)} %bitcast.50, bf16[1024,128]{1,0:T(8,128)(2,1)} %all_gather.6.refs_0_.refs_3_.v_ref), custom_call_target="tpu_custom_call" | custom-call | flops 1094713344 | bytes 1331200 | tf_op jit(solution)/shard_map/pallas_call | solution.py:58
  38.5 5.5 %all-gather = f32[4,1,1024]{2,1,0:T(1,128)S(1)} all-gather(f32[1,1,1024]{2,1,0:T(1,128)} %bitcast.49), channel_id=1, replica_groups=mesh['veh'=8,'req'=4] {'req'}, dimensions={0}, use_global_device_ids=true | all-gather | bytes 20480 | tf_op jit(solution)/shard_map/all_gather | solution.py:135
  44.0 0.6 copy.25
  44.6 7.3 %shard_map.57 = f32[8,4096]{1,0:T(8,128)} custom-call(bf16[1024,128]{1,0:T(8,128)(2,1)} %all_gather.6.refs_0_.refs_3_.v_ref, f32[4,1024]{1,0:T(4,128)} %bitcast.48, f32[1,1024]{1,0:T(1,128)} %bitcast.52, bf16[4096,128]{1,0:T(8,128)(2,1)} %r_ref.1), custom_call_target="tpu_custom_call" | custom-call | flops 1094713344 | bytes 1445888 | tf_op jit(solution)/shard_map/pallas_call | solution.py:58
  51.9 1.7 %copy.8 = f32[8,1,4096]{2,1,0:T(1,128)} copy(f32[8,1,4096]{2,0,1:T(8,128)} %bitcast.46) | data formatting | bytes 262144 | tf_op jit(solution)/shard_map/all_to_all | solution.py:131
  53.6 3.4 %all-to-all-start.1 = ((f32[8,1,4096]{2,1,0:T(1,128)}), f32[8,1,4096]{2,1,0:T(1,128)S(1)}, u32[]{:S(2)}, u32[]{:S(2)}) async-start(f32[8,1,4096]{2,1,0:T(1,128)} %copy.8), calls=%async_computation.1 | async-start | bytes 262144 | tf_op jit(solution)/shard_map/all_to_all | solution.py:131
  56.9 7.7 %all-to-all-done.1 = f32[8,1,4096]{2,1,0:T(1,128)S(1)} async-done(((f32[8,1,4096]{2,1,0:T(1,128)}), f32[8,1,4096]{2,1,0:T(1,128)S(1)}, u32[]{:S(2)}, u32[]{:S(2)}) %all-to-all-start.1) | async-done | bytes 131104 | tf_op jit(solution)/shard_map/all_to_all | solution.py:131
  64.6 0.7 copy.23
  65.3 15.0 %shard_map.58 = f32[4,264,256]{2,1,0:T(8,128)} custom-call(s32[1]{0:T(128)} %bitcast.rot_ref, bf16[1024,128]{1,0:T(8,128)(2,1)} %all_gather.6.refs_0_.refs_3_.v_ref, bf16[4096,128]{1,0:T(8,128)(2,1)} %r_ref.1, f32[8,4096]{1,0:T(8,128)} %bitcast.44, f32[1,4096]{1,0:T(1,128)} %bitcast.51, bf16[4096,256]{1,0:T(8,128)(2,1)} %f_ref.1), custom_call_target="tpu_custom_call" | custom-call | flops 3242196992 | bytes 4489216 | tf_op jit(solution)/shard_map/pallas_call | solution.py:112
  80.4 1.3 %fusion.4 = (f32[1,264,256]{2,1,0:T(8,128)S(1)}, f32[264,256]{1,0:T(8,128)S(1)}, f32[264,256]{1,0:T(8,128)S(1)}, f32[264,256]{1,0:T(8,128)S(1)}) fusion(f32[4,264,256]{2,1,0:T(8,128)} %shard_map.58), kind=kLoop, calls=%fused_computation.18 | loop fusion | bytes 2162688 | tf_op jit(solution)/shard_map/slice | solution.py:149
  81.7 0.1 collective-permute-start.2
  81.7 0.6 collective-permute-start.1
  82.4 0.1 collective-permute-start
  82.5 5.9 %collective-permute-done.2 = f32[264,256]{1,0:T(8,128)S(1)} collective-permute-done((f32[264,256]{1,0:T(8,128)S(1)}, f32[264,256]{1,0:T(8,128)S(1)}, u32[]{:S(2)}, u32[]{:S(2)}) %collective-permute-start.2) | collective-permute-done | bytes 270368 | tf_op jit(solution)/shard_map/ppermute | solution.py:152
  88.5 6.1 %collective-permute-done.1 = f32[264,256]{1,0:T(8,128)S(1)} collective-permute-done((f32[264,256]{1,0:T(8,128)S(1)}, f32[264,256]{1,0:T(8,128)S(1)}, u32[]{:S(2)}, u32[]{:S(2)}) %collective-permute-start.1) | collective-permute-done | bytes 270368 | tf_op jit(solution)/shard_map/ppermute | solution.py:152
  94.6 0.9 collective-permute-done
  95.5 0.1 pad_maximum_fusion
  95.7 0.1 fusion
  95.8 0.8 copy.10
  (4 shorter events, 0.1 us)
Async XLA Ops:
  53.6 11.0 %all-to-all-start.1 = ((f32[8,1,4096]{2,1,0:T(1,128)}), f32[8,1,4096]{2,1,0:T(1,128)S(1)}, u32[]{:S(2)}, u32[]{:S(2)}) async-start(f32[8,1,4096]{2,1,0:T(1,128)} %copy.8), calls=%async_computation.1 | async-start | bytes 262144 | tf_op jit(solution)/shard_map/all_to_all | solution.py:131
  81.7 6.8 %collective-permute-start.2 = (f32[264,256]{1,0:T(8,128)S(1)}, f32[264,256]{1,0:T(8,128)S(1)}, u32[]{:S(2)}, u32[]{:S(2)}) collective-permute-start(f32[264,256]{1,0:T(8,128)S(1)} %get-tuple-element.9), channel_id=1, source_target_pairs={{0,3},{1,0},{2,1},{3,2},{4,7},{5,4},{6,5},{7,6},{8,11},{9,8},{10,9... | collective-permute-start | bytes 811016 | tf_op jit(solution)/shard_map/ppermute | solution.py:152
  81.7 12.9 %collective-permute-start.1 = (f32[264,256]{1,0:T(8,128)S(1)}, f32[264,256]{1,0:T(8,128)S(1)}, u32[]{:S(2)}, u32[]{:S(2)}) collective-permute-start(f32[264,256]{1,0:T(8,128)S(1)} %get-tuple-element.10), channel_id=1, source_target_pairs={{0,2},{1,3},{2,0},{3,1},{4,6},{5,7},{6,4},{7,5},{8,10},{9,11},{10,... | collective-permute-start | bytes 811016 | tf_op jit(solution)/shard_map/ppermute | solution.py:152
  82.4 13.1 %collective-permute-start = (f32[264,256]{1,0:T(8,128)S(1)}, f32[264,256]{1,0:T(8,128)S(1)}, u32[]{:S(2)}, u32[]{:S(2)}) collective-permute-start(f32[264,256]{1,0:T(8,128)S(1)} %get-tuple-element.11), channel_id=1, source_target_pairs={{0,1},{1,2},{2,3},{3,0},{4,5},{5,6},{6,7},{7,4},{8,9},{9,10},{10,1... | collective-permute-start | bytes 811016 | tf_op jit(solution)/shard_map/ppermute | solution.py:152

commit v8 on v7

--- a/solution.py
+++ b/solution.py
@@ -10,8 +10,8 @@
 
 
 def merged_lse(parts):
-    top = jnp.max(parts, axis=0, keepdims=True)
-    return top + jnp.log(jnp.sum(jnp.exp(parts - top), axis=0, keepdims=True))
+    top = jnp.max(parts, axis=0)
+    return top + jnp.log(jnp.sum(jnp.exp(parts - top[None]), axis=0))
 
 
 def lse_kernel(*refs, scale, shifted, copies):
@@ -35,7 +35,7 @@
     top = jnp.max(logits, axis=0, keepdims=True)
     total = jnp.sum(jnp.exp(logits - top), axis=0, keepdims=True)
     result = top + jnp.log(total)
-    out_ref[...] = jnp.broadcast_to(result, (copies, result.shape[1]))
+    out_ref[...] = jnp.broadcast_to(result[None], (copies,) + result.shape)
 
 
 def lse_over_rows(a, b, scale, tile, copies, parts=None, base=None):
@@ -48,7 +48,7 @@
     scratch = []
     if shifted:
         in_specs += [
-            pl.BlockSpec(parts.shape, lambda j: (0, 0)),
+            pl.BlockSpec(parts.shape, lambda j: (0, 0, 0)),
             pl.BlockSpec((1, rows), lambda j: (0, 0)),
         ]
         operands += [parts, base.reshape(1, rows)]
@@ -57,10 +57,10 @@
     operands.append(b)
     return pl.pallas_call(
         functools.partial(lse_kernel, scale=scale, shifted=shifted, copies=copies),
-        out_shape=jax.ShapeDtypeStruct((copies, cols), jnp.float32),
+        out_shape=jax.ShapeDtypeStruct((copies, 1, cols), jnp.float32),
         grid=(cols // tile,),
         in_specs=in_specs,
-        out_specs=pl.BlockSpec((copies, tile), lambda j: (0, j)),
+        out_specs=pl.BlockSpec((copies, 1, tile), lambda j: (0, 0, j)),
         scratch_shapes=scratch,
         cost_estimate=pl.CostEstimate(
             flops=2 * rows * cols * width + 5 * rows * cols,
@@ -89,36 +89,31 @@
     out_ref[feat:, :] = extra.T[:8, :]
 
 
-def assign_rows(v, r, parts, base, f, scale, tile, owners, rotation):
+def assign_chunk(v, r, parts, base, f, scale, chunk, index):
     rows, width = v.shape
     cols, feat = f.shape
-    chunk = rows // owners
-    tiles = rows // tile
-    per_chunk = chunk // tile
     grid_spec = pltpu.PrefetchScalarGridSpec(
         num_scalar_prefetch=1,
-        grid=(tiles,),
+        grid=(1,),
         in_specs=[
-            pl.BlockSpec((tile, width), lambda i, rot: ((i + rot[0]) % tiles, 0)),
-            pl.BlockSpec((cols, width), lambda i, rot: (0, 0)),
-            pl.BlockSpec(parts.shape, lambda i, rot: (0, 0)),
-            pl.BlockSpec((1, cols), lambda i, rot: (0, 0)),
-            pl.BlockSpec((cols, feat), lambda i, rot: (0, 0)),
+            pl.BlockSpec((chunk, width), lambda i, at: (at[0], 0)),
+            pl.BlockSpec((cols, width), lambda i, at: (0, 0)),
+            pl.BlockSpec(parts.shape, lambda i, at: (0, 0, 0)),
+            pl.BlockSpec((1, cols), lambda i, at: (0, 0)),
+            pl.BlockSpec((cols, feat), lambda i, at: (0, 0)),
         ],
-        out_specs=pl.BlockSpec(
-            (None, feat + 8, tile), lambda i, rot: (i // per_chunk, 0, i % per_chunk)
-        ),
+        out_specs=pl.BlockSpec((feat + 8, chunk), lambda i, at: (0, 0)),
     )
     return pl.pallas_call(
         functools.partial(assign_kernel, scale=scale),
-        out_shape=jax.ShapeDtypeStruct((owners, feat + 8, chunk), jnp.float32),
+        out_shape=jax.ShapeDtypeStruct((feat + 8, chunk), jnp.float32),
         grid_spec=grid_spec,
         cost_estimate=pl.CostEstimate(
-            flops=2 * rows * cols * (width + feat) + 5 * rows * cols,
-            transcendentals=rows * cols,
-            bytes_accessed=2 * (rows + cols) * width + 2 * cols * feat + 4 * rows * (feat + 8),
+            flops=2 * chunk * cols * (width + feat) + 5 * chunk * cols,
+            transcendentals=chunk * cols,
+            bytes_accessed=2 * (chunk + cols) * width + 2 * cols * feat + 4 * chunk * (feat + 8),
         ),
-    )(rotation, v, r, parts, base.reshape(1, cols), f)
+    )(index, v, r, parts, base.reshape(1, cols), f)
 
 
 def local(vehicle_emb, request_emb, request_feat, log_supply, log_demand):
@@ -139,18 +134,17 @@
 
     owners = lax.axis_size("req")
     chunk = row_count // owners
-    tile = min(256, chunk)
     me = lax.axis_index("req")
-    rotation = jnp.reshape(me * (chunk // tile), (1,)).astype(jnp.int32)
-    packed = assign_rows(
-        own_rows, request_emb, second, log_demand, request_feat, scale, tile, owners, rotation
-    )
     feat = request_feat.shape[1]
-    pieces = [packed[0]]
-    for step in range(1, owners):
-        pieces.append(
-            lax.ppermute(packed[step], "req", [(i, (i + step) % owners) for i in range(owners)])
+    pieces = []
+    for step in list(range(1, owners)) + [0]:
+        index = jnp.reshape((me + step) % owners, (1,)).astype(jnp.int32)
+        piece = assign_chunk(
+            own_rows, request_emb, second, log_demand, request_feat, scale, chunk, index
         )
+        if step:
+            piece = lax.ppermute(piece, "req", [(i, (i + step) % owners) for i in range(owners)])
+        pieces.append(piece)
     arrived = jnp.stack(pieces)
     peaks = arrived[:, feat + 1, :]
     masses = arrived[:, feat, :]

time: 97.1 us -> 90.4 us (0.931)
  waiting for transfers between devices: 20.6 us -> 7.65 us
  Pallas kernels: 37.1 us -> 45.2 us
  local copies, waits for them, and re-layouts: 6.91 us -> 1.61 us
  starting transfers between devices: 4.23 us -> 6.1 us
    ppermute x3, waiting for transfers between devices: 13 us -> 0.01 us  [local(): lax.ppermute(piece, 'req', [(i, (i + step) % owners) for i in range(owner...]
    pallas_call x1 -> x4, Pallas kernels: 15 us -> 23 us  [assign_chunk(): pl.pallas_call(functools.partial(assign_kernel, scale=scale), out_shape=j...]
    all_to_all x2 -> x0, local copies, waits for them, and re-layouts: 2.71 us -> none  [exchange(): return lax.all_to_all(block, 'veh', 0, 0, tiled=True)]
    ppermute x3, starting transfers between devices: 0.86 us -> 2.73 us  [local(): lax.ppermute(piece, 'req', [(i, (i + step) % owners) for i in range(owner...]
    unnamed x3 -> x4, local copies, waits for them, and re-layouts: 2.07 us -> 0.77 us
    slice x1 -> x0, local copies, waits for them, and re-layouts: 1.29 us -> none  [local(): pieces = [packed[0]]]
  transfers between devices with their start and end apart: 4 -> 4, of which waited for: 4 -> 1; matrix products, arithmetic and copies ran while one was open for 0% -> 0% of each run, Pallas kernels for 0% -> 19%
where the time goes in v8:
time: 90.4 us; the launch traced here: 89.9 us
  Pallas kernels  45.2 us (50%)
  blocking collectives  28.2 us (31%)
  waiting for transfers between devices  7.65 us (8%)
  starting transfers between devices  6.1 us (7%)
  local copies, waits for them, and re-layouts  1.61 us (2%)
  other arithmetic  1.07 us (1%)
    pallas_call x4, Pallas kernels, assign_chunk(): pl.pallas_call(functools.partial(assign_kernel, scale=scale), out_shape=j...  23 us
    pallas_call x3, Pallas kernels, lse_over_rows(): pl.pallas_call(functools.partial(lse_kernel, scale=scale, shifted=shifted...  22.2 us
    all_to_all x1, blocking collectives, exchange(): return lax.all_to_all(block, 'veh', 0, 0, tiled=True)  13.4 us
    all_gather x1, blocking collectives, local(): own_rows = lax.all_gather(vehicle_emb, 'req', axis=0, tiled=True)  8.81 us
    all_to_all x1, waiting for transfers between devices, exchange(): return lax.all_to_all(block, 'veh', 0, 0, tiled=True)  7.64 us
    all_gather x1, blocking collectives, local(): row_parts = lax.all_gather(partial[0], 'req', axis=0, tiled=False)  5.98 us
    all_to_all x1, starting transfers between devices, exchange(): return lax.all_to_all(block, 'veh', 0, 0, tiled=True)  3.37 us
    ppermute x3, starting transfers between devices, local(): lax.ppermute(piece, 'req', [(i, (i + step) % owners) for i in range(owner...  2.73 us
  transfers between devices with their start and end apart: 4, of which 1 were waited for; matrix products, arithmetic and copies ran while one was open for 0% of the time, Pallas kernels for 19%

profile of v8, /device:TPU:0, one launch (start us, length us, event | category | flops | bytes accessed | tf_op | source)
XLA Modules:
  0.0 89.9 jit_solution(17042928225225460100)
XLA Ops:
  0.0 8.8 %all_gather.6.refs_0_.refs_3_.v_ref = bf16[1024,128]{1,0:T(8,128)(2,1)} all-gather(bf16[256,128]{1,0:T(8,128)(2,1)} %param.5), channel_id=1, replica_groups=mesh['veh'=8,'req'=4] {'req'}, dimensions={0}, use_global_device_ids=true | all-gather | bytes 327680 | tf_op jit(solution)/shard_map/all_gather | solution.py:120
  8.8 6.9 %shard_map.55 = f32[8,1,4096]{2,1,0:T(1,128)} custom-call(bf16[1024,128]{1,0:T(8,128)(2,1)} %all_gather.6.refs_0_.refs_3_.v_ref, bf16[4096,128]{1,0:T(8,128)(2,1)} %r_ref.7), custom_call_target="tpu_custom_call" | custom-call | flops 1094713344 | bytes 1445888 | tf_op jit(solution)/shard_map/pallas_call | solution.py:58
  15.7 13.4 %all_to_all.10.refs_1_ = f32[8,1,4096]{2,1,0:T(1,128)} all-to-all(f32[8,1,4096]{2,1,0:T(1,128)} %shard_map.55), channel_id=1, replica_groups=mesh['veh'=8,'req'=4] {'veh'}, dimensions={0} | all-to-all | bytes 262144 | tf_op jit(solution)/shard_map/all_to_all | solution.py:126
  29.1 7.7 %shard_map.56 = f32[1,1,1024]{2,1,0:T(1,128)} custom-call(bf16[4096,128]{1,0:T(8,128)(2,1)} %r_ref.7, f32[8,1,4096]{2,1,0:T(1,128)} %all_to_all.10.refs_1_, f32[1,4096]{1,0:T(1,128)} %bitcast.32, bf16[1024,128]{1,0:T(8,128)(2,1)} %all_gather.6.refs_0_.refs_3_.v_ref), custom_call_target="tpu_custom_call" | custom-call | flops 1094713344 | bytes 1331200 | tf_op jit(solution)/shard_map/pallas_call | solution.py:58
  36.8 6.0 %all_gather.7.refs_1_ = f32[4,1,1024]{2,1,0:T(1,128)} all-gather(f32[1,1,1024]{2,1,0:T(1,128)} %shard_map.56), channel_id=1, replica_groups=mesh['veh'=8,'req'=4] {'req'}, dimensions={0}, use_global_device_ids=true | all-gather | bytes 20480 | tf_op jit(solution)/shard_map/all_gather | solution.py:130
  42.8 7.6 %shard_map.57 = f32[8,1,4096]{2,1,0:T(1,128)} custom-call(bf16[1024,128]{1,0:T(8,128)(2,1)} %all_gather.6.refs_0_.refs_3_.v_ref, f32[4,1,1024]{2,1,0:T(1,128)} %all_gather.7.refs_1_, f32[1,1024]{1,0:T(1,128)} %bitcast.37, bf16[4096,128]{1,0:T(8,128)(2,1)} %r_ref.7), custom_call_target="tpu_custom_call" | custom-call | flops 1094713344 | bytes 1445888 | tf_op jit(solution)/shard_map/pallas_call | solution.py:58
  50.3 3.4 %all-to-all-start.1 = ((f32[8,1,4096]{2,1,0:T(1,128)}), f32[8,1,4096]{2,1,0:T(1,128)S(1)}, u32[]{:S(2)}, u32[]{:S(2)}) async-start(f32[8,1,4096]{2,1,0:T(1,128)} %shard_map.57), calls=%async_computation.1 | async-start | bytes 262144 | tf_op jit(solution)/shard_map/all_to_all | solution.py:126
  53.8 7.6 %all-to-all-done.1.parts_ref = f32[8,1,4096]{2,1,0:T(1,128)S(1)} async-done(((f32[8,1,4096]{2,1,0:T(1,128)}), f32[8,1,4096]{2,1,0:T(1,128)S(1)}, u32[]{:S(2)}, u32[]{:S(2)}) %all-to-all-start.1) | async-done | bytes 131104 | tf_op jit(solution)/shard_map/all_to_all | solution.py:126
  61.4 0.7 copy-done
  62.1 5.8 %shard_map.58 = f32[264,256]{1,0:T(8,128)} custom-call(s32[1]{0:T(128)} %bitcast.rot_ref, bf16[1024,128]{1,0:T(8,128)(2,1)} %all_gather.6.refs_0_.refs_3_.v_ref, bf16[4096,128]{1,0:T(8,128)(2,1)} %r_ref.7, f32[8,1,4096]{2,1,0:T(1,128)} %copy-done, f32[1,4096]{1,0:T(1,128)} %bitcast.33, bf16[4096,256]{1,0:T(8,128)(2,1)} %f_ref.7), custom_call_target="tpu_custom_call" | custom-call | flops 810549248 | bytes 3481600 | tf_op jit(solution)/shard_map/pallas_call | solution.py:107
  67.8 0.0 collective-permute-start
  67.8 5.8 %shard_map.59 = f32[264,256]{1,0:T(8,128)} custom-call(s32[1]{0:T(128)} %bitcast.4.rot_ref, bf16[1024,128]{1,0:T(8,128)(2,1)} %all_gather.6.refs_0_.refs_3_.v_ref, bf16[4096,128]{1,0:T(8,128)(2,1)} %r_ref.7, f32[8,1,4096]{2,1,0:T(1,128)} %copy-done, f32[1,4096]{1,0:T(1,128)} %bitcast.34, bf16[4096,256]{1,0:T(8,128)(2,1)} %f_ref.7), custom_call_target="tpu_custom_call" | custom-call | flops 810549248 | bytes 3481600 | tf_op jit(solution)/shard_map/pallas_call | solution.py:107
  73.6 1.3 %collective-permute-start.1 = (f32[264,256]{1,0:T(8,128)}, f32[264,256]{1,0:T(8,128)S(1)}, u32[]{:S(2)}, u32[]{:S(2)}) collective-permute-start(f32[264,256]{1,0:T(8,128)} %shard_map.59), channel_id=1, source_target_pairs={{0,2},{1,3},{2,0},{3,1},{4,6},{5,7},{6,4},{7,5},{8,10},{9,11},{10,... | collective-permute-start | bytes 811016 | tf_op jit(solution)/shard_map/ppermute | solution.py:146
  74.8 5.8 %shard_map.60 = f32[264,256]{1,0:T(8,128)} custom-call(s32[1]{0:T(128)} %bitcast.6.rot_ref, bf16[1024,128]{1,0:T(8,128)(2,1)} %all_gather.6.refs_0_.refs_3_.v_ref, bf16[4096,128]{1,0:T(8,128)(2,1)} %r_ref.7, f32[8,1,4096]{2,1,0:T(1,128)} %copy-done, f32[1,4096]{1,0:T(1,128)} %bitcast.35, bf16[4096,256]{1,0:T(8,128)(2,1)} %f_ref.7), custom_call_target="tpu_custom_call" | custom-call | flops 810549248 | bytes 3481600 | tf_op jit(solution)/shard_map/pallas_call | solution.py:107
  80.6 1.5 %collective-permute-start.2 = (f32[264,256]{1,0:T(8,128)}, f32[264,256]{1,0:T(8,128)S(1)}, u32[]{:S(2)}, u32[]{:S(2)}) collective-permute-start(f32[264,256]{1,0:T(8,128)} %shard_map.60), channel_id=1, source_target_pairs={{0,3},{1,0},{2,1},{3,2},{4,7},{5,4},{6,5},{7,6},{8,11},{9,8},{10,9... | collective-permute-start | bytes 811016 | tf_op jit(solution)/shard_map/ppermute | solution.py:146
  82.1 5.8 %shard_map.61 = f32[264,256]{1,0:T(8,128)} custom-call(s32[1]{0:T(128)} %bitcast.8.rot_ref, bf16[1024,128]{1,0:T(8,128)(2,1)} %all_gather.6.refs_0_.refs_3_.v_ref, bf16[4096,128]{1,0:T(8,128)(2,1)} %r_ref.7, f32[8,1,4096]{2,1,0:T(1,128)} %copy-done, f32[1,4096]{1,0:T(1,128)} %bitcast.36, bf16[4096,256]{1,0:T(8,128)(2,1)} %f_ref.7), custom_call_target="tpu_custom_call" | custom-call | flops 810549248 | bytes 3481600 | tf_op jit(solution)/shard_map/pallas_call | solution.py:107
  87.8 0.0 collective-permute-done
  87.8 0.0 collective-permute-done.1
  87.8 0.0 collective-permute-done.2
  87.8 0.8 fusion.3
  88.7 0.1 copy-done.1
  88.8 0.1 pad_maximum_fusion
  88.9 0.1 fusion
  89.1 0.8 copy.8
  (5 shorter events, 0.1 us)
Async XLA Ops:
  50.3 11.1 %all-to-all-start.1 = ((f32[8,1,4096]{2,1,0:T(1,128)}), f32[8,1,4096]{2,1,0:T(1,128)S(1)}, u32[]{:S(2)}, u32[]{:S(2)}) async-start(f32[8,1,4096]{2,1,0:T(1,128)} %shard_map.57), calls=%async_computation.1 | async-start | bytes 262144 | tf_op jit(solution)/shard_map/all_to_all | solution.py:126
  61.4 0.7 copy-start
  67.8 20.0 %collective-permute-start = (f32[264,256]{1,0:T(8,128)}, f32[264,256]{1,0:T(8,128)S(1)}, u32[]{:S(2)}, u32[]{:S(2)}) collective-permute-start(f32[264,256]{1,0:T(8,128)} %shard_map.58), channel_id=1, source_target_pairs={{0,1},{1,2},{2,3},{3,0},{4,5},{5,6},{6,7},{7,4},{8,9},{9,10},{10,1... | collective-permute-start | bytes 811016 | tf_op jit(solution)/shard_map/ppermute | solution.py:146
  73.6 14.3 %collective-permute-start.1 = (f32[264,256]{1,0:T(8,128)}, f32[264,256]{1,0:T(8,128)S(1)}, u32[]{:S(2)}, u32[]{:S(2)}) collective-permute-start(f32[264,256]{1,0:T(8,128)} %shard_map.59), channel_id=1, source_target_pairs={{0,2},{1,3},{2,0},{3,1},{4,6},{5,7},{6,4},{7,5},{8,10},{9,11},{10,... | collective-permute-start | bytes 811016 | tf_op jit(solution)/shard_map/ppermute | solution.py:146
  80.6 7.2 %collective-permute-start.2 = (f32[264,256]{1,0:T(8,128)}, f32[264,256]{1,0:T(8,128)S(1)}, u32[]{:S(2)}, u32[]{:S(2)}) collective-permute-start(f32[264,256]{1,0:T(8,128)} %shard_map.60), channel_id=1, source_target_pairs={{0,3},{1,0},{2,1},{3,2},{4,7},{5,4},{6,5},{7,6},{8,11},{9,8},{10,9... | collective-permute-start | bytes 811016 | tf_op jit(solution)/shard_map/ppermute | solution.py:146
  87.8 1.0 %copy-start.1 = (f32[264,256]{1,0:T(8,128)S(1)}, f32[264,256]{1,0:T(8,128)}, u32[]{:S(2)}) copy-start(f32[264,256]{1,0:T(8,128)} %shard_map.61) | copy-start | bytes 811012

commit v9 on v8

--- a/solution.py
+++ b/solution.py
@@ -70,7 +70,11 @@
     )(*operands)
 
 
-def assign_kernel(rot_ref, v_ref, r_ref, parts_ref, base_ref, f_ref, out_ref, *, scale):
+def assign_kernel(
+    rot_ref, v_ref, r_ref, parts_ref, base_ref, f_hbm, out_ref, f_ref, sem, *, scale
+):
+    fetch = pltpu.make_async_copy(f_hbm, f_ref, sem)
+    fetch.start()
     demand = base_ref[...] - merged_lse(parts_ref[...])
     scores = lax.dot_general(
         v_ref[...], r_ref[...], (((1,), (1,)), ((), ())), preferred_element_type=jnp.float32
@@ -80,6 +84,7 @@
     powers = jnp.exp(logits - top)
     mass = jnp.sum(powers, axis=1, keepdims=True)
     feat = f_ref.shape[1]
+    fetch.wait()
     block_feat = jnp.dot(
         powers.astype(jnp.bfloat16), f_ref[...], preferred_element_type=jnp.float32
     )
@@ -100,9 +105,10 @@
             pl.BlockSpec((cols, width), lambda i, at: (0, 0)),
             pl.BlockSpec(parts.shape, lambda i, at: (0, 0, 0)),
             pl.BlockSpec((1, cols), lambda i, at: (0, 0)),
-            pl.BlockSpec((cols, feat), lambda i, at: (0, 0)),
+            pl.BlockSpec(memory_space=pl.ANY),
         ],
         out_specs=pl.BlockSpec((feat + 8, chunk), lambda i, at: (0, 0)),
+        scratch_shapes=[pltpu.VMEM((cols, feat), f.dtype), pltpu.SemaphoreType.DMA(())],
     )
     return pl.pallas_call(
         functools.partial(assign_kernel, scale=scale),

time: 90.4 us -> 88.8 us (0.982)
  Pallas kernels: 45.2 us -> 43.1 us
    pallas_call x4, Pallas kernels: 23 us -> 21 us  [assign_chunk(): pl.pallas_call(functools.partial(assign_kernel, scale=scale), out_shape=j...]
  transfers between devices with their start and end apart: 4 -> 4, of which waited for: 1 -> 1; matrix products, arithmetic and copies ran while one was open for 0% -> 0% of each run, Pallas kernels for 19% -> 18%
where the time goes in v9:
time: 88.8 us; the launch traced here: 88.2 us
  Pallas kernels  43.1 us (49%)
  blocking collectives  28.2 us (32%)
  waiting for transfers between devices  7.65 us (9%)
  starting transfers between devices  6.48 us (7%)
  local copies, waits for them, and re-layouts  1.58 us (2%)
  other arithmetic  1.05 us (1%)
    pallas_call x3, Pallas kernels, lse_over_rows(): pl.pallas_call(functools.partial(lse_kernel, scale=scale, shifted=shifted...  22.2 us
    pallas_call x4, Pallas kernels, assign_chunk(): pl.pallas_call(functools.partial(assign_kernel, scale=scale), out_shape=j...  21 us
    all_to_all x1, blocking collectives, exchange(): return lax.all_to_all(block, 'veh', 0, 0, tiled=True)  13.4 us
    all_gather x1, blocking collectives, local(): own_rows = lax.all_gather(vehicle_emb, 'req', axis=0, tiled=True)  8.81 us
    all_to_all x1, waiting for transfers between devices, exchange(): return lax.all_to_all(block, 'veh', 0, 0, tiled=True)  7.64 us
    all_gather x1, blocking collectives, local(): row_parts = lax.all_gather(partial[0], 'req', axis=0, tiled=False)  5.98 us
    all_to_all x1, starting transfers between devices, exchange(): return lax.all_to_all(block, 'veh', 0, 0, tiled=True)  3.37 us
    ppermute x3, starting transfers between devices, local(): lax.ppermute(piece, 'req', [(i, (i + step) % owners) for i in range(owner...  3.11 us
  transfers between devices with their start and end apart: 4, of which 1 were waited for; matrix products, arithmetic and copies ran while one was open for 0% of the time, Pallas kernels for 18%

profile of v9, /device:TPU:0, one launch (start us, length us, event | category | flops | bytes accessed | tf_op | source)
XLA Modules:
  0.0 88.2 jit_solution(13321510924743207606)
XLA Ops:
  0.0 8.8 %all_gather.6.refs_0_.refs_3_.v_ref = bf16[1024,128]{1,0:T(8,128)(2,1)} all-gather(bf16[256,128]{1,0:T(8,128)(2,1)} %param.5), channel_id=1, replica_groups=mesh['veh'=8,'req'=4] {'req'}, dimensions={0}, use_global_device_ids=true | all-gather | bytes 327680 | tf_op jit(solution)/shard_map/all_gather | solution.py:126
  8.8 6.9 %shard_map.55 = f32[8,1,4096]{2,1,0:T(1,128)} custom-call(bf16[1024,128]{1,0:T(8,128)(2,1)} %all_gather.6.refs_0_.refs_3_.v_ref, bf16[4096,128]{1,0:T(8,128)(2,1)} %r_ref.7), custom_call_target="tpu_custom_call" | custom-call | flops 1094713344 | bytes 1445888 | tf_op jit(solution)/shard_map/pallas_call | solution.py:58
  15.7 13.4 %all_to_all.10.refs_1_ = f32[8,1,4096]{2,1,0:T(1,128)} all-to-all(f32[8,1,4096]{2,1,0:T(1,128)} %shard_map.55), channel_id=1, replica_groups=mesh['veh'=8,'req'=4] {'veh'}, dimensions={0} | all-to-all | bytes 262144 | tf_op jit(solution)/shard_map/all_to_all | solution.py:132
  29.1 7.7 %shard_map.56 = f32[1,1,1024]{2,1,0:T(1,128)} custom-call(bf16[4096,128]{1,0:T(8,128)(2,1)} %r_ref.7, f32[8,1,4096]{2,1,0:T(1,128)} %all_to_all.10.refs_1_, f32[1,4096]{1,0:T(1,128)} %bitcast.32, bf16[1024,128]{1,0:T(8,128)(2,1)} %all_gather.6.refs_0_.refs_3_.v_ref), custom_call_target="tpu_custom_call" | custom-call | flops 1094713344 | bytes 1331200 | tf_op jit(solution)/shard_map/pallas_call | solution.py:58
  36.8 6.0 %all_gather.7.refs_1_ = f32[4,1,1024]{2,1,0:T(1,128)} all-gather(f32[1,1,1024]{2,1,0:T(1,128)} %shard_map.56), channel_id=1, replica_groups=mesh['veh'=8,'req'=4] {'req'}, dimensions={0}, use_global_device_ids=true | all-gather | bytes 20480 | tf_op jit(solution)/shard_map/all_gather | solution.py:136
  42.8 7.6 %shard_map.57 = f32[8,1,4096]{2,1,0:T(1,128)} custom-call(bf16[1024,128]{1,0:T(8,128)(2,1)} %all_gather.6.refs_0_.refs_3_.v_ref, f32[4,1,1024]{2,1,0:T(1,128)} %all_gather.7.refs_1_, f32[1,1024]{1,0:T(1,128)} %bitcast.37, bf16[4096,128]{1,0:T(8,128)(2,1)} %r_ref.7), custom_call_target="tpu_custom_call" | custom-call | flops 1094713344 | bytes 1445888 | tf_op jit(solution)/shard_map/pallas_call | solution.py:58
  50.3 3.4 %all-to-all-start.1 = ((f32[8,1,4096]{2,1,0:T(1,128)}), f32[8,1,4096]{2,1,0:T(1,128)S(1)}, u32[]{:S(2)}, u32[]{:S(2)}) async-start(f32[8,1,4096]{2,1,0:T(1,128)} %shard_map.57), calls=%async_computation.1 | async-start | bytes 262144 | tf_op jit(solution)/shard_map/all_to_all | solution.py:132
  53.8 7.6 %all-to-all-done.1.parts_ref = f32[8,1,4096]{2,1,0:T(1,128)S(1)} async-done(((f32[8,1,4096]{2,1,0:T(1,128)}), f32[8,1,4096]{2,1,0:T(1,128)S(1)}, u32[]{:S(2)}, u32[]{:S(2)}) %all-to-all-start.1) | async-done | bytes 131104 | tf_op jit(solution)/shard_map/all_to_all | solution.py:132
  61.4 0.7 copy-done
  62.1 5.2 %shard_map.58 = f32[264,256]{1,0:T(8,128)} custom-call(s32[1]{0:T(128)} %bitcast.rot_ref, bf16[1024,128]{1,0:T(8,128)(2,1)} %all_gather.6.refs_0_.refs_3_.v_ref, bf16[4096,128]{1,0:T(8,128)(2,1)} %r_ref.7, f32[8,1,4096]{2,1,0:T(1,128)} %copy-done, f32[1,4096]{1,0:T(1,128)} %bitcast.33, bf16[4096,256]{1,0:T(8,128)(2,1)} %f_hbm.7), custom_call_target="tpu_custom_call" | custom-call | flops 810549248 | bytes 3481600 | tf_op jit(solution)/shard_map/pallas_call | solution.py:113
  67.3 0.1 collective-permute-start
  67.4 5.2 %shard_map.59 = f32[264,256]{1,0:T(8,128)} custom-call(s32[1]{0:T(128)} %bitcast.4.rot_ref, bf16[1024,128]{1,0:T(8,128)(2,1)} %all_gather.6.refs_0_.refs_3_.v_ref, bf16[4096,128]{1,0:T(8,128)(2,1)} %r_ref.7, f32[8,1,4096]{2,1,0:T(1,128)} %copy-done, f32[1,4096]{1,0:T(1,128)} %bitcast.34, bf16[4096,256]{1,0:T(8,128)(2,1)} %f_hbm.7), custom_call_target="tpu_custom_call" | custom-call | flops 810549248 | bytes 3481600 | tf_op jit(solution)/shard_map/pallas_call | solution.py:113
  72.6 1.3 %collective-permute-start.1 = (f32[264,256]{1,0:T(8,128)}, f32[264,256]{1,0:T(8,128)S(1)}, u32[]{:S(2)}, u32[]{:S(2)}) collective-permute-start(f32[264,256]{1,0:T(8,128)} %shard_map.59), channel_id=1, source_target_pairs={{0,2},{1,3},{2,0},{3,1},{4,6},{5,7},{6,4},{7,5},{8,10},{9,11},{10,... | collective-permute-start | bytes 811016 | tf_op jit(solution)/shard_map/ppermute | solution.py:152
  74.0 5.2 %shard_map.60 = f32[264,256]{1,0:T(8,128)} custom-call(s32[1]{0:T(128)} %bitcast.6.rot_ref, bf16[1024,128]{1,0:T(8,128)(2,1)} %all_gather.6.refs_0_.refs_3_.v_ref, bf16[4096,128]{1,0:T(8,128)(2,1)} %r_ref.7, f32[8,1,4096]{2,1,0:T(1,128)} %copy-done, f32[1,4096]{1,0:T(1,128)} %bitcast.35, bf16[4096,256]{1,0:T(8,128)(2,1)} %f_hbm.7), custom_call_target="tpu_custom_call" | custom-call | flops 810549248 | bytes 3481600 | tf_op jit(solution)/shard_map/pallas_call | solution.py:113
  79.2 1.7 %collective-permute-start.2 = (f32[264,256]{1,0:T(8,128)}, f32[264,256]{1,0:T(8,128)S(1)}, u32[]{:S(2)}, u32[]{:S(2)}) collective-permute-start(f32[264,256]{1,0:T(8,128)} %shard_map.60), channel_id=1, source_target_pairs={{0,3},{1,0},{2,1},{3,2},{4,7},{5,4},{6,5},{7,6},{8,11},{9,8},{10,9... | collective-permute-start | bytes 811016 | tf_op jit(solution)/shard_map/ppermute | solution.py:152
  80.9 5.2 %shard_map.61 = f32[264,256]{1,0:T(8,128)} custom-call(s32[1]{0:T(128)} %bitcast.8.rot_ref, bf16[1024,128]{1,0:T(8,128)(2,1)} %all_gather.6.refs_0_.refs_3_.v_ref, bf16[4096,128]{1,0:T(8,128)(2,1)} %r_ref.7, f32[8,1,4096]{2,1,0:T(1,128)} %copy-done, f32[1,4096]{1,0:T(1,128)} %bitcast.36, bf16[4096,256]{1,0:T(8,128)(2,1)} %f_hbm.7), custom_call_target="tpu_custom_call" | custom-call | flops 810549248 | bytes 3481600 | tf_op jit(solution)/shard_map/pallas_call | solution.py:113
  86.2 0.0 collective-permute-done
  86.2 0.0 collective-permute-done.1
  86.2 0.0 collective-permute-done.2
  86.2 0.8 fusion.3
  87.1 0.1 copy-done.1
  87.1 0.1 pad_maximum_fusion
  87.3 0.1 fusion
  87.4 0.8 copy.8
  (5 shorter events, 0.1 us)
Async XLA Ops:
  50.3 11.1 %all-to-all-start.1 = ((f32[8,1,4096]{2,1,0:T(1,128)}), f32[8,1,4096]{2,1,0:T(1,128)S(1)}, u32[]{:S(2)}, u32[]{:S(2)}) async-start(f32[8,1,4096]{2,1,0:T(1,128)} %shard_map.57), calls=%async_computation.1 | async-start | bytes 262144 | tf_op jit(solution)/shard_map/all_to_all | solution.py:132
  61.4 0.7 copy-start
  67.3 18.9 %collective-permute-start = (f32[264,256]{1,0:T(8,128)}, f32[264,256]{1,0:T(8,128)S(1)}, u32[]{:S(2)}, u32[]{:S(2)}) collective-permute-start(f32[264,256]{1,0:T(8,128)} %shard_map.58), channel_id=1, source_target_pairs={{0,1},{1,2},{2,3},{3,0},{4,5},{5,6},{6,7},{7,4},{8,9},{9,10},{10,1... | collective-permute-start | bytes 811016 | tf_op jit(solution)/shard_map/ppermute | solution.py:152
  72.6 13.6 %collective-permute-start.1 = (f32[264,256]{1,0:T(8,128)}, f32[264,256]{1,0:T(8,128)S(1)}, u32[]{:S(2)}, u32[]{:S(2)}) collective-permute-start(f32[264,256]{1,0:T(8,128)} %shard_map.59), channel_id=1, source_target_pairs={{0,2},{1,3},{2,0},{3,1},{4,6},{5,7},{6,4},{7,5},{8,10},{9,11},{10,... | collective-permute-start | bytes 811016 | tf_op jit(solution)/shard_map/ppermute | solution.py:152
  79.2 7.0 %collective-permute-start.2 = (f32[264,256]{1,0:T(8,128)}, f32[264,256]{1,0:T(8,128)S(1)}, u32[]{:S(2)}, u32[]{:S(2)}) collective-permute-start(f32[264,256]{1,0:T(8,128)} %shard_map.60), channel_id=1, source_target_pairs={{0,3},{1,0},{2,1},{3,2},{4,7},{5,4},{6,5},{7,6},{8,11},{9,8},{10,9... | collective-permute-start | bytes 811016 | tf_op jit(solution)/shard_map/ppermute | solution.py:152
  86.2 1.0 %copy-start.1 = (f32[264,256]{1,0:T(8,128)S(1)}, f32[264,256]{1,0:T(8,128)}, u32[]{:S(2)}) copy-start(f32[264,256]{1,0:T(8,128)} %shard_map.61) | copy-start | bytes 811012

commit v10 on v9

--- a/solution.py
+++ b/solution.py
@@ -114,6 +114,7 @@
         functools.partial(assign_kernel, scale=scale),
         out_shape=jax.ShapeDtypeStruct((feat + 8, chunk), jnp.float32),
         grid_spec=grid_spec,
+        compiler_params=pltpu.CompilerParams(vmem_limit_bytes=24 * 1024 * 1024),
         cost_estimate=pl.CostEstimate(
             flops=2 * chunk * cols * (width + feat) + 5 * chunk * cols,
             transcendentals=chunk * cols,

time: 88.8 us -> 85.6 us (0.964)
  Pallas kernels: 43.1 us -> 38.2 us
  other arithmetic: 1.05 us -> 2.17 us
    pallas_call x4, Pallas kernels: 21 us -> 15.9 us  [assign_chunk(): pl.pallas_call(functools.partial(assign_kernel, scale=scale), out_shape=j...]
    another operation x1, other arithmetic: 0.09 us -> 1.21 us  [local(): arrived = jnp.stack(pieces)]
  transfers between devices with their start and end apart: 4 -> 4, of which waited for: 1 -> 2; matrix products, arithmetic and copies ran while one was open for 0% -> 0% of each run, Pallas kernels for 18% -> 14%
where the time goes in v10:
time: 85.6 us; the launch traced here: 84.5 us
  Pallas kernels  38.2 us (45%)
  blocking collectives  28.2 us (33%)
  waiting for transfers between devices  8.49 us (10%)
  starting transfers between devices  6.49 us (8%)
  other arithmetic  2.17 us (3%)
    pallas_call x3, Pallas kernels, lse_over_rows(): pl.pallas_call(functools.partial(lse_kernel, scale=scale, shifted=shifted...  22.3 us
    pallas_call x4, Pallas kernels, assign_chunk(): pl.pallas_call(functools.partial(assign_kernel, scale=scale), out_shape=j...  15.9 us
    all_to_all x1, blocking collectives, exchange(): return lax.all_to_all(block, 'veh', 0, 0, tiled=True)  13.4 us
    all_gather x1, blocking collectives, local(): own_rows = lax.all_gather(vehicle_emb, 'req', axis=0, tiled=True)  8.82 us
    all_to_all x1, waiting for transfers between devices, exchange(): return lax.all_to_all(block, 'veh', 0, 0, tiled=True)  7.66 us
    all_gather x1, blocking collectives, local(): row_parts = lax.all_gather(partial[0], 'req', axis=0, tiled=False)  5.97 us
    all_to_all x1, starting transfers between devices, exchange(): return lax.all_to_all(block, 'veh', 0, 0, tiled=True)  3.37 us
    ppermute x3, starting transfers between devices, local(): lax.ppermute(piece, 'req', [(i, (i + step) % owners) for i in range(owner...  3.12 us
  transfers between devices with their start and end apart: 4, of which 2 were waited for; matrix products, arithmetic and copies ran while one was open for 0% of the time, Pallas kernels for 14%

profile of v10, /device:TPU:0, one launch (start us, length us, event | category | flops | bytes accessed | tf_op | source)
XLA Modules:
  0.0 84.5 jit_solution(10764044567649684377)
XLA Ops:
  0.0 8.8 %all_gather.6.refs_0_.refs_3_.v_ref = bf16[1024,128]{1,0:T(8,128)(2,1)} all-gather(bf16[256,128]{1,0:T(8,128)(2,1)} %param.5), channel_id=1, replica_groups=mesh['veh'=8,'req'=4] {'req'}, dimensions={0}, use_global_device_ids=true | all-gather | bytes 327680 | tf_op jit(solution)/shard_map/all_gather | solution.py:127
  8.8 6.9 %shard_map.55 = f32[8,1,4096]{2,1,0:T(1,128)} custom-call(bf16[1024,128]{1,0:T(8,128)(2,1)} %all_gather.6.refs_0_.refs_3_.v_ref, bf16[4096,128]{1,0:T(8,128)(2,1)} %r_ref.7), custom_call_target="tpu_custom_call" | custom-call | flops 1094713344 | bytes 1445888 | tf_op jit(solution)/shard_map/pallas_call | solution.py:58
  15.7 13.4 %all_to_all.10.refs_1_ = f32[8,1,4096]{2,1,0:T(1,128)} all-to-all(f32[8,1,4096]{2,1,0:T(1,128)} %shard_map.55), channel_id=1, replica_groups=mesh['veh'=8,'req'=4] {'veh'}, dimensions={0} | all-to-all | bytes 262144 | tf_op jit(solution)/shard_map/all_to_all | solution.py:133
  29.1 7.7 %shard_map.56 = f32[1,1,1024]{2,1,0:T(1,128)} custom-call(bf16[4096,128]{1,0:T(8,128)(2,1)} %r_ref.7, f32[8,1,4096]{2,1,0:T(1,128)} %all_to_all.10.refs_1_, f32[1,4096]{1,0:T(1,128)} %bitcast.26, bf16[1024,128]{1,0:T(8,128)(2,1)} %all_gather.6.refs_0_.refs_3_.v_ref), custom_call_target="tpu_custom_call" | custom-call | flops 1094713344 | bytes 1331200 | tf_op jit(solution)/shard_map/pallas_call | solution.py:58
  36.8 6.0 %all_gather.7.refs_1_ = f32[4,1,1024]{2,1,0:T(1,128)} all-gather(f32[1,1,1024]{2,1,0:T(1,128)} %shard_map.56), channel_id=1, replica_groups=mesh['veh'=8,'req'=4] {'req'}, dimensions={0}, use_global_device_ids=true | all-gather | bytes 20480 | tf_op jit(solution)/shard_map/all_gather | solution.py:137
  42.8 7.7 %shard_map.57 = f32[8,1,4096]{2,1,0:T(1,128)} custom-call(bf16[1024,128]{1,0:T(8,128)(2,1)} %all_gather.6.refs_0_.refs_3_.v_ref, f32[4,1,1024]{2,1,0:T(1,128)} %all_gather.7.refs_1_, f32[1,1024]{1,0:T(1,128)} %bitcast.31, bf16[4096,128]{1,0:T(8,128)(2,1)} %r_ref.7), custom_call_target="tpu_custom_call" | custom-call | flops 1094713344 | bytes 1445888 | tf_op jit(solution)/shard_map/pallas_call | solution.py:58
  50.5 3.4 %all-to-all-start.1 = ((f32[8,1,4096]{2,1,0:T(1,128)}), f32[8,1,4096]{2,1,0:T(1,128)S(1)}, u32[]{:S(2)}, u32[]{:S(2)}) async-start(f32[8,1,4096]{2,1,0:T(1,128)} %shard_map.57), calls=%async_computation.1 | async-start | bytes 262144 | tf_op jit(solution)/shard_map/all_to_all | solution.py:133
  53.9 7.7 %all-to-all-done.1.parts_ref = f32[8,1,4096]{2,1,0:T(1,128)S(1)} async-done(((f32[8,1,4096]{2,1,0:T(1,128)}), f32[8,1,4096]{2,1,0:T(1,128)S(1)}, u32[]{:S(2)}, u32[]{:S(2)}) %all-to-all-start.1) | async-done | bytes 131104 | tf_op jit(solution)/shard_map/all_to_all | solution.py:133
  61.6 0.0 copy-done
  61.6 0.0 copy-done.1
  61.6 4.2 %shard_map.58 = f32[264,256]{1,0:T(8,128)} custom-call(s32[1]{0:T(128)} %bitcast.rot_ref, bf16[1024,128]{1,0:T(8,128)(2,1)S(1)} %copy-done.2, bf16[4096,128]{1,0:T(8,128)(2,1)S(1)} %copy-done.1, f32[8,1,4096]{2,1,0:T(1,128)S(1)} %all-to-all-done.1.parts_ref, f32[1,4096]{1,0:T(1,128)S(1)} %bitcast.27, bf16[4096,256]{1,0:T(8,128)(2,1)S(1)} %copy-done), custom_call_target="tpu_custom_call" | custom-call | flops 810549248 | bytes 3481600 | tf_op jit(solution)/shard_map/pallas_call | solution.py:113
  65.8 0.1 collective-permute-start
  65.8 4.2 %shard_map.59 = f32[264,256]{1,0:T(8,128)} custom-call(s32[1]{0:T(128)} %bitcast.4.rot_ref, bf16[1024,128]{1,0:T(8,128)(2,1)S(1)} %copy-done.2, bf16[4096,128]{1,0:T(8,128)(2,1)S(1)} %copy-done.1, f32[8,1,4096]{2,1,0:T(1,128)S(1)} %all-to-all-done.1.parts_ref, f32[1,4096]{1,0:T(1,128)S(1)} %bitcast.28, bf16[4096,256]{1,0:T(8,128)(2,1)S(1)} %copy-done), custom_call_target="tpu_custom_call" | custom-call | flops 810549248 | bytes 3481600 | tf_op jit(solution)/shard_map/pallas_call | solution.py:113
  70.0 1.3 %collective-permute-start.1 = (f32[264,256]{1,0:T(8,128)}, f32[264,256]{1,0:T(8,128)}, u32[]{:S(2)}, u32[]{:S(2)}) collective-permute-start(f32[264,256]{1,0:T(8,128)} %shard_map.59), channel_id=1, source_target_pairs={{0,2},{1,3},{2,0},{3,1},{4,6},{5,7},{6,4},{7,5},{8,10},{9,11},{10,... | collective-permute-start | bytes 811016 | tf_op jit(solution)/shard_map/ppermute | solution.py:153
  71.3 4.1 %shard_map.60 = f32[264,256]{1,0:T(8,128)} custom-call(s32[1]{0:T(128)} %bitcast.6.rot_ref, bf16[1024,128]{1,0:T(8,128)(2,1)S(1)} %copy-done.2, bf16[4096,128]{1,0:T(8,128)(2,1)S(1)} %copy-done.1, f32[8,1,4096]{2,1,0:T(1,128)S(1)} %all-to-all-done.1.parts_ref, f32[1,4096]{1,0:T(1,128)S(1)} %bitcast.29, bf16[4096,256]{1,0:T(8,128)(2,1)S(1)} %copy-done), custom_call_target="tpu_custom_call" | custom-call | flops 810549248 | bytes 3481600 | tf_op jit(solution)/shard_map/pallas_call | solution.py:113
  75.5 1.7 %collective-permute-start.2 = (f32[264,256]{1,0:T(8,128)}, f32[264,256]{1,0:T(8,128)}, u32[]{:S(2)}, u32[]{:S(2)}) collective-permute-start(f32[264,256]{1,0:T(8,128)} %shard_map.60), channel_id=1, source_target_pairs={{0,3},{1,0},{2,1},{3,2},{4,7},{5,4},{6,5},{7,6},{8,11},{9,8},{10,9... | collective-permute-start | bytes 811016 | tf_op jit(solution)/shard_map/ppermute | solution.py:153
  77.2 3.4 %shard_map.61 = f32[264,256]{1,0:T(8,128)S(1)} custom-call(s32[1]{0:T(128)} %bitcast.8.rot_ref, bf16[1024,128]{1,0:T(8,128)(2,1)S(1)} %copy-done.2, bf16[4096,128]{1,0:T(8,128)(2,1)S(1)} %copy-done.1, f32[8,1,4096]{2,1,0:T(1,128)S(1)} %all-to-all-done.1.parts_ref, f32[1,4096]{1,0:T(1,128)S(1)} %bitcast.30, bf16[4096,256]{1,0:T(8,128)(2,1)S(1)} %copy-done), custom_call_target="tpu_custom_call" | custom-call | flops 810549248 | bytes 3481600 | tf_op jit(solution)/shard_map/pallas_call | solution.py:113
  80.6 0.0 collective-permute-done
  80.7 0.0 collective-permute-done.1
  80.7 0.8 collective-permute-done.2
  81.5 0.8 fusion.3
  82.3 1.2 %pad_maximum_fusion = f32[4,264,256]{2,1,0:T(8,128)S(1)} fusion(f32[1,264,256]{2,1,0:T(8,128)S(1)} %bitcast.25, f32[1,264,256]{2,1,0:T(8,128)} %bitcast.7, f32[1,264,256]{2,1,0:T(8,128)} %bitcast.5, f32[1,264,256]{2,1,0:T(8,128)} %bitcast.3), kind=kLoop, calls=%fused_computation | loop fusion | flops 811008 | bytes 2162688 | tf_op jit(solution)/shard_map/stack | solution.py:155
  83.6 0.1 fusion
  83.7 0.8 copy.8
  (9 shorter events, 0.1 us)
Async XLA Ops:
  42.8 18.8 %copy-start = (bf16[4096,256]{1,0:T(8,128)(2,1)S(1)}, bf16[4096,256]{1,0:T(8,128)(2,1)}, u32[]{:S(2)}) copy-start(bf16[4096,256]{1,0:T(8,128)(2,1)} %f_hbm.7) | copy-start | bytes 6291460
  42.8 18.8 %copy-start.1 = (bf16[4096,128]{1,0:T(8,128)(2,1)S(1)}, bf16[4096,128]{1,0:T(8,128)(2,1)}, u32[]{:S(2)}) copy-start(bf16[4096,128]{1,0:T(8,128)(2,1)} %r_ref.7) | copy-start | bytes 3145732
  42.8 18.8 %copy-start.2 = (bf16[1024,128]{1,0:T(8,128)(2,1)S(1)}, bf16[1024,128]{1,0:T(8,128)(2,1)}, u32[]{:S(2)}) copy-start(bf16[1024,128]{1,0:T(8,128)(2,1)} %all_gather.6.refs_0_.refs_3_.v_ref) | copy-start | bytes 786436
  42.8 18.8 %copy-start.3 = (f32[4096]{0:T(1024)S(1)}, f32[4096]{0:T(1024)}, u32[]{:S(2)}) copy-start(f32[4096]{0:T(1024)} %param.9) | copy-start | bytes 49156
  50.5 11.1 %all-to-all-start.1 = ((f32[8,1,4096]{2,1,0:T(1,128)}), f32[8,1,4096]{2,1,0:T(1,128)S(1)}, u32[]{:S(2)}, u32[]{:S(2)}) async-start(f32[8,1,4096]{2,1,0:T(1,128)} %shard_map.57), calls=%async_computation.1 | async-start | bytes 262144 | tf_op jit(solution)/shard_map/all_to_all | solution.py:133
  65.8 14.9 %collective-permute-start = (f32[264,256]{1,0:T(8,128)}, f32[264,256]{1,0:T(8,128)}, u32[]{:S(2)}, u32[]{:S(2)}) collective-permute-start(f32[264,256]{1,0:T(8,128)} %shard_map.58), channel_id=1, source_target_pairs={{0,1},{1,2},{2,3},{3,0},{4,5},{5,6},{6,7},{7,4},{8,9},{9,10},{10,1... | collective-permute-start | bytes 811016 | tf_op jit(solution)/shard_map/ppermute | solution.py:153
  70.0 10.7 %collective-permute-start.1 = (f32[264,256]{1,0:T(8,128)}, f32[264,256]{1,0:T(8,128)}, u32[]{:S(2)}, u32[]{:S(2)}) collective-permute-start(f32[264,256]{1,0:T(8,128)} %shard_map.59), channel_id=1, source_target_pairs={{0,2},{1,3},{2,0},{3,1},{4,6},{5,7},{6,4},{7,5},{8,10},{9,11},{10,... | collective-permute-start | bytes 811016 | tf_op jit(solution)/shard_map/ppermute | solution.py:153
  75.5 6.0 %collective-permute-start.2 = (f32[264,256]{1,0:T(8,128)}, f32[264,256]{1,0:T(8,128)}, u32[]{:S(2)}, u32[]{:S(2)}) collective-permute-start(f32[264,256]{1,0:T(8,128)} %shard_map.60), channel_id=1, source_target_pairs={{0,3},{1,0},{2,1},{3,2},{4,7},{5,4},{6,5},{7,6},{8,11},{9,8},{10,9... | collective-permute-start | bytes 811016 | tf_op jit(solution)/shard_map/ppermute | solution.py:153

commit v11 on v10

--- a/solution.py
+++ b/solution.py
@@ -38,7 +38,7 @@
     out_ref[...] = jnp.broadcast_to(result[None], (copies,) + result.shape)
 
 
-def lse_over_rows(a, b, scale, tile, copies, parts=None, base=None):
+def lse_over_rows(a, b, scale, tile, copies, vmem_limit, parts=None, base=None):
     rows, width = a.shape
     cols = b.shape[0]
     tile = min(tile, cols)
@@ -62,6 +62,7 @@
         in_specs=in_specs,
         out_specs=pl.BlockSpec((copies, 1, tile), lambda j: (0, 0, j)),
         scratch_shapes=scratch,
+        compiler_params=pltpu.CompilerParams(vmem_limit_bytes=vmem_limit),
         cost_estimate=pl.CostEstimate(
             flops=2 * rows * cols * width + 5 * rows * cols,
             transcendentals=rows * cols,
@@ -123,6 +124,39 @@
     )(index, v, r, parts, base.reshape(1, cols), f)
 
 
+def combine_kernel(*refs):
+    piece_refs, out_ref = refs[:-1], refs[-1]
+    feat = out_ref.shape[1]
+    peaks = [ref[feat + 1 : feat + 2, :] for ref in piece_refs]
+    top = peaks[0]
+    for peak in peaks[1:]:
+        top = jnp.maximum(top, peak)
+    numerator = None
+    denominator = None
+    for ref, peak in zip(piece_refs, peaks):
+        factor = jnp.exp(peak - top)
+        term = ref[:feat, :] * factor
+        mass = ref[feat : feat + 1, :] * factor
+        numerator = term if numerator is None else numerator + term
+        denominator = mass if denominator is None else denominator + mass
+    out_ref[...] = (numerator / denominator).T
+
+
+def combine(pieces, feat):
+    chunk = pieces[0].shape[1]
+    return pl.pallas_call(
+        combine_kernel,
+        out_shape=jax.ShapeDtypeStruct((chunk, feat), jnp.float32),
+        in_specs=[pl.BlockSpec(piece.shape, lambda: (0, 0)) for piece in pieces],
+        out_specs=pl.BlockSpec((chunk, feat), lambda: (0, 0)),
+        cost_estimate=pl.CostEstimate(
+            flops=3 * len(pieces) * chunk * feat,
+            transcendentals=len(pieces) * chunk,
+            bytes_accessed=4 * chunk * ((feat + 8) * len(pieces) + feat),
+        ),
+    )(*pieces)
+
+
 def local(vehicle_emb, request_emb, request_feat, log_supply, log_demand):
     own_rows = lax.all_gather(vehicle_emb, "req", axis=0, tiled=True)
     row_count = own_rows.shape[0]
@@ -132,11 +166,11 @@
     def exchange(block):
         return lax.all_to_all(block, "veh", 0, 0, tiled=True)
 
-    first = exchange(lse_over_rows(own_rows, request_emb, scale, 2048, spread))
-    partial = lse_over_rows(request_emb, own_rows, scale, 1024, 1, first, log_demand)
+    first = exchange(lse_over_rows(own_rows, request_emb, scale, 2048, spread, 24 << 20))
+    partial = lse_over_rows(request_emb, own_rows, scale, 1024, 1, 48 << 20, first, log_demand)
     row_parts = lax.all_gather(partial[0], "req", axis=0, tiled=False)
     second = exchange(
-        lse_over_rows(own_rows, request_emb, scale, 2048, spread, row_parts, log_supply)
+        lse_over_rows(own_rows, request_emb, scale, 2048, spread, 24 << 20, row_parts, log_supply)
     )
 
     owners = lax.axis_size("req")
@@ -152,13 +186,7 @@
         if step:
             piece = lax.ppermute(piece, "req", [(i, (i + step) % owners) for i in range(owners)])
         pieces.append(piece)
-    arrived = jnp.stack(pieces)
-    peaks = arrived[:, feat + 1, :]
-    masses = arrived[:, feat, :]
-    factor = jnp.exp(peaks - jnp.max(peaks, axis=0, keepdims=True))
-    numerator = jnp.sum(arrived[:, :feat, :] * factor[:, None, :], axis=0)
-    denominator = jnp.sum(masses * factor, axis=0)
-    return (numerator / denominator[None, :]).T
+    return combine(pieces, feat)
 
 
 def solution(mesh):

time: 85.6 us -> 78.2 us (0.914)
  Pallas kernels: 38.2 us -> 34.5 us
  blocking collectives: 28.2 us -> 25.9 us
  other arithmetic: 2.17 us -> 0 us
  local copies, waits for them, and re-layouts: 0.85 us -> 2.59 us
    pallas_call x3, Pallas kernels: 22.3 us -> 16.5 us  [lse_over_rows(): pl.pallas_call(functools.partial(lse_kernel, scale=scale, shifted=shifted...]
    unnamed x8 -> x14, local copies, waits for them, and re-layouts: 0.01 us -> 2.59 us
    pallas_call x0 -> x1, Pallas kernels: none -> 2.06 us  [combine(): pl.pallas_call(combine_kernel, out_shape=jax.ShapeDtypeStruct((chunk, fea...]
    all_gather x1, blocking collectives: 8.82 us -> 7.42 us  [local(): own_rows = lax.all_gather(vehicle_emb, 'req', axis=0, tiled=True)]
    another operation x1 -> x0, other arithmetic: 1.21 us -> none  [local(): arrived = jnp.stack(pieces)]
  transfers between devices with their start and end apart: 4 -> 4, of which waited for: 2 -> 2; matrix products, arithmetic and copies ran while one was open for 0% -> 0% of each run, Pallas kernels for 14% -> 15%
where the time goes in v11:
time: 78.2 us; the launch traced here: 77.6 us
  Pallas kernels  34.5 us (44%)
  blocking collectives  25.9 us (33%)
  waiting for transfers between devices  7.77 us (10%)
  starting transfers between devices  6.73 us (9%)
  local copies, waits for them, and re-layouts  2.59 us (3%)
    pallas_call x3, Pallas kernels, lse_over_rows(): pl.pallas_call(functools.partial(lse_kernel, scale=scale, shifted=shifted...  16.5 us
    pallas_call x4, Pallas kernels, assign_chunk(): pl.pallas_call(functools.partial(assign_kernel, scale=scale), out_shape=j...  15.9 us
    all_to_all x1, blocking collectives, exchange(): return lax.all_to_all(block, 'veh', 0, 0, tiled=True)  13.1 us
    all_to_all x1, waiting for transfers between devices, exchange(): return lax.all_to_all(block, 'veh', 0, 0, tiled=True)  7.63 us
    all_gather x1, blocking collectives, local(): own_rows = lax.all_gather(vehicle_emb, 'req', axis=0, tiled=True)  7.42 us
    all_gather x1, blocking collectives, local(): row_parts = lax.all_gather(partial[0], 'req', axis=0, tiled=False)  5.37 us
    all_to_all x1, starting transfers between devices, exchange(): return lax.all_to_all(block, 'veh', 0, 0, tiled=True)  3.37 us
    ppermute x3, starting transfers between devices, local(): lax.ppermute(piece, 'req', [(i, (i + step) % owners) for i in range(owner...  3.36 us
  transfers between devices with their start and end apart: 4, of which 2 were waited for; matrix products, arithmetic and copies ran while one was open for 0% of the time, Pallas kernels for 15%

profile of v11, /device:TPU:0, one launch (start us, length us, event | category | flops | bytes accessed | tf_op | source)
XLA Modules:
  0.0 77.6 jit_solution(6176779163519574941)
XLA Ops:
  0.0 7.4 %all_gather.6.refs_0_.refs_3_.v_ref = bf16[1024,128]{1,0:T(8,128)(2,1)S(1)} all-gather(bf16[256,128]{1,0:T(8,128)(2,1)} %param.5), channel_id=1, replica_groups=mesh['veh'=8,'req'=4] {'req'}, dimensions={0}, use_global_device_ids=true | all-gather | bytes 327680 | tf_op jit(solution)/shard_map/all_gather | solution.py:161
  7.4 1.2 %copy-done.1 = bf16[4096,128]{1,0:T(8,128)(2,1)S(1)} copy-done((bf16[4096,128]{1,0:T(8,128)(2,1)S(1)}, bf16[4096,128]{1,0:T(8,128)(2,1)}, u32[]{:S(2)}) %copy-start.1) | copy-done | bytes 1048600
  8.6 5.2 %shard_map.55 = f32[8,1,4096]{2,1,0:T(1,128)S(1)} custom-call(bf16[1024,128]{1,0:T(8,128)(2,1)S(1)} %all_gather.6.refs_0_.refs_3_.v_ref, bf16[4096,128]{1,0:T(8,128)(2,1)S(1)} %copy-done.1), custom_call_target="tpu_custom_call" | custom-call | flops 1094713344 | bytes 1445888 | tf_op jit(solution)/shard_map/pallas_call | solution.py:58
  13.8 13.1 %all_to_all.10.refs_1_ = f32[8,1,4096]{2,1,0:T(1,128)S(1)} all-to-all(f32[8,1,4096]{2,1,0:T(1,128)S(1)} %shard_map.55), channel_id=1, replica_groups=mesh['veh'=8,'req'=4] {'veh'}, dimensions={0} | all-to-all | bytes 262144 | tf_op jit(solution)/shard_map/all_to_all | solution.py:167
  26.9 0.0 copy-done.4
  27.0 5.7 %shard_map.56 = f32[1,1,1024]{2,1,0:T(1,128)S(1)} custom-call(bf16[4096,128]{1,0:T(8,128)(2,1)S(1)} %copy-done.2, f32[8,1,4096]{2,1,0:T(1,128)S(1)} %all_to_all.10.refs_1_, f32[1,4096]{1,0:T(1,128)S(1)} %bitcast.6, bf16[1024,128]{1,0:T(8,128)(2,1)S(1)} %all_gather.6.refs_0_.refs_3_.v_ref), custom_call_target="tpu_custom_call" | custom-call | flops 1094713344 | bytes 1331200 | tf_op jit(solution)/shard_map/pallas_call | solution.py:58
  32.7 5.4 %all_gather.7.refs_1_ = f32[4,1,1024]{2,1,0:T(1,128)S(1)} all-gather(f32[1,1,1024]{2,1,0:T(1,128)S(1)} %shard_map.56), channel_id=1, replica_groups=mesh['veh'=8,'req'=4] {'req'}, dimensions={0}, use_global_device_ids=true | all-gather | bytes 20480 | tf_op jit(solution)/shard_map/all_gather | solution.py:171
  38.0 5.6 %shard_map.57 = f32[8,1,4096]{2,1,0:T(1,128)S(1)} custom-call(bf16[1024,128]{1,0:T(8,128)(2,1)S(1)} %all_gather.6.refs_0_.refs_3_.v_ref, f32[4,1,1024]{2,1,0:T(1,128)S(1)} %all_gather.7.refs_1_, f32[1,1024]{1,0:T(1,128)S(1)} %bitcast.11, bf16[4096,128]{1,0:T(8,128)(2,1)S(1)} %copy-done.2), custom_call_target="tpu_custom_call" | custom-call | flops 1094713344 | bytes 1445888 | tf_op jit(solution)/shard_map/pallas_call | solution.py:58
  43.7 0.0 copy-start.5
  43.7 0.6 copy-done.5
  44.3 3.4 %all-to-all-start.1 = ((f32[8,1,4096]{2,1,0:T(1,128)}), f32[8,1,4096]{2,1,0:T(1,128)S(1)}, u32[]{:S(2)}, u32[]{:S(2)}) async-start(f32[8,1,4096]{2,1,0:T(1,128)} %copy-done.5), calls=%async_computation.1 | async-start | bytes 262144 | tf_op jit(solution)/shard_map/all_to_all | solution.py:167
  47.7 7.6 %all-to-all-done.1.parts_ref = f32[8,1,4096]{2,1,0:T(1,128)S(1)} async-done(((f32[8,1,4096]{2,1,0:T(1,128)}), f32[8,1,4096]{2,1,0:T(1,128)S(1)}, u32[]{:S(2)}, u32[]{:S(2)}) %all-to-all-start.1) | async-done | bytes 131104 | tf_op jit(solution)/shard_map/all_to_all | solution.py:167
  55.4 4.2 %shard_map.58 = f32[264,256]{1,0:T(8,128)} custom-call(s32[1]{0:T(128)} %bitcast.rot_ref, bf16[1024,128]{1,0:T(8,128)(2,1)S(1)} %all_gather.6.refs_0_.refs_3_.v_ref, bf16[4096,128]{1,0:T(8,128)(2,1)S(1)} %copy-done.2, f32[8,1,4096]{2,1,0:T(1,128)S(1)} %all-to-all-done.1.parts_ref, f32[1,4096]{1,0:T(1,128)S(1)} %bitcast.7, bf16[4096,256]{1,0:T(8,128)(2,1)S(1)} %copy-done), custom_call_target="tpu_custom_call" | custom-call | flops 810549248 | bytes 3481600 | tf_op jit(solution)/shard_map/pallas_call | solution.py:114
  59.5 0.1 collective-permute-start
  59.6 4.2 %shard_map.59 = f32[264,256]{1,0:T(8,128)} custom-call(s32[1]{0:T(128)} %bitcast.3.rot_ref, bf16[1024,128]{1,0:T(8,128)(2,1)S(1)} %all_gather.6.refs_0_.refs_3_.v_ref, bf16[4096,128]{1,0:T(8,128)(2,1)S(1)} %copy-done.2, f32[8,1,4096]{2,1,0:T(1,128)S(1)} %all-to-all-done.1.parts_ref, f32[1,4096]{1,0:T(1,128)S(1)} %bitcast.8, bf16[4096,256]{1,0:T(8,128)(2,1)S(1)} %copy-done), custom_call_target="tpu_custom_call" | custom-call | flops 810549248 | bytes 3481600 | tf_op jit(solution)/shard_map/pallas_call | solution.py:114
  63.8 1.6 %collective-permute-start.1 = (f32[264,256]{1,0:T(8,128)}, f32[264,256]{1,0:T(8,128)}, u32[]{:S(2)}, u32[]{:S(2)}) collective-permute-start(f32[264,256]{1,0:T(8,128)} %shard_map.59), channel_id=1, source_target_pairs={{0,2},{1,3},{2,0},{3,1},{4,6},{5,7},{6,4},{7,5},{8,10},{9,11},{10,... | collective-permute-start | bytes 811016 | tf_op jit(solution)/shard_map/ppermute | solution.py:187
  65.4 4.1 %shard_map.60 = f32[264,256]{1,0:T(8,128)} custom-call(s32[1]{0:T(128)} %bitcast.4.rot_ref, bf16[1024,128]{1,0:T(8,128)(2,1)S(1)} %all_gather.6.refs_0_.refs_3_.v_ref, bf16[4096,128]{1,0:T(8,128)(2,1)S(1)} %copy-done.2, f32[8,1,4096]{2,1,0:T(1,128)S(1)} %all-to-all-done.1.parts_ref, f32[1,4096]{1,0:T(1,128)S(1)} %bitcast.9, bf16[4096,256]{1,0:T(8,128)(2,1)S(1)} %copy-done), custom_call_target="tpu_custom_call" | custom-call | flops 810549248 | bytes 3481600 | tf_op jit(solution)/shard_map/pallas_call | solution.py:114
  69.5 1.7 %collective-permute-start.2 = (f32[264,256]{1,0:T(8,128)}, f32[264,256]{1,0:T(8,128)}, u32[]{:S(2)}, u32[]{:S(2)}) collective-permute-start(f32[264,256]{1,0:T(8,128)} %shard_map.60), channel_id=1, source_target_pairs={{0,3},{1,0},{2,1},{3,2},{4,7},{5,4},{6,5},{7,6},{8,11},{9,8},{10,9... | collective-permute-start | bytes 811016 | tf_op jit(solution)/shard_map/ppermute | solution.py:187
  71.2 3.4 %shard_map.61.refs_3_ = f32[264,256]{1,0:T(8,128)S(1)} custom-call(s32[1]{0:T(128)} %bitcast.5.rot_ref, bf16[1024,128]{1,0:T(8,128)(2,1)S(1)} %all_gather.6.refs_0_.refs_3_.v_ref, bf16[4096,128]{1,0:T(8,128)(2,1)S(1)} %copy-done.2, f32[8,1,4096]{2,1,0:T(1,128)S(1)} %all-to-all-done.1.parts_ref, f32[1,4096]{1,0:T(1,128)S(1)} %bitcast.10, ...), custom_call_target="tpu_custom_call" | custom-call | flops 810549248 | bytes 3481600 | tf_op jit(solution)/shard_map/pallas_call | solution.py:114
  74.7 0.7 copy-done.3
  75.4 0.0 collective-permute-done.refs_0_
  75.4 0.0 collective-permute-done.1.refs_1_
  75.4 0.1 collective-permute-done.2.refs_2_
  75.5 2.1 %shard_map.62 = f32[256,256]{1,0:T(8,128)} custom-call(f32[264,256]{1,0:T(8,128)} %collective-permute-done.refs_0_, f32[264,256]{1,0:T(8,128)} %collective-permute-done.1.refs_1_, f32[264,256]{1,0:T(8,128)} %collective-permute-done.2.refs_2_, f32[264,256]{1,0:T(8,128)} %copy-done.3), custom_call_target="tpu_custom_call" | custom-call | flops 786432 | bytes 1343488 | tf_op jit(solution)/shard_map/pallas_call | solution.py:147
  (9 shorter events, 0.0 us)
Async XLA Ops:
  7.4 1.2 %copy-start.1 = (bf16[4096,128]{1,0:T(8,128)(2,1)S(1)}, bf16[4096,128]{1,0:T(8,128)(2,1)}, u32[]{:S(2)}) copy-start(bf16[4096,128]{1,0:T(8,128)(2,1)} %r_ref.7) | copy-start | bytes 3145732
  8.6 18.3 %copy-start.2 = (bf16[4096,128]{1,0:T(8,128)(2,1)S(1)}, bf16[4096,128]{1,0:T(8,128)(2,1)}, u32[]{:S(2)}) copy-start(bf16[4096,128]{1,0:T(8,128)(2,1)} %r_ref.7) | copy-start | bytes 3145732
  8.6 18.3 %copy-start.4 = (f32[4096]{0:T(1024)S(1)}, f32[4096]{0:T(1024)}, u32[]{:S(2)}) copy-start(f32[4096]{0:T(1024)} %param.9) | copy-start | bytes 49156
  26.9 11.1 %copy-start.6 = (f32[1024]{0:T(1024)S(1)}, f32[1024]{0:T(1024)}, u32[]{:S(2)}) copy-start(f32[1024]{0:T(1024)} %param.8) | copy-start | bytes 12292
  38.0 17.3 %copy-start = (bf16[4096,256]{1,0:T(8,128)(2,1)S(1)}, bf16[4096,256]{1,0:T(8,128)(2,1)}, u32[]{:S(2)}) copy-start(bf16[4096,256]{1,0:T(8,128)(2,1)} %f_hbm.7) | copy-start | bytes 6291460
  43.7 0.7 copy-start.5
  44.3 11.0 %all-to-all-start.1 = ((f32[8,1,4096]{2,1,0:T(1,128)}), f32[8,1,4096]{2,1,0:T(1,128)S(1)}, u32[]{:S(2)}, u32[]{:S(2)}) async-start(f32[8,1,4096]{2,1,0:T(1,128)} %copy-done.5), calls=%async_computation.1 | async-start | bytes 262144 | tf_op jit(solution)/shard_map/all_to_all | solution.py:167
  59.5 15.9 %collective-permute-start = (f32[264,256]{1,0:T(8,128)}, f32[264,256]{1,0:T(8,128)}, u32[]{:S(2)}, u32[]{:S(2)}) collective-permute-start(f32[264,256]{1,0:T(8,128)} %shard_map.58), channel_id=1, source_target_pairs={{0,1},{1,2},{2,3},{3,0},{4,5},{5,6},{6,7},{7,4},{8,9},{9,10},{10,1... | collective-permute-start | bytes 811016 | tf_op jit(solution)/shard_map/ppermute | solution.py:187
  63.8 11.6 %collective-permute-start.1 = (f32[264,256]{1,0:T(8,128)}, f32[264,256]{1,0:T(8,128)}, u32[]{:S(2)}, u32[]{:S(2)}) collective-permute-start(f32[264,256]{1,0:T(8,128)} %shard_map.59), channel_id=1, source_target_pairs={{0,2},{1,3},{2,0},{3,1},{4,6},{5,7},{6,4},{7,5},{8,10},{9,11},{10,... | collective-permute-start | bytes 811016 | tf_op jit(solution)/shard_map/ppermute | solution.py:187
  69.5 6.0 %collective-permute-start.2 = (f32[264,256]{1,0:T(8,128)}, f32[264,256]{1,0:T(8,128)}, u32[]{:S(2)}, u32[]{:S(2)}) collective-permute-start(f32[264,256]{1,0:T(8,128)} %shard_map.60), channel_id=1, source_target_pairs={{0,3},{1,0},{2,1},{3,2},{4,7},{5,4},{6,5},{7,6},{8,11},{9,8},{10,9... | collective-permute-start | bytes 811016 | tf_op jit(solution)/shard_map/ppermute | solution.py:187
  74.7 0.7 copy-start.3

commit v12 on v11

--- a/solution.py
+++ b/solution.py
@@ -166,11 +166,11 @@
     def exchange(block):
         return lax.all_to_all(block, "veh", 0, 0, tiled=True)
 
-    first = exchange(lse_over_rows(own_rows, request_emb, scale, 2048, spread, 24 << 20))
+    first = exchange(lse_over_rows(own_rows, request_emb, scale, 4096, spread, 24 << 20))
     partial = lse_over_rows(request_emb, own_rows, scale, 1024, 1, 48 << 20, first, log_demand)
     row_parts = lax.all_gather(partial[0], "req", axis=0, tiled=False)
     second = exchange(
-        lse_over_rows(own_rows, request_emb, scale, 2048, spread, 24 << 20, row_parts, log_supply)
+        lse_over_rows(own_rows, request_emb, scale, 4096, spread, 24 << 20, row_parts, log_supply)
     )
 
     owners = lax.axis_size("req")

time: 78.2 us -> 77.7 us (level)
  no operation moved by 1% of the time
where the time goes in v12:
time: 77.7 us; the launch traced here: 76.9 us
  Pallas kernels  33.8 us (44%)
  blocking collectives  25.9 us (33%)
  waiting for transfers between devices  7.79 us (10%)
  starting transfers between devices  6.73 us (9%)
  local copies, waits for them, and re-layouts  2.59 us (3%)
    pallas_call x4, Pallas kernels, assign_chunk(): pl.pallas_call(functools.partial(assign_kernel, scale=scale), out_shape=j...  15.9 us
    pallas_call x3, Pallas kernels, lse_over_rows(): pl.pallas_call(functools.partial(lse_kernel, scale=scale, shifted=shifted...  15.8 us
    all_to_all x1, blocking collectives, exchange(): return lax.all_to_all(block, 'veh', 0, 0, tiled=True)  13.1 us
    all_to_all x1, waiting for transfers between devices, exchange(): return lax.all_to_all(block, 'veh', 0, 0, tiled=True)  7.65 us
    all_gather x1, blocking collectives, local(): own_rows = lax.all_gather(vehicle_emb, 'req', axis=0, tiled=True)  7.42 us
    all_gather x1, blocking collectives, local(): row_parts = lax.all_gather(partial[0], 'req', axis=0, tiled=False)  5.37 us
    all_to_all x1, starting transfers between devices, exchange(): return lax.all_to_all(block, 'veh', 0, 0, tiled=True)  3.37 us
    ppermute x3, starting transfers between devices, local(): lax.ppermute(piece, 'req', [(i, (i + step) % owners) for i in range(owner...  3.36 us
  transfers between devices with their start and end apart: 4, of which 2 were waited for; matrix products, arithmetic and copies ran while one was open for 0% of the time, Pallas kernels for 15%

profile of v12, /device:TPU:0, one launch (start us, length us, event | category | flops | bytes accessed | tf_op | source)
XLA Modules:
  0.0 76.9 jit_solution(7409338878475766250)
XLA Ops:
  0.0 7.4 %all_gather.6.refs_0_.refs_3_.v_ref = bf16[1024,128]{1,0:T(8,128)(2,1)S(1)} all-gather(bf16[256,128]{1,0:T(8,128)(2,1)} %param.5), channel_id=1, replica_groups=mesh['veh'=8,'req'=4] {'req'}, dimensions={0}, use_global_device_ids=true | all-gather | bytes 327680 | tf_op jit(solution)/shard_map/all_gather | solution.py:161
  7.4 1.2 %copy-done.1 = bf16[4096,128]{1,0:T(8,128)(2,1)S(1)} copy-done((bf16[4096,128]{1,0:T(8,128)(2,1)S(1)}, bf16[4096,128]{1,0:T(8,128)(2,1)}, u32[]{:S(2)}) %copy-start.1) | copy-done | bytes 1048600
  8.6 5.1 %shard_map.55 = f32[8,1,4096]{2,1,0:T(1,128)S(1)} custom-call(bf16[1024,128]{1,0:T(8,128)(2,1)S(1)} %all_gather.6.refs_0_.refs_3_.v_ref, bf16[4096,128]{1,0:T(8,128)(2,1)S(1)} %copy-done.1), custom_call_target="tpu_custom_call" | custom-call | flops 1094713344 | bytes 1445888 | tf_op jit(solution)/shard_map/pallas_call | solution.py:58
  13.7 13.1 %all_to_all.10.refs_1_ = f32[8,1,4096]{2,1,0:T(1,128)S(1)} all-to-all(f32[8,1,4096]{2,1,0:T(1,128)S(1)} %shard_map.55), channel_id=1, replica_groups=mesh['veh'=8,'req'=4] {'veh'}, dimensions={0} | all-to-all | bytes 262144 | tf_op jit(solution)/shard_map/all_to_all | solution.py:167
  26.9 0.0 copy-done.2
  26.9 5.7 %shard_map.56 = f32[1,1,1024]{2,1,0:T(1,128)S(1)} custom-call(bf16[4096,128]{1,0:T(8,128)(2,1)S(1)} %copy-done.2, f32[8,1,4096]{2,1,0:T(1,128)S(1)} %all_to_all.10.refs_1_, f32[1,4096]{1,0:T(1,128)S(1)} %bitcast.6, bf16[1024,128]{1,0:T(8,128)(2,1)S(1)} %all_gather.6.refs_0_.refs_3_.v_ref), custom_call_target="tpu_custom_call" | custom-call | flops 1094713344 | bytes 1331200 | tf_op jit(solution)/shard_map/pallas_call | solution.py:58
  32.6 5.4 %all_gather.7.refs_1_ = f32[4,1,1024]{2,1,0:T(1,128)S(1)} all-gather(f32[1,1,1024]{2,1,0:T(1,128)S(1)} %shard_map.56), channel_id=1, replica_groups=mesh['veh'=8,'req'=4] {'req'}, dimensions={0}, use_global_device_ids=true | all-gather | bytes 20480 | tf_op jit(solution)/shard_map/all_gather | solution.py:171
  37.9 5.0 %shard_map.57 = f32[8,1,4096]{2,1,0:T(1,128)S(1)} custom-call(bf16[1024,128]{1,0:T(8,128)(2,1)S(1)} %all_gather.6.refs_0_.refs_3_.v_ref, f32[4,1,1024]{2,1,0:T(1,128)S(1)} %all_gather.7.refs_1_, f32[1,1024]{1,0:T(1,128)S(1)} %bitcast.11, bf16[4096,128]{1,0:T(8,128)(2,1)S(1)} %copy-done.2), custom_call_target="tpu_custom_call" | custom-call | flops 1094713344 | bytes 1445888 | tf_op jit(solution)/shard_map/pallas_call | solution.py:58
  43.0 0.0 copy-start.5
  43.0 0.7 copy-done.5
  43.7 3.4 %all-to-all-start.1 = ((f32[8,1,4096]{2,1,0:T(1,128)}), f32[8,1,4096]{2,1,0:T(1,128)S(1)}, u32[]{:S(2)}, u32[]{:S(2)}) async-start(f32[8,1,4096]{2,1,0:T(1,128)} %copy-done.5), calls=%async_computation.1 | async-start | bytes 262144 | tf_op jit(solution)/shard_map/all_to_all | solution.py:167
  47.1 7.6 %all-to-all-done.1.parts_ref = f32[8,1,4096]{2,1,0:T(1,128)S(1)} async-done(((f32[8,1,4096]{2,1,0:T(1,128)}), f32[8,1,4096]{2,1,0:T(1,128)S(1)}, u32[]{:S(2)}, u32[]{:S(2)}) %all-to-all-start.1) | async-done | bytes 131104 | tf_op jit(solution)/shard_map/all_to_all | solution.py:167
  54.7 4.2 %shard_map.58 = f32[264,256]{1,0:T(8,128)} custom-call(s32[1]{0:T(128)} %bitcast.rot_ref, bf16[1024,128]{1,0:T(8,128)(2,1)S(1)} %all_gather.6.refs_0_.refs_3_.v_ref, bf16[4096,128]{1,0:T(8,128)(2,1)S(1)} %copy-done.2, f32[8,1,4096]{2,1,0:T(1,128)S(1)} %all-to-all-done.1.parts_ref, f32[1,4096]{1,0:T(1,128)S(1)} %bitcast.7, bf16[4096,256]{1,0:T(8,128)(2,1)S(1)} %copy-done), custom_call_target="tpu_custom_call" | custom-call | flops 810549248 | bytes 3481600 | tf_op jit(solution)/shard_map/pallas_call | solution.py:114
  58.9 0.3 collective-permute-start
  59.2 4.2 %shard_map.59 = f32[264,256]{1,0:T(8,128)} custom-call(s32[1]{0:T(128)} %bitcast.3.rot_ref, bf16[1024,128]{1,0:T(8,128)(2,1)S(1)} %all_gather.6.refs_0_.refs_3_.v_ref, bf16[4096,128]{1,0:T(8,128)(2,1)S(1)} %copy-done.2, f32[8,1,4096]{2,1,0:T(1,128)S(1)} %all-to-all-done.1.parts_ref, f32[1,4096]{1,0:T(1,128)S(1)} %bitcast.8, bf16[4096,256]{1,0:T(8,128)(2,1)S(1)} %copy-done), custom_call_target="tpu_custom_call" | custom-call | flops 810549248 | bytes 3481600 | tf_op jit(solution)/shard_map/pallas_call | solution.py:114
  63.3 1.6 %collective-permute-start.1 = (f32[264,256]{1,0:T(8,128)}, f32[264,256]{1,0:T(8,128)}, u32[]{:S(2)}, u32[]{:S(2)}) collective-permute-start(f32[264,256]{1,0:T(8,128)} %shard_map.59), channel_id=1, source_target_pairs={{0,2},{1,3},{2,0},{3,1},{4,6},{5,7},{6,4},{7,5},{8,10},{9,11},{10,... | collective-permute-start | bytes 811016 | tf_op jit(solution)/shard_map/ppermute | solution.py:187
  64.9 4.1 %shard_map.60 = f32[264,256]{1,0:T(8,128)} custom-call(s32[1]{0:T(128)} %bitcast.4.rot_ref, bf16[1024,128]{1,0:T(8,128)(2,1)S(1)} %all_gather.6.refs_0_.refs_3_.v_ref, bf16[4096,128]{1,0:T(8,128)(2,1)S(1)} %copy-done.2, f32[8,1,4096]{2,1,0:T(1,128)S(1)} %all-to-all-done.1.parts_ref, f32[1,4096]{1,0:T(1,128)S(1)} %bitcast.9, bf16[4096,256]{1,0:T(8,128)(2,1)S(1)} %copy-done), custom_call_target="tpu_custom_call" | custom-call | flops 810549248 | bytes 3481600 | tf_op jit(solution)/shard_map/pallas_call | solution.py:114
  69.1 1.5 %collective-permute-start.2 = (f32[264,256]{1,0:T(8,128)}, f32[264,256]{1,0:T(8,128)}, u32[]{:S(2)}, u32[]{:S(2)}) collective-permute-start(f32[264,256]{1,0:T(8,128)} %shard_map.60), channel_id=1, source_target_pairs={{0,3},{1,0},{2,1},{3,2},{4,7},{5,4},{6,5},{7,6},{8,11},{9,8},{10,9... | collective-permute-start | bytes 811016 | tf_op jit(solution)/shard_map/ppermute | solution.py:187
  70.6 3.4 %shard_map.61.refs_3_ = f32[264,256]{1,0:T(8,128)S(1)} custom-call(s32[1]{0:T(128)} %bitcast.5.rot_ref, bf16[1024,128]{1,0:T(8,128)(2,1)S(1)} %all_gather.6.refs_0_.refs_3_.v_ref, bf16[4096,128]{1,0:T(8,128)(2,1)S(1)} %copy-done.2, f32[8,1,4096]{2,1,0:T(1,128)S(1)} %all-to-all-done.1.parts_ref, f32[1,4096]{1,0:T(1,128)S(1)} %bitcast.10, ...), custom_call_target="tpu_custom_call" | custom-call | flops 810549248 | bytes 3481600 | tf_op jit(solution)/shard_map/pallas_call | solution.py:114
  74.0 0.7 copy-done.3
  74.7 0.0 collective-permute-done.refs_0_
  74.7 0.0 collective-permute-done.1.refs_1_
  74.7 0.1 collective-permute-done.2.refs_2_
  74.9 2.1 %shard_map.62 = f32[256,256]{1,0:T(8,128)} custom-call(f32[264,256]{1,0:T(8,128)} %collective-permute-done.refs_0_, f32[264,256]{1,0:T(8,128)} %collective-permute-done.1.refs_1_, f32[264,256]{1,0:T(8,128)} %collective-permute-done.2.refs_2_, f32[264,256]{1,0:T(8,128)} %copy-done.3), custom_call_target="tpu_custom_call" | custom-call | flops 786432 | bytes 1343488 | tf_op jit(solution)/shard_map/pallas_call | solution.py:147
  (9 shorter events, 0.0 us)
Async XLA Ops:
  7.4 1.2 %copy-start.1 = (bf16[4096,128]{1,0:T(8,128)(2,1)S(1)}, bf16[4096,128]{1,0:T(8,128)(2,1)}, u32[]{:S(2)}) copy-start(bf16[4096,128]{1,0:T(8,128)(2,1)} %r_ref.7) | copy-start | bytes 3145732
  8.6 18.2 %copy-start.2 = (bf16[4096,128]{1,0:T(8,128)(2,1)S(1)}, bf16[4096,128]{1,0:T(8,128)(2,1)}, u32[]{:S(2)}) copy-start(bf16[4096,128]{1,0:T(8,128)(2,1)} %r_ref.7) | copy-start | bytes 3145732
  8.6 18.2 %copy-start.4 = (f32[4096]{0:T(1024)S(1)}, f32[4096]{0:T(1024)}, u32[]{:S(2)}) copy-start(f32[4096]{0:T(1024)} %param.9) | copy-start | bytes 49156
  26.9 11.1 %copy-start.6 = (f32[1024]{0:T(1024)S(1)}, f32[1024]{0:T(1024)}, u32[]{:S(2)}) copy-start(f32[1024]{0:T(1024)} %param.8) | copy-start | bytes 12292
  37.9 16.8 %copy-start = (bf16[4096,256]{1,0:T(8,128)(2,1)S(1)}, bf16[4096,256]{1,0:T(8,128)(2,1)}, u32[]{:S(2)}) copy-start(bf16[4096,256]{1,0:T(8,128)(2,1)} %f_hbm.7) | copy-start | bytes 6291460
  43.0 0.7 copy-start.5
  43.7 11.1 %all-to-all-start.1 = ((f32[8,1,4096]{2,1,0:T(1,128)}), f32[8,1,4096]{2,1,0:T(1,128)S(1)}, u32[]{:S(2)}, u32[]{:S(2)}) async-start(f32[8,1,4096]{2,1,0:T(1,128)} %copy-done.5), calls=%async_computation.1 | async-start | bytes 262144 | tf_op jit(solution)/shard_map/all_to_all | solution.py:167
  58.9 15.9 %collective-permute-start = (f32[264,256]{1,0:T(8,128)}, f32[264,256]{1,0:T(8,128)}, u32[]{:S(2)}, u32[]{:S(2)}) collective-permute-start(f32[264,256]{1,0:T(8,128)} %shard_map.58), channel_id=1, source_target_pairs={{0,1},{1,2},{2,3},{3,0},{4,5},{5,6},{6,7},{7,4},{8,9},{9,10},{10,1... | collective-permute-start | bytes 811016 | tf_op jit(solution)/shard_map/ppermute | solution.py:187
  63.3 11.4 %collective-permute-start.1 = (f32[264,256]{1,0:T(8,128)}, f32[264,256]{1,0:T(8,128)}, u32[]{:S(2)}, u32[]{:S(2)}) collective-permute-start(f32[264,256]{1,0:T(8,128)} %shard_map.59), channel_id=1, source_target_pairs={{0,2},{1,3},{2,0},{3,1},{4,6},{5,7},{6,4},{7,5},{8,10},{9,11},{10,... | collective-permute-start | bytes 811016 | tf_op jit(solution)/shard_map/ppermute | solution.py:187
  69.1 5.8 %collective-permute-start.2 = (f32[264,256]{1,0:T(8,128)}, f32[264,256]{1,0:T(8,128)}, u32[]{:S(2)}, u32[]{:S(2)}) collective-permute-start(f32[264,256]{1,0:T(8,128)} %shard_map.60), channel_id=1, source_target_pairs={{0,3},{1,0},{2,1},{3,2},{4,7},{5,4},{6,5},{7,6},{8,11},{9,8},{10,9... | collective-permute-start | bytes 811016 | tf_op jit(solution)/shard_map/ppermute | solution.py:187
  74.0 0.7 copy-start.3

commit v13 on v12

--- a/solution.py
+++ b/solution.py
@@ -72,7 +72,8 @@
 
 
 def assign_kernel(
-    rot_ref, v_ref, r_ref, parts_ref, base_ref, f_hbm, out_ref, f_ref, sem, *, scale
+    at_ref, v_ref, r_ref, parts_ref, base_ref, f_hbm, out_ref, f_ref, sem, s_ref, p_ref, stat_ref,
+    *, scale, step
 ):
     fetch = pltpu.make_async_copy(f_hbm, f_ref, sem)
     fetch.start()
@@ -80,19 +81,25 @@
     scores = lax.dot_general(
         v_ref[...], r_ref[...], (((1,), (1,)), ((), ())), preferred_element_type=jnp.float32
     )
-    logits = scores * scale + demand
-    top = jnp.max(logits, axis=1, keepdims=True)
-    powers = jnp.exp(logits - top)
-    mass = jnp.sum(powers, axis=1, keepdims=True)
+    s_ref[...] = scores * scale + demand
+
+    def block(k, carry):
+        start = pl.multiple_of(k * step, step)
+        logits = s_ref[pl.ds(start, step), :]
+        top = jnp.max(logits, axis=1, keepdims=True)
+        powers = jnp.exp(logits - top)
+        mass = jnp.sum(powers, axis=1, keepdims=True)
+        p_ref[pl.ds(start, step), :] = powers.astype(jnp.bfloat16)
+        lane = lax.broadcasted_iota(jnp.int32, (step, 128), 1)
+        stat_ref[pl.ds(start, step), :] = jnp.where(lane == 0, mass, jnp.where(lane == 1, top, 0.0))
+        return carry
+
+    lax.fori_loop(0, s_ref.shape[0] // step, block, 0)
     feat = f_ref.shape[1]
     fetch.wait()
-    block_feat = jnp.dot(
-        powers.astype(jnp.bfloat16), f_ref[...], preferred_element_type=jnp.float32
-    )
+    block_feat = jnp.dot(p_ref[...], f_ref[...], preferred_element_type=jnp.float32)
     out_ref[:feat, :] = block_feat.T
-    lane = lax.broadcasted_iota(jnp.int32, (top.shape[0], 128), 1)
-    extra = jnp.where(lane == 0, mass, jnp.where(lane == 1, top, 0.0))
-    out_ref[feat:, :] = extra.T[:8, :]
+    out_ref[feat:, :] = stat_ref[...].T[:8, :]
 
 
 def assign_chunk(v, r, parts, base, f, scale, chunk, index):
@@ -109,10 +116,16 @@
             pl.BlockSpec(memory_space=pl.ANY),
         ],
         out_specs=pl.BlockSpec((feat + 8, chunk), lambda i, at: (0, 0)),
-        scratch_shapes=[pltpu.VMEM((cols, feat), f.dtype), pltpu.SemaphoreType.DMA(())],
+        scratch_shapes=[
+            pltpu.VMEM((cols, feat), f.dtype),
+            pltpu.SemaphoreType.DMA(()),
+            pltpu.VMEM((chunk, cols), jnp.float32),
+            pltpu.VMEM((chunk, cols), jnp.bfloat16),
+            pltpu.VMEM((chunk, 128), jnp.float32),
+        ],
     )
     return pl.pallas_call(
-        functools.partial(assign_kernel, scale=scale),
+        functools.partial(assign_kernel, scale=scale, step=16),
         out_shape=jax.ShapeDtypeStruct((feat + 8, chunk), jnp.float32),
         grid_spec=grid_spec,
         compiler_params=pltpu.CompilerParams(vmem_limit_bytes=24 * 1024 * 1024),

time: 77.7 us -> 87.9 us (1.13)
  Pallas kernels: 33.8 us -> 44.8 us
    pallas_call x4, Pallas kernels: 15.9 us -> 26.9 us  [assign_chunk(): pl.pallas_call(functools.partial(assign_kernel, scale=scale, step=16), ou...]
  transfers between devices with their start and end apart: 4 -> 4, of which waited for: 2 -> 1; matrix products, arithmetic and copies ran while one was open for 0% -> 0% of each run, Pallas kernels for 15% -> 23%
where the time goes in v13:
time: 87.9 us; the launch traced here: 87.6 us
  Pallas kernels  44.8 us (51%)
  blocking collectives  25.9 us (29%)
  waiting for transfers between devices  7.66 us (9%)
  starting transfers between devices  6.51 us (7%)
  local copies, waits for them, and re-layouts  2.59 us (3%)
    pallas_call x4, Pallas kernels, assign_chunk(): pl.pallas_call(functools.partial(assign_kernel, scale=scale, step=16), ou...  26.9 us
    pallas_call x3, Pallas kernels, lse_over_rows(): pl.pallas_call(functools.partial(lse_kernel, scale=scale, shifted=shifted...  15.8 us
    all_to_all x1, blocking collectives, exchange(): return lax.all_to_all(block, 'veh', 0, 0, tiled=True)  13.1 us
    all_to_all x1, waiting for transfers between devices, exchange(): return lax.all_to_all(block, 'veh', 0, 0, tiled=True)  7.65 us
    all_gather x1, blocking collectives, local(): own_rows = lax.all_gather(vehicle_emb, 'req', axis=0, tiled=True)  7.42 us
    all_gather x1, blocking collectives, local(): row_parts = lax.all_gather(partial[0], 'req', axis=0, tiled=False)  5.37 us
    all_to_all x1, starting transfers between devices, exchange(): return lax.all_to_all(block, 'veh', 0, 0, tiled=True)  3.37 us
    ppermute x3, starting transfers between devices, local(): lax.ppermute(piece, 'req', [(i, (i + step) % owners) for i in range(owner...  3.14 us
  transfers between devices with their start and end apart: 4, of which 1 were waited for; matrix products, arithmetic and copies ran while one was open for 0% of the time, Pallas kernels for 23%

profile of v13, /device:TPU:0, one launch (start us, length us, event | category | flops | bytes accessed | tf_op | source)
XLA Modules:
  0.0 87.6 jit_solution(16365905225648398018)
XLA Ops:
  0.0 7.4 %all_gather.6.refs_0_.refs_3_.v_ref = bf16[1024,128]{1,0:T(8,128)(2,1)S(1)} all-gather(bf16[256,128]{1,0:T(8,128)(2,1)} %param.5), channel_id=1, replica_groups=mesh['veh'=8,'req'=4] {'req'}, dimensions={0}, use_global_device_ids=true | all-gather | bytes 327680 | tf_op jit(solution)/shard_map/all_gather | solution.py:174
  7.4 1.2 %copy-done.1 = bf16[4096,128]{1,0:T(8,128)(2,1)S(1)} copy-done((bf16[4096,128]{1,0:T(8,128)(2,1)S(1)}, bf16[4096,128]{1,0:T(8,128)(2,1)}, u32[]{:S(2)}) %copy-start.1) | copy-done | bytes 1048600
  8.6 5.1 %shard_map.55 = f32[8,1,4096]{2,1,0:T(1,128)S(1)} custom-call(bf16[1024,128]{1,0:T(8,128)(2,1)S(1)} %all_gather.6.refs_0_.refs_3_.v_ref, bf16[4096,128]{1,0:T(8,128)(2,1)S(1)} %copy-done.1), custom_call_target="tpu_custom_call" | custom-call | flops 1094713344 | bytes 1445888 | tf_op jit(solution)/shard_map/pallas_call | solution.py:58
  13.7 13.1 %all_to_all.10.refs_1_ = f32[8,1,4096]{2,1,0:T(1,128)S(1)} all-to-all(f32[8,1,4096]{2,1,0:T(1,128)S(1)} %shard_map.55), channel_id=1, replica_groups=mesh['veh'=8,'req'=4] {'veh'}, dimensions={0} | all-to-all | bytes 262144 | tf_op jit(solution)/shard_map/all_to_all | solution.py:180
  26.9 0.0 copy-done.2
  26.9 5.7 %shard_map.56 = f32[1,1,1024]{2,1,0:T(1,128)S(1)} custom-call(bf16[4096,128]{1,0:T(8,128)(2,1)S(1)} %copy-done.2, f32[8,1,4096]{2,1,0:T(1,128)S(1)} %all_to_all.10.refs_1_, f32[1,4096]{1,0:T(1,128)S(1)} %bitcast.6, bf16[1024,128]{1,0:T(8,128)(2,1)S(1)} %all_gather.6.refs_0_.refs_3_.v_ref), custom_call_target="tpu_custom_call" | custom-call | flops 1094713344 | bytes 1331200 | tf_op jit(solution)/shard_map/pallas_call | solution.py:58
  32.6 5.4 %all_gather.7.refs_1_ = f32[4,1,1024]{2,1,0:T(1,128)S(1)} all-gather(f32[1,1,1024]{2,1,0:T(1,128)S(1)} %shard_map.56), channel_id=1, replica_groups=mesh['veh'=8,'req'=4] {'req'}, dimensions={0}, use_global_device_ids=true | all-gather | bytes 20480 | tf_op jit(solution)/shard_map/all_gather | solution.py:184
  37.9 5.0 %shard_map.57 = f32[8,1,4096]{2,1,0:T(1,128)S(1)} custom-call(bf16[1024,128]{1,0:T(8,128)(2,1)S(1)} %all_gather.6.refs_0_.refs_3_.v_ref, f32[4,1,1024]{2,1,0:T(1,128)S(1)} %all_gather.7.refs_1_, f32[1,1024]{1,0:T(1,128)S(1)} %bitcast.11, bf16[4096,128]{1,0:T(8,128)(2,1)S(1)} %copy-done.2), custom_call_target="tpu_custom_call" | custom-call | flops 1094713344 | bytes 1445888 | tf_op jit(solution)/shard_map/pallas_call | solution.py:58
  43.0 0.0 copy-start.5
  43.0 0.7 copy-done.5
  43.7 3.4 %all-to-all-start.1 = ((f32[8,1,4096]{2,1,0:T(1,128)}), f32[8,1,4096]{2,1,0:T(1,128)S(1)}, u32[]{:S(2)}, u32[]{:S(2)}) async-start(f32[8,1,4096]{2,1,0:T(1,128)} %copy-done.5), calls=%async_computation.1 | async-start | bytes 262144 | tf_op jit(solution)/shard_map/all_to_all | solution.py:180
  47.1 7.6 %all-to-all-done.1.parts_ref = f32[8,1,4096]{2,1,0:T(1,128)S(1)} async-done(((f32[8,1,4096]{2,1,0:T(1,128)}), f32[8,1,4096]{2,1,0:T(1,128)S(1)}, u32[]{:S(2)}, u32[]{:S(2)}) %all-to-all-start.1) | async-done | bytes 131104 | tf_op jit(solution)/shard_map/all_to_all | solution.py:180
  54.7 6.9 %shard_map.58 = f32[264,256]{1,0:T(8,128)} custom-call(s32[1]{0:T(128)} %bitcast.at_ref, bf16[1024,128]{1,0:T(8,128)(2,1)S(1)} %all_gather.6.refs_0_.refs_3_.v_ref, bf16[4096,128]{1,0:T(8,128)(2,1)S(1)} %copy-done.2, f32[8,1,4096]{2,1,0:T(1,128)S(1)} %all-to-all-done.1.parts_ref, f32[1,4096]{1,0:T(1,128)S(1)} %bitcast.7, bf16[4096,256]{1,0:T(8,128)(2,1)S(1)} %copy-done), custom_call_target="tpu_custom_call" | custom-call | flops 810549248 | bytes 3481600 | tf_op jit(solution)/shard_map/pallas_call | solution.py:127
  61.6 0.1 collective-permute-start
  61.7 6.9 %shard_map.59 = f32[264,256]{1,0:T(8,128)} custom-call(s32[1]{0:T(128)} %bitcast.3.at_ref, bf16[1024,128]{1,0:T(8,128)(2,1)S(1)} %all_gather.6.refs_0_.refs_3_.v_ref, bf16[4096,128]{1,0:T(8,128)(2,1)S(1)} %copy-done.2, f32[8,1,4096]{2,1,0:T(1,128)S(1)} %all-to-all-done.1.parts_ref, f32[1,4096]{1,0:T(1,128)S(1)} %bitcast.8, bf16[4096,256]{1,0:T(8,128)(2,1)S(1)} %copy-done), custom_call_target="tpu_custom_call" | custom-call | flops 810549248 | bytes 3481600 | tf_op jit(solution)/shard_map/pallas_call | solution.py:127
  68.6 1.6 %collective-permute-start.1 = (f32[264,256]{1,0:T(8,128)}, f32[264,256]{1,0:T(8,128)}, u32[]{:S(2)}, u32[]{:S(2)}) collective-permute-start(f32[264,256]{1,0:T(8,128)} %shard_map.59), channel_id=1, source_target_pairs={{0,2},{1,3},{2,0},{3,1},{4,6},{5,7},{6,4},{7,5},{8,10},{9,11},{10,... | collective-permute-start | bytes 811016 | tf_op jit(solution)/shard_map/ppermute | solution.py:200
  70.2 6.9 %shard_map.60 = f32[264,256]{1,0:T(8,128)} custom-call(s32[1]{0:T(128)} %bitcast.4.at_ref, bf16[1024,128]{1,0:T(8,128)(2,1)S(1)} %all_gather.6.refs_0_.refs_3_.v_ref, bf16[4096,128]{1,0:T(8,128)(2,1)S(1)} %copy-done.2, f32[8,1,4096]{2,1,0:T(1,128)S(1)} %all-to-all-done.1.parts_ref, f32[1,4096]{1,0:T(1,128)S(1)} %bitcast.9, bf16[4096,256]{1,0:T(8,128)(2,1)S(1)} %copy-done), custom_call_target="tpu_custom_call" | custom-call | flops 810549248 | bytes 3481600 | tf_op jit(solution)/shard_map/pallas_call | solution.py:127
  77.1 1.5 %collective-permute-start.2 = (f32[264,256]{1,0:T(8,128)}, f32[264,256]{1,0:T(8,128)}, u32[]{:S(2)}, u32[]{:S(2)}) collective-permute-start(f32[264,256]{1,0:T(8,128)} %shard_map.60), channel_id=1, source_target_pairs={{0,3},{1,0},{2,1},{3,2},{4,7},{5,4},{6,5},{7,6},{8,11},{9,8},{10,9... | collective-permute-start | bytes 811016 | tf_op jit(solution)/shard_map/ppermute | solution.py:200
  78.6 6.2 %shard_map.61.refs_3_ = f32[264,256]{1,0:T(8,128)S(1)} custom-call(s32[1]{0:T(128)} %bitcast.5.at_ref, bf16[1024,128]{1,0:T(8,128)(2,1)S(1)} %all_gather.6.refs_0_.refs_3_.v_ref, bf16[4096,128]{1,0:T(8,128)(2,1)S(1)} %copy-done.2, f32[8,1,4096]{2,1,0:T(1,128)S(1)} %all-to-all-done.1.parts_ref, f32[1,4096]{1,0:T(1,128)S(1)} %bitcast.10, ...), custom_call_target="tpu_custom_call" | custom-call | flops 810549248 | bytes 3481600 | tf_op jit(solution)/shard_map/pallas_call | solution.py:127
  84.8 0.7 copy-done.3
  85.5 0.0 collective-permute-done.refs_0_
  85.5 0.0 collective-permute-done.1.refs_1_
  85.5 0.0 collective-permute-done.2.refs_2_
  85.6 2.1 %shard_map.62 = f32[256,256]{1,0:T(8,128)} custom-call(f32[264,256]{1,0:T(8,128)} %collective-permute-done.refs_0_, f32[264,256]{1,0:T(8,128)} %collective-permute-done.1.refs_1_, f32[264,256]{1,0:T(8,128)} %collective-permute-done.2.refs_2_, f32[264,256]{1,0:T(8,128)} %copy-done.3), custom_call_target="tpu_custom_call" | custom-call | flops 786432 | bytes 1343488 | tf_op jit(solution)/shard_map/pallas_call | solution.py:160
  (9 shorter events, 0.0 us)
Async XLA Ops:
  7.4 1.2 %copy-start.1 = (bf16[4096,128]{1,0:T(8,128)(2,1)S(1)}, bf16[4096,128]{1,0:T(8,128)(2,1)}, u32[]{:S(2)}) copy-start(bf16[4096,128]{1,0:T(8,128)(2,1)} %r_ref.7) | copy-start | bytes 3145732
  8.6 18.2 %copy-start.2 = (bf16[4096,128]{1,0:T(8,128)(2,1)S(1)}, bf16[4096,128]{1,0:T(8,128)(2,1)}, u32[]{:S(2)}) copy-start(bf16[4096,128]{1,0:T(8,128)(2,1)} %r_ref.7) | copy-start | bytes 3145732
  8.6 18.2 %copy-start.4 = (f32[4096]{0:T(1024)S(1)}, f32[4096]{0:T(1024)}, u32[]{:S(2)}) copy-start(f32[4096]{0:T(1024)} %param.9) | copy-start | bytes 49156
  26.9 11.1 %copy-start.6 = (f32[1024]{0:T(1024)S(1)}, f32[1024]{0:T(1024)}, u32[]{:S(2)}) copy-start(f32[1024]{0:T(1024)} %param.8) | copy-start | bytes 12292
  37.9 16.8 %copy-start = (bf16[4096,256]{1,0:T(8,128)(2,1)S(1)}, bf16[4096,256]{1,0:T(8,128)(2,1)}, u32[]{:S(2)}) copy-start(bf16[4096,256]{1,0:T(8,128)(2,1)} %f_hbm.7) | copy-start | bytes 6291460
  43.0 0.7 copy-start.5
  43.7 11.1 %all-to-all-start.1 = ((f32[8,1,4096]{2,1,0:T(1,128)}), f32[8,1,4096]{2,1,0:T(1,128)S(1)}, u32[]{:S(2)}, u32[]{:S(2)}) async-start(f32[8,1,4096]{2,1,0:T(1,128)} %copy-done.5), calls=%async_computation.1 | async-start | bytes 262144 | tf_op jit(solution)/shard_map/all_to_all | solution.py:180
  61.6 23.9 %collective-permute-start = (f32[264,256]{1,0:T(8,128)}, f32[264,256]{1,0:T(8,128)}, u32[]{:S(2)}, u32[]{:S(2)}) collective-permute-start(f32[264,256]{1,0:T(8,128)} %shard_map.58), channel_id=1, source_target_pairs={{0,1},{1,2},{2,3},{3,0},{4,5},{5,6},{6,7},{7,4},{8,9},{9,10},{10,1... | collective-permute-start | bytes 811016 | tf_op jit(solution)/shard_map/ppermute | solution.py:200
  68.6 16.9 %collective-permute-start.1 = (f32[264,256]{1,0:T(8,128)}, f32[264,256]{1,0:T(8,128)}, u32[]{:S(2)}, u32[]{:S(2)}) collective-permute-start(f32[264,256]{1,0:T(8,128)} %shard_map.59), channel_id=1, source_target_pairs={{0,2},{1,3},{2,0},{3,1},{4,6},{5,7},{6,4},{7,5},{8,10},{9,11},{10,... | collective-permute-start | bytes 811016 | tf_op jit(solution)/shard_map/ppermute | solution.py:200
  77.1 8.4 %collective-permute-start.2 = (f32[264,256]{1,0:T(8,128)}, f32[264,256]{1,0:T(8,128)}, u32[]{:S(2)}, u32[]{:S(2)}) collective-permute-start(f32[264,256]{1,0:T(8,128)} %shard_map.60), channel_id=1, source_target_pairs={{0,3},{1,0},{2,1},{3,2},{4,7},{5,4},{6,5},{7,6},{8,11},{9,8},{10,9... | collective-permute-start | bytes 811016 | tf_op jit(solution)/shard_map/ppermute | solution.py:200
  84.8 0.7 copy-start.3

commit v14 on v12

--- a/solution.py
+++ b/solution.py
@@ -71,6 +71,43 @@
     )(*operands)
 
 
+def row_kernel(a_ref, parts_ref, base_ref, b_ref, out_ref, *, scale):
+    demand = base_ref[...] - merged_lse(parts_ref[...])
+    scores = lax.dot_general(
+        a_ref[...], b_ref[...], (((1,), (1,)), ((), ())), preferred_element_type=jnp.float32
+    )
+    logits = scores * scale + demand
+    top = jnp.max(logits, axis=1, keepdims=True)
+    total = jnp.sum(jnp.exp(logits - top), axis=1, keepdims=True)
+    result = top + jnp.log(total)
+    wide = jnp.broadcast_to(result, (result.shape[0], 128))
+    out_ref[...] = jnp.transpose(wide)[:1, :][None]
+
+
+def row_lse(a, b, scale, tile, vmem_limit, parts, base):
+    rows, width = a.shape
+    cols = b.shape[0]
+    tile = min(tile, rows)
+    return pl.pallas_call(
+        functools.partial(row_kernel, scale=scale),
+        out_shape=jax.ShapeDtypeStruct((1, 1, rows), jnp.float32),
+        grid=(rows // tile,),
+        in_specs=[
+            pl.BlockSpec((tile, width), lambda i: (i, 0)),
+            pl.BlockSpec(parts.shape, lambda i: (0, 0, 0)),
+            pl.BlockSpec((1, cols), lambda i: (0, 0)),
+            pl.BlockSpec((cols, width), lambda i: (0, 0)),
+        ],
+        out_specs=pl.BlockSpec((1, 1, tile), lambda i: (0, 0, i)),
+        compiler_params=pltpu.CompilerParams(vmem_limit_bytes=vmem_limit),
+        cost_estimate=pl.CostEstimate(
+            flops=2 * rows * cols * width + 5 * rows * cols,
+            transcendentals=rows * cols,
+            bytes_accessed=2 * (rows + cols) * width + 4 * (rows + 9 * cols),
+        ),
+    )(a, parts, base.reshape(1, cols), b)
+
+
 def assign_kernel(
     rot_ref, v_ref, r_ref, parts_ref, base_ref, f_hbm, out_ref, f_ref, sem, *, scale
 ):
@@ -144,11 +181,13 @@
 
 def combine(pieces, feat):
     chunk = pieces[0].shape[1]
+    width = min(128, chunk)
     return pl.pallas_call(
         combine_kernel,
         out_shape=jax.ShapeDtypeStruct((chunk, feat), jnp.float32),
-        in_specs=[pl.BlockSpec(piece.shape, lambda: (0, 0)) for piece in pieces],
-        out_specs=pl.BlockSpec((chunk, feat), lambda: (0, 0)),
+        grid=(chunk // width,),
+        in_specs=[pl.BlockSpec((feat + 8, width), lambda j: (0, j)) for piece in pieces],
+        out_specs=pl.BlockSpec((width, feat), lambda j: (j, 0)),
         cost_estimate=pl.CostEstimate(
             flops=3 * len(pieces) * chunk * feat,
             transcendentals=len(pieces) * chunk,
@@ -167,7 +206,7 @@
         return lax.all_to_all(block, "veh", 0, 0, tiled=True)
 
     first = exchange(lse_over_rows(own_rows, request_emb, scale, 4096, spread, 24 << 20))
-    partial = lse_over_rows(request_emb, own_rows, scale, 1024, 1, 48 << 20, first, log_demand)
+    partial = row_lse(own_rows, request_emb, scale, 1024, 48 << 20, first, log_demand)
     row_parts = lax.all_gather(partial[0], "req", axis=0, tiled=False)
     second = exchange(
         lse_over_rows(own_rows, request_emb, scale, 4096, spread, 24 << 20, row_parts, log_supply)

time: 77.7 us -> 77.3 us (level)
    pallas_call x3 -> x2, Pallas kernels: 15.8 us -> 10.1 us  [lse_over_rows(): pl.pallas_call(functools.partial(lse_kernel, scale=scale, shifted=shifted...]
    pallas_call x0 -> x1, Pallas kernels: none -> 5.26 us  [row_lse(): pl.pallas_call(functools.partial(row_kernel, scale=scale), out_shape=jax....]
where the time goes in v14:
time: 77.3 us; the launch traced here: 76.5 us
  Pallas kernels  33.4 us (43%)
  blocking collectives  25.9 us (34%)
  waiting for transfers between devices  7.77 us (10%)
  starting transfers between devices  6.73 us (9%)
  local copies, waits for them, and re-layouts  2.59 us (3%)
    pallas_call x4, Pallas kernels, assign_chunk(): pl.pallas_call(functools.partial(assign_kernel, scale=scale), out_shape=j...  15.9 us
    all_to_all x1, blocking collectives, exchange(): return lax.all_to_all(block, 'veh', 0, 0, tiled=True)  13.1 us
    pallas_call x2, Pallas kernels, lse_over_rows(): pl.pallas_call(functools.partial(lse_kernel, scale=scale, shifted=shifted...  10.1 us
    all_to_all x1, waiting for transfers between devices, exchange(): return lax.all_to_all(block, 'veh', 0, 0, tiled=True)  7.63 us
    all_gather x1, blocking collectives, local(): own_rows = lax.all_gather(vehicle_emb, 'req', axis=0, tiled=True)  7.42 us
    all_gather x1, blocking collectives, local(): row_parts = lax.all_gather(partial[0], 'req', axis=0, tiled=False)  5.38 us
    pallas_call x1, Pallas kernels, row_lse(): pl.pallas_call(functools.partial(row_kernel, scale=scale), out_shape=jax....  5.26 us
    all_to_all x1, starting transfers between devices, exchange(): return lax.all_to_all(block, 'veh', 0, 0, tiled=True)  3.37 us
  transfers between devices with their start and end apart: 4, of which 2 were waited for; matrix products, arithmetic and copies ran while one was open for 0% of the time, Pallas kernels for 15%

profile of v14, /device:TPU:0, one launch (start us, length us, event | category | flops | bytes accessed | tf_op | source)
XLA Modules:
  0.0 76.5 jit_solution(2043707804421252802)
XLA Ops:
  0.0 7.4 %all_gather.6.refs_0_.a_ref.v_ref = bf16[1024,128]{1,0:T(8,128)(2,1)S(1)} all-gather(bf16[256,128]{1,0:T(8,128)(2,1)} %param.5), channel_id=1, replica_groups=mesh['veh'=8,'req'=4] {'req'}, dimensions={0}, use_global_device_ids=true | all-gather | bytes 327680 | tf_op jit(solution)/shard_map/all_gather | solution.py:200
  7.4 1.2 %copy-done.1 = bf16[4096,128]{1,0:T(8,128)(2,1)S(1)} copy-done((bf16[4096,128]{1,0:T(8,128)(2,1)S(1)}, bf16[4096,128]{1,0:T(8,128)(2,1)}, u32[]{:S(2)}) %copy-start.1) | copy-done | bytes 1048600
  8.6 5.1 %shard_map.55 = f32[8,1,4096]{2,1,0:T(1,128)S(1)} custom-call(bf16[1024,128]{1,0:T(8,128)(2,1)S(1)} %all_gather.6.refs_0_.a_ref.v_ref, bf16[4096,128]{1,0:T(8,128)(2,1)S(1)} %copy-done.1), custom_call_target="tpu_custom_call" | custom-call | flops 1094713344 | bytes 1445888 | tf_op jit(solution)/shard_map/pallas_call | solution.py:58
  13.7 13.1 %all_to_all.10.parts_ref = f32[8,1,4096]{2,1,0:T(1,128)S(1)} all-to-all(f32[8,1,4096]{2,1,0:T(1,128)S(1)} %shard_map.55), channel_id=1, replica_groups=mesh['veh'=8,'req'=4] {'veh'}, dimensions={0} | all-to-all | bytes 262144 | tf_op jit(solution)/shard_map/all_to_all | solution.py:206
  26.9 5.3 %shard_map.56 = f32[1,1,1024]{2,1,0:T(1,128)S(1)} custom-call(bf16[1024,128]{1,0:T(8,128)(2,1)S(1)} %all_gather.6.refs_0_.a_ref.v_ref, f32[8,1,4096]{2,1,0:T(1,128)S(1)} %all_to_all.10.parts_ref, f32[1,4096]{1,0:T(1,128)S(1)} %bitcast.6, bf16[4096,128]{1,0:T(8,128)(2,1)S(1)} %copy-done.2), custom_call_target="tpu_custom_call" | custom-call | flops 1094713344 | bytes 1462272 | tf_op jit(solution)/shard_map/pallas_call | solution.py:91
  32.1 5.4 %all_gather.7.refs_1_ = f32[4,1,1024]{2,1,0:T(1,128)S(1)} all-gather(f32[1,1,1024]{2,1,0:T(1,128)S(1)} %shard_map.56), channel_id=1, replica_groups=mesh['veh'=8,'req'=4] {'req'}, dimensions={0}, use_global_device_ids=true | all-gather | bytes 20480 | tf_op jit(solution)/shard_map/all_gather | solution.py:210
  37.5 0.0 copy-done.6
  37.5 5.1 %shard_map.57 = f32[8,1,4096]{2,1,0:T(1,128)S(1)} custom-call(bf16[1024,128]{1,0:T(8,128)(2,1)S(1)} %all_gather.6.refs_0_.a_ref.v_ref, f32[4,1,1024]{2,1,0:T(1,128)S(1)} %all_gather.7.refs_1_, f32[1,1024]{1,0:T(1,128)S(1)} %bitcast.11, bf16[4096,128]{1,0:T(8,128)(2,1)S(1)} %copy-done.2), custom_call_target="tpu_custom_call" | custom-call | flops 1094713344 | bytes 1445888 | tf_op jit(solution)/shard_map/pallas_call | solution.py:58
  42.6 0.0 copy-start.5
  42.6 0.7 copy-done.5
  43.2 3.4 %all-to-all-start.1 = ((f32[8,1,4096]{2,1,0:T(1,128)}), f32[8,1,4096]{2,1,0:T(1,128)S(1)}, u32[]{:S(2)}, u32[]{:S(2)}) async-start(f32[8,1,4096]{2,1,0:T(1,128)} %copy-done.5), calls=%async_computation.1 | async-start | bytes 262144 | tf_op jit(solution)/shard_map/all_to_all | solution.py:206
  46.6 7.6 %all-to-all-done.1.parts_ref = f32[8,1,4096]{2,1,0:T(1,128)S(1)} async-done(((f32[8,1,4096]{2,1,0:T(1,128)}), f32[8,1,4096]{2,1,0:T(1,128)S(1)}, u32[]{:S(2)}, u32[]{:S(2)}) %all-to-all-start.1) | async-done | bytes 131104 | tf_op jit(solution)/shard_map/all_to_all | solution.py:206
  54.3 4.2 %shard_map.58 = f32[264,256]{1,0:T(8,128)} custom-call(s32[1]{0:T(128)} %bitcast.rot_ref, bf16[1024,128]{1,0:T(8,128)(2,1)S(1)} %all_gather.6.refs_0_.a_ref.v_ref, bf16[4096,128]{1,0:T(8,128)(2,1)S(1)} %copy-done.2, f32[8,1,4096]{2,1,0:T(1,128)S(1)} %all-to-all-done.1.parts_ref, f32[1,4096]{1,0:T(1,128)S(1)} %bitcast.7, bf16[4096,256]{1,0:T(8,128)(2,1)S(1)} %copy-done), custom_call_target="tpu_custom_call" | custom-call | flops 810549248 | bytes 3481600 | tf_op jit(solution)/shard_map/pallas_call | solution.py:151
  58.4 0.3 collective-permute-start
  58.7 4.2 %shard_map.59 = f32[264,256]{1,0:T(8,128)} custom-call(s32[1]{0:T(128)} %bitcast.3.rot_ref, bf16[1024,128]{1,0:T(8,128)(2,1)S(1)} %all_gather.6.refs_0_.a_ref.v_ref, bf16[4096,128]{1,0:T(8,128)(2,1)S(1)} %copy-done.2, f32[8,1,4096]{2,1,0:T(1,128)S(1)} %all-to-all-done.1.parts_ref, f32[1,4096]{1,0:T(1,128)S(1)} %bitcast.8, bf16[4096,256]{1,0:T(8,128)(2,1)S(1)} %copy-done), custom_call_target="tpu_custom_call" | custom-call | flops 810549248 | bytes 3481600 | tf_op jit(solution)/shard_map/pallas_call | solution.py:151
  62.9 1.6 %collective-permute-start.1 = (f32[264,256]{1,0:T(8,128)}, f32[264,256]{1,0:T(8,128)}, u32[]{:S(2)}, u32[]{:S(2)}) collective-permute-start(f32[264,256]{1,0:T(8,128)} %shard_map.59), channel_id=1, source_target_pairs={{0,2},{1,3},{2,0},{3,1},{4,6},{5,7},{6,4},{7,5},{8,10},{9,11},{10,... | collective-permute-start | bytes 811016 | tf_op jit(solution)/shard_map/ppermute | solution.py:226
  64.5 4.1 %shard_map.60 = f32[264,256]{1,0:T(8,128)} custom-call(s32[1]{0:T(128)} %bitcast.4.rot_ref, bf16[1024,128]{1,0:T(8,128)(2,1)S(1)} %all_gather.6.refs_0_.a_ref.v_ref, bf16[4096,128]{1,0:T(8,128)(2,1)S(1)} %copy-done.2, f32[8,1,4096]{2,1,0:T(1,128)S(1)} %all-to-all-done.1.parts_ref, f32[1,4096]{1,0:T(1,128)S(1)} %bitcast.9, bf16[4096,256]{1,0:T(8,128)(2,1)S(1)} %copy-done), custom_call_target="tpu_custom_call" | custom-call | flops 810549248 | bytes 3481600 | tf_op jit(solution)/shard_map/pallas_call | solution.py:151
  68.6 1.5 %collective-permute-start.2 = (f32[264,256]{1,0:T(8,128)}, f32[264,256]{1,0:T(8,128)}, u32[]{:S(2)}, u32[]{:S(2)}) collective-permute-start(f32[264,256]{1,0:T(8,128)} %shard_map.60), channel_id=1, source_target_pairs={{0,3},{1,0},{2,1},{3,2},{4,7},{5,4},{6,5},{7,6},{8,11},{9,8},{10,9... | collective-permute-start | bytes 811016 | tf_op jit(solution)/shard_map/ppermute | solution.py:226
  70.1 3.4 %shard_map.61.refs_3_ = f32[264,256]{1,0:T(8,128)S(1)} custom-call(s32[1]{0:T(128)} %bitcast.5.rot_ref, bf16[1024,128]{1,0:T(8,128)(2,1)S(1)} %all_gather.6.refs_0_.a_ref.v_ref, bf16[4096,128]{1,0:T(8,128)(2,1)S(1)} %copy-done.2, f32[8,1,4096]{2,1,0:T(1,128)S(1)} %all-to-all-done.1.parts_ref, f32[1,4096]{1,0:T(1,128)S(1)} %bitcast.10, ...), custom_call_target="tpu_custom_call" | custom-call | flops 810549248 | bytes 3481600 | tf_op jit(solution)/shard_map/pallas_call | solution.py:151
  73.6 0.7 copy-done.3
  74.3 0.0 collective-permute-done.refs_0_
  74.3 0.0 collective-permute-done.1.refs_1_
  74.3 0.1 collective-permute-done.2.refs_2_
  74.4 2.1 %shard_map.62 = f32[256,256]{1,0:T(8,128)} custom-call(f32[264,256]{1,0:T(8,128)} %collective-permute-done.refs_0_, f32[264,256]{1,0:T(8,128)} %collective-permute-done.1.refs_1_, f32[264,256]{1,0:T(8,128)} %collective-permute-done.2.refs_2_, f32[264,256]{1,0:T(8,128)} %copy-done.3), custom_call_target="tpu_custom_call" | custom-call | flops 786432 | bytes 1343488 | tf_op jit(solution)/shard_map/pallas_call | solution.py:185
  (9 shorter events, 0.0 us)
Async XLA Ops:
  7.4 1.2 %copy-start.1 = (bf16[4096,128]{1,0:T(8,128)(2,1)S(1)}, bf16[4096,128]{1,0:T(8,128)(2,1)}, u32[]{:S(2)}) copy-start(bf16[4096,128]{1,0:T(8,128)(2,1)} %r_ref.7) | copy-start | bytes 3145732
  8.6 18.2 %copy-start.2 = (bf16[4096,128]{1,0:T(8,128)(2,1)S(1)}, bf16[4096,128]{1,0:T(8,128)(2,1)}, u32[]{:S(2)}) copy-start(bf16[4096,128]{1,0:T(8,128)(2,1)} %r_ref.7) | copy-start | bytes 3145732
  8.6 18.2 %copy-start.4 = (f32[4096]{0:T(1024)S(1)}, f32[4096]{0:T(1024)}, u32[]{:S(2)}) copy-start(f32[4096]{0:T(1024)} %param.9) | copy-start | bytes 49156
  26.9 10.6 %copy-start.6 = (f32[1024]{0:T(1024)S(1)}, f32[1024]{0:T(1024)}, u32[]{:S(2)}) copy-start(f32[1024]{0:T(1024)} %param.8) | copy-start | bytes 12292
  37.5 16.8 %copy-start = (bf16[4096,256]{1,0:T(8,128)(2,1)S(1)}, bf16[4096,256]{1,0:T(8,128)(2,1)}, u32[]{:S(2)}) copy-start(bf16[4096,256]{1,0:T(8,128)(2,1)} %f_hbm.7) | copy-start | bytes 6291460
  42.6 0.7 copy-start.5
  43.2 11.0 %all-to-all-start.1 = ((f32[8,1,4096]{2,1,0:T(1,128)}), f32[8,1,4096]{2,1,0:T(1,128)S(1)}, u32[]{:S(2)}, u32[]{:S(2)}) async-start(f32[8,1,4096]{2,1,0:T(1,128)} %copy-done.5), calls=%async_computation.1 | async-start | bytes 262144 | tf_op jit(solution)/shard_map/all_to_all | solution.py:206
  58.4 15.9 %collective-permute-start = (f32[264,256]{1,0:T(8,128)}, f32[264,256]{1,0:T(8,128)}, u32[]{:S(2)}, u32[]{:S(2)}) collective-permute-start(f32[264,256]{1,0:T(8,128)} %shard_map.58), channel_id=1, source_target_pairs={{0,1},{1,2},{2,3},{3,0},{4,5},{5,6},{6,7},{7,4},{8,9},{9,10},{10,1... | collective-permute-start | bytes 811016 | tf_op jit(solution)/shard_map/ppermute | solution.py:226
  62.9 11.4 %collective-permute-start.1 = (f32[264,256]{1,0:T(8,128)}, f32[264,256]{1,0:T(8,128)}, u32[]{:S(2)}, u32[]{:S(2)}) collective-permute-start(f32[264,256]{1,0:T(8,128)} %shard_map.59), channel_id=1, source_target_pairs={{0,2},{1,3},{2,0},{3,1},{4,6},{5,7},{6,4},{7,5},{8,10},{9,11},{10,... | collective-permute-start | bytes 811016 | tf_op jit(solution)/shard_map/ppermute | solution.py:226
  68.6 5.8 %collective-permute-start.2 = (f32[264,256]{1,0:T(8,128)}, f32[264,256]{1,0:T(8,128)}, u32[]{:S(2)}, u32[]{:S(2)}) collective-permute-start(f32[264,256]{1,0:T(8,128)} %shard_map.60), channel_id=1, source_target_pairs={{0,3},{1,0},{2,1},{3,2},{4,7},{5,4},{6,5},{7,6},{8,11},{9,8},{10,9... | collective-permute-start | bytes 811016 | tf_op jit(solution)/shard_map/ppermute | solution.py:226
  73.6 0.7 copy-start.3

commit v15 on v14

--- a/solution.py
+++ b/solution.py
@@ -206,7 +206,7 @@
         return lax.all_to_all(block, "veh", 0, 0, tiled=True)
 
     first = exchange(lse_over_rows(own_rows, request_emb, scale, 4096, spread, 24 << 20))
-    partial = row_lse(own_rows, request_emb, scale, 1024, 48 << 20, first, log_demand)
+    partial = row_lse(own_rows, request_emb, scale, 512, 48 << 20, first, log_demand)
     row_parts = lax.all_gather(partial[0], "req", axis=0, tiled=False)
     second = exchange(
         lse_over_rows(own_rows, request_emb, scale, 4096, spread, 24 << 20, row_parts, log_supply)

time: 77.3 us -> 77.6 us (level)
  no operation moved by 1% of the time
where the time goes in v15:
time: 77.6 us; the launch traced here: 76.8 us
  Pallas kernels  33.7 us (43%)
  blocking collectives  25.9 us (33%)
  waiting for transfers between devices  7.78 us (10%)
  starting transfers between devices  6.73 us (9%)
  local copies, waits for them, and re-layouts  2.59 us (3%)
    pallas_call x4, Pallas kernels, assign_chunk(): pl.pallas_call(functools.partial(assign_kernel, scale=scale), out_shape=j...  15.9 us
    all_to_all x1, blocking collectives, exchange(): return lax.all_to_all(block, 'veh', 0, 0, tiled=True)  13.1 us
    pallas_call x2, Pallas kernels, lse_over_rows(): pl.pallas_call(functools.partial(lse_kernel, scale=scale, shifted=shifted...  10.1 us
    all_to_all x1, waiting for transfers between devices, exchange(): return lax.all_to_all(block, 'veh', 0, 0, tiled=True)  7.64 us
    all_gather x1, blocking collectives, local(): own_rows = lax.all_gather(vehicle_emb, 'req', axis=0, tiled=True)  7.42 us
    pallas_call x1, Pallas kernels, row_lse(): pl.pallas_call(functools.partial(row_kernel, scale=scale), out_shape=jax....  5.6 us
    all_gather x1, blocking collectives, local(): row_parts = lax.all_gather(partial[0], 'req', axis=0, tiled=False)  5.38 us
    all_to_all x1, starting transfers between devices, exchange(): return lax.all_to_all(block, 'veh', 0, 0, tiled=True)  3.37 us
  transfers between devices with their start and end apart: 4, of which 2 were waited for; matrix products, arithmetic and copies ran while one was open for 0% of the time, Pallas kernels for 15%

profile of v15, /device:TPU:0, one launch (start us, length us, event | category | flops | bytes accessed | tf_op | source)
XLA Modules:
  0.0 76.8 jit_solution(15612936639226969742)
XLA Ops:
  0.0 7.4 %all_gather.6.refs_0_.a_ref.v_ref = bf16[1024,128]{1,0:T(8,128)(2,1)S(1)} all-gather(bf16[256,128]{1,0:T(8,128)(2,1)} %param.5), channel_id=1, replica_groups=mesh['veh'=8,'req'=4] {'req'}, dimensions={0}, use_global_device_ids=true | all-gather | bytes 327680 | tf_op jit(solution)/shard_map/all_gather | solution.py:200
  7.4 1.2 %copy-done.1 = bf16[4096,128]{1,0:T(8,128)(2,1)S(1)} copy-done((bf16[4096,128]{1,0:T(8,128)(2,1)S(1)}, bf16[4096,128]{1,0:T(8,128)(2,1)}, u32[]{:S(2)}) %copy-start.1) | copy-done | bytes 1048600
  8.6 5.1 %shard_map.55 = f32[8,1,4096]{2,1,0:T(1,128)S(1)} custom-call(bf16[1024,128]{1,0:T(8,128)(2,1)S(1)} %all_gather.6.refs_0_.a_ref.v_ref, bf16[4096,128]{1,0:T(8,128)(2,1)S(1)} %copy-done.1), custom_call_target="tpu_custom_call" | custom-call | flops 1094713344 | bytes 1445888 | tf_op jit(solution)/shard_map/pallas_call | solution.py:58
  13.7 13.1 %all_to_all.10.parts_ref = f32[8,1,4096]{2,1,0:T(1,128)S(1)} all-to-all(f32[8,1,4096]{2,1,0:T(1,128)S(1)} %shard_map.55), channel_id=1, replica_groups=mesh['veh'=8,'req'=4] {'veh'}, dimensions={0} | all-to-all | bytes 262144 | tf_op jit(solution)/shard_map/all_to_all | solution.py:206
  26.9 5.6 %shard_map.56 = f32[1,1,1024]{2,1,0:T(1,128)S(1)} custom-call(bf16[1024,128]{1,0:T(8,128)(2,1)S(1)} %all_gather.6.refs_0_.a_ref.v_ref, f32[8,1,4096]{2,1,0:T(1,128)S(1)} %all_to_all.10.parts_ref, f32[1,4096]{1,0:T(1,128)S(1)} %bitcast.6, bf16[4096,128]{1,0:T(8,128)(2,1)S(1)} %copy-done.2), custom_call_target="tpu_custom_call" | custom-call | flops 1094713344 | bytes 1462272 | tf_op jit(solution)/shard_map/pallas_call | solution.py:91
  32.5 5.4 %all_gather.7.refs_1_ = f32[4,1,1024]{2,1,0:T(1,128)S(1)} all-gather(f32[1,1,1024]{2,1,0:T(1,128)S(1)} %shard_map.56), channel_id=1, replica_groups=mesh['veh'=8,'req'=4] {'req'}, dimensions={0}, use_global_device_ids=true | all-gather | bytes 20480 | tf_op jit(solution)/shard_map/all_gather | solution.py:210
  37.8 0.0 copy-done.6
  37.8 5.0 %shard_map.57 = f32[8,1,4096]{2,1,0:T(1,128)S(1)} custom-call(bf16[1024,128]{1,0:T(8,128)(2,1)S(1)} %all_gather.6.refs_0_.a_ref.v_ref, f32[4,1,1024]{2,1,0:T(1,128)S(1)} %all_gather.7.refs_1_, f32[1,1024]{1,0:T(1,128)S(1)} %bitcast.11, bf16[4096,128]{1,0:T(8,128)(2,1)S(1)} %copy-done.2), custom_call_target="tpu_custom_call" | custom-call | flops 1094713344 | bytes 1445888 | tf_op jit(solution)/shard_map/pallas_call | solution.py:58
  42.9 0.0 copy-start.5
  42.9 0.7 copy-done.5
  43.6 3.4 %all-to-all-start.1 = ((f32[8,1,4096]{2,1,0:T(1,128)}), f32[8,1,4096]{2,1,0:T(1,128)S(1)}, u32[]{:S(2)}, u32[]{:S(2)}) async-start(f32[8,1,4096]{2,1,0:T(1,128)} %copy-done.5), calls=%async_computation.1 | async-start | bytes 262144 | tf_op jit(solution)/shard_map/all_to_all | solution.py:206
  47.0 7.6 %all-to-all-done.1.parts_ref = f32[8,1,4096]{2,1,0:T(1,128)S(1)} async-done(((f32[8,1,4096]{2,1,0:T(1,128)}), f32[8,1,4096]{2,1,0:T(1,128)S(1)}, u32[]{:S(2)}, u32[]{:S(2)}) %all-to-all-start.1) | async-done | bytes 131104 | tf_op jit(solution)/shard_map/all_to_all | solution.py:206
  54.6 4.2 %shard_map.58 = f32[264,256]{1,0:T(8,128)} custom-call(s32[1]{0:T(128)} %bitcast.rot_ref, bf16[1024,128]{1,0:T(8,128)(2,1)S(1)} %all_gather.6.refs_0_.a_ref.v_ref, bf16[4096,128]{1,0:T(8,128)(2,1)S(1)} %copy-done.2, f32[8,1,4096]{2,1,0:T(1,128)S(1)} %all-to-all-done.1.parts_ref, f32[1,4096]{1,0:T(1,128)S(1)} %bitcast.7, bf16[4096,256]{1,0:T(8,128)(2,1)S(1)} %copy-done), custom_call_target="tpu_custom_call" | custom-call | flops 810549248 | bytes 3481600 | tf_op jit(solution)/shard_map/pallas_call | solution.py:151
  58.8 0.3 collective-permute-start
  59.1 4.2 %shard_map.59 = f32[264,256]{1,0:T(8,128)} custom-call(s32[1]{0:T(128)} %bitcast.3.rot_ref, bf16[1024,128]{1,0:T(8,128)(2,1)S(1)} %all_gather.6.refs_0_.a_ref.v_ref, bf16[4096,128]{1,0:T(8,128)(2,1)S(1)} %copy-done.2, f32[8,1,4096]{2,1,0:T(1,128)S(1)} %all-to-all-done.1.parts_ref, f32[1,4096]{1,0:T(1,128)S(1)} %bitcast.8, bf16[4096,256]{1,0:T(8,128)(2,1)S(1)} %copy-done), custom_call_target="tpu_custom_call" | custom-call | flops 810549248 | bytes 3481600 | tf_op jit(solution)/shard_map/pallas_call | solution.py:151
  63.2 1.6 %collective-permute-start.1 = (f32[264,256]{1,0:T(8,128)}, f32[264,256]{1,0:T(8,128)}, u32[]{:S(2)}, u32[]{:S(2)}) collective-permute-start(f32[264,256]{1,0:T(8,128)} %shard_map.59), channel_id=1, source_target_pairs={{0,2},{1,3},{2,0},{3,1},{4,6},{5,7},{6,4},{7,5},{8,10},{9,11},{10,... | collective-permute-start | bytes 811016 | tf_op jit(solution)/shard_map/ppermute | solution.py:226
  64.8 4.1 %shard_map.60 = f32[264,256]{1,0:T(8,128)} custom-call(s32[1]{0:T(128)} %bitcast.4.rot_ref, bf16[1024,128]{1,0:T(8,128)(2,1)S(1)} %all_gather.6.refs_0_.a_ref.v_ref, bf16[4096,128]{1,0:T(8,128)(2,1)S(1)} %copy-done.2, f32[8,1,4096]{2,1,0:T(1,128)S(1)} %all-to-all-done.1.parts_ref, f32[1,4096]{1,0:T(1,128)S(1)} %bitcast.9, bf16[4096,256]{1,0:T(8,128)(2,1)S(1)} %copy-done), custom_call_target="tpu_custom_call" | custom-call | flops 810549248 | bytes 3481600 | tf_op jit(solution)/shard_map/pallas_call | solution.py:151
  69.0 1.5 %collective-permute-start.2 = (f32[264,256]{1,0:T(8,128)}, f32[264,256]{1,0:T(8,128)}, u32[]{:S(2)}, u32[]{:S(2)}) collective-permute-start(f32[264,256]{1,0:T(8,128)} %shard_map.60), channel_id=1, source_target_pairs={{0,3},{1,0},{2,1},{3,2},{4,7},{5,4},{6,5},{7,6},{8,11},{9,8},{10,9... | collective-permute-start | bytes 811016 | tf_op jit(solution)/shard_map/ppermute | solution.py:226
  70.5 3.4 %shard_map.61.refs_3_ = f32[264,256]{1,0:T(8,128)S(1)} custom-call(s32[1]{0:T(128)} %bitcast.5.rot_ref, bf16[1024,128]{1,0:T(8,128)(2,1)S(1)} %all_gather.6.refs_0_.a_ref.v_ref, bf16[4096,128]{1,0:T(8,128)(2,1)S(1)} %copy-done.2, f32[8,1,4096]{2,1,0:T(1,128)S(1)} %all-to-all-done.1.parts_ref, f32[1,4096]{1,0:T(1,128)S(1)} %bitcast.10, ...), custom_call_target="tpu_custom_call" | custom-call | flops 810549248 | bytes 3481600 | tf_op jit(solution)/shard_map/pallas_call | solution.py:151
  73.9 0.7 copy-done.3
  74.6 0.0 collective-permute-done.refs_0_
  74.6 0.0 collective-permute-done.1.refs_1_
  74.6 0.1 collective-permute-done.2.refs_2_
  74.8 2.1 %shard_map.62 = f32[256,256]{1,0:T(8,128)} custom-call(f32[264,256]{1,0:T(8,128)} %collective-permute-done.refs_0_, f32[264,256]{1,0:T(8,128)} %collective-permute-done.1.refs_1_, f32[264,256]{1,0:T(8,128)} %collective-permute-done.2.refs_2_, f32[264,256]{1,0:T(8,128)} %copy-done.3), custom_call_target="tpu_custom_call" | custom-call | flops 786432 | bytes 1343488 | tf_op jit(solution)/shard_map/pallas_call | solution.py:185
  (9 shorter events, 0.0 us)
Async XLA Ops:
  7.4 1.2 %copy-start.1 = (bf16[4096,128]{1,0:T(8,128)(2,1)S(1)}, bf16[4096,128]{1,0:T(8,128)(2,1)}, u32[]{:S(2)}) copy-start(bf16[4096,128]{1,0:T(8,128)(2,1)} %r_ref.7) | copy-start | bytes 3145732
  8.6 18.2 %copy-start.2 = (bf16[4096,128]{1,0:T(8,128)(2,1)S(1)}, bf16[4096,128]{1,0:T(8,128)(2,1)}, u32[]{:S(2)}) copy-start(bf16[4096,128]{1,0:T(8,128)(2,1)} %r_ref.7) | copy-start | bytes 3145732
  8.6 18.2 %copy-start.4 = (f32[4096]{0:T(1024)S(1)}, f32[4096]{0:T(1024)}, u32[]{:S(2)}) copy-start(f32[4096]{0:T(1024)} %param.9) | copy-start | bytes 49156
  26.9 11.0 %copy-start.6 = (f32[1024]{0:T(1024)S(1)}, f32[1024]{0:T(1024)}, u32[]{:S(2)}) copy-start(f32[1024]{0:T(1024)} %param.8) | copy-start | bytes 12292
  37.8 16.8 %copy-start = (bf16[4096,256]{1,0:T(8,128)(2,1)S(1)}, bf16[4096,256]{1,0:T(8,128)(2,1)}, u32[]{:S(2)}) copy-start(bf16[4096,256]{1,0:T(8,128)(2,1)} %f_hbm.7) | copy-start | bytes 6291460
  42.9 0.7 copy-start.5
  43.6 11.0 %all-to-all-start.1 = ((f32[8,1,4096]{2,1,0:T(1,128)}), f32[8,1,4096]{2,1,0:T(1,128)S(1)}, u32[]{:S(2)}, u32[]{:S(2)}) async-start(f32[8,1,4096]{2,1,0:T(1,128)} %copy-done.5), calls=%async_computation.1 | async-start | bytes 262144 | tf_op jit(solution)/shard_map/all_to_all | solution.py:206
  58.8 15.9 %collective-permute-start = (f32[264,256]{1,0:T(8,128)}, f32[264,256]{1,0:T(8,128)}, u32[]{:S(2)}, u32[]{:S(2)}) collective-permute-start(f32[264,256]{1,0:T(8,128)} %shard_map.58), channel_id=1, source_target_pairs={{0,1},{1,2},{2,3},{3,0},{4,5},{5,6},{6,7},{7,4},{8,9},{9,10},{10,1... | collective-permute-start | bytes 811016 | tf_op jit(solution)/shard_map/ppermute | solution.py:226
  63.2 11.4 %collective-permute-start.1 = (f32[264,256]{1,0:T(8,128)}, f32[264,256]{1,0:T(8,128)}, u32[]{:S(2)}, u32[]{:S(2)}) collective-permute-start(f32[264,256]{1,0:T(8,128)} %shard_map.59), channel_id=1, source_target_pairs={{0,2},{1,3},{2,0},{3,1},{4,6},{5,7},{6,4},{7,5},{8,10},{9,11},{10,... | collective-permute-start | bytes 811016 | tf_op jit(solution)/shard_map/ppermute | solution.py:226
  69.0 5.8 %collective-permute-start.2 = (f32[264,256]{1,0:T(8,128)}, f32[264,256]{1,0:T(8,128)}, u32[]{:S(2)}, u32[]{:S(2)}) collective-permute-start(f32[264,256]{1,0:T(8,128)} %shard_map.60), channel_id=1, source_target_pairs={{0,3},{1,0},{2,1},{3,2},{4,7},{5,4},{6,5},{7,6},{8,11},{9,8},{10,9... | collective-permute-start | bytes 811016 | tf_op jit(solution)/shard_map/ppermute | solution.py:226
  73.9 0.7 copy-start.3

commit v16 on v14

--- a/solution.py
+++ b/solution.py
@@ -216,14 +216,18 @@
     chunk = row_count // owners
     me = lax.axis_index("req")
     feat = request_feat.shape[1]
+    if owners & (owners - 1) == 0:
+        order = [(step, lambda i, m=step: i ^ m) for step in list(range(2, owners)) + [1]]
+    else:
+        order = [(step, lambda i, m=step: (i + m) % owners) for step in range(1, owners)]
     pieces = []
-    for step in list(range(1, owners)) + [0]:
-        index = jnp.reshape((me + step) % owners, (1,)).astype(jnp.int32)
+    for step, partner in order + [(0, None)]:
+        index = jnp.reshape(partner(me) if step else me, (1,)).astype(jnp.int32)
         piece = assign_chunk(
             own_rows, request_emb, second, log_demand, request_feat, scale, chunk, index
         )
         if step:
-            piece = lax.ppermute(piece, "req", [(i, (i + step) % owners) for i in range(owners)])
+            piece = lax.ppermute(piece, "req", [(i, partner(i)) for i in range(owners)])
         pieces.append(piece)
     return combine(pieces, feat)
 

time: 77.3 us -> 74.9 us (0.969)
  Pallas kernels: 33.4 us -> 31.2 us
  local copies, waits for them, and re-layouts: 2.59 us -> 4.02 us
  starting transfers between devices: 6.73 us -> 5.69 us
    pallas_call x4, Pallas kernels: 15.9 us -> 13.8 us  [assign_chunk(): pl.pallas_call(functools.partial(assign_kernel, scale=scale), out_shape=j...]
    unnamed x14 -> x18, local copies, waits for them, and re-layouts: 2.59 us -> 4.02 us
    ppermute x3, starting transfers between devices: 3.36 us -> 2.32 us  [local(): piece = lax.ppermute(piece, 'req', [(i, partner(i)) for i in range(owners)])]
  transfers between devices with their start and end apart: 4 -> 4, of which waited for: 2 -> 1; matrix products, arithmetic and copies ran while one was open for 0% -> 0% of each run, Pallas kernels for 15% -> 14%
where the time goes in v16:
time: 74.9 us; the launch traced here: 74.6 us
  Pallas kernels  31.2 us (42%)
  blocking collectives  25.9 us (35%)
  waiting for transfers between devices  7.66 us (10%)
  starting transfers between devices  5.69 us (8%)
  local copies, waits for them, and re-layouts  4.02 us (5%)
    pallas_call x4, Pallas kernels, assign_chunk(): pl.pallas_call(functools.partial(assign_kernel, scale=scale), out_shape=j...  13.8 us
    all_to_all x1, blocking collectives, exchange(): return lax.all_to_all(block, 'veh', 0, 0, tiled=True)  13.1 us
    pallas_call x2, Pallas kernels, lse_over_rows(): pl.pallas_call(functools.partial(lse_kernel, scale=scale, shifted=shifted...  10.1 us
    all_to_all x1, waiting for transfers between devices, exchange(): return lax.all_to_all(block, 'veh', 0, 0, tiled=True)  7.65 us
    all_gather x1, blocking collectives, local(): own_rows = lax.all_gather(vehicle_emb, 'req', axis=0, tiled=True)  7.42 us
    all_gather x1, blocking collectives, local(): row_parts = lax.all_gather(partial[0], 'req', axis=0, tiled=False)  5.38 us
    pallas_call x1, Pallas kernels, row_lse(): pl.pallas_call(functools.partial(row_kernel, scale=scale), out_shape=jax....  5.26 us
    unnamed x18, local copies, waits for them, and re-layouts  4.02 us
  transfers between devices with their start and end apart: 4, of which 1 were waited for; matrix products, arithmetic and copies ran while one was open for 0% of the time, Pallas kernels for 14%

profile of v16, /device:TPU:0, one launch (start us, length us, event | category | flops | bytes accessed | tf_op | source)
XLA Modules:
  0.0 74.6 jit_solution(15503521465805184924)
XLA Ops:
  0.0 7.4 %all_gather.6.refs_0_.a_ref.v_ref = bf16[1024,128]{1,0:T(8,128)(2,1)S(1)} all-gather(bf16[256,128]{1,0:T(8,128)(2,1)} %param.5), channel_id=1, replica_groups=mesh['veh'=8,'req'=4] {'req'}, dimensions={0}, use_global_device_ids=true | all-gather | bytes 327680 | tf_op jit(solution)/shard_map/all_gather | solution.py:200
  7.4 1.2 %copy-done.1 = bf16[4096,128]{1,0:T(8,128)(2,1)S(1)} copy-done((bf16[4096,128]{1,0:T(8,128)(2,1)S(1)}, bf16[4096,128]{1,0:T(8,128)(2,1)}, u32[]{:S(2)}) %copy-start.1) | copy-done | bytes 1048600
  8.6 5.1 %shard_map.55 = f32[8,1,4096]{2,1,0:T(1,128)S(1)} custom-call(bf16[1024,128]{1,0:T(8,128)(2,1)S(1)} %all_gather.6.refs_0_.a_ref.v_ref, bf16[4096,128]{1,0:T(8,128)(2,1)S(1)} %copy-done.1), custom_call_target="tpu_custom_call" | custom-call | flops 1094713344 | bytes 1445888 | tf_op jit(solution)/shard_map/pallas_call | solution.py:58
  13.7 13.1 %all_to_all.10.parts_ref = f32[8,1,4096]{2,1,0:T(1,128)S(1)} all-to-all(f32[8,1,4096]{2,1,0:T(1,128)S(1)} %shard_map.55), channel_id=1, replica_groups=mesh['veh'=8,'req'=4] {'veh'}, dimensions={0} | all-to-all | bytes 262144 | tf_op jit(solution)/shard_map/all_to_all | solution.py:206
  26.9 5.3 %shard_map.56 = f32[1,1,1024]{2,1,0:T(1,128)S(1)} custom-call(bf16[1024,128]{1,0:T(8,128)(2,1)S(1)} %all_gather.6.refs_0_.a_ref.v_ref, f32[8,1,4096]{2,1,0:T(1,128)S(1)} %all_to_all.10.parts_ref, f32[1,4096]{1,0:T(1,128)S(1)} %bitcast.6, bf16[4096,128]{1,0:T(8,128)(2,1)S(1)} %copy-done.2), custom_call_target="tpu_custom_call" | custom-call | flops 1094713344 | bytes 1462272 | tf_op jit(solution)/shard_map/pallas_call | solution.py:91
  32.1 5.4 %all_gather.7.refs_1_ = f32[4,1,1024]{2,1,0:T(1,128)S(1)} all-gather(f32[1,1,1024]{2,1,0:T(1,128)S(1)} %shard_map.56), channel_id=1, replica_groups=mesh['veh'=8,'req'=4] {'req'}, dimensions={0}, use_global_device_ids=true | all-gather | bytes 20480 | tf_op jit(solution)/shard_map/all_gather | solution.py:210
  37.5 5.1 %shard_map.57 = f32[8,1,4096]{2,1,0:T(1,128)S(1)} custom-call(bf16[1024,128]{1,0:T(8,128)(2,1)S(1)} %all_gather.6.refs_0_.a_ref.v_ref, f32[4,1,1024]{2,1,0:T(1,128)S(1)} %all_gather.7.refs_1_, f32[1,1024]{1,0:T(1,128)S(1)} %bitcast.11, bf16[4096,128]{1,0:T(8,128)(2,1)S(1)} %copy-done.2), custom_call_target="tpu_custom_call" | custom-call | flops 1094713344 | bytes 1445888 | tf_op jit(solution)/shard_map/pallas_call | solution.py:58
  42.6 0.0 copy-start.5
  42.6 0.7 copy-done.5
  43.2 3.4 %all-to-all-start.1 = ((f32[8,1,4096]{2,1,0:T(1,128)}), f32[8,1,4096]{2,1,0:T(1,128)S(1)}, u32[]{:S(2)}, u32[]{:S(2)}) async-start(f32[8,1,4096]{2,1,0:T(1,128)} %copy-done.5), calls=%async_computation.1 | async-start | bytes 262144 | tf_op jit(solution)/shard_map/all_to_all | solution.py:206
  46.6 7.7 %all-to-all-done.1.parts_ref = f32[8,1,4096]{2,1,0:T(1,128)S(1)} async-done(((f32[8,1,4096]{2,1,0:T(1,128)}), f32[8,1,4096]{2,1,0:T(1,128)S(1)}, u32[]{:S(2)}, u32[]{:S(2)}) %all-to-all-start.1) | async-done | bytes 131104 | tf_op jit(solution)/shard_map/all_to_all | solution.py:206
  54.3 3.4 %shard_map.58 = f32[264,256]{1,0:T(8,128)S(1)} custom-call(s32[1]{0:T(128)} %bitcast.rot_ref, bf16[1024,128]{1,0:T(8,128)(2,1)S(1)} %all_gather.6.refs_0_.a_ref.v_ref, bf16[4096,128]{1,0:T(8,128)(2,1)S(1)} %copy-done.2, f32[8,1,4096]{2,1,0:T(1,128)S(1)} %all-to-all-done.1.parts_ref, f32[1,4096]{1,0:T(1,128)S(1)} %bitcast.7, bf16[4096,256]{1,0:T(8,128)(2,1)S(1)} %copy-done), custom_call_target="tpu_custom_call" | custom-call | flops 810549248 | bytes 3481600 | tf_op jit(solution)/shard_map/pallas_call | solution.py:151
  57.7 1.6 %collective-permute-start = (f32[264,256]{1,0:T(8,128)S(1)}, f32[264,256]{1,0:T(8,128)S(1)}, u32[]{:S(2)}, u32[]{:S(2)}) collective-permute-start(f32[264,256]{1,0:T(8,128)S(1)} %shard_map.58), channel_id=1, source_target_pairs={{0,2},{1,3},{2,0},{3,1},{4,6},{5,7},{6,4},{7,5},{8,10},{9,11},{10,... | collective-permute-start | bytes 811016 | tf_op jit(solution)/shard_map/ppermute | solution.py:230
  59.3 3.4 %shard_map.59 = f32[264,256]{1,0:T(8,128)S(1)} custom-call(s32[1]{0:T(128)} %bitcast.3.rot_ref, bf16[1024,128]{1,0:T(8,128)(2,1)S(1)} %all_gather.6.refs_0_.a_ref.v_ref, bf16[4096,128]{1,0:T(8,128)(2,1)S(1)} %copy-done.2, f32[8,1,4096]{2,1,0:T(1,128)S(1)} %all-to-all-done.1.parts_ref, f32[1,4096]{1,0:T(1,128)S(1)} %bitcast.8, bf16[4096,256]{1,0:T(8,128)(2,1)S(1)} %copy-done), custom_call_target="tpu_custom_call" | custom-call | flops 810549248 | bytes 3481600 | tf_op jit(solution)/shard_map/pallas_call | solution.py:151
  62.7 0.1 collective-permute-start.1
  62.8 3.5 %shard_map.60 = f32[264,256]{1,0:T(8,128)S(1)} custom-call(s32[1]{0:T(128)} %bitcast.4.rot_ref, bf16[1024,128]{1,0:T(8,128)(2,1)S(1)} %all_gather.6.refs_0_.a_ref.v_ref, bf16[4096,128]{1,0:T(8,128)(2,1)S(1)} %copy-done.2, f32[8,1,4096]{2,1,0:T(1,128)S(1)} %all-to-all-done.1.parts_ref, f32[1,4096]{1,0:T(1,128)S(1)} %bitcast.9, bf16[4096,256]{1,0:T(8,128)(2,1)S(1)} %copy-done), custom_call_target="tpu_custom_call" | custom-call | flops 810549248 | bytes 3481600 | tf_op jit(solution)/shard_map/pallas_call | solution.py:151
  66.3 0.7 collective-permute-start.2
  66.9 3.4 %shard_map.61.refs_3_ = f32[264,256]{1,0:T(8,128)S(1)} custom-call(s32[1]{0:T(128)} %bitcast.5.rot_ref, bf16[1024,128]{1,0:T(8,128)(2,1)S(1)} %all_gather.6.refs_0_.a_ref.v_ref, bf16[4096,128]{1,0:T(8,128)(2,1)S(1)} %copy-done.2, f32[8,1,4096]{2,1,0:T(1,128)S(1)} %all-to-all-done.1.parts_ref, f32[1,4096]{1,0:T(1,128)S(1)} %bitcast.10, ...), custom_call_target="tpu_custom_call" | custom-call | flops 810549248 | bytes 3481600 | tf_op jit(solution)/shard_map/pallas_call | solution.py:151
  70.4 0.7 copy-done.3
  71.1 0.0 collective-permute-done.refs_0_
  71.1 0.7 copy-done.7
  71.8 0.7 copy-done.8
  72.5 0.0 collective-permute-done.2.refs_2_
  72.5 2.1 %shard_map.62 = f32[256,256]{1,0:T(8,128)} custom-call(f32[264,256]{1,0:T(8,128)} %copy-done.7, f32[264,256]{1,0:T(8,128)} %copy-done.8, f32[264,256]{1,0:T(8,128)} %collective-permute-done.2.refs_2_, f32[264,256]{1,0:T(8,128)} %copy-done.3), custom_call_target="tpu_custom_call" | custom-call | flops 786432 | bytes 1343488 | tf_op jit(solution)/shard_map/pallas_call | solution.py:185
  (13 shorter events, 0.0 us)
Async XLA Ops:
  7.4 1.2 %copy-start.1 = (bf16[4096,128]{1,0:T(8,128)(2,1)S(1)}, bf16[4096,128]{1,0:T(8,128)(2,1)}, u32[]{:S(2)}) copy-start(bf16[4096,128]{1,0:T(8,128)(2,1)} %r_ref.7) | copy-start | bytes 3145732
  8.6 18.2 %copy-start.2 = (bf16[4096,128]{1,0:T(8,128)(2,1)S(1)}, bf16[4096,128]{1,0:T(8,128)(2,1)}, u32[]{:S(2)}) copy-start(bf16[4096,128]{1,0:T(8,128)(2,1)} %r_ref.7) | copy-start | bytes 3145732
  8.6 18.2 %copy-start.4 = (f32[4096]{0:T(1024)S(1)}, f32[4096]{0:T(1024)}, u32[]{:S(2)}) copy-start(f32[4096]{0:T(1024)} %param.9) | copy-start | bytes 49156
  26.9 10.6 %copy-start.6 = (f32[1024]{0:T(1024)S(1)}, f32[1024]{0:T(1024)}, u32[]{:S(2)}) copy-start(f32[1024]{0:T(1024)} %param.8) | copy-start | bytes 12292
  37.5 16.8 %copy-start = (bf16[4096,256]{1,0:T(8,128)(2,1)S(1)}, bf16[4096,256]{1,0:T(8,128)(2,1)}, u32[]{:S(2)}) copy-start(bf16[4096,256]{1,0:T(8,128)(2,1)} %f_hbm.7) | copy-start | bytes 6291460
  42.6 0.7 copy-start.5
  43.2 11.0 %all-to-all-start.1 = ((f32[8,1,4096]{2,1,0:T(1,128)}), f32[8,1,4096]{2,1,0:T(1,128)S(1)}, u32[]{:S(2)}, u32[]{:S(2)}) async-start(f32[8,1,4096]{2,1,0:T(1,128)} %copy-done.5), calls=%async_computation.1 | async-start | bytes 262144 | tf_op jit(solution)/shard_map/all_to_all | solution.py:206
  57.7 13.4 %collective-permute-start = (f32[264,256]{1,0:T(8,128)S(1)}, f32[264,256]{1,0:T(8,128)S(1)}, u32[]{:S(2)}, u32[]{:S(2)}) collective-permute-start(f32[264,256]{1,0:T(8,128)S(1)} %shard_map.58), channel_id=1, source_target_pairs={{0,2},{1,3},{2,0},{3,1},{4,6},{5,7},{6,4},{7,5},{8,10},{9,11},{10,... | collective-permute-start | bytes 811016 | tf_op jit(solution)/shard_map/ppermute | solution.py:230
  62.7 8.4 %collective-permute-start.1 = (f32[264,256]{1,0:T(8,128)S(1)}, f32[264,256]{1,0:T(8,128)S(1)}, u32[]{:S(2)}, u32[]{:S(2)}) collective-permute-start(f32[264,256]{1,0:T(8,128)S(1)} %shard_map.59), channel_id=1, source_target_pairs={{0,3},{1,2},{2,1},{3,0},{4,7},{5,6},{6,5},{7,4},{8,11},{9,10},{10,... | collective-permute-start | bytes 811016 | tf_op jit(solution)/shard_map/ppermute | solution.py:230
  66.3 6.3 %collective-permute-start.2 = (f32[264,256]{1,0:T(8,128)S(1)}, f32[264,256]{1,0:T(8,128)}, u32[]{:S(2)}, u32[]{:S(2)}) collective-permute-start(f32[264,256]{1,0:T(8,128)S(1)} %shard_map.60), channel_id=1, source_target_pairs={{0,1},{1,0},{2,3},{3,2},{4,5},{5,4},{6,7},{7,6},{8,9},{9,8},{10,11... | collective-permute-start | bytes 811016 | tf_op jit(solution)/shard_map/ppermute | solution.py:230
  70.4 0.7 copy-start.3
  71.1 0.7 copy-start.7
  71.8 0.7 copy-start.8

commit v17 on v16

--- a/solution.py
+++ b/solution.py
@@ -162,36 +162,45 @@
 
 
 def combine_kernel(*refs):
-    piece_refs, out_ref = refs[:-1], refs[-1]
+    count = len(refs) - 3
+    piece_refs, out_ref, held, sem = refs[:count], refs[count], refs[count + 1], refs[count + 2]
+    copies = [pltpu.make_async_copy(piece_refs[k], held.at[k], sem.at[k]) for k in range(count)]
+    for copy in copies:
+        copy.start()
+    for copy in copies:
+        copy.wait()
     feat = out_ref.shape[1]
-    peaks = [ref[feat + 1 : feat + 2, :] for ref in piece_refs]
+    peaks = [held[k, feat + 1 : feat + 2, :] for k in range(count)]
     top = peaks[0]
     for peak in peaks[1:]:
         top = jnp.maximum(top, peak)
     numerator = None
     denominator = None
-    for ref, peak in zip(piece_refs, peaks):
+    for k, peak in enumerate(peaks):
         factor = jnp.exp(peak - top)
-        term = ref[:feat, :] * factor
-        mass = ref[feat : feat + 1, :] * factor
+        term = held[k, :feat, :] * factor
+        mass = held[k, feat : feat + 1, :] * factor
         numerator = term if numerator is None else numerator + term
         denominator = mass if denominator is None else denominator + mass
     out_ref[...] = (numerator / denominator).T
 
 
 def combine(pieces, feat):
-    chunk = pieces[0].shape[1]
-    width = min(128, chunk)
+    rows, chunk = pieces[0].shape
+    count = len(pieces)
     return pl.pallas_call(
         combine_kernel,
         out_shape=jax.ShapeDtypeStruct((chunk, feat), jnp.float32),
-        grid=(chunk // width,),
-        in_specs=[pl.BlockSpec((feat + 8, width), lambda j: (0, j)) for piece in pieces],
-        out_specs=pl.BlockSpec((width, feat), lambda j: (j, 0)),
-        cost_estimate=pl.CostEstimate(
-            flops=3 * len(pieces) * chunk * feat,
-            transcendentals=len(pieces) * chunk,
-            bytes_accessed=4 * chunk * ((feat + 8) * len(pieces) + feat),
+        in_specs=[pl.BlockSpec(memory_space=pl.ANY) for piece in pieces],
+        out_specs=pl.BlockSpec((chunk, feat), lambda: (0, 0)),
+        scratch_shapes=[
+            pltpu.VMEM((count, rows, chunk), jnp.float32),
+            pltpu.SemaphoreType.DMA((count,)),
+        ],
+        cost_estimate=pl.CostEstimate(
+            flops=3 * count * chunk * feat,
+            transcendentals=count * chunk,
+            bytes_accessed=4 * chunk * (rows * count + feat),
         ),
     )(*pieces)
 

time: 74.9 us -> 75.1 us (level)
  no operation moved by 1% of the time
where the time goes in v17:
time: 75.1 us; the launch traced here: 74.8 us
  Pallas kernels  31.3 us (42%)
  blocking collectives  25.9 us (34%)
  waiting for transfers between devices  7.66 us (10%)
  starting transfers between devices  5.69 us (8%)
  local copies, waits for them, and re-layouts  4.02 us (5%)
    pallas_call x4, Pallas kernels, assign_chunk(): pl.pallas_call(functools.partial(assign_kernel, scale=scale), out_shape=j...  13.8 us
    all_to_all x1, blocking collectives, exchange(): return lax.all_to_all(block, 'veh', 0, 0, tiled=True)  13.1 us
    pallas_call x2, Pallas kernels, lse_over_rows(): pl.pallas_call(functools.partial(lse_kernel, scale=scale, shifted=shifted...  10.1 us
    all_to_all x1, waiting for transfers between devices, exchange(): return lax.all_to_all(block, 'veh', 0, 0, tiled=True)  7.65 us
    all_gather x1, blocking collectives, local(): own_rows = lax.all_gather(vehicle_emb, 'req', axis=0, tiled=True)  7.42 us
    all_gather x1, blocking collectives, local(): row_parts = lax.all_gather(partial[0], 'req', axis=0, tiled=False)  5.38 us
    pallas_call x1, Pallas kernels, row_lse(): pl.pallas_call(functools.partial(row_kernel, scale=scale), out_shape=jax....  5.26 us
    unnamed x18, local copies, waits for them, and re-layouts  4.02 us
  transfers between devices with their start and end apart: 4, of which 1 were waited for; matrix products, arithmetic and copies ran while one was open for 0% of the time, Pallas kernels for 14%

profile of v17, /device:TPU:0, one launch (start us, length us, event | category | flops | bytes accessed | tf_op | source)
XLA Modules:
  0.0 74.8 jit_solution(786699666787301449)
XLA Ops:
  0.0 7.4 %all_gather.6.refs_0_.a_ref.v_ref = bf16[1024,128]{1,0:T(8,128)(2,1)S(1)} all-gather(bf16[256,128]{1,0:T(8,128)(2,1)} %param.5), channel_id=1, replica_groups=mesh['veh'=8,'req'=4] {'req'}, dimensions={0}, use_global_device_ids=true | all-gather | bytes 327680 | tf_op jit(solution)/shard_map/all_gather | solution.py:209
  7.4 1.2 %copy-done.1 = bf16[4096,128]{1,0:T(8,128)(2,1)S(1)} copy-done((bf16[4096,128]{1,0:T(8,128)(2,1)S(1)}, bf16[4096,128]{1,0:T(8,128)(2,1)}, u32[]{:S(2)}) %copy-start.1) | copy-done | bytes 1048600
  8.6 5.1 %shard_map.55 = f32[8,1,4096]{2,1,0:T(1,128)S(1)} custom-call(bf16[1024,128]{1,0:T(8,128)(2,1)S(1)} %all_gather.6.refs_0_.a_ref.v_ref, bf16[4096,128]{1,0:T(8,128)(2,1)S(1)} %copy-done.1), custom_call_target="tpu_custom_call" | custom-call | flops 1094713344 | bytes 1445888 | tf_op jit(solution)/shard_map/pallas_call | solution.py:58
  13.7 13.1 %all_to_all.10.parts_ref = f32[8,1,4096]{2,1,0:T(1,128)S(1)} all-to-all(f32[8,1,4096]{2,1,0:T(1,128)S(1)} %shard_map.55), channel_id=1, replica_groups=mesh['veh'=8,'req'=4] {'veh'}, dimensions={0} | all-to-all | bytes 262144 | tf_op jit(solution)/shard_map/all_to_all | solution.py:215
  26.9 5.3 %shard_map.56 = f32[1,1,1024]{2,1,0:T(1,128)S(1)} custom-call(bf16[1024,128]{1,0:T(8,128)(2,1)S(1)} %all_gather.6.refs_0_.a_ref.v_ref, f32[8,1,4096]{2,1,0:T(1,128)S(1)} %all_to_all.10.parts_ref, f32[1,4096]{1,0:T(1,128)S(1)} %bitcast.6, bf16[4096,128]{1,0:T(8,128)(2,1)S(1)} %copy-done.2), custom_call_target="tpu_custom_call" | custom-call | flops 1094713344 | bytes 1462272 | tf_op jit(solution)/shard_map/pallas_call | solution.py:91
  32.1 5.4 %all_gather.7.refs_1_ = f32[4,1,1024]{2,1,0:T(1,128)S(1)} all-gather(f32[1,1,1024]{2,1,0:T(1,128)S(1)} %shard_map.56), channel_id=1, replica_groups=mesh['veh'=8,'req'=4] {'req'}, dimensions={0}, use_global_device_ids=true | all-gather | bytes 20480 | tf_op jit(solution)/shard_map/all_gather | solution.py:219
  37.5 5.1 %shard_map.57 = f32[8,1,4096]{2,1,0:T(1,128)S(1)} custom-call(bf16[1024,128]{1,0:T(8,128)(2,1)S(1)} %all_gather.6.refs_0_.a_ref.v_ref, f32[4,1,1024]{2,1,0:T(1,128)S(1)} %all_gather.7.refs_1_, f32[1,1024]{1,0:T(1,128)S(1)} %bitcast.11, bf16[4096,128]{1,0:T(8,128)(2,1)S(1)} %copy-done.2), custom_call_target="tpu_custom_call" | custom-call | flops 1094713344 | bytes 1445888 | tf_op jit(solution)/shard_map/pallas_call | solution.py:58
  42.6 0.0 copy-start.5
  42.6 0.7 copy-done.5
  43.2 3.4 %all-to-all-start.1 = ((f32[8,1,4096]{2,1,0:T(1,128)}), f32[8,1,4096]{2,1,0:T(1,128)S(1)}, u32[]{:S(2)}, u32[]{:S(2)}) async-start(f32[8,1,4096]{2,1,0:T(1,128)} %copy-done.5), calls=%async_computation.1 | async-start | bytes 262144 | tf_op jit(solution)/shard_map/all_to_all | solution.py:215
  46.6 7.7 %all-to-all-done.1.parts_ref = f32[8,1,4096]{2,1,0:T(1,128)S(1)} async-done(((f32[8,1,4096]{2,1,0:T(1,128)}), f32[8,1,4096]{2,1,0:T(1,128)S(1)}, u32[]{:S(2)}, u32[]{:S(2)}) %all-to-all-start.1) | async-done | bytes 131104 | tf_op jit(solution)/shard_map/all_to_all | solution.py:215
  54.3 3.4 %shard_map.58 = f32[264,256]{1,0:T(8,128)S(1)} custom-call(s32[1]{0:T(128)} %bitcast.rot_ref, bf16[1024,128]{1,0:T(8,128)(2,1)S(1)} %all_gather.6.refs_0_.a_ref.v_ref, bf16[4096,128]{1,0:T(8,128)(2,1)S(1)} %copy-done.2, f32[8,1,4096]{2,1,0:T(1,128)S(1)} %all-to-all-done.1.parts_ref, f32[1,4096]{1,0:T(1,128)S(1)} %bitcast.7, bf16[4096,256]{1,0:T(8,128)(2,1)S(1)} %copy-done), custom_call_target="tpu_custom_call" | custom-call | flops 810549248 | bytes 3481600 | tf_op jit(solution)/shard_map/pallas_call | solution.py:151
  57.7 1.6 %collective-permute-start = (f32[264,256]{1,0:T(8,128)S(1)}, f32[264,256]{1,0:T(8,128)S(1)}, u32[]{:S(2)}, u32[]{:S(2)}) collective-permute-start(f32[264,256]{1,0:T(8,128)S(1)} %shard_map.58), channel_id=1, source_target_pairs={{0,2},{1,3},{2,0},{3,1},{4,6},{5,7},{6,4},{7,5},{8,10},{9,11},{10,... | collective-permute-start | bytes 811016 | tf_op jit(solution)/shard_map/ppermute | solution.py:239
  59.3 3.4 %shard_map.59 = f32[264,256]{1,0:T(8,128)S(1)} custom-call(s32[1]{0:T(128)} %bitcast.3.rot_ref, bf16[1024,128]{1,0:T(8,128)(2,1)S(1)} %all_gather.6.refs_0_.a_ref.v_ref, bf16[4096,128]{1,0:T(8,128)(2,1)S(1)} %copy-done.2, f32[8,1,4096]{2,1,0:T(1,128)S(1)} %all-to-all-done.1.parts_ref, f32[1,4096]{1,0:T(1,128)S(1)} %bitcast.8, bf16[4096,256]{1,0:T(8,128)(2,1)S(1)} %copy-done), custom_call_target="tpu_custom_call" | custom-call | flops 810549248 | bytes 3481600 | tf_op jit(solution)/shard_map/pallas_call | solution.py:151
  62.7 0.1 collective-permute-start.1
  62.8 3.5 %shard_map.60 = f32[264,256]{1,0:T(8,128)S(1)} custom-call(s32[1]{0:T(128)} %bitcast.4.rot_ref, bf16[1024,128]{1,0:T(8,128)(2,1)S(1)} %all_gather.6.refs_0_.a_ref.v_ref, bf16[4096,128]{1,0:T(8,128)(2,1)S(1)} %copy-done.2, f32[8,1,4096]{2,1,0:T(1,128)S(1)} %all-to-all-done.1.parts_ref, f32[1,4096]{1,0:T(1,128)S(1)} %bitcast.9, bf16[4096,256]{1,0:T(8,128)(2,1)S(1)} %copy-done), custom_call_target="tpu_custom_call" | custom-call | flops 810549248 | bytes 3481600 | tf_op jit(solution)/shard_map/pallas_call | solution.py:151
  66.3 0.7 collective-permute-start.2
  66.9 3.4 %shard_map.61.refs_3_ = f32[264,256]{1,0:T(8,128)S(1)} custom-call(s32[1]{0:T(128)} %bitcast.5.rot_ref, bf16[1024,128]{1,0:T(8,128)(2,1)S(1)} %all_gather.6.refs_0_.a_ref.v_ref, bf16[4096,128]{1,0:T(8,128)(2,1)S(1)} %copy-done.2, f32[8,1,4096]{2,1,0:T(1,128)S(1)} %all-to-all-done.1.parts_ref, f32[1,4096]{1,0:T(1,128)S(1)} %bitcast.10, ...), custom_call_target="tpu_custom_call" | custom-call | flops 810549248 | bytes 3481600 | tf_op jit(solution)/shard_map/pallas_call | solution.py:151
  70.4 0.7 copy-done.3
  71.1 0.0 collective-permute-done.refs_0_
  71.1 0.0 collective-permute-done.1.refs_1_
  71.1 0.7 copy-done.7
  71.8 0.7 copy-done.8
  72.5 2.1 %shard_map.62 = f32[256,256]{1,0:T(8,128)} custom-call(f32[264,256]{1,0:T(8,128)} %copy-done.7, f32[264,256]{1,0:T(8,128)} %copy-done.8, f32[264,256]{1,0:T(8,128)} %collective-permute-done.2.refs_2_, f32[264,256]{1,0:T(8,128)} %copy-done.3), custom_call_target="tpu_custom_call" | custom-call | flops 786432 | bytes 1343488 | tf_op jit(solution)/shard_map/pallas_call | solution.py:191
  (13 shorter events, 0.0 us)
Async XLA Ops:
  7.4 1.2 %copy-start.1 = (bf16[4096,128]{1,0:T(8,128)(2,1)S(1)}, bf16[4096,128]{1,0:T(8,128)(2,1)}, u32[]{:S(2)}) copy-start(bf16[4096,128]{1,0:T(8,128)(2,1)} %r_ref.7) | copy-start | bytes 3145732
  8.6 18.2 %copy-start.2 = (bf16[4096,128]{1,0:T(8,128)(2,1)S(1)}, bf16[4096,128]{1,0:T(8,128)(2,1)}, u32[]{:S(2)}) copy-start(bf16[4096,128]{1,0:T(8,128)(2,1)} %r_ref.7) | copy-start | bytes 3145732
  8.6 18.2 %copy-start.4 = (f32[4096]{0:T(1024)S(1)}, f32[4096]{0:T(1024)}, u32[]{:S(2)}) copy-start(f32[4096]{0:T(1024)} %param.9) | copy-start | bytes 49156
  26.9 10.6 %copy-start.6 = (f32[1024]{0:T(1024)S(1)}, f32[1024]{0:T(1024)}, u32[]{:S(2)}) copy-start(f32[1024]{0:T(1024)} %param.8) | copy-start | bytes 12292
  37.5 16.8 %copy-start = (bf16[4096,256]{1,0:T(8,128)(2,1)S(1)}, bf16[4096,256]{1,0:T(8,128)(2,1)}, u32[]{:S(2)}) copy-start(bf16[4096,256]{1,0:T(8,128)(2,1)} %f_hbm.7) | copy-start | bytes 6291460
  42.6 0.7 copy-start.5
  43.2 11.0 %all-to-all-start.1 = ((f32[8,1,4096]{2,1,0:T(1,128)}), f32[8,1,4096]{2,1,0:T(1,128)S(1)}, u32[]{:S(2)}, u32[]{:S(2)}) async-start(f32[8,1,4096]{2,1,0:T(1,128)} %copy-done.5), calls=%async_computation.1 | async-start | bytes 262144 | tf_op jit(solution)/shard_map/all_to_all | solution.py:215
  57.7 13.4 %collective-permute-start = (f32[264,256]{1,0:T(8,128)S(1)}, f32[264,256]{1,0:T(8,128)S(1)}, u32[]{:S(2)}, u32[]{:S(2)}) collective-permute-start(f32[264,256]{1,0:T(8,128)S(1)} %shard_map.58), channel_id=1, source_target_pairs={{0,2},{1,3},{2,0},{3,1},{4,6},{5,7},{6,4},{7,5},{8,10},{9,11},{10,... | collective-permute-start | bytes 811016 | tf_op jit(solution)/shard_map/ppermute | solution.py:239
  62.7 8.4 %collective-permute-start.1 = (f32[264,256]{1,0:T(8,128)S(1)}, f32[264,256]{1,0:T(8,128)S(1)}, u32[]{:S(2)}, u32[]{:S(2)}) collective-permute-start(f32[264,256]{1,0:T(8,128)S(1)} %shard_map.59), channel_id=1, source_target_pairs={{0,3},{1,2},{2,1},{3,0},{4,7},{5,6},{6,5},{7,4},{8,11},{9,10},{10,... | collective-permute-start | bytes 811016 | tf_op jit(solution)/shard_map/ppermute | solution.py:239
  66.3 6.3 %collective-permute-start.2 = (f32[264,256]{1,0:T(8,128)S(1)}, f32[264,256]{1,0:T(8,128)}, u32[]{:S(2)}, u32[]{:S(2)}) collective-permute-start(f32[264,256]{1,0:T(8,128)S(1)} %shard_map.60), channel_id=1, source_target_pairs={{0,1},{1,0},{2,3},{3,2},{4,5},{5,4},{6,7},{7,6},{8,9},{9,8},{10,11... | collective-permute-start | bytes 811016 | tf_op jit(solution)/shard_map/ppermute | solution.py:239
  70.4 0.7 copy-start.3
  71.1 0.7 copy-start.7
  71.8 0.7 copy-start.8

commit v18 on v16

--- a/solution.py
+++ b/solution.py
@@ -229,7 +229,13 @@
         if step:
             piece = lax.ppermute(piece, "req", [(i, partner(i)) for i in range(owners)])
         pieces.append(piece)
-    return combine(pieces, feat)
+    arrived = jnp.stack(pieces)
+    peaks = arrived[:, feat + 1, :]
+    masses = arrived[:, feat, :]
+    factor = jnp.exp(peaks - jnp.max(peaks, axis=0, keepdims=True))
+    numerator = jnp.sum(arrived[:, :feat, :] * factor[:, None, :], axis=0)
+    denominator = jnp.sum(masses * factor, axis=0)
+    return (numerator / denominator[None, :]).T
 
 
 def solution(mesh):

time: 74.9 us -> 72.4 us (0.967)
  Pallas kernels: 31.2 us -> 29.2 us
  local copies, waits for them, and re-layouts: 4.02 us -> 2.73 us
    unnamed x18 -> x12, local copies, waits for them, and re-layouts: 4.02 us -> 1.89 us
    pallas_call x1 -> x0, Pallas kernels: 2.08 us -> none  [combine(): pl.pallas_call(combine_kernel, out_shape=jax.ShapeDtypeStruct((chunk, fea...]
    div x0 -> x1, local copies, waits for them, and re-layouts: none -> 0.84 us  [local(): return (numerator / denominator[None, :]).T]
  transfers between devices with their start and end apart: 4 -> 4, of which waited for: 1 -> 2; matrix products, arithmetic and copies ran while one was open for 0% -> 0% of each run, Pallas kernels for 14% -> 14%
where the time goes in v18:
time: 72.4 us; the launch traced here: 72.1 us
  Pallas kernels  29.2 us (40%)
  blocking collectives  25.9 us (36%)
  waiting for transfers between devices  8.23 us (11%)
  starting transfers between devices  5.69 us (8%)
  local copies, waits for them, and re-layouts  2.73 us (4%)
    pallas_call x4, Pallas kernels, assign_chunk(): pl.pallas_call(functools.partial(assign_kernel, scale=scale), out_shape=j...  13.8 us
    all_to_all x1, blocking collectives, exchange(): return lax.all_to_all(block, 'veh', 0, 0, tiled=True)  13.1 us
    pallas_call x2, Pallas kernels, lse_over_rows(): pl.pallas_call(functools.partial(lse_kernel, scale=scale, shifted=shifted...  10.1 us
    all_to_all x1, waiting for transfers between devices, exchange(): return lax.all_to_all(block, 'veh', 0, 0, tiled=True)  7.65 us
    all_gather x1, blocking collectives, local(): own_rows = lax.all_gather(vehicle_emb, 'req', axis=0, tiled=True)  7.42 us
    all_gather x1, blocking collectives, local(): row_parts = lax.all_gather(partial[0], 'req', axis=0, tiled=False)  5.38 us
    pallas_call x1, Pallas kernels, row_lse(): pl.pallas_call(functools.partial(row_kernel, scale=scale), out_shape=jax....  5.26 us
    all_to_all x1, starting transfers between devices, exchange(): return lax.all_to_all(block, 'veh', 0, 0, tiled=True)  3.37 us
  transfers between devices with their start and end apart: 4, of which 2 were waited for; matrix products, arithmetic and copies ran while one was open for 0% of the time, Pallas kernels for 14%

profile of v18, /device:TPU:0, one launch (start us, length us, event | category | flops | bytes accessed | tf_op | source)
XLA Modules:
  0.0 72.1 jit_solution(2628329027479933746)
XLA Ops:
  0.0 7.4 %all_gather.6.refs_0_.a_ref.v_ref = bf16[1024,128]{1,0:T(8,128)(2,1)S(1)} all-gather(bf16[256,128]{1,0:T(8,128)(2,1)} %param.5), channel_id=1, replica_groups=mesh['veh'=8,'req'=4] {'req'}, dimensions={0}, use_global_device_ids=true | all-gather | bytes 327680 | tf_op jit(solution)/shard_map/all_gather | solution.py:200
  7.4 1.2 %copy-done.1 = bf16[4096,128]{1,0:T(8,128)(2,1)S(1)} copy-done((bf16[4096,128]{1,0:T(8,128)(2,1)S(1)}, bf16[4096,128]{1,0:T(8,128)(2,1)}, u32[]{:S(2)}) %copy-start.1) | copy-done | bytes 1048600
  8.6 5.1 %shard_map.55 = f32[8,1,4096]{2,1,0:T(1,128)S(1)} custom-call(bf16[1024,128]{1,0:T(8,128)(2,1)S(1)} %all_gather.6.refs_0_.a_ref.v_ref, bf16[4096,128]{1,0:T(8,128)(2,1)S(1)} %copy-done.1), custom_call_target="tpu_custom_call" | custom-call | flops 1094713344 | bytes 1445888 | tf_op jit(solution)/shard_map/pallas_call | solution.py:58
  13.7 13.1 %all_to_all.10.parts_ref = f32[8,1,4096]{2,1,0:T(1,128)S(1)} all-to-all(f32[8,1,4096]{2,1,0:T(1,128)S(1)} %shard_map.55), channel_id=1, replica_groups=mesh['veh'=8,'req'=4] {'veh'}, dimensions={0} | all-to-all | bytes 262144 | tf_op jit(solution)/shard_map/all_to_all | solution.py:206
  26.9 5.3 %shard_map.56 = f32[1,1,1024]{2,1,0:T(1,128)S(1)} custom-call(bf16[1024,128]{1,0:T(8,128)(2,1)S(1)} %all_gather.6.refs_0_.a_ref.v_ref, f32[8,1,4096]{2,1,0:T(1,128)S(1)} %all_to_all.10.parts_ref, f32[1,4096]{1,0:T(1,128)S(1)} %bitcast.26, bf16[4096,128]{1,0:T(8,128)(2,1)S(1)} %copy-done.2), custom_call_target="tpu_custom_call" | custom-call | flops 1094713344 | bytes 1462272 | tf_op jit(solution)/shard_map/pallas_call | solution.py:91
  32.1 5.4 %all_gather.7.refs_1_ = f32[4,1,1024]{2,1,0:T(1,128)S(1)} all-gather(f32[1,1,1024]{2,1,0:T(1,128)S(1)} %shard_map.56), channel_id=1, replica_groups=mesh['veh'=8,'req'=4] {'req'}, dimensions={0}, use_global_device_ids=true | all-gather | bytes 20480 | tf_op jit(solution)/shard_map/all_gather | solution.py:210
  37.5 5.1 %shard_map.57 = f32[8,1,4096]{2,1,0:T(1,128)S(1)} custom-call(bf16[1024,128]{1,0:T(8,128)(2,1)S(1)} %all_gather.6.refs_0_.a_ref.v_ref, f32[4,1,1024]{2,1,0:T(1,128)S(1)} %all_gather.7.refs_1_, f32[1,1024]{1,0:T(1,128)S(1)} %bitcast.31, bf16[4096,128]{1,0:T(8,128)(2,1)S(1)} %copy-done.2), custom_call_target="tpu_custom_call" | custom-call | flops 1094713344 | bytes 1445888 | tf_op jit(solution)/shard_map/pallas_call | solution.py:58
  42.6 0.0 copy-start.4
  42.6 0.7 copy-done.4
  43.2 3.4 %all-to-all-start.1 = ((f32[8,1,4096]{2,1,0:T(1,128)}), f32[8,1,4096]{2,1,0:T(1,128)S(1)}, u32[]{:S(2)}, u32[]{:S(2)}) async-start(f32[8,1,4096]{2,1,0:T(1,128)} %copy-done.4), calls=%async_computation.1 | async-start | bytes 262144 | tf_op jit(solution)/shard_map/all_to_all | solution.py:206
  46.6 7.7 %all-to-all-done.1.parts_ref = f32[8,1,4096]{2,1,0:T(1,128)S(1)} async-done(((f32[8,1,4096]{2,1,0:T(1,128)}), f32[8,1,4096]{2,1,0:T(1,128)S(1)}, u32[]{:S(2)}, u32[]{:S(2)}) %all-to-all-start.1) | async-done | bytes 131104 | tf_op jit(solution)/shard_map/all_to_all | solution.py:206
  54.3 3.4 %shard_map.58 = f32[264,256]{1,0:T(8,128)S(1)} custom-call(s32[1]{0:T(128)} %bitcast.rot_ref, bf16[1024,128]{1,0:T(8,128)(2,1)S(1)} %all_gather.6.refs_0_.a_ref.v_ref, bf16[4096,128]{1,0:T(8,128)(2,1)S(1)} %copy-done.2, f32[8,1,4096]{2,1,0:T(1,128)S(1)} %all-to-all-done.1.parts_ref, f32[1,4096]{1,0:T(1,128)S(1)} %bitcast.27, bf16[4096,256]{1,0:T(8,128)(2,1)S(1)} %copy-done), custom_call_target="tpu_custom_call" | custom-call | flops 810549248 | bytes 3481600 | tf_op jit(solution)/shard_map/pallas_call | solution.py:151
  57.7 1.6 %collective-permute-start = (f32[264,256]{1,0:T(8,128)S(1)}, f32[264,256]{1,0:T(8,128)S(1)}, u32[]{:S(2)}, u32[]{:S(2)}) collective-permute-start(f32[264,256]{1,0:T(8,128)S(1)} %shard_map.58), channel_id=1, source_target_pairs={{0,2},{1,3},{2,0},{3,1},{4,6},{5,7},{6,4},{7,5},{8,10},{9,11},{10,... | collective-permute-start | bytes 811016 | tf_op jit(solution)/shard_map/ppermute | solution.py:230
  59.3 3.4 %shard_map.59 = f32[264,256]{1,0:T(8,128)S(1)} custom-call(s32[1]{0:T(128)} %bitcast.4.rot_ref, bf16[1024,128]{1,0:T(8,128)(2,1)S(1)} %all_gather.6.refs_0_.a_ref.v_ref, bf16[4096,128]{1,0:T(8,128)(2,1)S(1)} %copy-done.2, f32[8,1,4096]{2,1,0:T(1,128)S(1)} %all-to-all-done.1.parts_ref, f32[1,4096]{1,0:T(1,128)S(1)} %bitcast.28, bf16[4096,256]{1,0:T(8,128)(2,1)S(1)} %copy-done), custom_call_target="tpu_custom_call" | custom-call | flops 810549248 | bytes 3481600 | tf_op jit(solution)/shard_map/pallas_call | solution.py:151
  62.7 0.1 collective-permute-start.1
  62.8 3.5 %shard_map.60 = f32[264,256]{1,0:T(8,128)S(1)} custom-call(s32[1]{0:T(128)} %bitcast.6.rot_ref, bf16[1024,128]{1,0:T(8,128)(2,1)S(1)} %all_gather.6.refs_0_.a_ref.v_ref, bf16[4096,128]{1,0:T(8,128)(2,1)S(1)} %copy-done.2, f32[8,1,4096]{2,1,0:T(1,128)S(1)} %all-to-all-done.1.parts_ref, f32[1,4096]{1,0:T(1,128)S(1)} %bitcast.29, bf16[4096,256]{1,0:T(8,128)(2,1)S(1)} %copy-done), custom_call_target="tpu_custom_call" | custom-call | flops 810549248 | bytes 3481600 | tf_op jit(solution)/shard_map/pallas_call | solution.py:151
  66.3 0.7 collective-permute-start.2
  66.9 3.4 %shard_map.61 = f32[264,256]{1,0:T(8,128)S(1)} custom-call(s32[1]{0:T(128)} %bitcast.8.rot_ref, bf16[1024,128]{1,0:T(8,128)(2,1)S(1)} %all_gather.6.refs_0_.a_ref.v_ref, bf16[4096,128]{1,0:T(8,128)(2,1)S(1)} %copy-done.2, f32[8,1,4096]{2,1,0:T(1,128)S(1)} %all-to-all-done.1.parts_ref, f32[1,4096]{1,0:T(1,128)S(1)} %bitcast.30, bf16[4096,256]{1,0:T(8,128)(2,1)S(1)} %copy-done), custom_call_target="tpu_custom_call" | custom-call | flops 810549248 | bytes 3481600 | tf_op jit(solution)/shard_map/pallas_call | solution.py:151
  70.4 0.0 collective-permute-done
  70.4 0.6 collective-permute-done.1
  71.0 0.0 collective-permute-done.2
  71.0 0.1 pad_maximum_fusion
  71.1 0.1 fusion
  71.2 0.8 %copy.8 = f32[256,256]{1,0:T(8,128)} copy(f32[256,256]{0,1:T(8,128)S(1)} %divide_bitcast_fusion) | data formatting | bytes 524288 | tf_op jit(solution)/shard_map/div | solution.py:238
  (13 shorter events, 0.1 us)
Async XLA Ops:
  7.4 1.2 %copy-start.1 = (bf16[4096,128]{1,0:T(8,128)(2,1)S(1)}, bf16[4096,128]{1,0:T(8,128)(2,1)}, u32[]{:S(2)}) copy-start(bf16[4096,128]{1,0:T(8,128)(2,1)} %r_ref.7) | copy-start | bytes 3145732
  8.6 18.2 %copy-start.2 = (bf16[4096,128]{1,0:T(8,128)(2,1)S(1)}, bf16[4096,128]{1,0:T(8,128)(2,1)}, u32[]{:S(2)}) copy-start(bf16[4096,128]{1,0:T(8,128)(2,1)} %r_ref.7) | copy-start | bytes 3145732
  8.6 18.2 %copy-start.3 = (f32[4096]{0:T(1024)S(1)}, f32[4096]{0:T(1024)}, u32[]{:S(2)}) copy-start(f32[4096]{0:T(1024)} %param.9) | copy-start | bytes 49156
  26.9 10.6 %copy-start.5 = (f32[1024]{0:T(1024)S(1)}, f32[1024]{0:T(1024)}, u32[]{:S(2)}) copy-start(f32[1024]{0:T(1024)} %param.8) | copy-start | bytes 12292
  37.5 16.8 %copy-start = (bf16[4096,256]{1,0:T(8,128)(2,1)S(1)}, bf16[4096,256]{1,0:T(8,128)(2,1)}, u32[]{:S(2)}) copy-start(bf16[4096,256]{1,0:T(8,128)(2,1)} %f_hbm.7) | copy-start | bytes 6291460
  42.6 0.7 copy-start.4
  43.2 11.0 %all-to-all-start.1 = ((f32[8,1,4096]{2,1,0:T(1,128)}), f32[8,1,4096]{2,1,0:T(1,128)S(1)}, u32[]{:S(2)}, u32[]{:S(2)}) async-start(f32[8,1,4096]{2,1,0:T(1,128)} %copy-done.4), calls=%async_computation.1 | async-start | bytes 262144 | tf_op jit(solution)/shard_map/all_to_all | solution.py:206
  57.7 12.7 %collective-permute-start = (f32[264,256]{1,0:T(8,128)S(1)}, f32[264,256]{1,0:T(8,128)S(1)}, u32[]{:S(2)}, u32[]{:S(2)}) collective-permute-start(f32[264,256]{1,0:T(8,128)S(1)} %shard_map.58), channel_id=1, source_target_pairs={{0,2},{1,3},{2,0},{3,1},{4,6},{5,7},{6,4},{7,5},{8,10},{9,11},{10,... | collective-permute-start | bytes 811016 | tf_op jit(solution)/shard_map/ppermute | solution.py:230
  62.7 8.2 %collective-permute-start.1 = (f32[264,256]{1,0:T(8,128)S(1)}, f32[264,256]{1,0:T(8,128)S(1)}, u32[]{:S(2)}, u32[]{:S(2)}) collective-permute-start(f32[264,256]{1,0:T(8,128)S(1)} %shard_map.59), channel_id=1, source_target_pairs={{0,3},{1,2},{2,1},{3,0},{4,7},{5,6},{6,5},{7,4},{8,11},{9,10},{10,... | collective-permute-start | bytes 811016 | tf_op jit(solution)/shard_map/ppermute | solution.py:230
  66.3 4.7 %collective-permute-start.2 = (f32[264,256]{1,0:T(8,128)S(1)}, f32[264,256]{1,0:T(8,128)S(1)}, u32[]{:S(2)}, u32[]{:S(2)}) collective-permute-start(f32[264,256]{1,0:T(8,128)S(1)} %shard_map.60), channel_id=1, source_target_pairs={{0,1},{1,0},{2,3},{3,2},{4,5},{5,4},{6,7},{7,6},{8,9},{9,8},{10,11... | collective-permute-start | bytes 811016 | tf_op jit(solution)/shard_map/ppermute | solution.py:230

commit v19 on v18

--- a/solution.py
+++ b/solution.py
@@ -126,10 +126,9 @@
     block_feat = jnp.dot(
         powers.astype(jnp.bfloat16), f_ref[...], preferred_element_type=jnp.float32
     )
-    out_ref[:feat, :] = block_feat.T
+    out_ref[:, :feat] = block_feat
     lane = lax.broadcasted_iota(jnp.int32, (top.shape[0], 128), 1)
-    extra = jnp.where(lane == 0, mass, jnp.where(lane == 1, top, 0.0))
-    out_ref[feat:, :] = extra.T[:8, :]
+    out_ref[:, feat:] = jnp.where(lane == 0, mass, jnp.where(lane == 1, top, 0.0))
 
 
 def assign_chunk(v, r, parts, base, f, scale, chunk, index):
@@ -145,18 +144,18 @@
             pl.BlockSpec((1, cols), lambda i, at: (0, 0)),
             pl.BlockSpec(memory_space=pl.ANY),
         ],
-        out_specs=pl.BlockSpec((feat + 8, chunk), lambda i, at: (0, 0)),
+        out_specs=pl.BlockSpec((chunk, feat + 128), lambda i, at: (0, 0)),
         scratch_shapes=[pltpu.VMEM((cols, feat), f.dtype), pltpu.SemaphoreType.DMA(())],
     )
     return pl.pallas_call(
         functools.partial(assign_kernel, scale=scale),
-        out_shape=jax.ShapeDtypeStruct((feat + 8, chunk), jnp.float32),
+        out_shape=jax.ShapeDtypeStruct((chunk, feat + 128), jnp.float32),
         grid_spec=grid_spec,
         compiler_params=pltpu.CompilerParams(vmem_limit_bytes=24 * 1024 * 1024),
         cost_estimate=pl.CostEstimate(
             flops=2 * chunk * cols * (width + feat) + 5 * chunk * cols,
             transcendentals=chunk * cols,
-            bytes_accessed=2 * (chunk + cols) * width + 2 * cols * feat + 4 * chunk * (feat + 8),
+            bytes_accessed=2 * (chunk + cols) * width + 2 * cols * feat + 4 * chunk * (feat + 128),
         ),
     )(index, v, r, parts, base.reshape(1, cols), f)
 
@@ -230,12 +229,12 @@
             piece = lax.ppermute(piece, "req", [(i, partner(i)) for i in range(owners)])
         pieces.append(piece)
     arrived = jnp.stack(pieces)
-    peaks = arrived[:, feat + 1, :]
-    masses = arrived[:, feat, :]
+    peaks = arrived[:, :, feat + 1]
+    masses = arrived[:, :, feat]
     factor = jnp.exp(peaks - jnp.max(peaks, axis=0, keepdims=True))
-    numerator = jnp.sum(arrived[:, :feat, :] * factor[:, None, :], axis=0)
+    numerator = jnp.sum(arrived[:, :, :feat] * factor[:, :, None], axis=0)
     denominator = jnp.sum(masses * factor, axis=0)
-    return (numerator / denominator[None, :]).T
+    return numerator / denominator[:, None]
 
 
 def solution(mesh):

time: 72.4 us -> 78 us (1.077)
  waiting for transfers between devices: 8.23 us -> 12.7 us
  other arithmetic: 0.23 us -> 2.19 us
  local copies, waits for them, and re-layouts: 2.73 us -> 1.89 us
    ppermute x3, waiting for transfers between devices: 0.58 us -> 5.07 us  [local(): piece = lax.ppermute(piece, 'req', [(i, partner(i)) for i in range(owners)])]
    div x1 -> x0, local copies, waits for them, and re-layouts: 0.84 us -> none  [local(): return (numerator / denominator[None, :]).T]
    div x1, other arithmetic: 0.03 us -> 0.81 us  [local(): return numerator / denominator[:, None]]
  transfers between devices with their start and end apart: 4 -> 4, of which waited for: 2 -> 2; matrix products, arithmetic and copies ran while one was open for 0% -> 0% of each run, Pallas kernels for 14% -> 13%
where the time goes in v19:
time: 78 us; the launch traced here: 77.4 us
  Pallas kernels  28.9 us (37%)
  blocking collectives  25.9 us (33%)
  waiting for transfers between devices  12.7 us (16%)
  starting transfers between devices  5.69 us (7%)
  other arithmetic  2.19 us (3%)
  local copies, waits for them, and re-layouts  1.89 us (2%)
    pallas_call x4, Pallas kernels, assign_chunk(): pl.pallas_call(functools.partial(assign_kernel, scale=scale), out_shape=j...  13.5 us
    all_to_all x1, blocking collectives, exchange(): return lax.all_to_all(block, 'veh', 0, 0, tiled=True)  13.1 us
    pallas_call x2, Pallas kernels, lse_over_rows(): pl.pallas_call(functools.partial(lse_kernel, scale=scale, shifted=shifted...  10.1 us
    all_to_all x1, waiting for transfers between devices, exchange(): return lax.all_to_all(block, 'veh', 0, 0, tiled=True)  7.65 us
    all_gather x1, blocking collectives, local(): own_rows = lax.all_gather(vehicle_emb, 'req', axis=0, tiled=True)  7.42 us
    all_gather x1, blocking collectives, local(): row_parts = lax.all_gather(partial[0], 'req', axis=0, tiled=False)  5.38 us
    pallas_call x1, Pallas kernels, row_lse(): pl.pallas_call(functools.partial(row_kernel, scale=scale), out_shape=jax....  5.26 us
    ppermute x3, waiting for transfers between devices, local(): piece = lax.ppermute(piece, 'req', [(i, partner(i)) for i in range(owners)])  5.07 us
  transfers between devices with their start and end apart: 4, of which 2 were waited for; matrix products, arithmetic and copies ran while one was open for 0% of the time, Pallas kernels for 13%

profile of v19, /device:TPU:0, one launch (start us, length us, event | category | flops | bytes accessed | tf_op | source)
XLA Modules:
  0.0 77.4 jit_solution(9770671059036593930)
XLA Ops:
  0.0 7.4 %all_gather.6.refs_0_.a_ref.v_ref = bf16[1024,128]{1,0:T(8,128)(2,1)S(1)} all-gather(bf16[256,128]{1,0:T(8,128)(2,1)} %param.5), channel_id=1, replica_groups=mesh['veh'=8,'req'=4] {'req'}, dimensions={0}, use_global_device_ids=true | all-gather | bytes 327680 | tf_op jit(solution)/shard_map/all_gather | solution.py:199
  7.4 1.2 %copy-done.1 = bf16[4096,128]{1,0:T(8,128)(2,1)S(1)} copy-done((bf16[4096,128]{1,0:T(8,128)(2,1)S(1)}, bf16[4096,128]{1,0:T(8,128)(2,1)}, u32[]{:S(2)}) %copy-start.1) | copy-done | bytes 1048600
  8.6 5.1 %shard_map.55 = f32[8,1,4096]{2,1,0:T(1,128)S(1)} custom-call(bf16[1024,128]{1,0:T(8,128)(2,1)S(1)} %all_gather.6.refs_0_.a_ref.v_ref, bf16[4096,128]{1,0:T(8,128)(2,1)S(1)} %copy-done.1), custom_call_target="tpu_custom_call" | custom-call | flops 1094713344 | bytes 1445888 | tf_op jit(solution)/shard_map/pallas_call | solution.py:58
  13.7 13.1 %all_to_all.10.parts_ref = f32[8,1,4096]{2,1,0:T(1,128)S(1)} all-to-all(f32[8,1,4096]{2,1,0:T(1,128)S(1)} %shard_map.55), channel_id=1, replica_groups=mesh['veh'=8,'req'=4] {'veh'}, dimensions={0} | all-to-all | bytes 262144 | tf_op jit(solution)/shard_map/all_to_all | solution.py:205
  26.9 5.3 %shard_map.56 = f32[1,1,1024]{2,1,0:T(1,128)S(1)} custom-call(bf16[1024,128]{1,0:T(8,128)(2,1)S(1)} %all_gather.6.refs_0_.a_ref.v_ref, f32[8,1,4096]{2,1,0:T(1,128)S(1)} %all_to_all.10.parts_ref, f32[1,4096]{1,0:T(1,128)S(1)} %bitcast.11, bf16[4096,128]{1,0:T(8,128)(2,1)S(1)} %copy-done.2), custom_call_target="tpu_custom_call" | custom-call | flops 1094713344 | bytes 1462272 | tf_op jit(solution)/shard_map/pallas_call | solution.py:91
  32.1 5.4 %all_gather.7.refs_1_ = f32[4,1,1024]{2,1,0:T(1,128)S(1)} all-gather(f32[1,1,1024]{2,1,0:T(1,128)S(1)} %shard_map.56), channel_id=1, replica_groups=mesh['veh'=8,'req'=4] {'req'}, dimensions={0}, use_global_device_ids=true | all-gather | bytes 20480 | tf_op jit(solution)/shard_map/all_gather | solution.py:209
  37.5 5.1 %shard_map.57 = f32[8,1,4096]{2,1,0:T(1,128)S(1)} custom-call(bf16[1024,128]{1,0:T(8,128)(2,1)S(1)} %all_gather.6.refs_0_.a_ref.v_ref, f32[4,1,1024]{2,1,0:T(1,128)S(1)} %all_gather.7.refs_1_, f32[1,1024]{1,0:T(1,128)S(1)} %bitcast.16, bf16[4096,128]{1,0:T(8,128)(2,1)S(1)} %copy-done.2), custom_call_target="tpu_custom_call" | custom-call | flops 1094713344 | bytes 1445888 | tf_op jit(solution)/shard_map/pallas_call | solution.py:58
  42.6 0.0 copy-start.4
  42.6 0.7 copy-done.4
  43.2 3.4 %all-to-all-start.1 = ((f32[8,1,4096]{2,1,0:T(1,128)}), f32[8,1,4096]{2,1,0:T(1,128)S(1)}, u32[]{:S(2)}, u32[]{:S(2)}) async-start(f32[8,1,4096]{2,1,0:T(1,128)} %copy-done.4), calls=%async_computation.1 | async-start | bytes 262144 | tf_op jit(solution)/shard_map/all_to_all | solution.py:205
  46.6 7.7 %all-to-all-done.1.parts_ref = f32[8,1,4096]{2,1,0:T(1,128)S(1)} async-done(((f32[8,1,4096]{2,1,0:T(1,128)}), f32[8,1,4096]{2,1,0:T(1,128)S(1)}, u32[]{:S(2)}, u32[]{:S(2)}) %all-to-all-start.1) | async-done | bytes 131104 | tf_op jit(solution)/shard_map/all_to_all | solution.py:205
  54.3 3.4 %shard_map.58 = f32[256,384]{1,0:T(8,128)S(1)} custom-call(s32[1]{0:T(128)} %bitcast.rot_ref, bf16[1024,128]{1,0:T(8,128)(2,1)S(1)} %all_gather.6.refs_0_.a_ref.v_ref, bf16[4096,128]{1,0:T(8,128)(2,1)S(1)} %copy-done.2, f32[8,1,4096]{2,1,0:T(1,128)S(1)} %all-to-all-done.1.parts_ref, f32[1,4096]{1,0:T(1,128)S(1)} %bitcast.12, bf16[4096,256]{1,0:T(8,128)(2,1)S(1)} %copy-done), custom_call_target="tpu_custom_call" | custom-call | flops 810549248 | bytes 3604480 | tf_op jit(solution)/shard_map/pallas_call | solution.py:150
  57.6 1.6 %collective-permute-start = (f32[256,384]{1,0:T(8,128)S(1)}, f32[256,384]{1,0:T(8,128)S(1)}, u32[]{:S(2)}, u32[]{:S(2)}) collective-permute-start(f32[256,384]{1,0:T(8,128)S(1)} %shard_map.58), channel_id=1, source_target_pairs={{0,2},{1,3},{2,0},{3,1},{4,6},{5,7},{6,4},{7,5},{8,10},{9,11},{10,... | collective-permute-start | bytes 1179656 | tf_op jit(solution)/shard_map/ppermute | solution.py:229
  59.2 3.4 %shard_map.59 = f32[256,384]{1,0:T(8,128)S(1)} custom-call(s32[1]{0:T(128)} %bitcast.4.rot_ref, bf16[1024,128]{1,0:T(8,128)(2,1)S(1)} %all_gather.6.refs_0_.a_ref.v_ref, bf16[4096,128]{1,0:T(8,128)(2,1)S(1)} %copy-done.2, f32[8,1,4096]{2,1,0:T(1,128)S(1)} %all-to-all-done.1.parts_ref, f32[1,4096]{1,0:T(1,128)S(1)} %bitcast.13, bf16[4096,256]{1,0:T(8,128)(2,1)S(1)} %copy-done), custom_call_target="tpu_custom_call" | custom-call | flops 810549248 | bytes 3604480 | tf_op jit(solution)/shard_map/pallas_call | solution.py:150
  62.6 0.1 collective-permute-start.1
  62.7 3.4 %shard_map.60 = f32[256,384]{1,0:T(8,128)S(1)} custom-call(s32[1]{0:T(128)} %bitcast.6.rot_ref, bf16[1024,128]{1,0:T(8,128)(2,1)S(1)} %all_gather.6.refs_0_.a_ref.v_ref, bf16[4096,128]{1,0:T(8,128)(2,1)S(1)} %copy-done.2, f32[8,1,4096]{2,1,0:T(1,128)S(1)} %all-to-all-done.1.parts_ref, f32[1,4096]{1,0:T(1,128)S(1)} %bitcast.14, bf16[4096,256]{1,0:T(8,128)(2,1)S(1)} %copy-done), custom_call_target="tpu_custom_call" | custom-call | flops 810549248 | bytes 3604480 | tf_op jit(solution)/shard_map/pallas_call | solution.py:150
  66.1 0.7 collective-permute-start.2
  66.7 3.4 %shard_map.61 = f32[256,384]{1,0:T(8,128)S(1)} custom-call(s32[1]{0:T(128)} %bitcast.8.rot_ref, bf16[1024,128]{1,0:T(8,128)(2,1)S(1)} %all_gather.6.refs_0_.a_ref.v_ref, bf16[4096,128]{1,0:T(8,128)(2,1)S(1)} %copy-done.2, f32[8,1,4096]{2,1,0:T(1,128)S(1)} %all-to-all-done.1.parts_ref, f32[1,4096]{1,0:T(1,128)S(1)} %bitcast.15, bf16[4096,256]{1,0:T(8,128)(2,1)S(1)} %copy-done), custom_call_target="tpu_custom_call" | custom-call | flops 810549248 | bytes 3604480 | tf_op jit(solution)/shard_map/pallas_call | solution.py:150
  70.1 5.1 %collective-permute-done.1 = f32[256,384]{1,0:T(8,128)S(1)} collective-permute-done((f32[256,384]{1,0:T(8,128)S(1)}, f32[256,384]{1,0:T(8,128)S(1)}, u32[]{:S(2)}, u32[]{:S(2)}) %collective-permute-start.1) | collective-permute-done | bytes 393248 | tf_op jit(solution)/shard_map/ppermute | solution.py:229
  75.2 0.1 pad_maximum_fusion
  75.4 0.3 slice_reduce_fusion.2
  75.6 0.7 slice_reduce_fusion.1
  76.4 0.2 fusion
  76.6 0.8 %broadcast_divide_fusion = f32[256,256]{1,0:T(8,128)} fusion(f32[256,256]{1,0:T(8,128)S(1)} %fusion, f32[256]{0:T(256)S(1)} %multiply_reduce_fusion), kind=kLoop, calls=%fused_computation.7 | loop fusion | flops 65536 | bytes 525312 | tf_op jit(solution)/shard_map/div | solution.py:237
  (12 shorter events, 0.0 us)
Async XLA Ops:
  7.4 1.2 %copy-start.1 = (bf16[4096,128]{1,0:T(8,128)(2,1)S(1)}, bf16[4096,128]{1,0:T(8,128)(2,1)}, u32[]{:S(2)}) copy-start(bf16[4096,128]{1,0:T(8,128)(2,1)} %r_ref.7) | copy-start | bytes 3145732
  8.6 18.2 %copy-start.2 = (bf16[4096,128]{1,0:T(8,128)(2,1)S(1)}, bf16[4096,128]{1,0:T(8,128)(2,1)}, u32[]{:S(2)}) copy-start(bf16[4096,128]{1,0:T(8,128)(2,1)} %r_ref.7) | copy-start | bytes 3145732
  8.6 18.2 %copy-start.3 = (f32[4096]{0:T(1024)S(1)}, f32[4096]{0:T(1024)}, u32[]{:S(2)}) copy-start(f32[4096]{0:T(1024)} %param.9) | copy-start | bytes 49156
  26.9 10.6 %copy-start.5 = (f32[1024]{0:T(1024)S(1)}, f32[1024]{0:T(1024)}, u32[]{:S(2)}) copy-start(f32[1024]{0:T(1024)} %param.8) | copy-start | bytes 12292
  37.5 16.8 %copy-start = (bf16[4096,256]{1,0:T(8,128)(2,1)S(1)}, bf16[4096,256]{1,0:T(8,128)(2,1)}, u32[]{:S(2)}) copy-start(bf16[4096,256]{1,0:T(8,128)(2,1)} %f_hbm.7) | copy-start | bytes 6291460
  42.6 0.7 copy-start.4
  43.2 11.0 %all-to-all-start.1 = ((f32[8,1,4096]{2,1,0:T(1,128)}), f32[8,1,4096]{2,1,0:T(1,128)S(1)}, u32[]{:S(2)}, u32[]{:S(2)}) async-start(f32[8,1,4096]{2,1,0:T(1,128)} %copy-done.4), calls=%async_computation.1 | async-start | bytes 262144 | tf_op jit(solution)/shard_map/all_to_all | solution.py:205
  57.6 12.5 %collective-permute-start = (f32[256,384]{1,0:T(8,128)S(1)}, f32[256,384]{1,0:T(8,128)S(1)}, u32[]{:S(2)}, u32[]{:S(2)}) collective-permute-start(f32[256,384]{1,0:T(8,128)S(1)} %shard_map.58), channel_id=1, source_target_pairs={{0,2},{1,3},{2,0},{3,1},{4,6},{5,7},{6,4},{7,5},{8,10},{9,11},{10,... | collective-permute-start | bytes 1179656 | tf_op jit(solution)/shard_map/ppermute | solution.py:229
  62.6 12.6 %collective-permute-start.1 = (f32[256,384]{1,0:T(8,128)S(1)}, f32[256,384]{1,0:T(8,128)S(1)}, u32[]{:S(2)}, u32[]{:S(2)}) collective-permute-start(f32[256,384]{1,0:T(8,128)S(1)} %shard_map.59), channel_id=1, source_target_pairs={{0,3},{1,2},{2,1},{3,0},{4,7},{5,6},{6,5},{7,4},{8,11},{9,10},{10,... | collective-permute-start | bytes 1179656 | tf_op jit(solution)/shard_map/ppermute | solution.py:229
  66.1 9.1 %collective-permute-start.2 = (f32[256,384]{1,0:T(8,128)S(1)}, f32[256,384]{1,0:T(8,128)S(1)}, u32[]{:S(2)}, u32[]{:S(2)}) collective-permute-start(f32[256,384]{1,0:T(8,128)S(1)} %shard_map.60), channel_id=1, source_target_pairs={{0,1},{1,0},{2,3},{3,2},{4,5},{5,4},{6,7},{7,6},{8,9},{9,8},{10,11... | collective-permute-start | bytes 1179656 | tf_op jit(solution)/shard_map/ppermute | solution.py:229

commit v20 on v18

--- a/solution.py
+++ b/solution.py
@@ -152,7 +152,7 @@
         functools.partial(assign_kernel, scale=scale),
         out_shape=jax.ShapeDtypeStruct((feat + 8, chunk), jnp.float32),
         grid_spec=grid_spec,
-        compiler_params=pltpu.CompilerParams(vmem_limit_bytes=24 * 1024 * 1024),
+        compiler_params=pltpu.CompilerParams(vmem_limit_bytes=16 * 1024 * 1024),
         cost_estimate=pl.CostEstimate(
             flops=2 * chunk * cols * (width + feat) + 5 * chunk * cols,
             transcendentals=chunk * cols,
@@ -206,7 +206,7 @@
         return lax.all_to_all(block, "veh", 0, 0, tiled=True)
 
     first = exchange(lse_over_rows(own_rows, request_emb, scale, 4096, spread, 24 << 20))
-    partial = row_lse(own_rows, request_emb, scale, 1024, 48 << 20, first, log_demand)
+    partial = row_lse(own_rows, request_emb, scale, 1024, 24 << 20, first, log_demand)
     row_parts = lax.all_gather(partial[0], "req", axis=0, tiled=False)
     second = exchange(
         lse_over_rows(own_rows, request_emb, scale, 4096, spread, 24 << 20, row_parts, log_supply)

time: 72.4 us -> 72.3 us (level)
  no operation moved by 1% of the time
where the time goes in v20:
time: 72.3 us; the launch traced here: 72 us
  Pallas kernels  29.1 us (40%)
  blocking collectives  25.9 us (36%)
  waiting for transfers between devices  8.23 us (11%)
  starting transfers between devices  5.69 us (8%)
  local copies, waits for them, and re-layouts  2.73 us (4%)
    pallas_call x4, Pallas kernels, assign_chunk(): pl.pallas_call(functools.partial(assign_kernel, scale=scale), out_shape=j...  13.8 us
    all_to_all x1, blocking collectives, exchange(): return lax.all_to_all(block, 'veh', 0, 0, tiled=True)  13.1 us
    pallas_call x2, Pallas kernels, lse_over_rows(): pl.pallas_call(functools.partial(lse_kernel, scale=scale, shifted=shifted...  10.1 us
    all_to_all x1, waiting for transfers between devices, exchange(): return lax.all_to_all(block, 'veh', 0, 0, tiled=True)  7.65 us
    all_gather x1, blocking collectives, local(): own_rows = lax.all_gather(vehicle_emb, 'req', axis=0, tiled=True)  7.42 us
    all_gather x1, blocking collectives, local(): row_parts = lax.all_gather(partial[0], 'req', axis=0, tiled=False)  5.38 us
    pallas_call x1, Pallas kernels, row_lse(): pl.pallas_call(functools.partial(row_kernel, scale=scale), out_shape=jax....  5.26 us
    all_to_all x1, starting transfers between devices, exchange(): return lax.all_to_all(block, 'veh', 0, 0, tiled=True)  3.37 us
  transfers between devices with their start and end apart: 4, of which 2 were waited for; matrix products, arithmetic and copies ran while one was open for 0% of the time, Pallas kernels for 14%

profile of v20, /device:TPU:0, one launch (start us, length us, event | category | flops | bytes accessed | tf_op | source)
XLA Modules:
  0.0 72.0 jit_solution(15303025408945794275)
XLA Ops:
  0.0 7.4 %all_gather.6.refs_0_.a_ref.v_ref = bf16[1024,128]{1,0:T(8,128)(2,1)S(1)} all-gather(bf16[256,128]{1,0:T(8,128)(2,1)} %param.5), channel_id=1, replica_groups=mesh['veh'=8,'req'=4] {'req'}, dimensions={0}, use_global_device_ids=true | all-gather | bytes 327680 | tf_op jit(solution)/shard_map/all_gather | solution.py:200
  7.4 1.2 %copy-done.1 = bf16[4096,128]{1,0:T(8,128)(2,1)S(1)} copy-done((bf16[4096,128]{1,0:T(8,128)(2,1)S(1)}, bf16[4096,128]{1,0:T(8,128)(2,1)}, u32[]{:S(2)}) %copy-start.1) | copy-done | bytes 1048600
  8.6 5.1 %shard_map.55 = f32[8,1,4096]{2,1,0:T(1,128)S(1)} custom-call(bf16[1024,128]{1,0:T(8,128)(2,1)S(1)} %all_gather.6.refs_0_.a_ref.v_ref, bf16[4096,128]{1,0:T(8,128)(2,1)S(1)} %copy-done.1), custom_call_target="tpu_custom_call" | custom-call | flops 1094713344 | bytes 1445888 | tf_op jit(solution)/shard_map/pallas_call | solution.py:58
  13.7 13.1 %all_to_all.10.parts_ref = f32[8,1,4096]{2,1,0:T(1,128)S(1)} all-to-all(f32[8,1,4096]{2,1,0:T(1,128)S(1)} %shard_map.55), channel_id=1, replica_groups=mesh['veh'=8,'req'=4] {'veh'}, dimensions={0} | all-to-all | bytes 262144 | tf_op jit(solution)/shard_map/all_to_all | solution.py:206
  26.8 5.3 %shard_map.56 = f32[1,1,1024]{2,1,0:T(1,128)S(1)} custom-call(bf16[1024,128]{1,0:T(8,128)(2,1)S(1)} %all_gather.6.refs_0_.a_ref.v_ref, f32[8,1,4096]{2,1,0:T(1,128)S(1)} %all_to_all.10.parts_ref, f32[1,4096]{1,0:T(1,128)S(1)} %bitcast.26, bf16[4096,128]{1,0:T(8,128)(2,1)S(1)} %copy-done.1), custom_call_target="tpu_custom_call" | custom-call | flops 1094713344 | bytes 1462272 | tf_op jit(solution)/shard_map/pallas_call | solution.py:91
  32.1 5.4 %all_gather.7.refs_1_ = f32[4,1,1024]{2,1,0:T(1,128)S(1)} all-gather(f32[1,1,1024]{2,1,0:T(1,128)S(1)} %shard_map.56), channel_id=1, replica_groups=mesh['veh'=8,'req'=4] {'req'}, dimensions={0}, use_global_device_ids=true | all-gather | bytes 20480 | tf_op jit(solution)/shard_map/all_gather | solution.py:210
  37.5 5.1 %shard_map.57 = f32[8,1,4096]{2,1,0:T(1,128)S(1)} custom-call(bf16[1024,128]{1,0:T(8,128)(2,1)S(1)} %all_gather.6.refs_0_.a_ref.v_ref, f32[4,1,1024]{2,1,0:T(1,128)S(1)} %all_gather.7.refs_1_, f32[1,1024]{1,0:T(1,128)S(1)} %bitcast.31, bf16[4096,128]{1,0:T(8,128)(2,1)S(1)} %copy-done.1), custom_call_target="tpu_custom_call" | custom-call | flops 1094713344 | bytes 1445888 | tf_op jit(solution)/shard_map/pallas_call | solution.py:58
  42.5 0.0 copy-start.4
  42.5 0.7 copy-done.4
  43.2 3.4 %all-to-all-start.1 = ((f32[8,1,4096]{2,1,0:T(1,128)}), f32[8,1,4096]{2,1,0:T(1,128)S(1)}, u32[]{:S(2)}, u32[]{:S(2)}) async-start(f32[8,1,4096]{2,1,0:T(1,128)} %copy-done.4), calls=%async_computation.1 | async-start | bytes 262144 | tf_op jit(solution)/shard_map/all_to_all | solution.py:206
  46.6 7.7 %all-to-all-done.1.parts_ref = f32[8,1,4096]{2,1,0:T(1,128)S(1)} async-done(((f32[8,1,4096]{2,1,0:T(1,128)}), f32[8,1,4096]{2,1,0:T(1,128)S(1)}, u32[]{:S(2)}, u32[]{:S(2)}) %all-to-all-start.1) | async-done | bytes 131104 | tf_op jit(solution)/shard_map/all_to_all | solution.py:206
  54.2 3.4 %shard_map.58 = f32[264,256]{1,0:T(8,128)S(1)} custom-call(s32[1]{0:T(128)} %bitcast.rot_ref, bf16[1024,128]{1,0:T(8,128)(2,1)S(1)} %all_gather.6.refs_0_.a_ref.v_ref, bf16[4096,128]{1,0:T(8,128)(2,1)S(1)} %copy-done.2, f32[8,1,4096]{2,1,0:T(1,128)S(1)} %all-to-all-done.1.parts_ref, f32[1,4096]{1,0:T(1,128)S(1)} %bitcast.27, bf16[4096,256]{1,0:T(8,128)(2,1)S(1)} %copy-done), custom_call_target="tpu_custom_call" | custom-call | flops 810549248 | bytes 3481600 | tf_op jit(solution)/shard_map/pallas_call | solution.py:151
  57.7 1.6 %collective-permute-start = (f32[264,256]{1,0:T(8,128)S(1)}, f32[264,256]{1,0:T(8,128)S(1)}, u32[]{:S(2)}, u32[]{:S(2)}) collective-permute-start(f32[264,256]{1,0:T(8,128)S(1)} %shard_map.58), channel_id=1, source_target_pairs={{0,2},{1,3},{2,0},{3,1},{4,6},{5,7},{6,4},{7,5},{8,10},{9,11},{10,... | collective-permute-start | bytes 811016 | tf_op jit(solution)/shard_map/ppermute | solution.py:230
  59.3 3.4 %shard_map.59 = f32[264,256]{1,0:T(8,128)S(1)} custom-call(s32[1]{0:T(128)} %bitcast.4.rot_ref, bf16[1024,128]{1,0:T(8,128)(2,1)S(1)} %all_gather.6.refs_0_.a_ref.v_ref, bf16[4096,128]{1,0:T(8,128)(2,1)S(1)} %copy-done.2, f32[8,1,4096]{2,1,0:T(1,128)S(1)} %all-to-all-done.1.parts_ref, f32[1,4096]{1,0:T(1,128)S(1)} %bitcast.28, bf16[4096,256]{1,0:T(8,128)(2,1)S(1)} %copy-done), custom_call_target="tpu_custom_call" | custom-call | flops 810549248 | bytes 3481600 | tf_op jit(solution)/shard_map/pallas_call | solution.py:151
  62.7 0.1 collective-permute-start.1
  62.8 3.5 %shard_map.60 = f32[264,256]{1,0:T(8,128)S(1)} custom-call(s32[1]{0:T(128)} %bitcast.6.rot_ref, bf16[1024,128]{1,0:T(8,128)(2,1)S(1)} %all_gather.6.refs_0_.a_ref.v_ref, bf16[4096,128]{1,0:T(8,128)(2,1)S(1)} %copy-done.2, f32[8,1,4096]{2,1,0:T(1,128)S(1)} %all-to-all-done.1.parts_ref, f32[1,4096]{1,0:T(1,128)S(1)} %bitcast.29, bf16[4096,256]{1,0:T(8,128)(2,1)S(1)} %copy-done), custom_call_target="tpu_custom_call" | custom-call | flops 810549248 | bytes 3481600 | tf_op jit(solution)/shard_map/pallas_call | solution.py:151
  66.2 0.7 collective-permute-start.2
  66.9 3.4 %shard_map.61 = f32[264,256]{1,0:T(8,128)S(1)} custom-call(s32[1]{0:T(128)} %bitcast.8.rot_ref, bf16[1024,128]{1,0:T(8,128)(2,1)S(1)} %all_gather.6.refs_0_.a_ref.v_ref, bf16[4096,128]{1,0:T(8,128)(2,1)S(1)} %copy-done.2, f32[8,1,4096]{2,1,0:T(1,128)S(1)} %all-to-all-done.1.parts_ref, f32[1,4096]{1,0:T(1,128)S(1)} %bitcast.30, bf16[4096,256]{1,0:T(8,128)(2,1)S(1)} %copy-done), custom_call_target="tpu_custom_call" | custom-call | flops 810549248 | bytes 3481600 | tf_op jit(solution)/shard_map/pallas_call | solution.py:151
  70.4 0.0 collective-permute-done
  70.4 0.6 collective-permute-done.1
  70.9 0.0 collective-permute-done.2
  71.0 0.1 pad_maximum_fusion
  71.1 0.1 fusion
  71.2 0.8 %copy.8 = f32[256,256]{1,0:T(8,128)} copy(f32[256,256]{0,1:T(8,128)S(1)} %divide_bitcast_fusion) | data formatting | bytes 524288 | tf_op jit(solution)/shard_map/div | solution.py:238
  (13 shorter events, 0.1 us)
Async XLA Ops:
  7.4 1.2 %copy-start.1 = (bf16[4096,128]{1,0:T(8,128)(2,1)S(1)}, bf16[4096,128]{1,0:T(8,128)(2,1)}, u32[]{:S(2)}) copy-start(bf16[4096,128]{1,0:T(8,128)(2,1)} %r_ref.7) | copy-start | bytes 3145732
  8.6 18.2 %copy-start.3 = (f32[4096]{0:T(1024)S(1)}, f32[4096]{0:T(1024)}, u32[]{:S(2)}) copy-start(f32[4096]{0:T(1024)} %param.9) | copy-start | bytes 49156
  26.8 10.6 %copy-start.5 = (f32[1024]{0:T(1024)S(1)}, f32[1024]{0:T(1024)}, u32[]{:S(2)}) copy-start(f32[1024]{0:T(1024)} %param.8) | copy-start | bytes 12292
  37.5 16.8 %copy-start = (bf16[4096,256]{1,0:T(8,128)(2,1)S(1)}, bf16[4096,256]{1,0:T(8,128)(2,1)}, u32[]{:S(2)}) copy-start(bf16[4096,256]{1,0:T(8,128)(2,1)} %f_hbm.7) | copy-start | bytes 6291460
  37.5 16.8 %copy-start.2 = (bf16[4096,128]{1,0:T(8,128)(2,1)S(1)}, bf16[4096,128]{1,0:T(8,128)(2,1)}, u32[]{:S(2)}) copy-start(bf16[4096,128]{1,0:T(8,128)(2,1)} %r_ref.7) | copy-start | bytes 3145732
  42.5 0.7 copy-start.4
  43.2 11.0 %all-to-all-start.1 = ((f32[8,1,4096]{2,1,0:T(1,128)}), f32[8,1,4096]{2,1,0:T(1,128)S(1)}, u32[]{:S(2)}, u32[]{:S(2)}) async-start(f32[8,1,4096]{2,1,0:T(1,128)} %copy-done.4), calls=%async_computation.1 | async-start | bytes 262144 | tf_op jit(solution)/shard_map/all_to_all | solution.py:206
  57.7 12.7 %collective-permute-start = (f32[264,256]{1,0:T(8,128)S(1)}, f32[264,256]{1,0:T(8,128)S(1)}, u32[]{:S(2)}, u32[]{:S(2)}) collective-permute-start(f32[264,256]{1,0:T(8,128)S(1)} %shard_map.58), channel_id=1, source_target_pairs={{0,2},{1,3},{2,0},{3,1},{4,6},{5,7},{6,4},{7,5},{8,10},{9,11},{10,... | collective-permute-start | bytes 811016 | tf_op jit(solution)/shard_map/ppermute | solution.py:230
  62.7 8.2 %collective-permute-start.1 = (f32[264,256]{1,0:T(8,128)S(1)}, f32[264,256]{1,0:T(8,128)S(1)}, u32[]{:S(2)}, u32[]{:S(2)}) collective-permute-start(f32[264,256]{1,0:T(8,128)S(1)} %shard_map.59), channel_id=1, source_target_pairs={{0,3},{1,2},{2,1},{3,0},{4,7},{5,6},{6,5},{7,4},{8,11},{9,10},{10,... | collective-permute-start | bytes 811016 | tf_op jit(solution)/shard_map/ppermute | solution.py:230
  66.2 4.7 %collective-permute-start.2 = (f32[264,256]{1,0:T(8,128)S(1)}, f32[264,256]{1,0:T(8,128)S(1)}, u32[]{:S(2)}, u32[]{:S(2)}) collective-permute-start(f32[264,256]{1,0:T(8,128)S(1)} %shard_map.60), channel_id=1, source_target_pairs={{0,1},{1,0},{2,3},{3,2},{4,5},{5,4},{6,7},{7,6},{8,9},{9,8},{10,11... | collective-permute-start | bytes 811016 | tf_op jit(solution)/shard_map/ppermute | solution.py:230

commit v21 on v18

--- a/solution.py
+++ b/solution.py
@@ -217,7 +217,7 @@
     me = lax.axis_index("req")
     feat = request_feat.shape[1]
     if owners & (owners - 1) == 0:
-        order = [(step, lambda i, m=step: i ^ m) for step in list(range(2, owners)) + [1]]
+        order = [(step, lambda i, m=step: i ^ m) for step in list(range(owners - 1, 1, -1)) + [1]]
     else:
         order = [(step, lambda i, m=step: (i + m) % owners) for step in range(1, owners)]
     pieces = []

time: 72.4 us -> 73.7 us (1.018)
  waiting for transfers between devices: 8.23 us -> 9.88 us
    ppermute x3, waiting for transfers between devices: 0.58 us -> 2.23 us  [local(): piece = lax.ppermute(piece, 'req', [(i, partner(i)) for i in range(owners)])]
where the time goes in v21:
time: 73.7 us; the launch traced here: 73.4 us
  Pallas kernels  29.2 us (40%)
  blocking collectives  25.9 us (35%)
  waiting for transfers between devices  9.88 us (13%)
  starting transfers between devices  5.43 us (7%)
  local copies, waits for them, and re-layouts  2.73 us (4%)
    pallas_call x4, Pallas kernels, assign_chunk(): pl.pallas_call(functools.partial(assign_kernel, scale=scale), out_shape=j...  13.8 us
    all_to_all x1, blocking collectives, exchange(): return lax.all_to_all(block, 'veh', 0, 0, tiled=True)  13.1 us
    pallas_call x2, Pallas kernels, lse_over_rows(): pl.pallas_call(functools.partial(lse_kernel, scale=scale, shifted=shifted...  10.1 us
    all_to_all x1, waiting for transfers between devices, exchange(): return lax.all_to_all(block, 'veh', 0, 0, tiled=True)  7.65 us
    all_gather x1, blocking collectives, local(): own_rows = lax.all_gather(vehicle_emb, 'req', axis=0, tiled=True)  7.42 us
    all_gather x1, blocking collectives, local(): row_parts = lax.all_gather(partial[0], 'req', axis=0, tiled=False)  5.38 us
    pallas_call x1, Pallas kernels, row_lse(): pl.pallas_call(functools.partial(row_kernel, scale=scale), out_shape=jax....  5.26 us
    all_to_all x1, starting transfers between devices, exchange(): return lax.all_to_all(block, 'veh', 0, 0, tiled=True)  3.37 us
  transfers between devices with their start and end apart: 4, of which 2 were waited for; matrix products, arithmetic and copies ran while one was open for 0% of the time, Pallas kernels for 14%

profile of v21, /device:TPU:0, one launch (start us, length us, event | category | flops | bytes accessed | tf_op | source)
XLA Modules:
  0.0 73.4 jit_solution(6713713405409767438)
XLA Ops:
  0.0 7.4 %all_gather.6.refs_0_.a_ref.v_ref = bf16[1024,128]{1,0:T(8,128)(2,1)S(1)} all-gather(bf16[256,128]{1,0:T(8,128)(2,1)} %param.5), channel_id=1, replica_groups=mesh['veh'=8,'req'=4] {'req'}, dimensions={0}, use_global_device_ids=true | all-gather | bytes 327680 | tf_op jit(solution)/shard_map/all_gather | solution.py:200
  7.4 1.2 %copy-done.1 = bf16[4096,128]{1,0:T(8,128)(2,1)S(1)} copy-done((bf16[4096,128]{1,0:T(8,128)(2,1)S(1)}, bf16[4096,128]{1,0:T(8,128)(2,1)}, u32[]{:S(2)}) %copy-start.1) | copy-done | bytes 1048600
  8.6 5.1 %shard_map.55 = f32[8,1,4096]{2,1,0:T(1,128)S(1)} custom-call(bf16[1024,128]{1,0:T(8,128)(2,1)S(1)} %all_gather.6.refs_0_.a_ref.v_ref, bf16[4096,128]{1,0:T(8,128)(2,1)S(1)} %copy-done.1), custom_call_target="tpu_custom_call" | custom-call | flops 1094713344 | bytes 1445888 | tf_op jit(solution)/shard_map/pallas_call | solution.py:58
  13.7 13.1 %all_to_all.10.parts_ref = f32[8,1,4096]{2,1,0:T(1,128)S(1)} all-to-all(f32[8,1,4096]{2,1,0:T(1,128)S(1)} %shard_map.55), channel_id=1, replica_groups=mesh['veh'=8,'req'=4] {'veh'}, dimensions={0} | all-to-all | bytes 262144 | tf_op jit(solution)/shard_map/all_to_all | solution.py:206
  26.9 5.3 %shard_map.56 = f32[1,1,1024]{2,1,0:T(1,128)S(1)} custom-call(bf16[1024,128]{1,0:T(8,128)(2,1)S(1)} %all_gather.6.refs_0_.a_ref.v_ref, f32[8,1,4096]{2,1,0:T(1,128)S(1)} %all_to_all.10.parts_ref, f32[1,4096]{1,0:T(1,128)S(1)} %bitcast.26, bf16[4096,128]{1,0:T(8,128)(2,1)S(1)} %copy-done.2), custom_call_target="tpu_custom_call" | custom-call | flops 1094713344 | bytes 1462272 | tf_op jit(solution)/shard_map/pallas_call | solution.py:91
  32.1 5.4 %all_gather.7.refs_1_ = f32[4,1,1024]{2,1,0:T(1,128)S(1)} all-gather(f32[1,1,1024]{2,1,0:T(1,128)S(1)} %shard_map.56), channel_id=1, replica_groups=mesh['veh'=8,'req'=4] {'req'}, dimensions={0}, use_global_device_ids=true | all-gather | bytes 20480 | tf_op jit(solution)/shard_map/all_gather | solution.py:210
  37.5 5.1 %shard_map.57 = f32[8,1,4096]{2,1,0:T(1,128)S(1)} custom-call(bf16[1024,128]{1,0:T(8,128)(2,1)S(1)} %all_gather.6.refs_0_.a_ref.v_ref, f32[4,1,1024]{2,1,0:T(1,128)S(1)} %all_gather.7.refs_1_, f32[1,1024]{1,0:T(1,128)S(1)} %bitcast.31, bf16[4096,128]{1,0:T(8,128)(2,1)S(1)} %copy-done.2), custom_call_target="tpu_custom_call" | custom-call | flops 1094713344 | bytes 1445888 | tf_op jit(solution)/shard_map/pallas_call | solution.py:58
  42.6 0.0 copy-start.4
  42.6 0.7 copy-done.4
  43.2 3.4 %all-to-all-start.1 = ((f32[8,1,4096]{2,1,0:T(1,128)}), f32[8,1,4096]{2,1,0:T(1,128)S(1)}, u32[]{:S(2)}, u32[]{:S(2)}) async-start(f32[8,1,4096]{2,1,0:T(1,128)} %copy-done.4), calls=%async_computation.1 | async-start | bytes 262144 | tf_op jit(solution)/shard_map/all_to_all | solution.py:206
  46.6 7.7 %all-to-all-done.1.parts_ref = f32[8,1,4096]{2,1,0:T(1,128)S(1)} async-done(((f32[8,1,4096]{2,1,0:T(1,128)}), f32[8,1,4096]{2,1,0:T(1,128)S(1)}, u32[]{:S(2)}, u32[]{:S(2)}) %all-to-all-start.1) | async-done | bytes 131104 | tf_op jit(solution)/shard_map/all_to_all | solution.py:206
  54.3 3.4 %shard_map.58 = f32[264,256]{1,0:T(8,128)S(1)} custom-call(s32[1]{0:T(128)} %bitcast.rot_ref, bf16[1024,128]{1,0:T(8,128)(2,1)S(1)} %all_gather.6.refs_0_.a_ref.v_ref, bf16[4096,128]{1,0:T(8,128)(2,1)S(1)} %copy-done.2, f32[8,1,4096]{2,1,0:T(1,128)S(1)} %all-to-all-done.1.parts_ref, f32[1,4096]{1,0:T(1,128)S(1)} %bitcast.27, bf16[4096,256]{1,0:T(8,128)(2,1)S(1)} %copy-done), custom_call_target="tpu_custom_call" | custom-call | flops 810549248 | bytes 3481600 | tf_op jit(solution)/shard_map/pallas_call | solution.py:151
  57.7 0.2 collective-permute-start
  57.9 3.4 %shard_map.59 = f32[264,256]{1,0:T(8,128)S(1)} custom-call(s32[1]{0:T(128)} %bitcast.4.rot_ref, bf16[1024,128]{1,0:T(8,128)(2,1)S(1)} %all_gather.6.refs_0_.a_ref.v_ref, bf16[4096,128]{1,0:T(8,128)(2,1)S(1)} %copy-done.2, f32[8,1,4096]{2,1,0:T(1,128)S(1)} %all-to-all-done.1.parts_ref, f32[1,4096]{1,0:T(1,128)S(1)} %bitcast.28, bf16[4096,256]{1,0:T(8,128)(2,1)S(1)} %copy-done), custom_call_target="tpu_custom_call" | custom-call | flops 810549248 | bytes 3481600 | tf_op jit(solution)/shard_map/pallas_call | solution.py:151
  61.4 1.5 %collective-permute-start.1 = (f32[264,256]{1,0:T(8,128)S(1)}, f32[264,256]{1,0:T(8,128)S(1)}, u32[]{:S(2)}, u32[]{:S(2)}) collective-permute-start(f32[264,256]{1,0:T(8,128)S(1)} %shard_map.59), channel_id=1, source_target_pairs={{0,2},{1,3},{2,0},{3,1},{4,6},{5,7},{6,4},{7,5},{8,10},{9,11},{10,... | collective-permute-start | bytes 811016 | tf_op jit(solution)/shard_map/ppermute | solution.py:230
  62.8 3.4 %shard_map.60 = f32[264,256]{1,0:T(8,128)S(1)} custom-call(s32[1]{0:T(128)} %bitcast.6.rot_ref, bf16[1024,128]{1,0:T(8,128)(2,1)S(1)} %all_gather.6.refs_0_.a_ref.v_ref, bf16[4096,128]{1,0:T(8,128)(2,1)S(1)} %copy-done.2, f32[8,1,4096]{2,1,0:T(1,128)S(1)} %all-to-all-done.1.parts_ref, f32[1,4096]{1,0:T(1,128)S(1)} %bitcast.29, bf16[4096,256]{1,0:T(8,128)(2,1)S(1)} %copy-done), custom_call_target="tpu_custom_call" | custom-call | flops 810549248 | bytes 3481600 | tf_op jit(solution)/shard_map/pallas_call | solution.py:151
  66.3 0.4 collective-permute-start.2
  66.7 3.4 %shard_map.61 = f32[264,256]{1,0:T(8,128)S(1)} custom-call(s32[1]{0:T(128)} %bitcast.8.rot_ref, bf16[1024,128]{1,0:T(8,128)(2,1)S(1)} %all_gather.6.refs_0_.a_ref.v_ref, bf16[4096,128]{1,0:T(8,128)(2,1)S(1)} %copy-done.2, f32[8,1,4096]{2,1,0:T(1,128)S(1)} %all-to-all-done.1.parts_ref, f32[1,4096]{1,0:T(1,128)S(1)} %bitcast.30, bf16[4096,256]{1,0:T(8,128)(2,1)S(1)} %copy-done), custom_call_target="tpu_custom_call" | custom-call | flops 810549248 | bytes 3481600 | tf_op jit(solution)/shard_map/pallas_call | solution.py:151
  70.1 0.0 collective-permute-done
  70.1 2.2 %collective-permute-done.1 = f32[264,256]{1,0:T(8,128)S(1)} collective-permute-done((f32[264,256]{1,0:T(8,128)S(1)}, f32[264,256]{1,0:T(8,128)S(1)}, u32[]{:S(2)}, u32[]{:S(2)}) %collective-permute-start.1) | collective-permute-done | bytes 270368 | tf_op jit(solution)/shard_map/ppermute | solution.py:230
  72.3 0.0 collective-permute-done.2
  72.4 0.1 pad_maximum_fusion
  72.5 0.1 fusion
  72.6 0.8 %copy.8 = f32[256,256]{1,0:T(8,128)} copy(f32[256,256]{0,1:T(8,128)S(1)} %divide_bitcast_fusion) | data formatting | bytes 524288 | tf_op jit(solution)/shard_map/div | solution.py:238
  (13 shorter events, 0.1 us)
Async XLA Ops:
  7.4 1.2 %copy-start.1 = (bf16[4096,128]{1,0:T(8,128)(2,1)S(1)}, bf16[4096,128]{1,0:T(8,128)(2,1)}, u32[]{:S(2)}) copy-start(bf16[4096,128]{1,0:T(8,128)(2,1)} %r_ref.7) | copy-start | bytes 3145732
  8.6 18.2 %copy-start.2 = (bf16[4096,128]{1,0:T(8,128)(2,1)S(1)}, bf16[4096,128]{1,0:T(8,128)(2,1)}, u32[]{:S(2)}) copy-start(bf16[4096,128]{1,0:T(8,128)(2,1)} %r_ref.7) | copy-start | bytes 3145732
  8.6 18.2 %copy-start.3 = (f32[4096]{0:T(1024)S(1)}, f32[4096]{0:T(1024)}, u32[]{:S(2)}) copy-start(f32[4096]{0:T(1024)} %param.9) | copy-start | bytes 49156
  26.9 10.6 %copy-start.5 = (f32[1024]{0:T(1024)S(1)}, f32[1024]{0:T(1024)}, u32[]{:S(2)}) copy-start(f32[1024]{0:T(1024)} %param.8) | copy-start | bytes 12292
  37.5 16.8 %copy-start = (bf16[4096,256]{1,0:T(8,128)(2,1)S(1)}, bf16[4096,256]{1,0:T(8,128)(2,1)}, u32[]{:S(2)}) copy-start(bf16[4096,256]{1,0:T(8,128)(2,1)} %f_hbm.7) | copy-start | bytes 6291460
  42.6 0.7 copy-start.4
  43.2 11.0 %all-to-all-start.1 = ((f32[8,1,4096]{2,1,0:T(1,128)}), f32[8,1,4096]{2,1,0:T(1,128)S(1)}, u32[]{:S(2)}, u32[]{:S(2)}) async-start(f32[8,1,4096]{2,1,0:T(1,128)} %copy-done.4), calls=%async_computation.1 | async-start | bytes 262144 | tf_op jit(solution)/shard_map/all_to_all | solution.py:206
  57.7 12.4 %collective-permute-start = (f32[264,256]{1,0:T(8,128)S(1)}, f32[264,256]{1,0:T(8,128)S(1)}, u32[]{:S(2)}, u32[]{:S(2)}) collective-permute-start(f32[264,256]{1,0:T(8,128)S(1)} %shard_map.58), channel_id=1, source_target_pairs={{0,3},{1,2},{2,1},{3,0},{4,7},{5,6},{6,5},{7,4},{8,11},{9,10},{10,... | collective-permute-start | bytes 811016 | tf_op jit(solution)/shard_map/ppermute | solution.py:230
  61.4 11.0 %collective-permute-start.1 = (f32[264,256]{1,0:T(8,128)S(1)}, f32[264,256]{1,0:T(8,128)S(1)}, u32[]{:S(2)}, u32[]{:S(2)}) collective-permute-start(f32[264,256]{1,0:T(8,128)S(1)} %shard_map.59), channel_id=1, source_target_pairs={{0,2},{1,3},{2,0},{3,1},{4,6},{5,7},{6,4},{7,5},{8,10},{9,11},{10,... | collective-permute-start | bytes 811016 | tf_op jit(solution)/shard_map/ppermute | solution.py:230
  66.3 6.1 %collective-permute-start.2 = (f32[264,256]{1,0:T(8,128)S(1)}, f32[264,256]{1,0:T(8,128)S(1)}, u32[]{:S(2)}, u32[]{:S(2)}) collective-permute-start(f32[264,256]{1,0:T(8,128)S(1)} %shard_map.60), channel_id=1, source_target_pairs={{0,1},{1,0},{2,3},{3,2},{4,5},{5,4},{6,7},{7,6},{8,9},{9,8},{10,11... | collective-permute-start | bytes 811016 | tf_op jit(solution)/shard_map/ppermute | solution.py:230

commit v22 on v18

--- a/solution.py
+++ b/solution.py
@@ -71,7 +71,7 @@
     )(*operands)
 
 
-def row_kernel(a_ref, parts_ref, base_ref, b_ref, out_ref, *, scale):
+def row_kernel(a_ref, parts_ref, base_ref, b_ref, out_ref, *, scale, copies):
     demand = base_ref[...] - merged_lse(parts_ref[...])
     scores = lax.dot_general(
         a_ref[...], b_ref[...], (((1,), (1,)), ((), ())), preferred_element_type=jnp.float32
@@ -81,16 +81,17 @@
     total = jnp.sum(jnp.exp(logits - top), axis=1, keepdims=True)
     result = top + jnp.log(total)
     wide = jnp.broadcast_to(result, (result.shape[0], 128))
-    out_ref[...] = jnp.transpose(wide)[:1, :][None]
-
-
-def row_lse(a, b, scale, tile, vmem_limit, parts, base):
+    row = jnp.transpose(wide)[:1, :]
+    out_ref[...] = jnp.broadcast_to(row[None], (copies,) + row.shape)
+
+
+def row_lse(a, b, scale, tile, vmem_limit, parts, base, copies):
     rows, width = a.shape
     cols = b.shape[0]
     tile = min(tile, rows)
     return pl.pallas_call(
-        functools.partial(row_kernel, scale=scale),
-        out_shape=jax.ShapeDtypeStruct((1, 1, rows), jnp.float32),
+        functools.partial(row_kernel, scale=scale, copies=copies),
+        out_shape=jax.ShapeDtypeStruct((copies, 1, rows), jnp.float32),
         grid=(rows // tile,),
         in_specs=[
             pl.BlockSpec((tile, width), lambda i: (i, 0)),
@@ -98,7 +99,7 @@
             pl.BlockSpec((1, cols), lambda i: (0, 0)),
             pl.BlockSpec((cols, width), lambda i: (0, 0)),
         ],
-        out_specs=pl.BlockSpec((1, 1, tile), lambda i: (0, 0, i)),
+        out_specs=pl.BlockSpec((copies, 1, tile), lambda i: (0, 0, i)),
         compiler_params=pltpu.CompilerParams(vmem_limit_bytes=vmem_limit),
         cost_estimate=pl.CostEstimate(
             flops=2 * rows * cols * width + 5 * rows * cols,
@@ -206,8 +207,10 @@
         return lax.all_to_all(block, "veh", 0, 0, tiled=True)
 
     first = exchange(lse_over_rows(own_rows, request_emb, scale, 4096, spread, 24 << 20))
-    partial = row_lse(own_rows, request_emb, scale, 1024, 48 << 20, first, log_demand)
-    row_parts = lax.all_gather(partial[0], "req", axis=0, tiled=False)
+    partial = row_lse(
+        own_rows, request_emb, scale, 1024, 48 << 20, first, log_demand, lax.axis_size("req")
+    )
+    row_parts = lax.all_to_all(partial, "req", 0, 0, tiled=True)
     second = exchange(
         lse_over_rows(own_rows, request_emb, scale, 4096, spread, 24 << 20, row_parts, log_supply)
     )

time: 72.4 us -> 72.6 us (level)
  blocking collectives: 25.9 us -> 27 us
  waiting for transfers between devices: 8.23 us -> 7.28 us
    all_to_all x0 -> x1, blocking collectives: none -> 6.46 us  [local(): row_parts = lax.all_to_all(partial, 'req', 0, 0, tiled=True)]
    all_gather x1 -> x0, blocking collectives: 5.38 us -> none  [local(): row_parts = lax.all_gather(partial[0], 'req', axis=0, tiled=False)]
  transfers between devices with their start and end apart: 4 -> 4, of which waited for: 2 -> 1; matrix products, arithmetic and copies ran while one was open for 0% -> 0% of each run, Pallas kernels for 14% -> 14%
where the time goes in v22:
time: 72.6 us; the launch traced here: 72.2 us
  Pallas kernels  29.2 us (40%)
  blocking collectives  27 us (37%)
  waiting for transfers between devices  7.28 us (10%)
  starting transfers between devices  5.68 us (8%)
  local copies, waits for them, and re-layouts  2.73 us (4%)
    pallas_call x4, Pallas kernels, assign_chunk(): pl.pallas_call(functools.partial(assign_kernel, scale=scale), out_shape=j...  13.8 us
    all_to_all x1, blocking collectives, exchange(): return lax.all_to_all(block, 'veh', 0, 0, tiled=True)  13.1 us
    pallas_call x2, Pallas kernels, lse_over_rows(): pl.pallas_call(functools.partial(lse_kernel, scale=scale, shifted=shifted...  10.1 us
    all_gather x1, blocking collectives, local(): own_rows = lax.all_gather(vehicle_emb, 'req', axis=0, tiled=True)  7.42 us
    all_to_all x1, waiting for transfers between devices, exchange(): return lax.all_to_all(block, 'veh', 0, 0, tiled=True)  7.28 us
    all_to_all x1, blocking collectives, local(): row_parts = lax.all_to_all(partial, 'req', 0, 0, tiled=True)  6.46 us
    pallas_call x1, Pallas kernels, row_lse(): pl.pallas_call(functools.partial(row_kernel, scale=scale, copies=copies),...  5.26 us
    all_to_all x1, starting transfers between devices, exchange(): return lax.all_to_all(block, 'veh', 0, 0, tiled=True)  3.37 us
  transfers between devices with their start and end apart: 4, of which 1 were waited for; matrix products, arithmetic and copies ran while one was open for 0% of the time, Pallas kernels for 14%

profile of v22, /device:TPU:0, one launch (start us, length us, event | category | flops | bytes accessed | tf_op | source)
XLA Modules:
  0.0 72.2 jit_solution(14080284810598777248)
XLA Ops:
  0.0 7.4 %all_gather.3.refs_0_.a_ref.v_ref = bf16[1024,128]{1,0:T(8,128)(2,1)S(1)} all-gather(bf16[256,128]{1,0:T(8,128)(2,1)} %param.5), channel_id=1, replica_groups=mesh['veh'=8,'req'=4] {'req'}, dimensions={0}, use_global_device_ids=true | all-gather | bytes 327680 | tf_op jit(solution)/shard_map/all_gather | solution.py:201
  7.4 1.2 %copy-done.1 = bf16[4096,128]{1,0:T(8,128)(2,1)S(1)} copy-done((bf16[4096,128]{1,0:T(8,128)(2,1)S(1)}, bf16[4096,128]{1,0:T(8,128)(2,1)}, u32[]{:S(2)}) %copy-start.1) | copy-done | bytes 1048600
  8.6 5.1 %shard_map.55 = f32[8,1,4096]{2,1,0:T(1,128)S(1)} custom-call(bf16[1024,128]{1,0:T(8,128)(2,1)S(1)} %all_gather.3.refs_0_.a_ref.v_ref, bf16[4096,128]{1,0:T(8,128)(2,1)S(1)} %copy-done.1), custom_call_target="tpu_custom_call" | custom-call | flops 1094713344 | bytes 1445888 | tf_op jit(solution)/shard_map/pallas_call | solution.py:58
  13.7 13.1 %all_to_all.15.parts_ref = f32[8,1,4096]{2,1,0:T(1,128)S(1)} all-to-all(f32[8,1,4096]{2,1,0:T(1,128)S(1)} %shard_map.55), channel_id=1, replica_groups=mesh['veh'=8,'req'=4] {'veh'}, dimensions={0} | all-to-all | bytes 262144 | tf_op jit(solution)/shard_map/all_to_all | solution.py:207
  26.9 5.3 %shard_map.56 = f32[4,1,1024]{2,1,0:T(1,128)S(1)} custom-call(bf16[1024,128]{1,0:T(8,128)(2,1)S(1)} %all_gather.3.refs_0_.a_ref.v_ref, f32[8,1,4096]{2,1,0:T(1,128)S(1)} %all_to_all.15.parts_ref, f32[1,4096]{1,0:T(1,128)S(1)} %bitcast.26, bf16[4096,128]{1,0:T(8,128)(2,1)S(1)} %copy-done.2), custom_call_target="tpu_custom_call" | custom-call | flops 1094713344 | bytes 1462272 | tf_op jit(solution)/shard_map/pallas_call | solution.py:92
  32.1 6.5 %all_to_all.16.refs_1_ = f32[4,1,1024]{2,1,0:T(1,128)S(1)} all-to-all(f32[4,1,1024]{2,1,0:T(1,128)S(1)} %shard_map.56), channel_id=1, replica_groups=mesh['veh'=8,'req'=4] {'req'}, dimensions={0} | all-to-all | bytes 32768 | tf_op jit(solution)/shard_map/all_to_all | solution.py:213
  38.6 5.1 %shard_map.57 = f32[8,1,4096]{2,1,0:T(1,128)S(1)} custom-call(bf16[1024,128]{1,0:T(8,128)(2,1)S(1)} %all_gather.3.refs_0_.a_ref.v_ref, f32[4,1,1024]{2,1,0:T(1,128)S(1)} %all_to_all.16.refs_1_, f32[1,1024]{1,0:T(1,128)S(1)} %bitcast.31, bf16[4096,128]{1,0:T(8,128)(2,1)S(1)} %copy-done.2), custom_call_target="tpu_custom_call" | custom-call | flops 1094713344 | bytes 1445888 | tf_op jit(solution)/shard_map/pallas_call | solution.py:58
  43.6 0.0 copy-start.4
  43.6 0.7 copy-done.4
  44.3 3.4 %all-to-all-start.2 = ((f32[8,1,4096]{2,1,0:T(1,128)}), f32[8,1,4096]{2,1,0:T(1,128)S(1)}, u32[]{:S(2)}, u32[]{:S(2)}) async-start(f32[8,1,4096]{2,1,0:T(1,128)} %copy-done.4), calls=%async_computation.2 | async-start | bytes 262144 | tf_op jit(solution)/shard_map/all_to_all | solution.py:207
  47.7 7.3 %all-to-all-done.2.parts_ref = f32[8,1,4096]{2,1,0:T(1,128)S(1)} async-done(((f32[8,1,4096]{2,1,0:T(1,128)}), f32[8,1,4096]{2,1,0:T(1,128)S(1)}, u32[]{:S(2)}, u32[]{:S(2)}) %all-to-all-start.2) | async-done | bytes 131104 | tf_op jit(solution)/shard_map/all_to_all | solution.py:207
  55.0 3.4 %shard_map.58 = f32[264,256]{1,0:T(8,128)S(1)} custom-call(s32[1]{0:T(128)} %bitcast.rot_ref, bf16[1024,128]{1,0:T(8,128)(2,1)S(1)} %all_gather.3.refs_0_.a_ref.v_ref, bf16[4096,128]{1,0:T(8,128)(2,1)S(1)} %copy-done.2, f32[8,1,4096]{2,1,0:T(1,128)S(1)} %all-to-all-done.2.parts_ref, f32[1,4096]{1,0:T(1,128)S(1)} %bitcast.27, bf16[4096,256]{1,0:T(8,128)(2,1)S(1)} %copy-done), custom_call_target="tpu_custom_call" | custom-call | flops 810549248 | bytes 3481600 | tf_op jit(solution)/shard_map/pallas_call | solution.py:152
  58.4 0.1 collective-permute-start
  58.5 3.5 %shard_map.59 = f32[264,256]{1,0:T(8,128)S(1)} custom-call(s32[1]{0:T(128)} %bitcast.4.rot_ref, bf16[1024,128]{1,0:T(8,128)(2,1)S(1)} %all_gather.3.refs_0_.a_ref.v_ref, bf16[4096,128]{1,0:T(8,128)(2,1)S(1)} %copy-done.2, f32[8,1,4096]{2,1,0:T(1,128)S(1)} %all-to-all-done.2.parts_ref, f32[1,4096]{1,0:T(1,128)S(1)} %bitcast.28, bf16[4096,256]{1,0:T(8,128)(2,1)S(1)} %copy-done), custom_call_target="tpu_custom_call" | custom-call | flops 810549248 | bytes 3481600 | tf_op jit(solution)/shard_map/pallas_call | solution.py:152
  62.0 0.1 collective-permute-start.1
  62.0 3.5 %shard_map.60 = f32[264,256]{1,0:T(8,128)S(1)} custom-call(s32[1]{0:T(128)} %bitcast.6.rot_ref, bf16[1024,128]{1,0:T(8,128)(2,1)S(1)} %all_gather.3.refs_0_.a_ref.v_ref, bf16[4096,128]{1,0:T(8,128)(2,1)S(1)} %copy-done.2, f32[8,1,4096]{2,1,0:T(1,128)S(1)} %all-to-all-done.2.parts_ref, f32[1,4096]{1,0:T(1,128)S(1)} %bitcast.29, bf16[4096,256]{1,0:T(8,128)(2,1)S(1)} %copy-done), custom_call_target="tpu_custom_call" | custom-call | flops 810549248 | bytes 3481600 | tf_op jit(solution)/shard_map/pallas_call | solution.py:152
  65.5 2.2 %collective-permute-start.2 = (f32[264,256]{1,0:T(8,128)S(1)}, f32[264,256]{1,0:T(8,128)S(1)}, u32[]{:S(2)}, u32[]{:S(2)}) collective-permute-start(f32[264,256]{1,0:T(8,128)S(1)} %shard_map.60), channel_id=1, source_target_pairs={{0,1},{1,0},{2,3},{3,2},{4,5},{5,4},{6,7},{7,6},{8,9},{9,8},{10,11... | collective-permute-start | bytes 811016 | tf_op jit(solution)/shard_map/ppermute | solution.py:233
  67.6 3.4 %shard_map.61 = f32[264,256]{1,0:T(8,128)S(1)} custom-call(s32[1]{0:T(128)} %bitcast.8.rot_ref, bf16[1024,128]{1,0:T(8,128)(2,1)S(1)} %all_gather.3.refs_0_.a_ref.v_ref, bf16[4096,128]{1,0:T(8,128)(2,1)S(1)} %copy-done.2, f32[8,1,4096]{2,1,0:T(1,128)S(1)} %all-to-all-done.2.parts_ref, f32[1,4096]{1,0:T(1,128)S(1)} %bitcast.30, bf16[4096,256]{1,0:T(8,128)(2,1)S(1)} %copy-done), custom_call_target="tpu_custom_call" | custom-call | flops 810549248 | bytes 3481600 | tf_op jit(solution)/shard_map/pallas_call | solution.py:152
  71.1 0.0 collective-permute-done
  71.1 0.0 collective-permute-done.1
  71.1 0.0 collective-permute-done.2
  71.2 0.1 pad_maximum_fusion
  71.3 0.1 fusion
  71.4 0.8 %copy.8 = f32[256,256]{1,0:T(8,128)} copy(f32[256,256]{0,1:T(8,128)S(1)} %divide_bitcast_fusion) | data formatting | bytes 524288 | tf_op jit(solution)/shard_map/div | solution.py:241
  (13 shorter events, 0.1 us)
Async XLA Ops:
  7.4 1.2 %copy-start.1 = (bf16[4096,128]{1,0:T(8,128)(2,1)S(1)}, bf16[4096,128]{1,0:T(8,128)(2,1)}, u32[]{:S(2)}) copy-start(bf16[4096,128]{1,0:T(8,128)(2,1)} %r_ref.7) | copy-start | bytes 3145732
  8.6 18.2 %copy-start.2 = (bf16[4096,128]{1,0:T(8,128)(2,1)S(1)}, bf16[4096,128]{1,0:T(8,128)(2,1)}, u32[]{:S(2)}) copy-start(bf16[4096,128]{1,0:T(8,128)(2,1)} %r_ref.7) | copy-start | bytes 3145732
  8.6 18.2 %copy-start.3 = (f32[4096]{0:T(1024)S(1)}, f32[4096]{0:T(1024)}, u32[]{:S(2)}) copy-start(f32[4096]{0:T(1024)} %param.9) | copy-start | bytes 49156
  26.9 11.7 %copy-start.5 = (f32[1024]{0:T(1024)S(1)}, f32[1024]{0:T(1024)}, u32[]{:S(2)}) copy-start(f32[1024]{0:T(1024)} %param.8) | copy-start | bytes 12292
  38.6 16.4 %copy-start = (bf16[4096,256]{1,0:T(8,128)(2,1)S(1)}, bf16[4096,256]{1,0:T(8,128)(2,1)}, u32[]{:S(2)}) copy-start(bf16[4096,256]{1,0:T(8,128)(2,1)} %f_hbm.7) | copy-start | bytes 6291460
  43.6 0.7 copy-start.4
  44.3 10.7 %all-to-all-start.2 = ((f32[8,1,4096]{2,1,0:T(1,128)}), f32[8,1,4096]{2,1,0:T(1,128)S(1)}, u32[]{:S(2)}, u32[]{:S(2)}) async-start(f32[8,1,4096]{2,1,0:T(1,128)} %copy-done.4), calls=%async_computation.2 | async-start | bytes 262144 | tf_op jit(solution)/shard_map/all_to_all | solution.py:207
  58.4 12.7 %collective-permute-start = (f32[264,256]{1,0:T(8,128)S(1)}, f32[264,256]{1,0:T(8,128)S(1)}, u32[]{:S(2)}, u32[]{:S(2)}) collective-permute-start(f32[264,256]{1,0:T(8,128)S(1)} %shard_map.58), channel_id=1, source_target_pairs={{0,2},{1,3},{2,0},{3,1},{4,6},{5,7},{6,4},{7,5},{8,10},{9,11},{10,... | collective-permute-start | bytes 811016 | tf_op jit(solution)/shard_map/ppermute | solution.py:233
  62.0 9.2 %collective-permute-start.1 = (f32[264,256]{1,0:T(8,128)S(1)}, f32[264,256]{1,0:T(8,128)S(1)}, u32[]{:S(2)}, u32[]{:S(2)}) collective-permute-start(f32[264,256]{1,0:T(8,128)S(1)} %shard_map.59), channel_id=1, source_target_pairs={{0,3},{1,2},{2,1},{3,0},{4,7},{5,6},{6,5},{7,4},{8,11},{9,10},{10,... | collective-permute-start | bytes 811016 | tf_op jit(solution)/shard_map/ppermute | solution.py:233
  65.5 5.6 %collective-permute-start.2 = (f32[264,256]{1,0:T(8,128)S(1)}, f32[264,256]{1,0:T(8,128)S(1)}, u32[]{:S(2)}, u32[]{:S(2)}) collective-permute-start(f32[264,256]{1,0:T(8,128)S(1)} %shard_map.60), channel_id=1, source_target_pairs={{0,1},{1,0},{2,3},{3,2},{4,5},{5,4},{6,7},{7,6},{8,9},{9,8},{10,11... | collective-permute-start | bytes 811016 | tf_op jit(solution)/shard_map/ppermute | solution.py:233

commit v23 on v18

--- a/solution.py
+++ b/solution.py
@@ -108,16 +108,13 @@
     )(a, parts, base.reshape(1, cols), b)
 
 
-def assign_kernel(
-    rot_ref, v_ref, r_ref, parts_ref, base_ref, f_hbm, out_ref, f_ref, sem, *, scale
-):
+def assign_kernel(rot_ref, v_ref, r_ref, demand_ref, f_hbm, out_ref, f_ref, sem, *, scale):
     fetch = pltpu.make_async_copy(f_hbm, f_ref, sem)
     fetch.start()
-    demand = base_ref[...] - merged_lse(parts_ref[...])
     scores = lax.dot_general(
         v_ref[...], r_ref[...], (((1,), (1,)), ((), ())), preferred_element_type=jnp.float32
     )
-    logits = scores * scale + demand
+    logits = scores * scale + demand_ref[...]
     top = jnp.max(logits, axis=1, keepdims=True)
     powers = jnp.exp(logits - top)
     mass = jnp.sum(powers, axis=1, keepdims=True)
@@ -132,7 +129,7 @@
     out_ref[feat:, :] = extra.T[:8, :]
 
 
-def assign_chunk(v, r, parts, base, f, scale, chunk, index):
+def assign_chunk(v, r, demand, f, scale, chunk, index):
     rows, width = v.shape
     cols, feat = f.shape
     grid_spec = pltpu.PrefetchScalarGridSpec(
@@ -141,7 +138,6 @@
         in_specs=[
             pl.BlockSpec((chunk, width), lambda i, at: (at[0], 0)),
             pl.BlockSpec((cols, width), lambda i, at: (0, 0)),
-            pl.BlockSpec(parts.shape, lambda i, at: (0, 0, 0)),
             pl.BlockSpec((1, cols), lambda i, at: (0, 0)),
             pl.BlockSpec(memory_space=pl.ANY),
         ],
@@ -158,7 +154,7 @@
             transcendentals=chunk * cols,
             bytes_accessed=2 * (chunk + cols) * width + 2 * cols * feat + 4 * chunk * (feat + 8),
         ),
-    )(index, v, r, parts, base.reshape(1, cols), f)
+    )(index, v, r, demand, f)
 
 
 def combine_kernel(*refs):
@@ -220,12 +216,11 @@
         order = [(step, lambda i, m=step: i ^ m) for step in list(range(2, owners)) + [1]]
     else:
         order = [(step, lambda i, m=step: (i + m) % owners) for step in range(1, owners)]
+    demand = log_demand.reshape(1, -1) - merged_lse(second)
     pieces = []
     for step, partner in order + [(0, None)]:
         index = jnp.reshape(partner(me) if step else me, (1,)).astype(jnp.int32)
-        piece = assign_chunk(
-            own_rows, request_emb, second, log_demand, request_feat, scale, chunk, index
-        )
+        piece = assign_chunk(own_rows, request_emb, demand, request_feat, scale, chunk, index)
         if step:
             piece = lax.ppermute(piece, "req", [(i, partner(i)) for i in range(owners)])
         pieces.append(piece)

time: 72.4 us -> 81.3 us (1.12)
  waiting for transfers between devices: 8.23 us -> 14.3 us
  other arithmetic: 0.23 us -> 2.6 us
    ppermute x3, waiting for transfers between devices: 0.58 us -> 6.67 us  [local(): piece = lax.ppermute(piece, 'req', [(i, partner(i)) for i in range(owners)])]
    reduce_sum x0 -> x1, other arithmetic: none -> 0.92 us  [merged_lse(): return top + jnp.log(jnp.sum(jnp.exp(parts - top[None]), axis=0))]
    unnamed x12 -> x10, local copies, waits for them, and re-layouts: 1.89 us -> 1.24 us
  transfers between devices with their start and end apart: 4 -> 4, of which waited for: 2 -> 3; matrix products, arithmetic and copies ran while one was open for 0% -> 0% of each run, Pallas kernels for 14% -> 4%
where the time goes in v23:
time: 81.3 us; the launch traced here: 80.5 us
  Pallas kernels  29.9 us (37%)
  blocking collectives  25.9 us (32%)
  waiting for transfers between devices  14.3 us (18%)
  starting transfers between devices  5.58 us (7%)
  other arithmetic  2.6 us (3%)
  local copies, waits for them, and re-layouts  2.08 us (3%)
    pallas_call x4, Pallas kernels, assign_chunk(): pl.pallas_call(functools.partial(assign_kernel, scale=scale), out_shape=j...  13.8 us
    all_to_all x1, blocking collectives, exchange(): return lax.all_to_all(block, 'veh', 0, 0, tiled=True)  13.1 us
    pallas_call x2, Pallas kernels, lse_over_rows(): pl.pallas_call(functools.partial(lse_kernel, scale=scale, shifted=shifted...  10.9 us
    all_to_all x1, waiting for transfers between devices, exchange(): return lax.all_to_all(block, 'veh', 0, 0, tiled=True)  7.65 us
    all_gather x1, blocking collectives, local(): own_rows = lax.all_gather(vehicle_emb, 'req', axis=0, tiled=True)  7.42 us
    ppermute x3, waiting for transfers between devices, local(): piece = lax.ppermute(piece, 'req', [(i, partner(i)) for i in range(owners)])  6.67 us
    all_gather x1, blocking collectives, local(): row_parts = lax.all_gather(partial[0], 'req', axis=0, tiled=False)  5.38 us
    pallas_call x1, Pallas kernels, row_lse(): pl.pallas_call(functools.partial(row_kernel, scale=scale), out_shape=jax....  5.25 us
  transfers between devices with their start and end apart: 4, of which 3 were waited for; matrix products, arithmetic and copies ran while one was open for 0% of the time, Pallas kernels for 4%

profile of v23, /device:TPU:0, one launch (start us, length us, event | category | flops | bytes accessed | tf_op | source)
XLA Modules:
  0.0 80.5 jit_solution(16915124402295692951)
XLA Ops:
  0.0 7.4 %all_gather.6.refs_0_.a_ref.v_ref = bf16[1024,128]{1,0:T(8,128)(2,1)S(1)} all-gather(bf16[256,128]{1,0:T(8,128)(2,1)} %param.5), channel_id=1, replica_groups=mesh['veh'=8,'req'=4] {'req'}, dimensions={0}, use_global_device_ids=true | all-gather | bytes 327680 | tf_op jit(solution)/shard_map/all_gather | solution.py:196
  7.4 1.2 %copy-done.1 = bf16[4096,128]{1,0:T(8,128)(2,1)S(1)} copy-done((bf16[4096,128]{1,0:T(8,128)(2,1)S(1)}, bf16[4096,128]{1,0:T(8,128)(2,1)}, u32[]{:S(2)}) %copy-start.1) | copy-done | bytes 1048600
  8.6 5.1 %shard_map.55 = f32[8,1,4096]{2,1,0:T(1,128)S(1)} custom-call(bf16[1024,128]{1,0:T(8,128)(2,1)S(1)} %all_gather.6.refs_0_.a_ref.v_ref, bf16[4096,128]{1,0:T(8,128)(2,1)S(1)} %copy-done.1), custom_call_target="tpu_custom_call" | custom-call | flops 1094713344 | bytes 1445888 | tf_op jit(solution)/shard_map/pallas_call | solution.py:58
  13.8 13.1 %all_to_all.10.parts_ref = f32[8,1,4096]{2,1,0:T(1,128)S(1)} all-to-all(f32[8,1,4096]{2,1,0:T(1,128)S(1)} %shard_map.55), channel_id=1, replica_groups=mesh['veh'=8,'req'=4] {'veh'}, dimensions={0} | all-to-all | bytes 262144 | tf_op jit(solution)/shard_map/all_to_all | solution.py:202
  26.9 5.3 %shard_map.56 = f32[1,1,1024]{2,1,0:T(1,128)S(1)} custom-call(bf16[1024,128]{1,0:T(8,128)(2,1)S(1)} %all_gather.6.refs_0_.a_ref.v_ref, f32[8,1,4096]{2,1,0:T(1,128)S(1)} %all_to_all.10.parts_ref, f32[1,4096]{1,0:T(1,128)S(1)} %bitcast.31, bf16[4096,128]{1,0:T(8,128)(2,1)S(1)} %copy-done.2), custom_call_target="tpu_custom_call" | custom-call | flops 1094713344 | bytes 1462272 | tf_op jit(solution)/shard_map/pallas_call | solution.py:91
  32.1 5.4 %all_gather.7.refs_1_ = f32[4,1,1024]{2,1,0:T(1,128)S(1)} all-gather(f32[1,1,1024]{2,1,0:T(1,128)S(1)} %shard_map.56), channel_id=1, replica_groups=mesh['veh'=8,'req'=4] {'req'}, dimensions={0}, use_global_device_ids=true | all-gather | bytes 20480 | tf_op jit(solution)/shard_map/all_gather | solution.py:206
  37.5 5.7 %shard_map.57 = f32[8,1,4096]{2,1,0:T(1,128)} custom-call(bf16[1024,128]{1,0:T(8,128)(2,1)S(1)} %all_gather.6.refs_0_.a_ref.v_ref, f32[4,1,1024]{2,1,0:T(1,128)S(1)} %all_gather.7.refs_1_, f32[1,1024]{1,0:T(1,128)S(1)} %bitcast.32, bf16[4096,128]{1,0:T(8,128)(2,1)S(1)} %copy-done.2), custom_call_target="tpu_custom_call" | custom-call | flops 1094713344 | bytes 1445888 | tf_op jit(solution)/shard_map/pallas_call | solution.py:58
  43.2 3.4 %all-to-all-start.1 = ((f32[8,1,4096]{2,1,0:T(1,128)}), f32[8,1,4096]{2,1,0:T(1,128)S(1)}, u32[]{:S(2)}, u32[]{:S(2)}) async-start(f32[8,1,4096]{2,1,0:T(1,128)} %shard_map.57), calls=%async_computation.1 | async-start | bytes 262144 | tf_op jit(solution)/shard_map/all_to_all | solution.py:202
  46.6 7.7 %all-to-all-done.1 = f32[8,1,4096]{2,1,0:T(1,128)S(1)} async-done(((f32[8,1,4096]{2,1,0:T(1,128)}), f32[8,1,4096]{2,1,0:T(1,128)S(1)}, u32[]{:S(2)}, u32[]{:S(2)}) %all-to-all-start.1) | async-done | bytes 131104 | tf_op jit(solution)/shard_map/all_to_all | solution.py:202
  54.3 0.7 reduce_max.18
  55.0 0.9 %exponential_reduce_fusion = f32[4096]{0:T(1024)S(1)} fusion(f32[8,1,4096]{2,1,0:T(1,128)S(1)} %all-to-all-done.1, f32[4096]{0:T(1024)} %reduce_max.18), kind=kLoop, calls=%fused_computation.4 | loop fusion | flops 61440 | bytes 163840 | tf_op jit(solution)/shard_map/reduce_sum | solution.py:14
  55.9 0.7 add_subtract_fusion
  56.6 3.5 %shard_map.60 = f32[264,256]{1,0:T(8,128)S(1)} custom-call(s32[1]{0:T(128)} %bitcast.7.rot_ref, bf16[1024,128]{1,0:T(8,128)(2,1)S(1)} %all_gather.6.refs_0_.a_ref.v_ref, bf16[4096,128]{1,0:T(8,128)(2,1)S(1)} %copy-done.2, f32[1,4096]{1,0:T(1,128)S(1)} %bitcast.27, bf16[4096,256]{1,0:T(8,128)(2,1)S(1)} %copy-done), custom_call_target="tpu_custom_call" | custom-call | flops 810549248 | bytes 3481600 | tf_op jit(solution)/shard_map/pallas_call | solution.py:147
  60.1 3.5 %shard_map.59 = f32[264,256]{1,0:T(8,128)S(1)} custom-call(s32[1]{0:T(128)} %bitcast.5.rot_ref, bf16[1024,128]{1,0:T(8,128)(2,1)S(1)} %all_gather.6.refs_0_.a_ref.v_ref, bf16[4096,128]{1,0:T(8,128)(2,1)S(1)} %copy-done.2, f32[1,4096]{1,0:T(1,128)S(1)} %bitcast.28, bf16[4096,256]{1,0:T(8,128)(2,1)S(1)} %copy-done), custom_call_target="tpu_custom_call" | custom-call | flops 810549248 | bytes 3481600 | tf_op jit(solution)/shard_map/pallas_call | solution.py:147
  63.6 3.5 %shard_map.58 = f32[264,256]{1,0:T(8,128)S(1)} custom-call(s32[1]{0:T(128)} %bitcast.rot_ref, bf16[1024,128]{1,0:T(8,128)(2,1)S(1)} %all_gather.6.refs_0_.a_ref.v_ref, bf16[4096,128]{1,0:T(8,128)(2,1)S(1)} %copy-done.2, f32[1,4096]{1,0:T(1,128)S(1)} %bitcast.29, bf16[4096,256]{1,0:T(8,128)(2,1)S(1)} %copy-done), custom_call_target="tpu_custom_call" | custom-call | flops 810549248 | bytes 3481600 | tf_op jit(solution)/shard_map/pallas_call | solution.py:147
  67.0 1.6 %collective-permute-start = (f32[264,256]{1,0:T(8,128)S(1)}, f32[264,256]{1,0:T(8,128)S(1)}, u32[]{:S(2)}, u32[]{:S(2)}) collective-permute-start(f32[264,256]{1,0:T(8,128)S(1)} %shard_map.58), channel_id=1, source_target_pairs={{0,2},{1,3},{2,0},{3,1},{4,6},{5,7},{6,4},{7,5},{8,10},{9,11},{10,... | collective-permute-start | bytes 811016 | tf_op jit(solution)/shard_map/ppermute | solution.py:225
  68.6 0.0 collective-permute-start.1
  68.6 0.6 collective-permute-start.2
  69.2 3.4 %shard_map.61 = f32[264,256]{1,0:T(8,128)S(1)} custom-call(s32[1]{0:T(128)} %bitcast.9.rot_ref, bf16[1024,128]{1,0:T(8,128)(2,1)S(1)} %all_gather.6.refs_0_.a_ref.v_ref, bf16[4096,128]{1,0:T(8,128)(2,1)S(1)} %copy-done.2, f32[1,4096]{1,0:T(1,128)S(1)} %bitcast.30, bf16[4096,256]{1,0:T(8,128)(2,1)S(1)} %copy-done), custom_call_target="tpu_custom_call" | custom-call | flops 810549248 | bytes 3481600 | tf_op jit(solution)/shard_map/pallas_call | solution.py:147
  72.7 3.8 %collective-permute-done = f32[264,256]{1,0:T(8,128)S(1)} collective-permute-done((f32[264,256]{1,0:T(8,128)S(1)}, f32[264,256]{1,0:T(8,128)S(1)}, u32[]{:S(2)}, u32[]{:S(2)}) %collective-permute-start) | collective-permute-done | bytes 270368 | tf_op jit(solution)/shard_map/ppermute | solution.py:225
  76.5 2.9 %collective-permute-done.1 = f32[264,256]{1,0:T(8,128)S(1)} collective-permute-done((f32[264,256]{1,0:T(8,128)S(1)}, f32[264,256]{1,0:T(8,128)S(1)}, u32[]{:S(2)}, u32[]{:S(2)}) %collective-permute-start.1) | collective-permute-done | bytes 270368 | tf_op jit(solution)/shard_map/ppermute | solution.py:225
  79.4 0.1 pad_maximum_fusion
  79.5 0.1 fusion
  79.6 0.8 %copy.8 = f32[256,256]{1,0:T(8,128)} copy(f32[256,256]{0,1:T(8,128)S(1)} %divide_bitcast_fusion) | data formatting | bytes 524288 | tf_op jit(solution)/shard_map/div | solution.py:233
  (14 shorter events, 0.1 us)
Async XLA Ops:
  7.4 1.2 %copy-start.1 = (bf16[4096,128]{1,0:T(8,128)(2,1)S(1)}, bf16[4096,128]{1,0:T(8,128)(2,1)}, u32[]{:S(2)}) copy-start(bf16[4096,128]{1,0:T(8,128)(2,1)} %r_ref.7) | copy-start | bytes 3145732
  8.6 18.2 %copy-start.2 = (bf16[4096,128]{1,0:T(8,128)(2,1)S(1)}, bf16[4096,128]{1,0:T(8,128)(2,1)}, u32[]{:S(2)}) copy-start(bf16[4096,128]{1,0:T(8,128)(2,1)} %r_ref.7) | copy-start | bytes 3145732
  8.6 18.2 %copy-start.3 = (f32[4096]{0:T(1024)S(1)}, f32[4096]{0:T(1024)}, u32[]{:S(2)}) copy-start(f32[4096]{0:T(1024)} %param.9) | copy-start | bytes 49156
  26.9 10.6 %copy-start.4 = (f32[1024]{0:T(1024)S(1)}, f32[1024]{0:T(1024)}, u32[]{:S(2)}) copy-start(f32[1024]{0:T(1024)} %param.8) | copy-start | bytes 12292
  37.5 19.1 %copy-start = (bf16[4096,256]{1,0:T(8,128)(2,1)S(1)}, bf16[4096,256]{1,0:T(8,128)(2,1)}, u32[]{:S(2)}) copy-start(bf16[4096,256]{1,0:T(8,128)(2,1)} %f_hbm.7) | copy-start | bytes 6291460
  43.2 11.0 %all-to-all-start.1 = ((f32[8,1,4096]{2,1,0:T(1,128)}), f32[8,1,4096]{2,1,0:T(1,128)S(1)}, u32[]{:S(2)}, u32[]{:S(2)}) async-start(f32[8,1,4096]{2,1,0:T(1,128)} %shard_map.57), calls=%async_computation.1 | async-start | bytes 262144 | tf_op jit(solution)/shard_map/all_to_all | solution.py:202
  67.0 9.5 %collective-permute-start = (f32[264,256]{1,0:T(8,128)S(1)}, f32[264,256]{1,0:T(8,128)S(1)}, u32[]{:S(2)}, u32[]{:S(2)}) collective-permute-start(f32[264,256]{1,0:T(8,128)S(1)} %shard_map.58), channel_id=1, source_target_pairs={{0,2},{1,3},{2,0},{3,1},{4,6},{5,7},{6,4},{7,5},{8,10},{9,11},{10,... | collective-permute-start | bytes 811016 | tf_op jit(solution)/shard_map/ppermute | solution.py:225
  68.6 10.7 %collective-permute-start.1 = (f32[264,256]{1,0:T(8,128)S(1)}, f32[264,256]{1,0:T(8,128)S(1)}, u32[]{:S(2)}, u32[]{:S(2)}) collective-permute-start(f32[264,256]{1,0:T(8,128)S(1)} %shard_map.59), channel_id=1, source_target_pairs={{0,3},{1,2},{2,1},{3,0},{4,7},{5,6},{6,5},{7,4},{8,11},{9,10},{10,... | collective-permute-start | bytes 811016 | tf_op jit(solution)/shard_map/ppermute | solution.py:225
  68.6 10.7 %collective-permute-start.2 = (f32[264,256]{1,0:T(8,128)S(1)}, f32[264,256]{1,0:T(8,128)S(1)}, u32[]{:S(2)}, u32[]{:S(2)}) collective-permute-start(f32[264,256]{1,0:T(8,128)S(1)} %shard_map.60), channel_id=1, source_target_pairs={{0,1},{1,0},{2,3},{3,2},{4,5},{5,4},{6,7},{7,6},{8,9},{9,8},{10,11... | collective-permute-start | bytes 811016 | tf_op jit(solution)/shard_map/ppermute | solution.py:225
